TPU v7x, 256 devices: a whole 4x4x8 slice. The times are simulated.
256 devices in a mesh: sp: 64 (over y, z_lo, x), dp: 4 (over z_hi, core).
Axes of the slice: x: 4, y: 4, z: 8 (z_hi: 2, z_lo: 4; z = z_hi * 4 + z_lo), core: 2. Of those that a mesh axis runs over, the one named last changes fastest.
Arguments:
- queries: bfloat16 [4, 64, 384, 768], P('dp', 'sp'), may hold values from -7 to 7
- keys: bfloat16 [4, 64, 384, 768], P('dp', 'sp'), may hold values from -7 to 7
- values: bfloat16 [4, 64, 384, 768], P('dp', 'sp'), may hold values from -6 to 6
- tile_lists: int32 [64, 5], P('sp'), may hold values from -1 to 63, as said below
- grad_out: bfloat16 [4, 64, 384, 3072], P('dp', 'sp'), may hold values from -16 to 16
- w_out: bfloat16 [768, 3072], replicated, may hold values from -0.21875 to 0.21875
Outputs:
- grad_queries: bfloat16 [4, 64, 384, 768], P('dp', 'sp')
- grad_keys: bfloat16 [4, 64, 384, 768], P('dp', 'sp')
- grad_values: bfloat16 [4, 64, 384, 768], P('dp', 'sp')
- grad_w_out: float32 [768, 3072], P('dp', 'sp')
Inputs may be any that keep to these rules, and one draw needn't show every extreme that they name: `tile_lists`: row i lists distinct tiles of the 3 x 3 block of time-height tile positions around tile i (clipped at the clip's borders), tile i itself first; -1 marks an empty entry and comes only after all tiles of the clipped block are listed.
All inputs are finite; a program needn't handle non-finite values.
Results may differ from a plain program's by a relative error of at most 0.014.
The roundings to bfloat16 on the way count: a program that leaves them out, or rounds other values in their place, can miss the bound.
Values may be sent and summed in bfloat16 or wider, within the bound.
No kernel may reach another device: no remote copies, remote signals or barrier semaphores. Data moves between devices by JAX's collectives and lax.ppermute only.
A program may use at most 128 MiB of HBM per device.

v0:
```python
import math

import jax
import jax.numpy as jnp
from jax import lax
from jax.sharding import PartitionSpec as P

HEAD = 128
H_TILES = 4


def from_behind(value, axis, steps):
    count = lax.axis_size(axis)
    initial, last = (max(0, -steps), min(count, count - steps))
    return lax.ppermute(value, axis, [(source, source + steps) for source in range(initial, last)])


def body(queries, keys, values, tile_lists, grad_out, w_out):
    query_tile = queries[0, 0]
    key_tile = keys[0, 0]
    value_tile = values[0, 0]
    grad_tile = grad_out[0, 0]
    listed = tile_lists[0]
    tile_tok, inner_width = query_tile.shape
    slot_count = listed.shape[0]
    height_tiles = H_TILES
    score_scale = 1.0 / math.sqrt(HEAD)
    own_tile = lax.axis_index("sp")
    key_value = jnp.stack([key_tile, value_tile])
    offsets = [(time_step, height_step) for time_step in (-1, 0, 1) for height_step in (-1, 0, 1)]
    pieces = []
    for time_step, height_step in offsets:
        if time_step == 0 and height_step == 0:
            pieces.append(key_value)
        else:
            pieces.append(from_behind(key_value, "sp", -(time_step * height_tiles + height_step)))
    window = jnp.stack(pieces)
    valid_slot = listed >= 0
    time_gap = listed // height_tiles - own_tile // height_tiles
    height_gap = listed % height_tiles - own_tile % height_tiles
    slot_index = jnp.where(valid_slot, (time_gap + 1) * 3 + height_gap + 1, 4)
    picked = jnp.take(window, slot_index, axis=0)
    key_rows = picked[:, 0].reshape(slot_count * tile_tok, inner_width)
    value_rows = picked[:, 1].reshape(slot_count * tile_tok, inner_width)
    key_mask = jnp.repeat(valid_slot, tile_tok)
    grad_attn = lax.dot_general(
        grad_tile, w_out, (((1,), (1,)), ((), ())), preferred_element_type=jnp.float32
    ).astype(jnp.bfloat16)
    block_width = 128
    heads_block = block_width // HEAD

    def head_block(block_index, carry):
        attn_all, grad_query, grad_key, grad_value = carry
        block_start = block_index * block_width
        query_part = lax.dynamic_slice_in_dim(query_tile, block_start, block_width, 1).reshape(
            tile_tok, heads_block, HEAD
        )
        key_part = lax.dynamic_slice_in_dim(key_rows, block_start, block_width, 1).reshape(
            -1, heads_block, HEAD
        )
        value_part = lax.dynamic_slice_in_dim(value_rows, block_start, block_width, 1).reshape(
            -1, heads_block, HEAD
        )
        grad_part = lax.dynamic_slice_in_dim(grad_attn, block_start, block_width, 1).reshape(
            tile_tok, heads_block, HEAD
        )
        scores = (
            jnp.einsum("qhd,khd->hqk", query_part, key_part, preferred_element_type=jnp.float32)
            * score_scale
        )
        scores = jnp.where(key_mask[None, None, :], scores, -1e30)
        row_peak = jnp.max(scores, axis=2, keepdims=True)
        exp_scores = jnp.exp(scores - row_peak)
        attn_probs = exp_scores / jnp.sum(exp_scores, axis=2, keepdims=True)
        probs_low = attn_probs.astype(jnp.bfloat16)
        attn_part = jnp.einsum(
            "hqk,khd->qhd", probs_low, value_part, preferred_element_type=jnp.float32
        ).astype(jnp.bfloat16)
        row_delta = jnp.einsum(
            "qhd,qhd->hq", grad_part.astype(jnp.float32), attn_part.astype(jnp.float32)
        )
        dprobs = jnp.einsum(
            "qhd,khd->hqk", grad_part, value_part, preferred_element_type=jnp.float32
        )
        dscores = (attn_probs * (dprobs - row_delta[:, :, None])).astype(jnp.bfloat16)
        query_grad = (
            jnp.einsum("hqk,khd->qhd", dscores, key_part, preferred_element_type=jnp.float32)
            * score_scale
        )
        key_grad = (
            jnp.einsum("hqk,qhd->khd", dscores, query_part, preferred_element_type=jnp.float32)
            * score_scale
        )
        value_grad = jnp.einsum(
            "hqk,qhd->khd", probs_low, grad_part, preferred_element_type=jnp.float32
        )
        attn_all = lax.dynamic_update_slice_in_dim(
            attn_all, attn_part.reshape(tile_tok, block_width), block_start, 1
        )
        grad_query = lax.dynamic_update_slice_in_dim(
            grad_query,
            query_grad.astype(jnp.bfloat16).reshape(tile_tok, block_width),
            block_start,
            1,
        )
        grad_key = lax.dynamic_update_slice_in_dim(
            grad_key, key_grad.astype(jnp.bfloat16).reshape(-1, block_width), block_start, 1
        )
        grad_value = lax.dynamic_update_slice_in_dim(
            grad_value, value_grad.astype(jnp.bfloat16).reshape(-1, block_width), block_start, 1
        )
        return (attn_all, grad_query, grad_key, grad_value)

    start_state = (
        jnp.zeros((tile_tok, inner_width), jnp.bfloat16),
        jnp.zeros((tile_tok, inner_width), jnp.bfloat16),
        jnp.zeros((slot_count * tile_tok, inner_width), jnp.bfloat16),
        jnp.zeros((slot_count * tile_tok, inner_width), jnp.bfloat16),
    )
    attn_all, grad_query, grad_key, grad_value = lax.fori_loop(
        0, inner_width // block_width, head_block, start_state
    )
    tile_sum = lax.psum_scatter(
        lax.dot_general(
            grad_tile, attn_all, (((0,), (0,)), ((), ())), preferred_element_type=jnp.float32
        ),
        "sp",
        scatter_dimension=0,
        tiled=True,
    )
    weight_grad = (
        lax.psum_scatter(tile_sum.astype(jnp.bfloat16), "dp", scatter_dimension=1, tiled=True)
        .astype(jnp.float32)
        .T
    )
    slot_terms = jnp.stack(
        [
            grad_key.reshape(slot_count, tile_tok, inner_width),
            grad_value.reshape(slot_count, tile_tok, inner_width),
        ],
        axis=1,
    )
    selector = (
        (slot_index[:, None] == jnp.arange(9, dtype=jnp.int32)[None, :]) & valid_slot[:, None]
    ).astype(jnp.bfloat16)
    by_slot = jnp.einsum(
        "js,jctd->sctd", selector, slot_terms, preferred_element_type=jnp.float32
    ).astype(jnp.bfloat16)
    grad_total = by_slot[4].astype(jnp.float32)
    for time_step, height_step in offsets:
        if time_step == 0 and height_step == 0:
            continue
        slot_number = (time_step + 1) * 3 + height_step + 1
        arrived = from_behind(by_slot[slot_number], "sp", time_step * height_tiles + height_step)
        grad_total = grad_total + arrived.astype(jnp.float32)
    grad_kv = grad_total.astype(jnp.bfloat16)
    return (grad_query[None, None], grad_kv[0][None, None], grad_kv[1][None, None], weight_grad)


def solution(mesh):
    in_specs = (
        P("dp", "sp", None, None),
        P("dp", "sp", None, None),
        P("dp", "sp", None, None),
        P("sp", None),
        P("dp", "sp", None, None),
        P(),
    )
    out_specs = (
        P("dp", "sp", None, None),
        P("dp", "sp", None, None),
        P("dp", "sp", None, None),
        P("dp", "sp"),
    )
    return jax.shard_map(body, mesh=mesh, in_specs=in_specs, out_specs=out_specs, check_vma=False)
```

profile of v0, /device:TPU:24, one launch (start us, length us, event | category | flops | bytes accessed | tf_op | source)
XLA Modules:
  0.0 1003.6 jit_solution(16910948961080448136)
XLA Ops:
  33.7 38.3 %collective-permute-done = bf16[2,384,768]{2,1,0:T(8,128)(2,1)} collective-permute-done((bf16[2,384,768]{2,1,0:T(8,128)(2,1)S(1)}, bf16[2,384,768]{2,1,0:T(8,128)(2,1)}, u32[]{:S(2)}, u32[]{:S(2)}) %collective-permute-start) | collective-permute-done | bytes 1179680 | tf_op jit(solution)/shard_map/ppermute | solution.py:15
  77.1 66.5 %collective-permute-done.1 = bf16[2,384,768]{2,1,0:T(8,128)(2,1)} collective-permute-done((bf16[2,384,768]{2,1,0:T(8,128)(2,1)S(1)}, bf16[2,384,768]{2,1,0:T(8,128)(2,1)}, u32[]{:S(2)}, u32[]{:S(2)}) %collective-permute-start.1) | collective-permute-done | bytes 1179680 | tf_op jit(solution)/shard_map/ppermute | solution.py:15
  143.6 21.0 %collective-permute-start.5 = (bf16[2,384,768]{2,1,0:T(8,128)(2,1)S(1)}, bf16[2,384,768]{2,1,0:T(8,128)(2,1)S(1)}, u32[]{:S(2)}, u32[]{:S(2)}) collective-permute-start(bf16[2,384,768]{2,1,0:T(8,128)(2,1)S(1)} %pad_maximum_fusion), channel_id=1, source_target_pairs={{12,0},{16,4},{20,8},{24,12},{28,16},{32,20},{36,24},{40,28},{44,3... | collective-permute-start | bytes 3538952 | tf_op jit(solution)/shard_map/ppermute | solution.py:15
  167.0 10.9 %collective-permute-start.7 = (bf16[2,384,768]{2,1,0:T(8,128)(2,1)S(1)}, bf16[2,384,768]{2,1,0:T(8,128)(2,1)S(1)}, u32[]{:S(2)}, u32[]{:S(2)}) collective-permute-start(bf16[2,384,768]{2,1,0:T(8,128)(2,1)S(1)} %pad_maximum_fusion), channel_id=1, source_target_pairs={{20,0},{24,4},{28,8},{32,12},{36,16},{40,20},{44,24},{48,28},{52,3... | collective-permute-start | bytes 3538952 | tf_op jit(solution)/shard_map/ppermute | solution.py:15
  184.9 18.7 %collective-permute-done.5 = bf16[2,384,768]{2,1,0:T(8,128)(2,1)S(1)} collective-permute-done((bf16[2,384,768]{2,1,0:T(8,128)(2,1)S(1)}, bf16[2,384,768]{2,1,0:T(8,128)(2,1)S(1)}, u32[]{:S(2)}, u32[]{:S(2)}) %collective-permute-start.5) | collective-permute-done | bytes 1179680 | tf_op jit(solution)/shard_map/ppermute | solution.py:15
  207.1 7.1 collective-permute-done.7
  215.4 8.0 gather_fusion
  234.9 117.0 %while.20 = (s32[]{:T(128)}, bf16[384,768]{0,1:T(8,128)(2,1)}, bf16[384,768]{1,0:T(8,128)(2,1)}, bf16[1920,768]{1,0:T(8,128)(2,1)}, bf16[1920,768]{1,0:T(8,128)(...) while((s32[]{:T(128)}, bf16[384,768]{0,1:T(8,128)(2,1)}, ...), condition=%wide.region_3.4_spmd.clone, body=%wide.region_0.3_spmd.clone.sunk | while | flops 1142389632 | bytes 57627912 | solution.py:120
  351.8 6.2 convolution_bitcast_fusion
  358.0 9.6 copy.107
  373.6 10.0 convolution_convert_fusion.2
  383.6 35.8 %fusion.58 = (bf16[1,2,384,768]{3,0,2,1:T(2,128)(2,1)}, bf16[1,2,384,768]{3,0,2,1:T(2,128)(2,1)}, bf16[1,2,384,768]{3,0,2,1:T(2,128)(2,1)S(1)}, bf16[1,2,384,768...) fusion(bf16[9,2,384,768]{3,0,2,1:T(8,128)(2,1)} %convolution_co, ...), kind=kLoop, calls=%fused_computation.114 | loop fusion | flops 589824 | bytes 22413312 | tf_op jit(solution)/shard_map/slice | solution.py:154
  422.0 12.9 %collective-permute-start.9 = (bf16[2,384,768]{2,1,0:T(8,128)(2,1)S(1)}, bf16[2,384,768]{2,1,0:T(8,128)(2,1)S(1)}, u32[]{:S(2)}, u32[]{:S(2)}) collective-permute-start(bf16[2,384,768]{2,1,0:T(8,128)(2,1)S(1)} %bitcast.176), channel_id=1, source_target_pairs={{16,0},{20,4},{24,8},{28,12},{32,16},{36,20},{40,24},{44,28},{48,3... | collective-permute-start | bytes 3538952 | tf_op jit(solution)/shard_map/ppermute | solution.py:15
  434.9 9.4 collective-permute-start.10
  444.5 16.6 %collective-permute-start.11 = (bf16[2,384,768]{2,1,0:T(8,128)(2,1)S(1)}, bf16[2,384,768]{2,1,0:T(8,128)(2,1)S(1)}, u32[]{:S(2)}, u32[]{:S(2)}) collective-permute-start(bf16[2,384,768]{2,1,0:T(8,128)(2,1)S(1)} %bitcast.174), channel_id=1, source_target_pairs={{4,0},{8,4},{12,8},{16,12},{20,16},{24,20},{28,24},{32,28},{36,32}... | collective-permute-start | bytes 3538952 | tf_op jit(solution)/shard_map/ppermute | solution.py:15
  463.9 6.6 collective-permute-start.13
  470.5 13.1 %collective-permute-done.9 = bf16[2,384,768]{2,1,0:T(8,128)(2,1)S(1)} collective-permute-done((bf16[2,384,768]{2,1,0:T(8,128)(2,1)S(1)}, bf16[2,384,768]{2,1,0:T(8,128)(2,1)S(1)}, u32[]{:S(2)}, u32[]{:S(2)}) %collective-permute-start.9) | collective-permute-done | bytes 1179680 | tf_op jit(solution)/shard_map/ppermute | solution.py:15
  485.6 15.1 %collective-permute-done.10 = bf16[2,384,768]{2,1,0:T(8,128)(2,1)S(1)} collective-permute-done((bf16[2,384,768]{2,1,0:T(8,128)(2,1)S(1)}, bf16[2,384,768]{2,1,0:T(8,128)(2,1)S(1)}, u32[]{:S(2)}, u32[]{:S(2)}) %collective-permute-start.10) | collective-permute-done | bytes 1179680 | tf_op jit(solution)/shard_map/ppermute | solution.py:15
  500.7 13.7 %collective-permute-start.15 = (bf16[2,384,768]{2,1,0:T(8,128)(2,1)S(1)}, bf16[2,384,768]{2,1,0:T(8,128)(2,1)S(1)}, u32[]{:S(2)}, u32[]{:S(2)}) collective-permute-start(bf16[2,384,768]{2,1,0:T(8,128)(2,1)S(1)} %bitcast.171), channel_id=1, source_target_pairs={{0,20},{4,24},{8,28},{12,32},{16,36},{20,40},{24,44},{28,48},{32,5... | collective-permute-start | bytes 3538952 | tf_op jit(solution)/shard_map/ppermute | solution.py:15
  514.4 32.9 %collective-permute-done.11 = bf16[2,384,768]{2,1,0:T(8,128)(2,1)S(1)} collective-permute-done((bf16[2,384,768]{2,1,0:T(8,128)(2,1)S(1)}, bf16[2,384,768]{2,1,0:T(8,128)(2,1)S(1)}, u32[]{:S(2)}, u32[]{:S(2)}) %collective-permute-start.11) | collective-permute-done | bytes 1179680 | tf_op jit(solution)/shard_map/ppermute | solution.py:15
  551.2 30.2 %collective-permute-done.14 = bf16[2,384,768]{2,1,0:T(8,128)(2,1)S(1)} collective-permute-done((bf16[2,384,768]{2,1,0:T(8,128)(2,1)S(1)}, bf16[2,384,768]{2,1,0:T(8,128)(2,1)S(1)}, u32[]{:S(2)}, u32[]{:S(2)}) %collective-permute-start.14) | collective-permute-done | bytes 1179680 | tf_op jit(solution)/shard_map/ppermute | solution.py:15
  581.4 91.2 %collective-permute-done.15 = bf16[2,384,768]{2,1,0:T(8,128)(2,1)S(1)} collective-permute-done((bf16[2,384,768]{2,1,0:T(8,128)(2,1)S(1)}, bf16[2,384,768]{2,1,0:T(8,128)(2,1)S(1)}, u32[]{:S(2)}, u32[]{:S(2)}) %collective-permute-start.15) | collective-permute-done | bytes 1179680 | tf_op jit(solution)/shard_map/ppermute | solution.py:15
  674.1 227.2 %reduce-scatter.7.cloned.1.call-done = f32[48,768]{1,0:T(8,128)} async-done(((f32[3072,768]{1,0:T(8,128)}), f32[48,768]{1,0:T(8,128)}) %reduce-scatter.7.cloned.1.call-update) | async-done | bytes 147472
  904.1 91.2 %reduce-scatter.5.cloned.1.call-done = bf16[48,192]{0,1:T(8,128)(2,1)} async-done(((bf16[48,768]{0,1:T(8,128)(2,1)}), bf16[48,192]{0,1:T(8,128)(2,1)}) %reduce-scatter.5.cloned.1.call-update) | async-done | bytes 18448 | tf_op jit(solution)/shard_map/reduce_scatter | solution.py:132
  (207 shorter events, 196.8 us)
Async XLA Ops:
  7.2 20.6 %copy-start = (bf16[1,1,384,3072]{3,2,1,0:T(8,128)(2,1)S(1)}, bf16[1,1,384,3072]{3,2,1,0:T(8,128)(2,1)}, u32[]{:S(2)}) copy-start(bf16[1,1,384,3072]{3,2,1,0:T(8,128)(2,1)} %param.12) | copy-start | bytes 7077892
  7.2 894.1 %reduce-scatter.7.cloned.1.call-start = ((), (), s32[]{:S(2)}) async-start(), calls=%async_computation.3 | async-start | bytes 9584640
  8.7 24.3 %copy-start.11 = (s32[1,5]{1,0:T(1,128)S(1)}, s32[1,5]{1,0:T(1,128)}, u32[]{:S(2)}) copy-start(s32[1,5]{1,0:T(1,128)} %param.11) | copy-start | bytes 64
  8.7 63.2 %collective-permute-start = (bf16[2,384,768]{2,1,0:T(8,128)(2,1)S(1)}, bf16[2,384,768]{2,1,0:T(8,128)(2,1)}, u32[]{:S(2)}, u32[]{:S(2)}) collective-permute-start(bf16[2,384,768]{2,1,0:T(8,128)(2,1)S(1)} %pad_maximum_fusion), channel_id=1, source_target_pairs={{0,20},{4,24},{8,28},{12,32},{16,36},{20,40},{24,44},{28,48},{32,5... | collective-permute-start | bytes 3538952 | tf_op jit(solution)/shard_map/ppermute | solution.py:15
  13.5 191.2 %collective-permute-start.6 = (bf16[2,384,768]{2,1,0:T(8,128)(2,1)S(1)}, bf16[2,384,768]{2,1,0:T(8,128)(2,1)}, u32[]{:S(2)}, u32[]{:S(2)}) collective-permute-start(bf16[2,384,768]{2,1,0:T(8,128)(2,1)S(1)} %pad_maximum_fusion), channel_id=1, source_target_pairs={{16,0},{20,4},{24,8},{28,12},{32,16},{36,20},{40,24},{44,28},{48,3... | collective-permute-start | bytes 3538952 | tf_op jit(solution)/shard_map/ppermute | solution.py:15
  18.2 162.0 %collective-permute-start.3 = (bf16[2,384,768]{2,1,0:T(8,128)(2,1)S(1)}, bf16[2,384,768]{2,1,0:T(8,128)(2,1)}, u32[]{:S(2)}, u32[]{:S(2)}) collective-permute-start(bf16[2,384,768]{2,1,0:T(8,128)(2,1)S(1)} %pad_maximum_fusion), channel_id=1, source_target_pairs={{0,4},{4,8},{8,12},{12,16},{16,20},{20,24},{24,28},{28,32},{32,36}... | collective-permute-start | bytes 3538952 | tf_op jit(solution)/shard_map/ppermute | solution.py:15
  21.6 145.3 %collective-permute-start.2 = (bf16[2,384,768]{2,1,0:T(8,128)(2,1)S(1)}, bf16[2,384,768]{2,1,0:T(8,128)(2,1)}, u32[]{:S(2)}, u32[]{:S(2)}) collective-permute-start(bf16[2,384,768]{2,1,0:T(8,128)(2,1)S(1)} %pad_maximum_fusion), channel_id=1, source_target_pairs={{0,12},{4,16},{8,20},{12,24},{16,28},{20,32},{24,36},{28,40},{32,4... | collective-permute-start | bytes 3538952 | tf_op jit(solution)/shard_map/ppermute | solution.py:15
  24.3 119.3 %collective-permute-start.1 = (bf16[2,384,768]{2,1,0:T(8,128)(2,1)S(1)}, bf16[2,384,768]{2,1,0:T(8,128)(2,1)}, u32[]{:S(2)}, u32[]{:S(2)}) collective-permute-start(bf16[2,384,768]{2,1,0:T(8,128)(2,1)S(1)} %pad_maximum_fusion), channel_id=1, source_target_pairs={{0,16},{4,20},{8,24},{12,28},{16,32},{20,36},{24,40},{28,44},{32,4... | collective-permute-start | bytes 3538952 | tf_op jit(solution)/shard_map/ppermute | solution.py:15
  71.9 111.8 %collective-permute-start.4 = (bf16[2,384,768]{2,1,0:T(8,128)(2,1)S(1)}, bf16[2,384,768]{2,1,0:T(8,128)(2,1)S(1)}, u32[]{:S(2)}, u32[]{:S(2)}) collective-permute-start(bf16[2,384,768]{2,1,0:T(8,128)(2,1)S(1)} %pad_maximum_fusion), channel_id=1, source_target_pairs={{4,0},{8,4},{12,8},{16,12},{20,16},{24,20},{28,24},{32,28},{36,32}... | collective-permute-start | bytes 3538952 | tf_op jit(solution)/shard_map/ppermute | solution.py:15
  143.6 59.9 %collective-permute-start.5 = (bf16[2,384,768]{2,1,0:T(8,128)(2,1)S(1)}, bf16[2,384,768]{2,1,0:T(8,128)(2,1)S(1)}, u32[]{:S(2)}, u32[]{:S(2)}) collective-permute-start(bf16[2,384,768]{2,1,0:T(8,128)(2,1)S(1)} %pad_maximum_fusion), channel_id=1, source_target_pairs={{12,0},{16,4},{20,8},{24,12},{28,16},{32,20},{36,24},{40,28},{44,3... | collective-permute-start | bytes 3538952 | tf_op jit(solution)/shard_map/ppermute | solution.py:15
  167.0 47.3 %collective-permute-start.7 = (bf16[2,384,768]{2,1,0:T(8,128)(2,1)S(1)}, bf16[2,384,768]{2,1,0:T(8,128)(2,1)S(1)}, u32[]{:S(2)}, u32[]{:S(2)}) collective-permute-start(bf16[2,384,768]{2,1,0:T(8,128)(2,1)S(1)} %pad_maximum_fusion), channel_id=1, source_target_pairs={{20,0},{24,4},{28,8},{32,12},{36,16},{40,20},{44,24},{48,28},{52,3... | collective-permute-start | bytes 3538952 | tf_op jit(solution)/shard_map/ppermute | solution.py:15
  367.6 627.7 %reduce-scatter.5.cloned.1.call-start = ((), (), s32[]{:S(2)}) async-start(), calls=%async_computation.2 | async-start | bytes 245760 | tf_op jit(solution)/shard_map/reduce_scatter | solution.py:132
  419.4 24.8 %copy-start.7 = (bf16[1,2,384,768]{3,0,2,1:T(2,128)(2,1)S(1)}, bf16[1,2,384,768]{3,0,2,1:T(2,128)(2,1)}, u32[]{:S(2)}) copy-start(bf16[1,2,384,768]{3,0,2,1:T(2,128)(2,1)} %get-tuple-element.276) | copy-start | bytes 3538948
  421.8 39.2 %copy-start.6 = (bf16[1,2,384,768]{3,0,2,1:T(2,128)(2,1)S(1)}, bf16[1,2,384,768]{3,0,2,1:T(2,128)(2,1)}, u32[]{:S(2)}) copy-start(bf16[1,2,384,768]{3,0,2,1:T(2,128)(2,1)} %get-tuple-element.271) | copy-start | bytes 3538948
  422.0 61.7 %collective-permute-start.9 = (bf16[2,384,768]{2,1,0:T(8,128)(2,1)S(1)}, bf16[2,384,768]{2,1,0:T(8,128)(2,1)S(1)}, u32[]{:S(2)}, u32[]{:S(2)}) collective-permute-start(bf16[2,384,768]{2,1,0:T(8,128)(2,1)S(1)} %bitcast.176), channel_id=1, source_target_pairs={{16,0},{20,4},{24,8},{28,12},{32,16},{36,20},{40,24},{44,28},{48,3... | collective-permute-start | bytes 3538952 | tf_op jit(solution)/shard_map/ppermute | solution.py:15
  434.9 65.8 %collective-permute-start.10 = (bf16[2,384,768]{2,1,0:T(8,128)(2,1)S(1)}, bf16[2,384,768]{2,1,0:T(8,128)(2,1)S(1)}, u32[]{:S(2)}, u32[]{:S(2)}) collective-permute-start(bf16[2,384,768]{2,1,0:T(8,128)(2,1)S(1)} %bitcast.173), channel_id=1, source_target_pairs={{12,0},{16,4},{20,8},{24,12},{28,16},{32,20},{36,24},{40,28},{44,3... | collective-permute-start | bytes 3538952 | tf_op jit(solution)/shard_map/ppermute | solution.py:15
  444.3 17.0 %copy-start.5 = (bf16[1,2,384,768]{3,0,2,1:T(2,128)(2,1)S(1)}, bf16[1,2,384,768]{3,0,2,1:T(2,128)(2,1)}, u32[]{:S(2)}) copy-start(bf16[1,2,384,768]{3,0,2,1:T(2,128)(2,1)} %get-tuple-element.272) | copy-start | bytes 3538948
  444.5 102.8 %collective-permute-start.11 = (bf16[2,384,768]{2,1,0:T(8,128)(2,1)S(1)}, bf16[2,384,768]{2,1,0:T(8,128)(2,1)S(1)}, u32[]{:S(2)}, u32[]{:S(2)}) collective-permute-start(bf16[2,384,768]{2,1,0:T(8,128)(2,1)S(1)} %bitcast.174), channel_id=1, source_target_pairs={{4,0},{8,4},{12,8},{16,12},{20,16},{24,20},{28,24},{32,28},{36,32}... | collective-permute-start | bytes 3538952 | tf_op jit(solution)/shard_map/ppermute | solution.py:15
  462.0 89.1 %collective-permute-start.12 = (bf16[2,384,768]{2,1,0:T(8,128)(2,1)S(1)}, bf16[2,384,768]{2,1,0:T(8,128)(2,1)S(1)}, u32[]{:S(2)}, u32[]{:S(2)}) collective-permute-start(bf16[2,384,768]{2,1,0:T(8,128)(2,1)S(1)} %bitcast.177), channel_id=1, source_target_pairs={{0,4},{4,8},{8,12},{12,16},{16,20},{20,24},{24,28},{28,32},{32,36}... | collective-permute-start | bytes 3538952 | tf_op jit(solution)/shard_map/ppermute | solution.py:15
  463.9 87.3 %collective-permute-start.13 = (bf16[2,384,768]{2,1,0:T(8,128)(2,1)S(1)}, bf16[2,384,768]{2,1,0:T(8,128)(2,1)S(1)}, u32[]{:S(2)}, u32[]{:S(2)}) collective-permute-start(bf16[2,384,768]{2,1,0:T(8,128)(2,1)S(1)} %bitcast.175), channel_id=1, source_target_pairs={{0,12},{4,16},{8,20},{12,24},{16,28},{20,32},{24,36},{28,40},{32,4... | collective-permute-start | bytes 3538952 | tf_op jit(solution)/shard_map/ppermute | solution.py:15
  483.7 97.7 %collective-permute-start.14 = (bf16[2,384,768]{2,1,0:T(8,128)(2,1)S(1)}, bf16[2,384,768]{2,1,0:T(8,128)(2,1)S(1)}, u32[]{:S(2)}, u32[]{:S(2)}) collective-permute-start(bf16[2,384,768]{2,1,0:T(8,128)(2,1)S(1)} %bitcast.172), channel_id=1, source_target_pairs={{0,16},{4,20},{8,24},{12,28},{16,32},{20,36},{24,40},{28,44},{32,4... | collective-permute-start | bytes 3538952 | tf_op jit(solution)/shard_map/ppermute | solution.py:15
  500.7 172.0 %collective-permute-start.15 = (bf16[2,384,768]{2,1,0:T(8,128)(2,1)S(1)}, bf16[2,384,768]{2,1,0:T(8,128)(2,1)S(1)}, u32[]{:S(2)}, u32[]{:S(2)}) collective-permute-start(bf16[2,384,768]{2,1,0:T(8,128)(2,1)S(1)} %bitcast.171), channel_id=1, source_target_pairs={{0,20},{4,24},{8,28},{12,32},{16,36},{20,40},{24,44},{28,48},{32,5... | collective-permute-start | bytes 3538952 | tf_op jit(solution)/shard_map/ppermute | solution.py:15
  547.3 125.3 %collective-permute-start.8 = (bf16[2,384,768]{2,1,0:T(8,128)(2,1)S(1)}, bf16[2,384,768]{2,1,0:T(8,128)(2,1)S(1)}, u32[]{:S(2)}, u32[]{:S(2)}) collective-permute-start(bf16[2,384,768]{2,1,0:T(8,128)(2,1)S(1)} %bitcast.170), channel_id=1, source_target_pairs={{20,0},{24,4},{28,8},{32,12},{36,16},{40,20},{44,24},{48,28},{52,3... | collective-permute-start | bytes 3538952 | tf_op jit(solution)/shard_map/ppermute | solution.py:15
  672.7 324.1 %copy-start.1 = (bf16[1,1,384,3072]{3,2,1,0:T(8,128)(2,1)S(1)}, bf16[1,1,384,3072]{3,2,1,0:T(8,128)(2,1)}, u32[]{:S(2)}) copy-start(bf16[1,1,384,3072]{3,2,1,0:T(8,128)(2,1)} %param.12) | copy-start | bytes 7077892
  (16 other events, 68.0 us)
Sparse Core Ops, SparseCore 0:
  367.8 533.4 reduce-scatter.6
  904.0 91.2 reduce-scatter.4
where the time goes:
time: 1010 us; the launch traced here: 1000 us
  waiting for transfers between devices  634 us (63%)
  starting transfers between devices  119 us (12%)
  matrix products  93.2 us (9%)
  local copies, waits for them, and re-layouts  85.8 us (8%)
  other arithmetic  57.5 us (6%)
  between operations  14.3 us (1%)
    ppermute x16, waiting for transfers between devices, from_behind(): lax.ppermute(value, axis, [(source, source + steps) for source in range(i...  315 us
    unnamed x3, waiting for transfers between devices  227 us
    ppermute x16, starting transfers between devices, from_behind(): lax.ppermute(value, axis, [(source, source + steps) for source in range(i...  119 us
    reduce_scatter x1, waiting for transfers between devices, body(): lax.psum_scatter(tile_sum.astype(jnp.bfloat16), 'dp', scatter_dimension=1...  91.2 us
    slice x1, other arithmetic, body(): by_slot[slot_number]  35.8 us
    unnamed x38, local copies, waits for them, and re-layouts  29.9 us
    dot_general x6, matrix products, head_block(): jnp.einsum('hqk,khd->qhd', probs_low, value_part, preferred_element_type=...  20.3 us
  transfers between devices with their start and end apart: 18, of which 13 were waited for; matrix products, arithmetic and copies ran while one was open for 8% of the time, Pallas kernels for 0%

commit v1 on v0

--- a/solution.py
+++ b/solution.py
@@ -120,19 +120,33 @@
     attn_all, grad_query, grad_key, grad_value = lax.fori_loop(
         0, inner_width // block_width, head_block, start_state
     )
-    tile_sum = lax.psum_scatter(
-        lax.dot_general(
-            grad_tile, attn_all, (((0,), (0,)), ((), ())), preferred_element_type=jnp.float32
-        ),
-        "sp",
-        scatter_dimension=0,
-        tiled=True,
+    dp_count = lax.axis_size("dp")
+    sp_count = lax.axis_size("sp")
+    dp_index = lax.axis_index("dp")
+    core, high = dp_index % 2, dp_index // 2
+    row_block = inner_width // dp_count
+    model_width = grad_tile.shape[1]
+    col_block = model_width // sp_count
+    attn_blocks = attn_all.reshape(tile_tok, dp_count // 2, 2, row_block)
+    kept_rows = lax.dynamic_index_in_dim(attn_blocks, core, 2, keepdims=False).reshape(tile_tok, -1)
+    sent_rows = lax.dynamic_index_in_dim(attn_blocks, 1 - core, 2, keepdims=False).reshape(tile_tok, -1)
+    contract_tokens = (((0,), (0,)), ((), ()))
+    kept_part = lax.dot_general(grad_tile, kept_rows, contract_tokens, preferred_element_type=jnp.float32)
+    sent_part = lax.dot_general(grad_tile, sent_rows, contract_tokens, preferred_element_type=jnp.float32)
+    sibling_part = lax.ppermute(
+        sent_part.astype(jnp.bfloat16), "dp", [(index, index ^ 1) for index in range(dp_count)]
     )
+    core_sum = (kept_part + sibling_part.astype(jnp.float32)).astype(jnp.bfloat16)
+    by_column = lax.all_to_all(
+        core_sum.reshape(sp_count, col_block, -1), "sp", 0, 0, tiled=True
+    )
+    column_sum = by_column.astype(jnp.float32).sum(0).reshape(col_block, dp_count // 2, row_block)
+    own_half = lax.dynamic_index_in_dim(column_sum, high, 1, keepdims=False)
+    other_half = lax.dynamic_index_in_dim(column_sum, 1 - high, 1, keepdims=False)
     weight_grad = (
-        lax.psum_scatter(tile_sum.astype(jnp.bfloat16), "dp", scatter_dimension=1, tiled=True)
-        .astype(jnp.float32)
-        .T
-    )
+        own_half
+        + lax.ppermute(other_half, "dp", [(index, (index + 2) % dp_count) for index in range(dp_count)])
+    ).T
     slot_terms = jnp.stack(
         [
             grad_key.reshape(slot_count, tile_tok, inner_width),

time: 1010 us -> 799 us (0.79)
  the two profiles are of different devices: /device:TPU:24 before, /device:TPU:112 now
where the time goes in v1:
time: 799 us; the launch traced here: 796 us
  waiting for transfers between devices  336 us (42%)
  starting transfers between devices  217 us (27%)
  matrix products  91.5 us (11%)
  local copies, waits for them, and re-layouts  85.2 us (11%)
  other arithmetic  64.8 us (8%)
    ppermute x16, waiting for transfers between devices, from_behind(): lax.ppermute(value, axis, [(source, source + steps) for source in range(i...  332 us
    ppermute x16, starting transfers between devices, from_behind(): lax.ppermute(value, axis, [(source, source + steps) for source in range(i...  154 us
    all_to_all x1, starting transfers between devices, body(): lax.all_to_all(core_sum.reshape(sp_count, col_block, -1), 'sp', 0, 0, til...  59.9 us
    slice x1, other arithmetic, body(): by_slot[slot_number]  36.3 us
    unnamed x38, local copies, waits for them, and re-layouts  23.2 us
    dot_general x6, matrix products, head_block(): jnp.einsum('hqk,khd->qhd', probs_low, value_part, preferred_element_type=...  20.3 us
  transfers between devices with their start and end apart: 19, of which 9 were waited for; matrix products, arithmetic and copies ran while one was open for 11% of the time, Pallas kernels for 0%

profile of v1, /device:TPU:112, one launch (start us, length us, event | category | flops | bytes accessed | tf_op | source)
XLA Modules:
  0.0 796.4 jit_solution(5614290880269272678)
XLA Ops:
  7.6 7.7 collective-permute-start.2
  19.3 5.2 fusion.46
  25.2 136.7 %collective-permute-done = bf16[2,384,768]{2,1,0:T(8,128)(2,1)} collective-permute-done((bf16[2,384,768]{2,1,0:T(8,128)(2,1)S(1)}, bf16[2,384,768]{2,1,0:T(8,128)(2,1)}, u32[]{:S(2)}, u32[]{:S(2)}) %collective-permute-start) | collective-permute-done | bytes 1179680 | tf_op jit(solution)/shard_map/ppermute | solution.py:15
  161.9 30.6 %collective-permute-start.4 = (bf16[2,384,768]{2,1,0:T(8,128)(2,1)S(1)}, bf16[2,384,768]{2,1,0:T(8,128)(2,1)S(1)}, u32[]{:S(2)}, u32[]{:S(2)}) collective-permute-start(bf16[2,384,768]{2,1,0:T(8,128)(2,1)S(1)} %pad_maximum_fusion), channel_id=1, source_target_pairs={{4,0},{8,4},{12,8},{16,12},{20,16},{24,20},{28,24},{32,28},{36,32}... | collective-permute-start | bytes 3538952 | tf_op jit(solution)/shard_map/ppermute | solution.py:15
  207.1 11.8 %collective-permute-done.4 = bf16[2,384,768]{2,1,0:T(8,128)(2,1)S(1)} collective-permute-done((bf16[2,384,768]{2,1,0:T(8,128)(2,1)S(1)}, bf16[2,384,768]{2,1,0:T(8,128)(2,1)S(1)}, u32[]{:S(2)}, u32[]{:S(2)}) %collective-permute-start.4) | collective-permute-done | bytes 1179680 | tf_op jit(solution)/shard_map/ppermute | solution.py:15
  220.0 24.2 %collective-permute-done.5 = bf16[2,384,768]{2,1,0:T(8,128)(2,1)S(1)} collective-permute-done((bf16[2,384,768]{2,1,0:T(8,128)(2,1)S(1)}, bf16[2,384,768]{2,1,0:T(8,128)(2,1)S(1)}, u32[]{:S(2)}, u32[]{:S(2)}) %collective-permute-start.5) | collective-permute-done | bytes 1179680 | tf_op jit(solution)/shard_map/ppermute | solution.py:15
  247.8 20.8 %collective-permute-done.7 = bf16[2,384,768]{2,1,0:T(8,128)(2,1)S(1)} collective-permute-done((bf16[2,384,768]{2,1,0:T(8,128)(2,1)S(1)}, bf16[2,384,768]{2,1,0:T(8,128)(2,1)S(1)}, u32[]{:S(2)}, u32[]{:S(2)}) %collective-permute-start.7) | collective-permute-done | bytes 1179680 | tf_op jit(solution)/shard_map/ppermute | solution.py:15
  269.7 8.0 %gather_fusion = bf16[5,2,384,768]{3,2,1,0:T(8,128)(2,1)} fusion(bf16[9,2,384,768]{3,2,1,0:T(8,128)(2,1)} %bitcast_dynamic-update-slice_fusion, s32[1024]{0:T(1024)S(1)} %pad_clamp_fusion), kind=kCustom, calls=%fused_computation | custom fusion | bytes 11796500 | tf_op jit(solution)/shard_map/jit(_take)/gather | solution.py:42
  289.2 116.9 %while.20 = (s32[]{:T(128)}, bf16[384,768]{0,1:T(8,128)(2,1)}, bf16[384,768]{1,0:T(8,128)(2,1)}, bf16[1920,768]{1,0:T(8,128)(2,1)}, bf16[1920,768]{1,0:T(8,128)(...) while((s32[]{:T(128)}, bf16[384,768]{0,1:T(8,128)(2,1)}, ...), condition=%wide.region_3.4_spmd.clone, body=%wide.region_0.3_spmd.clone.sunk | while | flops 1142389632 | bytes 57627912 | solution.py:120
  412.9 10.2 %convolution_convert_fusion.2 = bf16[9,2,384,768]{3,0,2,1:T(8,128)(2,1)} fusion(bf16[5,1,384,768]{3,0,2,1:T(8,128)(2,1)S(1)} %copy.93, bf16[5,1,384,768]{3,0,2,1:T(8,128)(2,1)S(1)} %copy.92, s32[5]{0:T(128)S(1)} %get-tuple-element.224, pred[5]{0:T(512)(128)(4,1)S(1)} %get-tuple-element.385), kind=kOutput, calls=%fused_computation.42 | convolution fusion | flops 70189144 | bytes 16515097 | tf_op jit(solution)/shard_map/js,jctd->sctd/dot_general | solution.py:160
  425.9 4.3 copy.94
  430.2 59.9 %all-to-all-start = ((bf16[64,48,384]{2,1,0:T(8,128)(2,1)}), bf16[64,48,384]{2,1,0:T(8,128)(2,1)}, u32[]{:S(2)}, u32[]{:S(2)}) async-start(bf16[64,48,384]{2,1,0:T(8,128)(2,1)} %bitcast.183), calls=%async_computation | async-start | bytes 4718592 | tf_op jit(solution)/shard_map/all_to_all | solution.py:140
  490.1 36.3 %fusion.62 = (bf16[1,2,384,768]{3,0,2,1:T(2,128)(2,1)}, bf16[1,2,384,768]{3,0,2,1:T(2,128)(2,1)}, bf16[1,2,384,768]{3,0,2,1:T(2,128)(2,1)S(1)}, bf16[1,2,384,768...) fusion(bf16[9,2,384,768]{3,0,2,1:T(8,128)(2,1)} %convolution_co, ...), kind=kLoop, calls=%fused_computation.125 | loop fusion | flops 589824 | bytes 22413312 | tf_op jit(solution)/shard_map/slice | solution.py:168
  535.3 3.8 collective-permute-start.11
  547.4 8.5 %collective-permute-start.13 = (bf16[2,384,768]{2,1,0:T(8,128)(2,1)}, bf16[2,384,768]{2,1,0:T(8,128)(2,1)}, u32[]{:S(2)}, u32[]{:S(2)}) collective-permute-start(bf16[2,384,768]{2,1,0:T(8,128)(2,1)} %bitcast.162), channel_id=1, source_target_pairs={{0,12},{4,16},{8,20},{12,24},{16,28},{20,32},{24,36},{28,40},{32,4... | collective-permute-start | bytes 3538952 | tf_op jit(solution)/shard_map/ppermute | solution.py:15
  555.9 7.9 collective-permute-done.9
  563.8 3.8 collective-permute-start.14
  567.6 15.8 %collective-permute-done.10 = bf16[2,384,768]{2,1,0:T(8,128)(2,1)} collective-permute-done((bf16[2,384,768]{2,1,0:T(8,128)(2,1)S(1)}, bf16[2,384,768]{2,1,0:T(8,128)(2,1)}, u32[]{:S(2)}, u32[]{:S(2)}) %collective-permute-start.10) | collective-permute-done | bytes 1179680 | tf_op jit(solution)/shard_map/ppermute | solution.py:15
  583.4 10.4 %collective-permute-start.15 = (bf16[2,384,768]{2,1,0:T(8,128)(2,1)}, bf16[2,384,768]{2,1,0:T(8,128)(2,1)}, u32[]{:S(2)}, u32[]{:S(2)}) collective-permute-start(bf16[2,384,768]{2,1,0:T(8,128)(2,1)} %bitcast.160), channel_id=1, source_target_pairs={{0,20},{4,24},{8,28},{12,32},{16,36},{20,40},{24,44},{28,48},{32,5... | collective-permute-start | bytes 3538952 | tf_op jit(solution)/shard_map/ppermute | solution.py:15
  593.8 15.6 %collective-permute-done.11 = bf16[2,384,768]{2,1,0:T(8,128)(2,1)} collective-permute-done((bf16[2,384,768]{2,1,0:T(8,128)(2,1)S(1)}, bf16[2,384,768]{2,1,0:T(8,128)(2,1)}, u32[]{:S(2)}, u32[]{:S(2)}) %collective-permute-start.11) | collective-permute-done | bytes 1179680 | tf_op jit(solution)/shard_map/ppermute | solution.py:15
  609.4 68.0 %collective-permute-start.8 = (bf16[2,384,768]{2,1,0:T(8,128)(2,1)}, bf16[2,384,768]{2,1,0:T(8,128)(2,1)}, u32[]{:S(2)}, u32[]{:S(2)}) collective-permute-start(bf16[2,384,768]{2,1,0:T(8,128)(2,1)} %bitcast.167), channel_id=1, source_target_pairs={{20,0},{24,4},{28,8},{32,12},{36,16},{40,20},{44,24},{48,28},{52,3... | collective-permute-start | bytes 3538952 | tf_op jit(solution)/shard_map/ppermute | solution.py:15
  677.4 99.2 %collective-permute-done.15 = bf16[2,384,768]{2,1,0:T(8,128)(2,1)} collective-permute-done((bf16[2,384,768]{2,1,0:T(8,128)(2,1)}, bf16[2,384,768]{2,1,0:T(8,128)(2,1)}, u32[]{:S(2)}, u32[]{:S(2)}) %collective-permute-start.15) | collective-permute-done | bytes 1179680 | tf_op jit(solution)/shard_map/ppermute | solution.py:15
  776.6 5.6 fusion.41
  791.7 4.0 collective-permute-done.17
  (213 shorter events, 196.7 us)
Async XLA Ops:
  0.6 18.6 %copy-start = (bf16[1,1,384,3072]{3,2,1,0:T(8,128)(2,1)S(1)}, bf16[1,1,384,3072]{3,2,1,0:T(8,128)(2,1)}, u32[]{:S(2)}) copy-start(bf16[1,1,384,3072]{3,2,1,0:T(8,128)(2,1)} %param.12) | copy-start | bytes 7077892
  2.2 22.3 %copy-start.12 = (s32[1,5]{1,0:T(1,128)S(1)}, s32[1,5]{1,0:T(1,128)}, u32[]{:S(2)}) copy-start(s32[1,5]{1,0:T(1,128)} %param.11) | copy-start | bytes 64
  2.2 243.2 %collective-permute-start.6 = (bf16[2,384,768]{2,1,0:T(8,128)(2,1)S(1)}, bf16[2,384,768]{2,1,0:T(8,128)(2,1)}, u32[]{:S(2)}, u32[]{:S(2)}) collective-permute-start(bf16[2,384,768]{2,1,0:T(8,128)(2,1)S(1)} %pad_maximum_fusion), channel_id=1, source_target_pairs={{16,0},{20,4},{24,8},{28,12},{32,16},{36,20},{40,24},{44,28},{48,3... | collective-permute-start | bytes 3538952 | tf_op jit(solution)/shard_map/ppermute | solution.py:15
  4.2 199.4 %collective-permute-start.3 = (bf16[2,384,768]{2,1,0:T(8,128)(2,1)S(1)}, bf16[2,384,768]{2,1,0:T(8,128)(2,1)}, u32[]{:S(2)}, u32[]{:S(2)}) collective-permute-start(bf16[2,384,768]{2,1,0:T(8,128)(2,1)S(1)} %pad_maximum_fusion), channel_id=1, source_target_pairs={{0,4},{4,8},{8,12},{12,16},{16,20},{20,24},{24,28},{28,32},{32,36}... | collective-permute-start | bytes 3538952 | tf_op jit(solution)/shard_map/ppermute | solution.py:15
  7.6 191.5 %collective-permute-start.2 = (bf16[2,384,768]{2,1,0:T(8,128)(2,1)S(1)}, bf16[2,384,768]{2,1,0:T(8,128)(2,1)}, u32[]{:S(2)}, u32[]{:S(2)}) collective-permute-start(bf16[2,384,768]{2,1,0:T(8,128)(2,1)S(1)} %pad_maximum_fusion), channel_id=1, source_target_pairs={{0,12},{4,16},{8,20},{12,24},{16,28},{20,32},{24,36},{28,40},{32,4... | collective-permute-start | bytes 3538952 | tf_op jit(solution)/shard_map/ppermute | solution.py:15
  15.3 179.5 %collective-permute-start.1 = (bf16[2,384,768]{2,1,0:T(8,128)(2,1)S(1)}, bf16[2,384,768]{2,1,0:T(8,128)(2,1)}, u32[]{:S(2)}, u32[]{:S(2)}) collective-permute-start(bf16[2,384,768]{2,1,0:T(8,128)(2,1)S(1)} %pad_maximum_fusion), channel_id=1, source_target_pairs={{0,16},{4,20},{8,24},{12,28},{16,32},{20,36},{24,40},{28,44},{32,4... | collective-permute-start | bytes 3538952 | tf_op jit(solution)/shard_map/ppermute | solution.py:15
  17.3 144.5 %collective-permute-start = (bf16[2,384,768]{2,1,0:T(8,128)(2,1)S(1)}, bf16[2,384,768]{2,1,0:T(8,128)(2,1)}, u32[]{:S(2)}, u32[]{:S(2)}) collective-permute-start(bf16[2,384,768]{2,1,0:T(8,128)(2,1)S(1)} %pad_maximum_fusion), channel_id=1, source_target_pairs={{0,20},{4,24},{8,28},{12,32},{16,36},{20,40},{24,44},{28,48},{32,5... | collective-permute-start | bytes 3538952 | tf_op jit(solution)/shard_map/ppermute | solution.py:15
  161.9 57.0 %collective-permute-start.4 = (bf16[2,384,768]{2,1,0:T(8,128)(2,1)S(1)}, bf16[2,384,768]{2,1,0:T(8,128)(2,1)S(1)}, u32[]{:S(2)}, u32[]{:S(2)}) collective-permute-start(bf16[2,384,768]{2,1,0:T(8,128)(2,1)S(1)} %pad_maximum_fusion), channel_id=1, source_target_pairs={{4,0},{8,4},{12,8},{16,12},{20,16},{24,20},{28,24},{32,28},{36,32}... | collective-permute-start | bytes 3538952 | tf_op jit(solution)/shard_map/ppermute | solution.py:15
  194.8 49.3 %collective-permute-start.5 = (bf16[2,384,768]{2,1,0:T(8,128)(2,1)S(1)}, bf16[2,384,768]{2,1,0:T(8,128)(2,1)S(1)}, u32[]{:S(2)}, u32[]{:S(2)}) collective-permute-start(bf16[2,384,768]{2,1,0:T(8,128)(2,1)S(1)} %pad_maximum_fusion), channel_id=1, source_target_pairs={{12,0},{16,4},{20,8},{24,12},{28,16},{32,20},{36,24},{40,28},{44,3... | collective-permute-start | bytes 3538952 | tf_op jit(solution)/shard_map/ppermute | solution.py:15
  199.1 6.8 copy-start.10
  199.1 69.5 %collective-permute-start.7 = (bf16[2,384,768]{2,1,0:T(8,128)(2,1)S(1)}, bf16[2,384,768]{2,1,0:T(8,128)(2,1)S(1)}, u32[]{:S(2)}, u32[]{:S(2)}) collective-permute-start(bf16[2,384,768]{2,1,0:T(8,128)(2,1)S(1)} %pad_maximum_fusion), channel_id=1, source_target_pairs={{20,0},{24,4},{28,8},{32,12},{36,16},{40,20},{44,24},{48,28},{52,3... | collective-permute-start | bytes 3538952 | tf_op jit(solution)/shard_map/ppermute | solution.py:15
  408.7 14.4 %collective-permute-start.16 = (bf16[3072,384]{0,1:T(8,128)(2,1)S(1)}, bf16[3072,384]{0,1:T(8,128)(2,1)S(1)}, u32[]{:S(2)}, u32[]{:S(2)}) collective-permute-start(bf16[3072,384]{0,1:T(8,128)(2,1)S(1)} %fusion.33), channel_id=1, source_target_pairs={{0,1},{1,0},{2,3},{3,2},{4,5},{5,4},{6,7},{7,6},{8,9},{9,8},{10,11... | collective-permute-start | bytes 7077896 | tf_op jit(solution)/shard_map/ppermute | solution.py:136
  430.2 352.1 %all-to-all-start = ((bf16[64,48,384]{2,1,0:T(8,128)(2,1)}), bf16[64,48,384]{2,1,0:T(8,128)(2,1)}, u32[]{:S(2)}, u32[]{:S(2)}) async-start(bf16[64,48,384]{2,1,0:T(8,128)(2,1)} %bitcast.183), calls=%async_computation | async-start | bytes 4718592 | tf_op jit(solution)/shard_map/all_to_all | solution.py:140
  529.0 10.1 %copy-start.6 = (bf16[1,2,384,768]{3,0,2,1:T(2,128)(2,1)S(1)}, bf16[1,2,384,768]{3,0,2,1:T(2,128)(2,1)}, u32[]{:S(2)}) copy-start(bf16[1,2,384,768]{3,0,2,1:T(2,128)(2,1)} %get-tuple-element.231) | copy-start | bytes 3538948
  529.0 34.8 %collective-permute-start.9 = (bf16[2,384,768]{2,1,0:T(8,128)(2,1)S(1)}, bf16[2,384,768]{2,1,0:T(8,128)(2,1)}, u32[]{:S(2)}, u32[]{:S(2)}) collective-permute-start(bf16[2,384,768]{2,1,0:T(8,128)(2,1)S(1)} %bitcast.192), channel_id=1, source_target_pairs={{16,0},{20,4},{24,8},{28,12},{32,16},{36,20},{40,24},{44,28},{48,3... | collective-permute-start | bytes 3538952 | tf_op jit(solution)/shard_map/ppermute | solution.py:15
  531.7 51.7 %collective-permute-start.10 = (bf16[2,384,768]{2,1,0:T(8,128)(2,1)S(1)}, bf16[2,384,768]{2,1,0:T(8,128)(2,1)}, u32[]{:S(2)}, u32[]{:S(2)}) collective-permute-start(bf16[2,384,768]{2,1,0:T(8,128)(2,1)S(1)} %bitcast.190), channel_id=1, source_target_pairs={{12,0},{16,4},{20,8},{24,12},{28,16},{32,20},{36,24},{40,28},{44,3... | collective-permute-start | bytes 3538952 | tf_op jit(solution)/shard_map/ppermute | solution.py:15
  535.3 74.1 %collective-permute-start.11 = (bf16[2,384,768]{2,1,0:T(8,128)(2,1)S(1)}, bf16[2,384,768]{2,1,0:T(8,128)(2,1)}, u32[]{:S(2)}, u32[]{:S(2)}) collective-permute-start(bf16[2,384,768]{2,1,0:T(8,128)(2,1)S(1)} %bitcast.191), channel_id=1, source_target_pairs={{4,0},{8,4},{12,8},{16,12},{20,16},{24,20},{28,24},{32,28},{36,32}... | collective-permute-start | bytes 3538952 | tf_op jit(solution)/shard_map/ppermute | solution.py:15
  545.2 132.2 %collective-permute-start.12 = (bf16[2,384,768]{2,1,0:T(8,128)(2,1)}, bf16[2,384,768]{2,1,0:T(8,128)(2,1)S(1)}, u32[]{:S(2)}, u32[]{:S(2)}) collective-permute-start(bf16[2,384,768]{2,1,0:T(8,128)(2,1)} %bitcast.163), channel_id=1, source_target_pairs={{0,4},{4,8},{8,12},{12,16},{16,20},{20,24},{24,28},{28,32},{32,36}... | collective-permute-start | bytes 3538952 | tf_op jit(solution)/shard_map/ppermute | solution.py:15
  547.4 130.1 %collective-permute-start.13 = (bf16[2,384,768]{2,1,0:T(8,128)(2,1)}, bf16[2,384,768]{2,1,0:T(8,128)(2,1)}, u32[]{:S(2)}, u32[]{:S(2)}) collective-permute-start(bf16[2,384,768]{2,1,0:T(8,128)(2,1)} %bitcast.162), channel_id=1, source_target_pairs={{0,12},{4,16},{8,20},{12,24},{16,28},{20,32},{24,36},{28,40},{32,4... | collective-permute-start | bytes 3538952 | tf_op jit(solution)/shard_map/ppermute | solution.py:15
  563.8 113.6 %collective-permute-start.14 = (bf16[2,384,768]{2,1,0:T(8,128)(2,1)}, bf16[2,384,768]{2,1,0:T(8,128)(2,1)}, u32[]{:S(2)}, u32[]{:S(2)}) collective-permute-start(bf16[2,384,768]{2,1,0:T(8,128)(2,1)} %bitcast.161), channel_id=1, source_target_pairs={{0,16},{4,20},{8,24},{12,28},{16,32},{20,36},{24,40},{28,44},{32,4... | collective-permute-start | bytes 3538952 | tf_op jit(solution)/shard_map/ppermute | solution.py:15
  583.4 193.2 %collective-permute-start.15 = (bf16[2,384,768]{2,1,0:T(8,128)(2,1)}, bf16[2,384,768]{2,1,0:T(8,128)(2,1)}, u32[]{:S(2)}, u32[]{:S(2)}) collective-permute-start(bf16[2,384,768]{2,1,0:T(8,128)(2,1)} %bitcast.160), channel_id=1, source_target_pairs={{0,20},{4,24},{8,28},{12,32},{16,36},{20,40},{24,44},{28,48},{32,5... | collective-permute-start | bytes 3538952 | tf_op jit(solution)/shard_map/ppermute | solution.py:15
  609.4 167.2 %collective-permute-start.8 = (bf16[2,384,768]{2,1,0:T(8,128)(2,1)}, bf16[2,384,768]{2,1,0:T(8,128)(2,1)}, u32[]{:S(2)}, u32[]{:S(2)}) collective-permute-start(bf16[2,384,768]{2,1,0:T(8,128)(2,1)} %bitcast.167), channel_id=1, source_target_pairs={{20,0},{24,4},{28,8},{32,12},{36,16},{40,20},{44,24},{48,28},{52,3... | collective-permute-start | bytes 3538952 | tf_op jit(solution)/shard_map/ppermute | solution.py:15
  677.4 99.2 %copy-start.11 = (bf16[2,384,768]{2,1,0:T(8,128)(2,1)}, bf16[2,384,768]{2,1,0:T(8,128)(2,1)S(1)}, u32[]{:S(2)}) copy-start(bf16[2,384,768]{2,1,0:T(8,128)(2,1)S(1)} %collective-permute-done.12) | copy-start | bytes 3538948
  787.7 8.1 %collective-permute-start.17 = (f32[48,192]{1,0:T(8,128)S(1)}, f32[48,192]{1,0:T(8,128)S(1)}, u32[]{:S(2)}, u32[]{:S(2)}) collective-permute-start(f32[48,192]{1,0:T(8,128)S(1)} %bitcast.195), channel_id=1, source_target_pairs={{0,2},{1,3},{2,0},{3,1},{4,6},{5,7},{6,4},{7,5},{8,10},{9,11},{10,... | collective-permute-start | bytes 110600 | tf_op jit(solution)/shard_map/ppermute | solution.py:148
  (18 other events, 54.8 us)

commit v2 on v1

--- a/solution.py
+++ b/solution.py
@@ -9,10 +9,16 @@
 H_TILES = 4
 
 
-def from_behind(value, axis, steps):
+def neighbour_shift(value, axis, time_step, height_step, height_tiles, toward):
     count = lax.axis_size(axis)
-    initial, last = (max(0, -steps), min(count, count - steps))
-    return lax.ppermute(value, axis, [(source, source + steps) for source in range(initial, last)])
+    time_tiles = count // height_tiles
+    offset = time_step * height_tiles + height_step
+    pairs = []
+    for tile in range(count):
+        time_row, height_col = divmod(tile, height_tiles)
+        if 0 <= time_row + time_step < time_tiles and 0 <= height_col + height_step < height_tiles:
+            pairs.append((tile, tile + offset) if toward else (tile + offset, tile))
+    return lax.ppermute(value, axis, pairs)
 
 
 def body(queries, keys, values, tile_lists, grad_out, w_out):
@@ -33,7 +39,7 @@
         if time_step == 0 and height_step == 0:
             pieces.append(key_value)
         else:
-            pieces.append(from_behind(key_value, "sp", -(time_step * height_tiles + height_step)))
+            pieces.append(neighbour_shift(key_value, "sp", time_step, height_step, height_tiles, False))
     window = jnp.stack(pieces)
     valid_slot = listed >= 0
     time_gap = listed // height_tiles - own_tile // height_tiles
@@ -147,25 +153,30 @@
         own_half
         + lax.ppermute(other_half, "dp", [(index, (index + 2) % dp_count) for index in range(dp_count)])
     ).T
-    slot_terms = jnp.stack(
-        [
-            grad_key.reshape(slot_count, tile_tok, inner_width),
-            grad_value.reshape(slot_count, tile_tok, inner_width),
-        ],
-        axis=1,
-    )
-    selector = (
-        (slot_index[:, None] == jnp.arange(9, dtype=jnp.int32)[None, :]) & valid_slot[:, None]
-    ).astype(jnp.bfloat16)
-    by_slot = jnp.einsum(
-        "js,jctd->sctd", selector, slot_terms, preferred_element_type=jnp.float32
-    ).astype(jnp.bfloat16)
-    grad_total = by_slot[4].astype(jnp.float32)
+    key_terms = grad_key.reshape(slot_count, tile_tok, inner_width)
+    value_terms = grad_value.reshape(slot_count, tile_tok, inner_width)
+    matches = (slot_index[:, None] == jnp.arange(9, dtype=jnp.int32)[None, :]) & valid_slot[:, None]
+    match_slot = jnp.argmax(matches, axis=0)
+    match_any = jnp.any(matches, axis=0)
+
+    def slot_payload(slot_number):
+        picked_slot = match_slot[slot_number]
+        payload = jnp.stack(
+            [
+                lax.dynamic_index_in_dim(key_terms, picked_slot, 0, keepdims=False),
+                lax.dynamic_index_in_dim(value_terms, picked_slot, 0, keepdims=False),
+            ]
+        )
+        return jnp.where(match_any[slot_number], payload, jnp.zeros_like(payload))
+
+    grad_total = slot_payload(4).astype(jnp.float32)
     for time_step, height_step in offsets:
         if time_step == 0 and height_step == 0:
             continue
         slot_number = (time_step + 1) * 3 + height_step + 1
-        arrived = from_behind(by_slot[slot_number], "sp", time_step * height_tiles + height_step)
+        arrived = neighbour_shift(
+            slot_payload(slot_number), "sp", time_step, height_step, height_tiles, True
+        )
         grad_total = grad_total + arrived.astype(jnp.float32)
     grad_kv = grad_total.astype(jnp.bfloat16)
     return (grad_query[None, None], grad_kv[0][None, None], grad_kv[1][None, None], weight_grad)

time: 799 us -> 645 us (0.81)
  the two profiles are of different devices: /device:TPU:112 before, /device:TPU:220 now
where the time goes in v2:
time: 645 us; the launch traced here: 642 us
  waiting for transfers between devices  262 us (41%)
  starting transfers between devices  149 us (23%)
  matrix products  89.5 us (14%)
  local copies, waits for them, and re-layouts  87.4 us (14%)
  other arithmetic  35.8 us (6%)
  between operations  17.6 us (3%)
    ppermute x16, waiting for transfers between devices, neighbour_shift(): return lax.ppermute(value, axis, pairs)  251 us
    all_to_all x1, starting transfers between devices, body(): lax.all_to_all(core_sum.reshape(sp_count, col_block, -1), 'sp', 0, 0, til...  93.1 us
    ppermute x16, starting transfers between devices, neighbour_shift(): return lax.ppermute(value, axis, pairs)  55.2 us
    dot_general x6, matrix products, head_block(): jnp.einsum('hqk,qhd->khd', probs_low, grad_part, preferred_element_type=j...  19 us
    while x54, local copies, waits for them, and re-layouts  17.5 us
    dot_general x6, matrix products, head_block(): jnp.einsum('qhd,khd->hqk', grad_part, value_part, preferred_element_type=...  15.6 us
    dynamic_update_slice x12, local copies, waits for them, and re-layouts, head_block(): lax.dynamic_update_slice_in_dim(grad_value, value_grad.astype(jnp.bfloat1...  14.5 us
    unnamed x18, local copies, waits for them, and re-layouts  14.2 us
  transfers between devices with their start and end apart: 19, of which 12 were waited for; matrix products, arithmetic and copies ran while one was open for 7% of the time, Pallas kernels for 0%

profile of v2, /device:TPU:220, one launch (start us, length us, event | category | flops | bytes accessed | tf_op | source)
XLA Modules:
  0.0 641.7 jit_solution(1296783661913186449)
XLA Ops:
  3.2 3.7 collective-permute-start
  16.6 4.4 fusion.35
  21.1 14.2 %collective-permute-done = bf16[2,384,768]{2,1,0:T(8,128)(2,1)} collective-permute-done((bf16[2,384,768]{2,1,0:T(8,128)(2,1)}, bf16[2,384,768]{2,1,0:T(8,128)(2,1)}, u32[]{:S(2)}, u32[]{:S(2)}) %collective-permute-start) | collective-permute-done | bytes 1179680 | tf_op jit(solution)/shard_map/ppermute | solution.py:21
  41.2 19.1 %collective-permute-done.1 = bf16[2,384,768]{2,1,0:T(8,128)(2,1)} collective-permute-done((bf16[2,384,768]{2,1,0:T(8,128)(2,1)}, bf16[2,384,768]{2,1,0:T(8,128)(2,1)}, u32[]{:S(2)}, u32[]{:S(2)}) %collective-permute-start.1) | collective-permute-done | bytes 1179680 | tf_op jit(solution)/shard_map/ppermute | solution.py:21
  60.3 8.2 %collective-permute-start.6 = (bf16[2,384,768]{2,1,0:T(8,128)(2,1)}, bf16[2,384,768]{2,1,0:T(8,128)(2,1)S(1)}, u32[]{:S(2)}, u32[]{:S(2)}) collective-permute-start(bf16[2,384,768]{2,1,0:T(8,128)(2,1)} %pad_maximum_fusion), channel_id=1, source_target_pairs={{16,0},{20,4},{24,8},{28,12},{32,16},{36,20},{40,24},{44,28},{48,3... | collective-permute-start | bytes 3538952 | tf_op jit(solution)/shard_map/ppermute | solution.py:21
  70.8 12.3 %collective-permute-done.2 = bf16[2,384,768]{2,1,0:T(8,128)(2,1)} collective-permute-done((bf16[2,384,768]{2,1,0:T(8,128)(2,1)}, bf16[2,384,768]{2,1,0:T(8,128)(2,1)}, u32[]{:S(2)}, u32[]{:S(2)}) %collective-permute-start.2) | collective-permute-done | bytes 1179680 | tf_op jit(solution)/shard_map/ppermute | solution.py:21
  83.1 6.3 collective-permute-start.7
  100.0 16.3 %collective-permute-done.7 = bf16[2,384,768]{2,1,0:T(8,128)(2,1)S(1)} collective-permute-done((bf16[2,384,768]{2,1,0:T(8,128)(2,1)}, bf16[2,384,768]{2,1,0:T(8,128)(2,1)S(1)}, u32[]{:S(2)}, u32[]{:S(2)}) %collective-permute-start.7) | collective-permute-done | bytes 1179680 | tf_op jit(solution)/shard_map/ppermute | solution.py:21
  117.4 8.0 %gather_fusion = bf16[5,2,384,768]{3,2,1,0:T(8,128)(2,1)} fusion(bf16[9,2,384,768]{3,2,1,0:T(8,128)(2,1)} %bitcast_dynamic-update-slice_fusion, s32[1024]{0:T(1024)S(1)} %pad_clamp_fusion), kind=kCustom, calls=%fused_computation | custom fusion | bytes 11796500 | tf_op jit(solution)/shard_map/jit(_take)/gather | solution.py:48
  137.0 127.7 %while.20 = (s32[]{:T(128)}, bf16[384,768]{0,1:T(8,128)(2,1)}, bf16[384,768]{1,0:T(8,128)(2,1)}, bf16[1920,768]{1,0:T(8,128)(2,1)}, bf16[1920,768]{1,0:T(8,128)(...) while((s32[]{:T(128)}, bf16[384,768]{0,1:T(8,128)(2,1)}, ...), condition=%wide.region_3.4_spmd.clone, body=%wide.region_0.3_spmd.clone.sunk | while | flops 1142389632 | bytes 56448832 | solution.py:126
  267.5 4.5 collective-permute-done.16
  274.9 4.3 copy.20
  279.2 93.1 %all-to-all-start = ((bf16[64,48,384]{2,1,0:T(8,128)(2,1)}), bf16[64,48,384]{2,1,0:T(8,128)(2,1)}, u32[]{:S(2)}, u32[]{:S(2)}) async-start(bf16[64,48,384]{2,1,0:T(8,128)(2,1)} %bitcast.154), calls=%async_computation | async-start | bytes 4718592 | tf_op jit(solution)/shard_map/all_to_all | solution.py:146
  390.9 6.4 %constant_dynamic-slice_fusion.20 = (bf16[1,384,768]{2,1,0:T(8,128)(2,1)}, bf16[1,384,768]{2,1,0:T(8,128)(2,1)S(1)}, bf16[1,384,768]{2,1,0:T(8,128)(2,1)S(1)}, b...) fusion(bf16[5,384,768]{2,1,0:T(8,128)(2,1)} %bitcast.151, ...), kind=kLoop, calls=%fused_computation.98 | loop fusion | bytes 21233700 | tf_op jit(solution)/shard_map/jit(dynamic_index_in_dim)/dynamic_slice | solution.py:167
  404.5 7.4 %collective-permute-start.10 = (bf16[2,384,768]{2,1,0:T(8,128)(2,1)S(1)}, bf16[2,384,768]{2,1,0:T(8,128)(2,1)}, u32[]{:S(2)}, u32[]{:S(2)}) collective-permute-start(bf16[2,384,768]{2,1,0:T(8,128)(2,1)S(1)} %maximum_select_fusion.3), channel_id=1, source_target_pairs={{16,4},{20,8},{24,12},{32,20},{36,24},{40,28},{48,36},{52,40},{56,... | collective-permute-start | bytes 3538952 | tf_op jit(solution)/shard_map/ppermute | solution.py:21
  417.3 4.0 collective-permute-start.12
  426.8 22.0 %collective-permute-done.8 = bf16[2,384,768]{2,1,0:T(8,128)(2,1)} collective-permute-done((bf16[2,384,768]{2,1,0:T(8,128)(2,1)S(1)}, bf16[2,384,768]{2,1,0:T(8,128)(2,1)}, u32[]{:S(2)}, u32[]{:S(2)}) %collective-permute-start.8) | collective-permute-done | bytes 1179680 | tf_op jit(solution)/shard_map/ppermute | solution.py:21
  450.7 23.4 %collective-permute-done.9 = bf16[2,384,768]{2,1,0:T(8,128)(2,1)} collective-permute-done((bf16[2,384,768]{2,1,0:T(8,128)(2,1)S(1)}, bf16[2,384,768]{2,1,0:T(8,128)(2,1)}, u32[]{:S(2)}, u32[]{:S(2)}) %collective-permute-start.9) | collective-permute-done | bytes 1179680 | tf_op jit(solution)/shard_map/ppermute | solution.py:21
  476.0 22.3 %collective-permute-done.10 = bf16[2,384,768]{2,1,0:T(8,128)(2,1)} collective-permute-done((bf16[2,384,768]{2,1,0:T(8,128)(2,1)S(1)}, bf16[2,384,768]{2,1,0:T(8,128)(2,1)}, u32[]{:S(2)}, u32[]{:S(2)}) %collective-permute-start.10) | collective-permute-done | bytes 1179680 | tf_op jit(solution)/shard_map/ppermute | solution.py:21
  500.3 17.5 %collective-permute-done.13 = bf16[2,384,768]{2,1,0:T(8,128)(2,1)} collective-permute-done((bf16[2,384,768]{2,1,0:T(8,128)(2,1)}, bf16[2,384,768]{2,1,0:T(8,128)(2,1)}, u32[]{:S(2)}, u32[]{:S(2)}) %collective-permute-start.13) | collective-permute-done | bytes 1179680 | tf_op jit(solution)/shard_map/ppermute | solution.py:21
  517.8 34.5 %collective-permute-done.14 = bf16[2,384,768]{2,1,0:T(8,128)(2,1)} collective-permute-done((bf16[2,384,768]{2,1,0:T(8,128)(2,1)}, bf16[2,384,768]{2,1,0:T(8,128)(2,1)}, u32[]{:S(2)}, u32[]{:S(2)}) %collective-permute-start.14) | collective-permute-done | bytes 1179680 | tf_op jit(solution)/shard_map/ppermute | solution.py:21
  552.4 69.2 %collective-permute-done.15 = bf16[2,384,768]{2,1,0:T(8,128)(2,1)} collective-permute-done((bf16[2,384,768]{2,1,0:T(8,128)(2,1)}, bf16[2,384,768]{2,1,0:T(8,128)(2,1)}, u32[]{:S(2)}, u32[]{:S(2)}) %collective-permute-start.15) | collective-permute-done | bytes 1179680 | tf_op jit(solution)/shard_map/ppermute | solution.py:21
  621.6 6.1 add_convert_fusion
  634.2 6.9 %collective-permute-done.17 = f32[48,192]{1,0:T(8,128)S(1)} collective-permute-done((f32[48,192]{1,0:T(8,128)S(1)}, f32[48,192]{1,0:T(8,128)S(1)}, u32[]{:S(2)}, u32[]{:S(2)}) %collective-permute-start.17) | collective-permute-done | bytes 36896 | tf_op jit(solution)/shard_map/ppermute | solution.py:154
  (226 shorter events, 209.7 us)
Async XLA Ops:
  0.6 15.9 %copy-start = (bf16[1,1,384,3072]{3,2,1,0:T(8,128)(2,1)S(1)}, bf16[1,1,384,3072]{3,2,1,0:T(8,128)(2,1)}, u32[]{:S(2)}) copy-start(bf16[1,1,384,3072]{3,2,1,0:T(8,128)(2,1)} %param.12) | copy-start | bytes 7077892
  3.2 17.8 %copy-start.8 = (s32[1,5]{1,0:T(1,128)S(1)}, s32[1,5]{1,0:T(1,128)}, u32[]{:S(2)}) copy-start(s32[1,5]{1,0:T(1,128)} %param.11) | copy-start | bytes 64
  3.2 32.1 %collective-permute-start = (bf16[2,384,768]{2,1,0:T(8,128)(2,1)}, bf16[2,384,768]{2,1,0:T(8,128)(2,1)}, u32[]{:S(2)}, u32[]{:S(2)}) collective-permute-start(bf16[2,384,768]{2,1,0:T(8,128)(2,1)} %pad_maximum_fusion), channel_id=1, source_target_pairs={{0,20},{4,24},{8,28},{16,36},{20,40},{24,44},{32,52},{36,56},{40,6... | collective-permute-start | bytes 3538952 | tf_op jit(solution)/shard_map/ppermute | solution.py:21
  6.9 53.5 %collective-permute-start.1 = (bf16[2,384,768]{2,1,0:T(8,128)(2,1)}, bf16[2,384,768]{2,1,0:T(8,128)(2,1)}, u32[]{:S(2)}, u32[]{:S(2)}) collective-permute-start(bf16[2,384,768]{2,1,0:T(8,128)(2,1)} %pad_maximum_fusion), channel_id=1, source_target_pairs={{0,16},{4,20},{8,24},{12,28},{16,32},{20,36},{24,40},{28,44},{32,4... | collective-permute-start | bytes 3538952 | tf_op jit(solution)/shard_map/ppermute | solution.py:21
  8.8 74.3 %collective-permute-start.2 = (bf16[2,384,768]{2,1,0:T(8,128)(2,1)}, bf16[2,384,768]{2,1,0:T(8,128)(2,1)}, u32[]{:S(2)}, u32[]{:S(2)}) collective-permute-start(bf16[2,384,768]{2,1,0:T(8,128)(2,1)} %pad_maximum_fusion), channel_id=1, source_target_pairs={{4,16},{8,20},{12,24},{20,32},{24,36},{28,40},{36,48},{40,52},{44,... | collective-permute-start | bytes 3538952 | tf_op jit(solution)/shard_map/ppermute | solution.py:21
  10.7 81.1 %collective-permute-start.3 = (bf16[2,384,768]{2,1,0:T(8,128)(2,1)}, bf16[2,384,768]{2,1,0:T(8,128)(2,1)}, u32[]{:S(2)}, u32[]{:S(2)}) collective-permute-start(bf16[2,384,768]{2,1,0:T(8,128)(2,1)} %pad_maximum_fusion), channel_id=1, source_target_pairs={{0,4},{4,8},{8,12},{16,20},{20,24},{24,28},{32,36},{36,40},{40,44}... | collective-permute-start | bytes 3538952 | tf_op jit(solution)/shard_map/ppermute | solution.py:21
  13.2 82.1 %collective-permute-start.4 = (bf16[2,384,768]{2,1,0:T(8,128)(2,1)}, bf16[2,384,768]{2,1,0:T(8,128)(2,1)}, u32[]{:S(2)}, u32[]{:S(2)}) collective-permute-start(bf16[2,384,768]{2,1,0:T(8,128)(2,1)} %pad_maximum_fusion), channel_id=1, source_target_pairs={{4,0},{8,4},{12,8},{20,16},{24,20},{28,24},{36,32},{40,36},{44,40}... | collective-permute-start | bytes 3538952 | tf_op jit(solution)/shard_map/ppermute | solution.py:21
  35.3 62.4 %collective-permute-start.5 = (bf16[2,384,768]{2,1,0:T(8,128)(2,1)}, bf16[2,384,768]{2,1,0:T(8,128)(2,1)S(1)}, u32[]{:S(2)}, u32[]{:S(2)}) collective-permute-start(bf16[2,384,768]{2,1,0:T(8,128)(2,1)} %pad_maximum_fusion), channel_id=1, source_target_pairs={{16,4},{20,8},{24,12},{32,20},{36,24},{40,28},{48,36},{52,40},{56,... | collective-permute-start | bytes 3538952 | tf_op jit(solution)/shard_map/ppermute | solution.py:21
  60.3 38.5 %collective-permute-start.6 = (bf16[2,384,768]{2,1,0:T(8,128)(2,1)}, bf16[2,384,768]{2,1,0:T(8,128)(2,1)S(1)}, u32[]{:S(2)}, u32[]{:S(2)}) collective-permute-start(bf16[2,384,768]{2,1,0:T(8,128)(2,1)} %pad_maximum_fusion), channel_id=1, source_target_pairs={{16,0},{20,4},{24,8},{28,12},{32,16},{36,20},{40,24},{44,28},{48,3... | collective-permute-start | bytes 3538952 | tf_op jit(solution)/shard_map/ppermute | solution.py:21
  70.8 23.3 %copy-start.5 = (bf16[1,1,384,768]{3,2,1,0:T(8,128)(2,1)S(1)}, bf16[1,1,384,768]{3,2,1,0:T(8,128)(2,1)}, u32[]{:S(2)}) copy-start(bf16[1,1,384,768]{3,2,1,0:T(8,128)(2,1)} %param.10) | copy-start | bytes 1769476
  70.8 23.3 %copy-start.6 = (bf16[1,1,384,768]{3,2,1,0:T(8,128)(2,1)S(1)}, bf16[1,1,384,768]{3,2,1,0:T(8,128)(2,1)}, u32[]{:S(2)}) copy-start(bf16[1,1,384,768]{3,2,1,0:T(8,128)(2,1)} %param.9) | copy-start | bytes 1769476
  83.1 33.2 %collective-permute-start.7 = (bf16[2,384,768]{2,1,0:T(8,128)(2,1)}, bf16[2,384,768]{2,1,0:T(8,128)(2,1)S(1)}, u32[]{:S(2)}, u32[]{:S(2)}) collective-permute-start(bf16[2,384,768]{2,1,0:T(8,128)(2,1)} %pad_maximum_fusion), channel_id=1, source_target_pairs={{20,0},{24,4},{28,8},{36,16},{40,20},{44,24},{52,32},{56,36},{60,4... | collective-permute-start | bytes 3538952 | tf_op jit(solution)/shard_map/ppermute | solution.py:21
  267.2 4.8 collective-permute-start.16
  279.2 348.5 %all-to-all-start = ((bf16[64,48,384]{2,1,0:T(8,128)(2,1)}), bf16[64,48,384]{2,1,0:T(8,128)(2,1)}, u32[]{:S(2)}, u32[]{:S(2)}) async-start(bf16[64,48,384]{2,1,0:T(8,128)(2,1)} %bitcast.154), calls=%async_computation | async-start | bytes 4718592 | tf_op jit(solution)/shard_map/all_to_all | solution.py:146
  398.1 50.8 %collective-permute-start.8 = (bf16[2,384,768]{2,1,0:T(8,128)(2,1)S(1)}, bf16[2,384,768]{2,1,0:T(8,128)(2,1)}, u32[]{:S(2)}, u32[]{:S(2)}) collective-permute-start(bf16[2,384,768]{2,1,0:T(8,128)(2,1)S(1)} %maximum_select_fusion.1), channel_id=1, source_target_pairs={{20,0},{24,4},{28,8},{36,16},{40,20},{44,24},{52,32},{56,36},{60,4... | collective-permute-start | bytes 3538952 | tf_op jit(solution)/shard_map/ppermute | solution.py:21
  401.3 72.8 %collective-permute-start.9 = (bf16[2,384,768]{2,1,0:T(8,128)(2,1)S(1)}, bf16[2,384,768]{2,1,0:T(8,128)(2,1)}, u32[]{:S(2)}, u32[]{:S(2)}) collective-permute-start(bf16[2,384,768]{2,1,0:T(8,128)(2,1)S(1)} %maximum_select_fusion.2), channel_id=1, source_target_pairs={{16,0},{20,4},{24,8},{28,12},{32,16},{36,20},{40,24},{44,28},{48,3... | collective-permute-start | bytes 3538952 | tf_op jit(solution)/shard_map/ppermute | solution.py:21
  404.5 93.8 %collective-permute-start.10 = (bf16[2,384,768]{2,1,0:T(8,128)(2,1)S(1)}, bf16[2,384,768]{2,1,0:T(8,128)(2,1)}, u32[]{:S(2)}, u32[]{:S(2)}) collective-permute-start(bf16[2,384,768]{2,1,0:T(8,128)(2,1)S(1)} %maximum_select_fusion.3), channel_id=1, source_target_pairs={{16,4},{20,8},{24,12},{32,20},{36,24},{40,28},{48,36},{52,40},{56,... | collective-permute-start | bytes 3538952 | tf_op jit(solution)/shard_map/ppermute | solution.py:21
  413.6 86.6 %collective-permute-start.11 = (bf16[2,384,768]{2,1,0:T(8,128)(2,1)}, bf16[2,384,768]{2,1,0:T(8,128)(2,1)S(1)}, u32[]{:S(2)}, u32[]{:S(2)}) collective-permute-start(bf16[2,384,768]{2,1,0:T(8,128)(2,1)} %maximum_select_fusion.4), channel_id=1, source_target_pairs={{4,0},{8,4},{12,8},{20,16},{24,20},{28,24},{36,32},{40,36},{44,40}... | collective-permute-start | bytes 3538952 | tf_op jit(solution)/shard_map/ppermute | solution.py:21
  417.3 83.0 %collective-permute-start.12 = (bf16[2,384,768]{2,1,0:T(8,128)(2,1)}, bf16[2,384,768]{2,1,0:T(8,128)(2,1)}, u32[]{:S(2)}, u32[]{:S(2)}) collective-permute-start(bf16[2,384,768]{2,1,0:T(8,128)(2,1)} %maximum_select_fusion.5), channel_id=1, source_target_pairs={{0,4},{4,8},{8,12},{16,20},{20,24},{24,28},{32,36},{36,40},{40,44}... | collective-permute-start | bytes 3538952 | tf_op jit(solution)/shard_map/ppermute | solution.py:21
  448.8 69.0 %collective-permute-start.13 = (bf16[2,384,768]{2,1,0:T(8,128)(2,1)}, bf16[2,384,768]{2,1,0:T(8,128)(2,1)}, u32[]{:S(2)}, u32[]{:S(2)}) collective-permute-start(bf16[2,384,768]{2,1,0:T(8,128)(2,1)} %maximum_select_fusion.6), channel_id=1, source_target_pairs={{4,16},{8,20},{12,24},{20,32},{24,36},{28,40},{36,48},{40,52},{44,... | collective-permute-start | bytes 3538952 | tf_op jit(solution)/shard_map/ppermute | solution.py:21
  474.1 78.3 %collective-permute-start.14 = (bf16[2,384,768]{2,1,0:T(8,128)(2,1)}, bf16[2,384,768]{2,1,0:T(8,128)(2,1)}, u32[]{:S(2)}, u32[]{:S(2)}) collective-permute-start(bf16[2,384,768]{2,1,0:T(8,128)(2,1)} %maximum_select_fusion.7), channel_id=1, source_target_pairs={{0,16},{4,20},{8,24},{12,28},{16,32},{20,36},{24,40},{28,44},{32,4... | collective-permute-start | bytes 3538952 | tf_op jit(solution)/shard_map/ppermute | solution.py:21
  498.3 123.2 %collective-permute-start.15 = (bf16[2,384,768]{2,1,0:T(8,128)(2,1)}, bf16[2,384,768]{2,1,0:T(8,128)(2,1)}, u32[]{:S(2)}, u32[]{:S(2)}) collective-permute-start(bf16[2,384,768]{2,1,0:T(8,128)(2,1)} %maximum_select_fusion.8), channel_id=1, source_target_pairs={{0,20},{4,24},{8,28},{16,36},{20,40},{24,44},{32,52},{36,56},{40,6... | collective-permute-start | bytes 3538952 | tf_op jit(solution)/shard_map/ppermute | solution.py:21
  500.3 121.3 %copy-start.7 = (bf16[2,384,768]{2,1,0:T(8,128)(2,1)}, bf16[2,384,768]{2,1,0:T(8,128)(2,1)S(1)}, u32[]{:S(2)}) copy-start(bf16[2,384,768]{2,1,0:T(8,128)(2,1)S(1)} %collective-permute-done.11) | copy-start | bytes 3538948
  633.0 8.1 %collective-permute-start.17 = (f32[48,192]{1,0:T(8,128)S(1)}, f32[48,192]{1,0:T(8,128)S(1)}, u32[]{:S(2)}, u32[]{:S(2)}) collective-permute-start(f32[48,192]{1,0:T(8,128)S(1)} %bitcast.164), channel_id=1, source_target_pairs={{0,2},{1,3},{2,0},{3,1},{4,6},{5,7},{6,4},{7,5},{8,10},{9,11},{10,... | collective-permute-start | bytes 110600 | tf_op jit(solution)/shard_map/ppermute | solution.py:154
  (24 other events, 78.4 us)

commit v3 on v2

--- a/solution.py
+++ b/solution.py
@@ -1,8 +1,10 @@
+import functools
 import math
 
 import jax
 import jax.numpy as jnp
 from jax import lax
+from jax.experimental import pallas as pl
 from jax.sharding import PartitionSpec as P
 
 HEAD = 128
@@ -19,6 +21,31 @@
         if 0 <= time_row + time_step < time_tiles and 0 <= height_col + height_step < height_tiles:
             pairs.append((tile, tile + offset) if toward else (tile + offset, tile))
     return lax.ppermute(value, axis, pairs)
+
+
+def tile_attention(mask_ref, query_ref, key_ref, value_ref, grad_ref, attn_ref, dq_ref, dk_ref, dv_ref, *, score_scale):
+    rows_by_rows = (((1,), (1,)), ((), ()))
+    cols_by_cols = (((0,), (0,)), ((), ()))
+    query = query_ref[...]
+    key = key_ref[...]
+    value = value_ref[...]
+    grad = grad_ref[...]
+    scores = lax.dot_general(query, key, rows_by_rows, preferred_element_type=jnp.float32) * score_scale
+    scores = jnp.where(mask_ref[...] > 0, scores, -1e30)
+    row_peak = jnp.max(scores, axis=1, keepdims=True)
+    exp_scores = jnp.exp(scores - row_peak)
+    probs = exp_scores / jnp.sum(exp_scores, axis=1, keepdims=True)
+    probs_low = probs.astype(jnp.bfloat16)
+    attn = jnp.dot(probs_low, value, preferred_element_type=jnp.float32).astype(jnp.bfloat16)
+    attn_ref[...] = attn
+    row_delta = jnp.sum(grad.astype(jnp.float32) * attn.astype(jnp.float32), axis=1, keepdims=True)
+    dprobs = lax.dot_general(grad, value, rows_by_rows, preferred_element_type=jnp.float32)
+    dscores = (probs * (dprobs - row_delta)).astype(jnp.bfloat16)
+    dq_ref[...] = (jnp.dot(dscores, key, preferred_element_type=jnp.float32) * score_scale).astype(jnp.bfloat16)
+    dk_ref[...] = (
+        lax.dot_general(dscores, query, cols_by_cols, preferred_element_type=jnp.float32) * score_scale
+    ).astype(jnp.bfloat16)
+    dv_ref[...] = lax.dot_general(probs_low, grad, cols_by_cols, preferred_element_type=jnp.float32).astype(jnp.bfloat16)
 
 
 def body(queries, keys, values, tile_lists, grad_out, w_out):
@@ -52,80 +79,34 @@
     grad_attn = lax.dot_general(
         grad_tile, w_out, (((1,), (1,)), ((), ())), preferred_element_type=jnp.float32
     ).astype(jnp.bfloat16)
-    block_width = 128
-    heads_block = block_width // HEAD
-
-    def head_block(block_index, carry):
-        attn_all, grad_query, grad_key, grad_value = carry
-        block_start = block_index * block_width
-        query_part = lax.dynamic_slice_in_dim(query_tile, block_start, block_width, 1).reshape(
-            tile_tok, heads_block, HEAD
-        )
-        key_part = lax.dynamic_slice_in_dim(key_rows, block_start, block_width, 1).reshape(
-            -1, heads_block, HEAD
-        )
-        value_part = lax.dynamic_slice_in_dim(value_rows, block_start, block_width, 1).reshape(
-            -1, heads_block, HEAD
-        )
-        grad_part = lax.dynamic_slice_in_dim(grad_attn, block_start, block_width, 1).reshape(
-            tile_tok, heads_block, HEAD
-        )
-        scores = (
-            jnp.einsum("qhd,khd->hqk", query_part, key_part, preferred_element_type=jnp.float32)
-            * score_scale
-        )
-        scores = jnp.where(key_mask[None, None, :], scores, -1e30)
-        row_peak = jnp.max(scores, axis=2, keepdims=True)
-        exp_scores = jnp.exp(scores - row_peak)
-        attn_probs = exp_scores / jnp.sum(exp_scores, axis=2, keepdims=True)
-        probs_low = attn_probs.astype(jnp.bfloat16)
-        attn_part = jnp.einsum(
-            "hqk,khd->qhd", probs_low, value_part, preferred_element_type=jnp.float32
-        ).astype(jnp.bfloat16)
-        row_delta = jnp.einsum(
-            "qhd,qhd->hq", grad_part.astype(jnp.float32), attn_part.astype(jnp.float32)
-        )
-        dprobs = jnp.einsum(
-            "qhd,khd->hqk", grad_part, value_part, preferred_element_type=jnp.float32
-        )
-        dscores = (attn_probs * (dprobs - row_delta[:, :, None])).astype(jnp.bfloat16)
-        query_grad = (
-            jnp.einsum("hqk,khd->qhd", dscores, key_part, preferred_element_type=jnp.float32)
-            * score_scale
-        )
-        key_grad = (
-            jnp.einsum("hqk,qhd->khd", dscores, query_part, preferred_element_type=jnp.float32)
-            * score_scale
-        )
-        value_grad = jnp.einsum(
-            "hqk,qhd->khd", probs_low, grad_part, preferred_element_type=jnp.float32
-        )
-        attn_all = lax.dynamic_update_slice_in_dim(
-            attn_all, attn_part.reshape(tile_tok, block_width), block_start, 1
-        )
-        grad_query = lax.dynamic_update_slice_in_dim(
-            grad_query,
-            query_grad.astype(jnp.bfloat16).reshape(tile_tok, block_width),
-            block_start,
-            1,
-        )
-        grad_key = lax.dynamic_update_slice_in_dim(
-            grad_key, key_grad.astype(jnp.bfloat16).reshape(-1, block_width), block_start, 1
-        )
-        grad_value = lax.dynamic_update_slice_in_dim(
-            grad_value, value_grad.astype(jnp.bfloat16).reshape(-1, block_width), block_start, 1
-        )
-        return (attn_all, grad_query, grad_key, grad_value)
-
-    start_state = (
-        jnp.zeros((tile_tok, inner_width), jnp.bfloat16),
-        jnp.zeros((tile_tok, inner_width), jnp.bfloat16),
-        jnp.zeros((slot_count * tile_tok, inner_width), jnp.bfloat16),
-        jnp.zeros((slot_count * tile_tok, inner_width), jnp.bfloat16),
-    )
-    attn_all, grad_query, grad_key, grad_value = lax.fori_loop(
-        0, inner_width // block_width, head_block, start_state
-    )
+    key_count = slot_count * tile_tok
+    mask_row = key_mask.astype(jnp.int32).reshape(1, key_count)
+    head_count = inner_width // HEAD
+    tile_spec = pl.BlockSpec((tile_tok, HEAD), lambda head: (0, head))
+    key_spec = pl.BlockSpec((key_count, HEAD), lambda head: (0, head))
+    attn_all, grad_query, grad_key, grad_value = pl.pallas_call(
+        functools.partial(tile_attention, score_scale=score_scale),
+        grid=(head_count,),
+        in_specs=[
+            pl.BlockSpec((1, key_count), lambda head: (0, 0)),
+            tile_spec,
+            key_spec,
+            key_spec,
+            tile_spec,
+        ],
+        out_specs=[tile_spec, tile_spec, key_spec, key_spec],
+        out_shape=[
+            jax.ShapeDtypeStruct((tile_tok, inner_width), jnp.bfloat16),
+            jax.ShapeDtypeStruct((tile_tok, inner_width), jnp.bfloat16),
+            jax.ShapeDtypeStruct((key_count, inner_width), jnp.bfloat16),
+            jax.ShapeDtypeStruct((key_count, inner_width), jnp.bfloat16),
+        ],
+        cost_estimate=pl.CostEstimate(
+            flops=2 * 5 * tile_tok * key_count * inner_width,
+            transcendentals=head_count * tile_tok * key_count,
+            bytes_accessed=2 * 2 * (2 * tile_tok + 2 * key_count) * inner_width,
+        ),
+    )(mask_row, query_tile, key_rows, value_rows, grad_attn)
     dp_count = lax.axis_size("dp")
     sp_count = lax.axis_size("sp")
     dp_index = lax.axis_index("dp")

time: 645 us -> 530 us (0.82)
  the two profiles are of different devices: /device:TPU:220 before, /device:TPU:212 now
where the time goes in v3:
time: 530 us; the launch traced here: 528 us
  waiting for transfers between devices  318 us (60%)
  starting transfers between devices  91.6 us (17%)
  local copies, waits for them, and re-layouts  42.6 us (8%)
  other arithmetic  26 us (5%)
  Pallas kernels  23.2 us (4%)
  between operations  17.7 us (3%)
  matrix products  9.5 us (2%)
    ppermute x16, waiting for transfers between devices, neighbour_shift(): return lax.ppermute(value, axis, pairs)  306 us
    ppermute x16, starting transfers between devices, neighbour_shift(): return lax.ppermute(value, axis, pairs)  59.1 us
    all_to_all x1, starting transfers between devices, body(): lax.all_to_all(core_sum.reshape(sp_count, col_block, -1), 'sp', 0, 0, til...  32.1 us
    pallas_call x1, Pallas kernels, body(): pl.pallas_call(functools.partial(tile_attention, score_scale=score_scale)...  23.2 us
    unnamed x24, local copies, waits for them, and re-layouts  15 us
    select_n x8, other arithmetic, slot_payload(): return jnp.where(match_any[slot_number], payload, jnp.zeros_like(payload))  11.1 us
  transfers between devices with their start and end apart: 19, of which 11 were waited for; matrix products, arithmetic and copies ran while one was open for 9% of the time, Pallas kernels for 0%

profile of v3, /device:TPU:212, one launch (start us, length us, event | category | flops | bytes accessed | tf_op | source)
XLA Modules:
  0.0 528.3 jit_solution(9799762654189487385)
XLA Ops:
  5.7 4.5 collective-permute-start.1
  13.5 4.1 collective-permute-start.3
  19.5 5.2 fusion.6.grad_ref
  26.0 8.0 %collective-permute-done = bf16[2,384,768]{2,1,0:T(8,128)(2,1)} collective-permute-done((bf16[2,384,768]{2,1,0:T(8,128)(2,1)S(1)}, bf16[2,384,768]{2,1,0:T(8,128)(2,1)}, u32[]{:S(2)}, u32[]{:S(2)}) %collective-permute-start) | collective-permute-done | bytes 1179680 | tf_op jit(solution)/shard_map/ppermute | solution.py:23
  39.9 19.1 %collective-permute-done.1 = bf16[2,384,768]{2,1,0:T(8,128)(2,1)} collective-permute-done((bf16[2,384,768]{2,1,0:T(8,128)(2,1)S(1)}, bf16[2,384,768]{2,1,0:T(8,128)(2,1)}, u32[]{:S(2)}, u32[]{:S(2)}) %collective-permute-start.1) | collective-permute-done | bytes 1179680 | tf_op jit(solution)/shard_map/ppermute | solution.py:23
  59.0 8.2 %collective-permute-start.6 = (bf16[2,384,768]{2,1,0:T(8,128)(2,1)S(1)}, bf16[2,384,768]{2,1,0:T(8,128)(2,1)S(1)}, u32[]{:S(2)}, u32[]{:S(2)}) collective-permute-start(bf16[2,384,768]{2,1,0:T(8,128)(2,1)S(1)} %pad_maximum_fusion), channel_id=1, source_target_pairs={{16,0},{20,4},{24,8},{28,12},{32,16},{36,20},{40,24},{44,28},{48,3... | collective-permute-start | bytes 3538952 | tf_op jit(solution)/shard_map/ppermute | solution.py:23
  69.5 12.1 %collective-permute-done.2 = bf16[2,384,768]{2,1,0:T(8,128)(2,1)} collective-permute-done((bf16[2,384,768]{2,1,0:T(8,128)(2,1)S(1)}, bf16[2,384,768]{2,1,0:T(8,128)(2,1)}, u32[]{:S(2)}, u32[]{:S(2)}) %collective-permute-start.2) | collective-permute-done | bytes 1179680 | tf_op jit(solution)/shard_map/ppermute | solution.py:23
  81.7 6.4 %collective-permute-start.7 = (bf16[2,384,768]{2,1,0:T(8,128)(2,1)S(1)}, bf16[2,384,768]{2,1,0:T(8,128)(2,1)S(1)}, u32[]{:S(2)}, u32[]{:S(2)}) collective-permute-start(bf16[2,384,768]{2,1,0:T(8,128)(2,1)S(1)} %pad_maximum_fusion), channel_id=1, source_target_pairs={{20,0},{24,4},{28,8},{36,16},{40,20},{44,24},{52,32},{56,36},{60,4... | collective-permute-start | bytes 3538952 | tf_op jit(solution)/shard_map/ppermute | solution.py:23
  96.4 14.9 %collective-permute-done.5 = bf16[2,384,768]{2,1,0:T(8,128)(2,1)S(1)} collective-permute-done((bf16[2,384,768]{2,1,0:T(8,128)(2,1)S(1)}, bf16[2,384,768]{2,1,0:T(8,128)(2,1)S(1)}, u32[]{:S(2)}, u32[]{:S(2)}) %collective-permute-start.5) | collective-permute-done | bytes 1179680 | tf_op jit(solution)/shard_map/ppermute | solution.py:23
  112.5 62.2 %collective-permute-done.6 = bf16[2,384,768]{2,1,0:T(8,128)(2,1)S(1)} collective-permute-done((bf16[2,384,768]{2,1,0:T(8,128)(2,1)S(1)}, bf16[2,384,768]{2,1,0:T(8,128)(2,1)S(1)}, u32[]{:S(2)}, u32[]{:S(2)}) %collective-permute-start.6) | collective-permute-done | bytes 1179680 | tf_op jit(solution)/shard_map/ppermute | solution.py:23
  177.0 8.1 %gather_fusion = bf16[5,2,384,768]{3,2,1,0:T(8,128)(2,1)} fusion(bf16[9,2,384,768]{3,2,1,0:T(8,128)(2,1)} %bitcast_dynamic-update-slice_fusion, s32[1024]{0:T(1024)S(1)} %pad_clamp_fusion), kind=kCustom, calls=%fused_computation | custom fusion | bytes 11796500 | tf_op jit(solution)/shard_map/jit(_take)/gather | solution.py:75
  191.2 23.2 %shard_map.93 = (bf16[384,768]{1,0:T(8,128)(2,1)}, bf16[384,768]{1,0:T(8,128)(2,1)}, bf16[1920,768]{1,0:T(8,128)(2,1)}, bf16[1920,768]{1,0:T(8,128)(2,1)}) custom-call(s32[1,1920]{1,0:T(1,128)} %bitcast.133, bf16[384,768]{1,0:T(8,128)(2,1)} %bitcast.134, bf16[1920,768]{1,0:T(8,128)(2,1)} %bitcast.124, bf16[1920,768]{1,0:T(8,128)(2,1)} %bitcast.123, ...), custom_call_target="tpu_custom_call" | custom-call | flops 5662310400 | bytes 14155776 | tf_op jit(solution)/shard_map/pallas_call | solution.py:87
  217.6 4.5 collective-permute-done.16
  225.0 4.3 copy.13
  229.3 32.1 %all-to-all-start = ((bf16[64,48,384]{2,1,0:T(8,128)(2,1)}), bf16[64,48,384]{2,1,0:T(8,128)(2,1)S(1)}, u32[]{:S(2)}, u32[]{:S(2)}) async-start(bf16[64,48,384]{2,1,0:T(8,128)(2,1)} %bitcast.122), calls=%async_computation | async-start | bytes 4718592 | tf_op jit(solution)/shard_map/all_to_all | solution.py:127
  280.2 6.2 %constant_dynamic-slice_fusion.20 = (bf16[1,384,768]{2,1,0:T(8,128)(2,1)}, bf16[1,384,768]{2,1,0:T(8,128)(2,1)S(1)}, bf16[1,384,768]{2,1,0:T(8,128)(2,1)S(1)}, b...) fusion(bf16[5,384,768]{2,1,0:T(8,128)(2,1)} %bitcast.121, ...), kind=kLoop, calls=%fused_computation.58 | loop fusion | bytes 21233700 | tf_op jit(solution)/shard_map/jit(dynamic_index_in_dim)/dynamic_slice | solution.py:148
  293.6 7.1 %collective-permute-start.10 = (bf16[2,384,768]{2,1,0:T(8,128)(2,1)S(1)}, bf16[2,384,768]{2,1,0:T(8,128)(2,1)}, u32[]{:S(2)}, u32[]{:S(2)}) collective-permute-start(bf16[2,384,768]{2,1,0:T(8,128)(2,1)S(1)} %maximum_select_fusion.3), channel_id=1, source_target_pairs={{16,4},{20,8},{24,12},{32,20},{36,24},{40,28},{48,36},{52,40},{56,... | collective-permute-start | bytes 3538952 | tf_op jit(solution)/shard_map/ppermute | solution.py:23
  306.3 4.0 collective-permute-start.12
  315.6 22.7 %collective-permute-done.8 = bf16[2,384,768]{2,1,0:T(8,128)(2,1)} collective-permute-done((bf16[2,384,768]{2,1,0:T(8,128)(2,1)S(1)}, bf16[2,384,768]{2,1,0:T(8,128)(2,1)}, u32[]{:S(2)}, u32[]{:S(2)}) %collective-permute-start.8) | collective-permute-done | bytes 1179680 | tf_op jit(solution)/shard_map/ppermute | solution.py:23
  340.2 23.4 %collective-permute-done.9 = bf16[2,384,768]{2,1,0:T(8,128)(2,1)} collective-permute-done((bf16[2,384,768]{2,1,0:T(8,128)(2,1)S(1)}, bf16[2,384,768]{2,1,0:T(8,128)(2,1)}, u32[]{:S(2)}, u32[]{:S(2)}) %collective-permute-start.9) | collective-permute-done | bytes 1179680 | tf_op jit(solution)/shard_map/ppermute | solution.py:23
  365.4 98.2 %collective-permute-done.10 = bf16[2,384,768]{2,1,0:T(8,128)(2,1)} collective-permute-done((bf16[2,384,768]{2,1,0:T(8,128)(2,1)S(1)}, bf16[2,384,768]{2,1,0:T(8,128)(2,1)}, u32[]{:S(2)}, u32[]{:S(2)}) %collective-permute-start.10) | collective-permute-done | bytes 1179680 | tf_op jit(solution)/shard_map/ppermute | solution.py:23
  465.6 45.8 %collective-permute-done.15 = bf16[2,384,768]{2,1,0:T(8,128)(2,1)} collective-permute-done((bf16[2,384,768]{2,1,0:T(8,128)(2,1)}, bf16[2,384,768]{2,1,0:T(8,128)(2,1)}, u32[]{:S(2)}, u32[]{:S(2)}) %collective-permute-start.15) | collective-permute-done | bytes 1179680 | tf_op jit(solution)/shard_map/ppermute | solution.py:23
  511.4 6.1 %add_convert_fusion = bf16[2,384,768]{2,1,0:T(8,128)(2,1)S(1)} fusion(bf16[2,384,768]{2,1,0:T(8,128)(2,1)} %collective-permute-done.15, bf16[2,384,768]{2,1,0:T(8,128)(2,1)} %collective-permute-done.14, bf16[2,384,768]{2,1,0:T(8,128)(2,1)} %collective-permute-done.13, bf16[2,384,768]{2,1,0:T(8,128)(2,1)} %collective-permute-done.12, ...), kind=kLoop, calls=%fused_computation.11 | loop fusion | flops 11796480 | bytes 11796481 | tf_op jit(solution)/shard_map/convert_element_type | solution.py:162
  520.7 6.9 %collective-permute-done.17 = f32[48,192]{1,0:T(8,128)S(1)} collective-permute-done((f32[48,192]{1,0:T(8,128)S(1)}, f32[48,192]{1,0:T(8,128)S(1)}, u32[]{:S(2)}, u32[]{:S(2)}) %collective-permute-start.17) | collective-permute-done | bytes 36896 | tf_op jit(solution)/shard_map/ppermute | solution.py:135
  (73 shorter events, 73.4 us)
Async XLA Ops:
  0.6 18.9 %copy-start = (bf16[1,1,384,3072]{3,2,1,0:T(8,128)(2,1)S(1)}, bf16[1,1,384,3072]{3,2,1,0:T(8,128)(2,1)}, u32[]{:S(2)}) copy-start(bf16[1,1,384,3072]{3,2,1,0:T(8,128)(2,1)} %param.10) | copy-start | bytes 7077892
  2.2 22.6 %copy-start.5 = (s32[1,5]{1,0:T(1,128)S(1)}, s32[1,5]{1,0:T(1,128)}, u32[]{:S(2)}) copy-start(s32[1,5]{1,0:T(1,128)} %param.9) | copy-start | bytes 64
  2.2 31.8 %collective-permute-start = (bf16[2,384,768]{2,1,0:T(8,128)(2,1)S(1)}, bf16[2,384,768]{2,1,0:T(8,128)(2,1)}, u32[]{:S(2)}, u32[]{:S(2)}) collective-permute-start(bf16[2,384,768]{2,1,0:T(8,128)(2,1)S(1)} %pad_maximum_fusion), channel_id=1, source_target_pairs={{0,20},{4,24},{8,28},{16,36},{20,40},{24,44},{32,52},{36,56},{40,6... | collective-permute-start | bytes 3538952 | tf_op jit(solution)/shard_map/ppermute | solution.py:23
  5.7 53.2 %collective-permute-start.1 = (bf16[2,384,768]{2,1,0:T(8,128)(2,1)S(1)}, bf16[2,384,768]{2,1,0:T(8,128)(2,1)}, u32[]{:S(2)}, u32[]{:S(2)}) collective-permute-start(bf16[2,384,768]{2,1,0:T(8,128)(2,1)S(1)} %pad_maximum_fusion), channel_id=1, source_target_pairs={{0,16},{4,20},{8,24},{12,28},{16,32},{20,36},{24,40},{28,44},{32,4... | collective-permute-start | bytes 3538952 | tf_op jit(solution)/shard_map/ppermute | solution.py:23
  10.3 71.4 %collective-permute-start.2 = (bf16[2,384,768]{2,1,0:T(8,128)(2,1)S(1)}, bf16[2,384,768]{2,1,0:T(8,128)(2,1)}, u32[]{:S(2)}, u32[]{:S(2)}) collective-permute-start(bf16[2,384,768]{2,1,0:T(8,128)(2,1)S(1)} %pad_maximum_fusion), channel_id=1, source_target_pairs={{4,16},{8,20},{12,24},{20,32},{24,36},{28,40},{36,48},{40,52},{44,... | collective-permute-start | bytes 3538952 | tf_op jit(solution)/shard_map/ppermute | solution.py:23
  13.5 77.0 %collective-permute-start.3 = (bf16[2,384,768]{2,1,0:T(8,128)(2,1)S(1)}, bf16[2,384,768]{2,1,0:T(8,128)(2,1)}, u32[]{:S(2)}, u32[]{:S(2)}) collective-permute-start(bf16[2,384,768]{2,1,0:T(8,128)(2,1)S(1)} %pad_maximum_fusion), channel_id=1, source_target_pairs={{0,4},{4,8},{8,12},{16,20},{20,24},{24,28},{32,36},{36,40},{40,44}... | collective-permute-start | bytes 3538952 | tf_op jit(solution)/shard_map/ppermute | solution.py:23
  17.6 76.5 %collective-permute-start.4 = (bf16[2,384,768]{2,1,0:T(8,128)(2,1)S(1)}, bf16[2,384,768]{2,1,0:T(8,128)(2,1)}, u32[]{:S(2)}, u32[]{:S(2)}) collective-permute-start(bf16[2,384,768]{2,1,0:T(8,128)(2,1)S(1)} %pad_maximum_fusion), channel_id=1, source_target_pairs={{4,0},{8,4},{12,8},{20,16},{24,20},{28,24},{36,32},{40,36},{44,40}... | collective-permute-start | bytes 3538952 | tf_op jit(solution)/shard_map/ppermute | solution.py:23
  34.0 77.4 %collective-permute-start.5 = (bf16[2,384,768]{2,1,0:T(8,128)(2,1)S(1)}, bf16[2,384,768]{2,1,0:T(8,128)(2,1)S(1)}, u32[]{:S(2)}, u32[]{:S(2)}) collective-permute-start(bf16[2,384,768]{2,1,0:T(8,128)(2,1)S(1)} %pad_maximum_fusion), channel_id=1, source_target_pairs={{16,4},{20,8},{24,12},{32,20},{36,24},{40,28},{48,36},{52,40},{56,... | collective-permute-start | bytes 3538952 | tf_op jit(solution)/shard_map/ppermute | solution.py:23
  59.0 115.7 %collective-permute-start.6 = (bf16[2,384,768]{2,1,0:T(8,128)(2,1)S(1)}, bf16[2,384,768]{2,1,0:T(8,128)(2,1)S(1)}, u32[]{:S(2)}, u32[]{:S(2)}) collective-permute-start(bf16[2,384,768]{2,1,0:T(8,128)(2,1)S(1)} %pad_maximum_fusion), channel_id=1, source_target_pairs={{16,0},{20,4},{24,8},{28,12},{32,16},{36,20},{40,24},{44,28},{48,3... | collective-permute-start | bytes 3538952 | tf_op jit(solution)/shard_map/ppermute | solution.py:23
  81.7 94.2 %collective-permute-start.7 = (bf16[2,384,768]{2,1,0:T(8,128)(2,1)S(1)}, bf16[2,384,768]{2,1,0:T(8,128)(2,1)S(1)}, u32[]{:S(2)}, u32[]{:S(2)}) collective-permute-start(bf16[2,384,768]{2,1,0:T(8,128)(2,1)S(1)} %pad_maximum_fusion), channel_id=1, source_target_pairs={{20,0},{24,4},{28,8},{36,16},{40,20},{44,24},{52,32},{56,36},{60,4... | collective-permute-start | bytes 3538952 | tf_op jit(solution)/shard_map/ppermute | solution.py:23
  217.3 4.8 collective-permute-start.16
  229.3 32.1 %copy-start.6 = (s32[5]{0:T(128)S(1)}, s32[5]{0:T(128)}, u32[]{:S(2)}) copy-start(s32[5]{0:T(128)} %get-tuple-element.63) | copy-start | bytes 64
  229.3 288.1 %all-to-all-start = ((bf16[64,48,384]{2,1,0:T(8,128)(2,1)}), bf16[64,48,384]{2,1,0:T(8,128)(2,1)S(1)}, u32[]{:S(2)}, u32[]{:S(2)}) async-start(bf16[64,48,384]{2,1,0:T(8,128)(2,1)} %bitcast.122), calls=%async_computation | async-start | bytes 4718592 | tf_op jit(solution)/shard_map/all_to_all | solution.py:127
  287.2 51.0 %collective-permute-start.8 = (bf16[2,384,768]{2,1,0:T(8,128)(2,1)S(1)}, bf16[2,384,768]{2,1,0:T(8,128)(2,1)}, u32[]{:S(2)}, u32[]{:S(2)}) collective-permute-start(bf16[2,384,768]{2,1,0:T(8,128)(2,1)S(1)} %maximum_select_fusion.1), channel_id=1, source_target_pairs={{20,0},{24,4},{28,8},{36,16},{40,20},{44,24},{52,32},{56,36},{60,4... | collective-permute-start | bytes 3538952 | tf_op jit(solution)/shard_map/ppermute | solution.py:23
  290.5 73.0 %collective-permute-start.9 = (bf16[2,384,768]{2,1,0:T(8,128)(2,1)S(1)}, bf16[2,384,768]{2,1,0:T(8,128)(2,1)}, u32[]{:S(2)}, u32[]{:S(2)}) collective-permute-start(bf16[2,384,768]{2,1,0:T(8,128)(2,1)S(1)} %maximum_select_fusion.2), channel_id=1, source_target_pairs={{16,0},{20,4},{24,8},{28,12},{32,16},{36,20},{40,24},{44,28},{48,3... | collective-permute-start | bytes 3538952 | tf_op jit(solution)/shard_map/ppermute | solution.py:23
  293.6 170.0 %collective-permute-start.10 = (bf16[2,384,768]{2,1,0:T(8,128)(2,1)S(1)}, bf16[2,384,768]{2,1,0:T(8,128)(2,1)}, u32[]{:S(2)}, u32[]{:S(2)}) collective-permute-start(bf16[2,384,768]{2,1,0:T(8,128)(2,1)S(1)} %maximum_select_fusion.3), channel_id=1, source_target_pairs={{16,4},{20,8},{24,12},{32,20},{36,24},{40,28},{48,36},{52,40},{56,... | collective-permute-start | bytes 3538952 | tf_op jit(solution)/shard_map/ppermute | solution.py:23
  302.6 163.0 %collective-permute-start.11 = (bf16[2,384,768]{2,1,0:T(8,128)(2,1)}, bf16[2,384,768]{2,1,0:T(8,128)(2,1)S(1)}, u32[]{:S(2)}, u32[]{:S(2)}) collective-permute-start(bf16[2,384,768]{2,1,0:T(8,128)(2,1)} %maximum_select_fusion.4), channel_id=1, source_target_pairs={{4,0},{8,4},{12,8},{20,16},{24,20},{28,24},{36,32},{40,36},{44,40}... | collective-permute-start | bytes 3538952 | tf_op jit(solution)/shard_map/ppermute | solution.py:23
  306.3 159.3 %collective-permute-start.12 = (bf16[2,384,768]{2,1,0:T(8,128)(2,1)}, bf16[2,384,768]{2,1,0:T(8,128)(2,1)}, u32[]{:S(2)}, u32[]{:S(2)}) collective-permute-start(bf16[2,384,768]{2,1,0:T(8,128)(2,1)} %maximum_select_fusion.5), channel_id=1, source_target_pairs={{0,4},{4,8},{8,12},{16,20},{20,24},{24,28},{32,36},{36,40},{40,44}... | collective-permute-start | bytes 3538952 | tf_op jit(solution)/shard_map/ppermute | solution.py:23
  338.2 127.3 %collective-permute-start.13 = (bf16[2,384,768]{2,1,0:T(8,128)(2,1)}, bf16[2,384,768]{2,1,0:T(8,128)(2,1)}, u32[]{:S(2)}, u32[]{:S(2)}) collective-permute-start(bf16[2,384,768]{2,1,0:T(8,128)(2,1)} %maximum_select_fusion.6), channel_id=1, source_target_pairs={{4,16},{8,20},{12,24},{20,32},{24,36},{28,40},{36,48},{40,52},{44,... | collective-permute-start | bytes 3538952 | tf_op jit(solution)/shard_map/ppermute | solution.py:23
  363.5 102.1 %collective-permute-start.14 = (bf16[2,384,768]{2,1,0:T(8,128)(2,1)}, bf16[2,384,768]{2,1,0:T(8,128)(2,1)}, u32[]{:S(2)}, u32[]{:S(2)}) collective-permute-start(bf16[2,384,768]{2,1,0:T(8,128)(2,1)} %maximum_select_fusion.7), channel_id=1, source_target_pairs={{0,16},{4,20},{8,24},{12,28},{16,32},{20,36},{24,40},{28,44},{32,4... | collective-permute-start | bytes 3538952 | tf_op jit(solution)/shard_map/ppermute | solution.py:23
  463.6 47.8 %collective-permute-start.15 = (bf16[2,384,768]{2,1,0:T(8,128)(2,1)}, bf16[2,384,768]{2,1,0:T(8,128)(2,1)}, u32[]{:S(2)}, u32[]{:S(2)}) collective-permute-start(bf16[2,384,768]{2,1,0:T(8,128)(2,1)} %maximum_select_fusion.8), channel_id=1, source_target_pairs={{0,20},{4,24},{8,28},{16,36},{20,40},{24,44},{32,52},{36,56},{40,6... | collective-permute-start | bytes 3538952 | tf_op jit(solution)/shard_map/ppermute | solution.py:23
  465.6 45.8 %copy-start.4 = (bf16[2,384,768]{2,1,0:T(8,128)(2,1)}, bf16[2,384,768]{2,1,0:T(8,128)(2,1)S(1)}, u32[]{:S(2)}) copy-start(bf16[2,384,768]{2,1,0:T(8,128)(2,1)S(1)} %collective-permute-done.11) | copy-start | bytes 3538948
  519.5 8.7 %copy-start.1 = (bf16[1,1,384,3072]{3,2,1,0:T(8,128)(2,1)S(1)}, bf16[1,1,384,3072]{3,2,1,0:T(8,128)(2,1)}, u32[]{:S(2)}) copy-start(bf16[1,1,384,3072]{3,2,1,0:T(8,128)(2,1)} %param.10) | copy-start | bytes 7077892
  519.6 8.1 %collective-permute-start.17 = (f32[48,192]{1,0:T(8,128)S(1)}, f32[48,192]{1,0:T(8,128)S(1)}, u32[]{:S(2)}, u32[]{:S(2)}) collective-permute-start(f32[48,192]{1,0:T(8,128)S(1)} %bitcast.132), channel_id=1, source_target_pairs={{0,2},{1,3},{2,0},{3,1},{4,6},{5,7},{6,4},{7,5},{8,10},{9,11},{10,... | collective-permute-start | bytes 110600 | tf_op jit(solution)/shard_map/ppermute | solution.py:135
  (2 other events, 5.0 us)

commit v4 on v3

--- a/solution.py
+++ b/solution.py
@@ -60,13 +60,24 @@
     score_scale = 1.0 / math.sqrt(HEAD)
     own_tile = lax.axis_index("sp")
     key_value = jnp.stack([key_tile, value_tile])
-    offsets = [(time_step, height_step) for time_step in (-1, 0, 1) for height_step in (-1, 0, 1)]
+    def shifted(value, time_step, height_step, toward):
+        return neighbour_shift(value, "sp", time_step, height_step, height_tiles, toward)
+
+    earlier = shifted(key_value, -1, 0, False)
+    later = shifted(key_value, 1, 0, False)
+    column = [earlier, key_value, later]
+    relayed = jnp.stack([earlier, later])
+    side_own = {step: shifted(key_value, 0, step, False) for step in (-1, 1)}
+    side_relayed = {step: shifted(relayed, 0, step, False) for step in (-1, 1)}
     pieces = []
-    for time_step, height_step in offsets:
-        if time_step == 0 and height_step == 0:
-            pieces.append(key_value)
-        else:
-            pieces.append(neighbour_shift(key_value, "sp", time_step, height_step, height_tiles, False))
+    for time_step in (-1, 0, 1):
+        for height_step in (-1, 0, 1):
+            if height_step == 0:
+                pieces.append(column[time_step + 1])
+            elif time_step == 0:
+                pieces.append(side_own[height_step])
+            else:
+                pieces.append(side_relayed[height_step][(time_step + 1) // 2])
     window = jnp.stack(pieces)
     valid_slot = listed >= 0
     time_gap = listed // height_tiles - own_tile // height_tiles
@@ -150,15 +161,23 @@
         )
         return jnp.where(match_any[slot_number], payload, jnp.zeros_like(payload))
 
-    grad_total = slot_payload(4).astype(jnp.float32)
-    for time_step, height_step in offsets:
-        if time_step == 0 and height_step == 0:
-            continue
-        slot_number = (time_step + 1) * 3 + height_step + 1
-        arrived = neighbour_shift(
-            slot_payload(slot_number), "sp", time_step, height_step, height_tiles, True
-        )
-        grad_total = grad_total + arrived.astype(jnp.float32)
+    from_side = {
+        step: shifted(
+            jnp.stack([slot_payload(time_step * 3 + step + 4) for time_step in (-1, 0, 1)]), 0, step, True
+        ).astype(jnp.float32)
+        for step in (-1, 1)
+    }
+    column_sums = [
+        slot_payload(time_step * 3 + 4).astype(jnp.float32)
+        + from_side[-1][time_step + 1]
+        + from_side[1][time_step + 1]
+        for time_step in (-1, 0, 1)
+    ]
+    grad_total = (
+        column_sums[1]
+        + shifted(column_sums[0].astype(jnp.bfloat16), -1, 0, True).astype(jnp.float32)
+        + shifted(column_sums[2].astype(jnp.bfloat16), 1, 0, True).astype(jnp.float32)
+    )
     grad_kv = grad_total.astype(jnp.bfloat16)
     return (grad_query[None, None], grad_kv[0][None, None], grad_kv[1][None, None], weight_grad)
 

time: 530 us -> 400 us (0.75)
  the two profiles are of different devices: /device:TPU:212 before, /device:TPU:24 now
where the time goes in v4:
time: 400 us; the launch traced here: 394 us
  waiting for transfers between devices  207 us (52%)
  starting transfers between devices  56.4 us (14%)
  local copies, waits for them, and re-layouts  43.2 us (11%)
  other arithmetic  35.9 us (9%)
  Pallas kernels  23.1 us (6%)
  between operations  18.1 us (5%)
  matrix products  10.8 us (3%)
    ppermute x10, waiting for transfers between devices, neighbour_shift(): return lax.ppermute(value, axis, pairs)  206 us
    ppermute x10, starting transfers between devices, neighbour_shift(): return lax.ppermute(value, axis, pairs)  38.3 us
    pallas_call x1, Pallas kernels, body(): pl.pallas_call(functools.partial(tile_attention, score_scale=score_scale)...  23.1 us
    unnamed x58, local copies, waits for them, and re-layouts  15 us
    all_to_all x1, starting transfers between devices, body(): lax.all_to_all(core_sum.reshape(sp_count, col_block, -1), 'sp', 0, 0, til...  11.5 us
  transfers between devices with their start and end apart: 13, of which 11 were waited for; matrix products, arithmetic and copies ran while one was open for 13% of the time, Pallas kernels for 0%

profile of v4, /device:TPU:24, one launch (start us, length us, event | category | flops | bytes accessed | tf_op | source)
XLA Modules:
  0.0 394.3 jit_solution(12268719090858468455)
XLA Ops:
  3.2 3.8 collective-permute-start
  7.0 4.8 %collective-permute-start.1 = (bf16[2,384,768]{2,1,0:T(8,128)(2,1)}, bf16[2,384,768]{2,1,0:T(8,128)(2,1)S(1)}, u32[]{:S(2)}, u32[]{:S(2)}) collective-permute-start(bf16[2,384,768]{2,1,0:T(8,128)(2,1)} %pad_maximum_fusion.3), channel_id=1, source_target_pairs={{16,0},{20,4},{24,8},{28,12},{32,16},{36,20},{40,24},{44,28},{48,3... | collective-permute-start | bytes 3538952 | tf_op jit(solution)/shard_map/ppermute | solution.py:23
  11.8 25.1 %collective-permute-done = bf16[2,384,768]{2,1,0:T(8,128)(2,1)S(1)} collective-permute-done((bf16[2,384,768]{2,1,0:T(8,128)(2,1)}, bf16[2,384,768]{2,1,0:T(8,128)(2,1)S(1)}, u32[]{:S(2)}, u32[]{:S(2)}) %collective-permute-start) | collective-permute-done | bytes 1179680 | tf_op jit(solution)/shard_map/ppermute | solution.py:23
  36.9 20.9 %collective-permute-done.1 = bf16[2,384,768]{2,1,0:T(8,128)(2,1)S(1)} collective-permute-done((bf16[2,384,768]{2,1,0:T(8,128)(2,1)}, bf16[2,384,768]{2,1,0:T(8,128)(2,1)S(1)}, u32[]{:S(2)}, u32[]{:S(2)}) %collective-permute-start.1) | collective-permute-done | bytes 1179680 | tf_op jit(solution)/shard_map/ppermute | solution.py:23
  59.4 4.8 %collective-permute-start.2 = (bf16[2,2,384,768]{3,2,1,0:T(8,128)(2,1)}, bf16[2,2,384,768]{3,2,1,0:T(8,128)(2,1)}, u32[]{:S(2)}, u32[]{:S(2)}) collective-permute-start(bf16[2,2,384,768]{3,2,1,0:T(8,128)(2,1)} %pad_maximum_fusion.2), channel_id=1, source_target_pairs={{0,4},{4,8},{8,12},{16,20},{20,24},{24,28},{32,36},{36,40},{40,44}... | collective-permute-start | bytes 7077896 | tf_op jit(solution)/shard_map/ppermute | solution.py:23
  65.5 5.6 %collective-permute-start.4 = (bf16[2,384,768]{2,1,0:T(8,128)(2,1)}, bf16[2,384,768]{2,1,0:T(8,128)(2,1)}, u32[]{:S(2)}, u32[]{:S(2)}) collective-permute-start(bf16[2,384,768]{2,1,0:T(8,128)(2,1)} %pad_maximum_fusion.3), channel_id=1, source_target_pairs={{0,4},{4,8},{8,12},{16,20},{20,24},{24,28},{32,36},{36,40},{40,44}... | collective-permute-start | bytes 3538952 | tf_op jit(solution)/shard_map/ppermute | solution.py:23
  91.5 5.2 %fusion.17.grad_ref = bf16[384,768]{1,0:T(8,128)(2,1)} fusion(bf16[768,3072]{1,0:T(8,128)(2,1)} %param.11, bf16[1,1,384,3072]{3,2,1,0:T(8,128)(2,1)S(1)} %copy-done), kind=kOutput, calls=%fused_computation.31 | convolution fusion | flops 1812234240 | bytes 7667712 | tf_op jit(solution)/shard_map/dot_general | solution.py:90
  96.7 18.2 %collective-permute-done.2 = bf16[2,2,384,768]{3,2,1,0:T(8,128)(2,1)} collective-permute-done((bf16[2,2,384,768]{3,2,1,0:T(8,128)(2,1)}, bf16[2,2,384,768]{3,2,1,0:T(8,128)(2,1)}, u32[]{:S(2)}, u32[]{:S(2)}) %collective-permute-start.2) | collective-permute-done | bytes 2359328 | tf_op jit(solution)/shard_map/ppermute | solution.py:23
  123.0 15.1 %collective-permute-done.4 = bf16[2,384,768]{2,1,0:T(8,128)(2,1)} collective-permute-done((bf16[2,384,768]{2,1,0:T(8,128)(2,1)}, bf16[2,384,768]{2,1,0:T(8,128)(2,1)}, u32[]{:S(2)}, u32[]{:S(2)}) %collective-permute-start.4) | collective-permute-done | bytes 1179680 | tf_op jit(solution)/shard_map/ppermute | solution.py:23
  151.9 8.0 %gather_fusion = bf16[5,2,384,768]{3,2,1,0:T(8,128)(2,1)} fusion(bf16[9,2,384,768]{3,2,1,0:T(8,128)(2,1)} %slice_dynamic-update-slice_fusion, s32[1024]{0:T(1024)S(1)} %pad_clamp_fusion), kind=kCustom, calls=%fused_computation | custom fusion | bytes 11796500 | tf_op jit(solution)/shard_map/jit(_take)/gather | solution.py:86
  159.9 3.3 broadcast_select_fusion
  166.1 23.1 %shard_map.93 = (bf16[384,768]{1,0:T(8,128)(2,1)}, bf16[384,768]{1,0:T(8,128)(2,1)}, bf16[1920,768]{1,0:T(8,128)(2,1)}, bf16[1920,768]{1,0:T(8,128)(2,1)}) custom-call(s32[1,1920]{1,0:T(1,128)} %bitcast.191, bf16[384,768]{1,0:T(8,128)(2,1)} %bitcast.192, bf16[1920,768]{1,0:T(8,128)(2,1)} %bitcast.182, bf16[1920,768]{1,0:T(8,128)(2,1)} %bitcast.181, ...), custom_call_target="tpu_custom_call" | custom-call | flops 5662310400 | bytes 14155776 | tf_op jit(solution)/shard_map/pallas_call | solution.py:98
  195.0 3.3 constant_dynamic-slice_fusion.8
  209.8 6.4 %collective-permute-start.7 = (bf16[3,2,384,768]{3,2,1,0:T(8,128)(2,1)}, bf16[3,2,384,768]{3,2,1,0:T(8,128)(2,1)}, u32[]{:S(2)}, u32[]{:S(2)}) collective-permute-start(bf16[3,2,384,768]{3,2,1,0:T(8,128)(2,1)} %pad_maximum_fusion.1), channel_id=1, source_target_pairs={{0,4},{4,8},{8,12},{16,20},{20,24},{24,28},{32,36},{36,40},{40,44}... | collective-permute-start | bytes 10616840 | tf_op jit(solution)/shard_map/ppermute | solution.py:23
  219.1 4.3 %copy.13 = bf16[3072,384]{1,0:T(8,128)(2,1)} copy(bf16[3072,384]{0,1:T(8,128)(2,1)} %fusion) | data formatting | bytes 4718592 | tf_op jit(solution)/shard_map/convert_element_type | solution.py:137
  223.4 11.5 %all-to-all-start = ((bf16[64,48,384]{2,1,0:T(8,128)(2,1)}), bf16[64,48,384]{2,1,0:T(8,128)(2,1)}, u32[]{:S(2)}, u32[]{:S(2)}) async-start(bf16[64,48,384]{2,1,0:T(8,128)(2,1)} %bitcast.178), calls=%async_computation | async-start | bytes 4718592 | tf_op jit(solution)/shard_map/all_to_all | solution.py:138
  234.8 69.7 %collective-permute-done.6 = bf16[3,2,384,768]{3,2,1,0:T(8,128)(2,1)} collective-permute-done((bf16[3,2,384,768]{3,2,1,0:T(8,128)(2,1)}, bf16[3,2,384,768]{3,2,1,0:T(8,128)(2,1)}, u32[]{:S(2)}, u32[]{:S(2)}) %collective-permute-start.6) | collective-permute-done | bytes 3538976 | tf_op jit(solution)/shard_map/ppermute | solution.py:23
  307.2 3.3 collective-permute-done.7
  313.2 3.5 fusion.6
  316.7 7.0 %collective-permute-start.8 = (bf16[2,384,768]{2,1,0:T(8,128)(2,1)}, bf16[2,384,768]{2,1,0:T(8,128)(2,1)S(1)}, u32[]{:S(2)}, u32[]{:S(2)}) collective-permute-start(bf16[2,384,768]{2,1,0:T(8,128)(2,1)} %get-tuple-element.16), channel_id=1, source_target_pairs={{16,0},{20,4},{24,8},{28,12},{32,16},{36,20},{40,24},{44,28},{48,3... | collective-permute-start | bytes 3538952 | tf_op jit(solution)/shard_map/ppermute | solution.py:23
  325.6 24.8 %collective-permute-done.8 = bf16[2,384,768]{2,1,0:T(8,128)(2,1)S(1)} collective-permute-done((bf16[2,384,768]{2,1,0:T(8,128)(2,1)}, bf16[2,384,768]{2,1,0:T(8,128)(2,1)S(1)}, u32[]{:S(2)}, u32[]{:S(2)}) %collective-permute-start.8) | collective-permute-done | bytes 1179680 | tf_op jit(solution)/shard_map/ppermute | solution.py:23
  350.4 24.5 %collective-permute-done.9 = bf16[2,384,768]{2,1,0:T(8,128)(2,1)} collective-permute-done((bf16[2,384,768]{2,1,0:T(8,128)(2,1)}, bf16[2,384,768]{2,1,0:T(8,128)(2,1)}, u32[]{:S(2)}, u32[]{:S(2)}) %collective-permute-start.9) | collective-permute-done | bytes 1179680 | tf_op jit(solution)/shard_map/ppermute | solution.py:23
  374.9 4.6 %fusion.11 = bf16[2,384,768]{2,1,0:T(8,128)(2,1)S(1)} fusion(f32[3,2,384,768]{3,2,1,0:T(8,128)} %copy-done.2, f32[3,2,384,768]{3,2,1,0:T(8,128)} %copy-done.1, bf16[2,384,768]{2,1,0:T(8,128)(2,1)} %collective-permute-done.9, bf16[2,384,768]{2,1,0:T(8,128)(2,1)} %copy-done.20, bf16[1,384,768]{2,1,0:T(8,128)(2,1)} %get-tuple-element.29, ...), kind=kLoop, calls=%fused_computation.23 | loop fusion | flops 5898240 | bytes 9437185 | tf_op jit(solution)/shard_map/convert_element_type | solution.py:181
  384.9 6.7 %collective-permute-start.11 = (f32[48,192]{1,0:T(8,128)S(1)}, f32[48,192]{1,0:T(8,128)S(1)}, u32[]{:S(2)}, u32[]{:S(2)}) collective-permute-start(f32[48,192]{1,0:T(8,128)S(1)} %bitcast.190), channel_id=1, source_target_pairs={{0,2},{1,3},{2,0},{3,1},{4,6},{5,7},{6,4},{7,5},{8,10},{9,11},{10,... | collective-permute-start | bytes 110600 | tf_op jit(solution)/shard_map/ppermute | solution.py:146
  (99 shorter events, 68.8 us)
Async XLA Ops:
  0.6 90.8 %copy-start = (bf16[1,1,384,3072]{3,2,1,0:T(8,128)(2,1)S(1)}, bf16[1,1,384,3072]{3,2,1,0:T(8,128)(2,1)}, u32[]{:S(2)}) copy-start(bf16[1,1,384,3072]{3,2,1,0:T(8,128)(2,1)} %param.10) | copy-start | bytes 7077892
  3.2 33.7 %collective-permute-start = (bf16[2,384,768]{2,1,0:T(8,128)(2,1)}, bf16[2,384,768]{2,1,0:T(8,128)(2,1)S(1)}, u32[]{:S(2)}, u32[]{:S(2)}) collective-permute-start(bf16[2,384,768]{2,1,0:T(8,128)(2,1)} %pad_maximum_fusion.3), channel_id=1, source_target_pairs={{0,16},{4,20},{8,24},{12,28},{16,32},{20,36},{24,40},{28,44},{32,4... | collective-permute-start | bytes 3538952 | tf_op jit(solution)/shard_map/ppermute | solution.py:23
  7.0 50.8 %collective-permute-start.1 = (bf16[2,384,768]{2,1,0:T(8,128)(2,1)}, bf16[2,384,768]{2,1,0:T(8,128)(2,1)S(1)}, u32[]{:S(2)}, u32[]{:S(2)}) collective-permute-start(bf16[2,384,768]{2,1,0:T(8,128)(2,1)} %pad_maximum_fusion.3), channel_id=1, source_target_pairs={{16,0},{20,4},{24,8},{28,12},{32,16},{36,20},{40,24},{44,28},{48,3... | collective-permute-start | bytes 3538952 | tf_op jit(solution)/shard_map/ppermute | solution.py:23
  36.9 22.5 %copy-start.5 = (bf16[2,384,768]{2,1,0:T(8,128)(2,1)}, bf16[2,384,768]{2,1,0:T(8,128)(2,1)S(1)}, u32[]{:S(2)}) copy-start(bf16[2,384,768]{2,1,0:T(8,128)(2,1)S(1)} %collective-permute-done) | copy-start | bytes 3538948
  57.8 14.6 %copy-start.21 = (s32[1,5]{1,0:T(1,128)S(1)}, s32[1,5]{1,0:T(1,128)}, u32[]{:S(2)}) copy-start(s32[1,5]{1,0:T(1,128)} %param.9) | copy-start | bytes 64
  59.4 55.4 %collective-permute-start.2 = (bf16[2,2,384,768]{3,2,1,0:T(8,128)(2,1)}, bf16[2,2,384,768]{3,2,1,0:T(8,128)(2,1)}, u32[]{:S(2)}, u32[]{:S(2)}) collective-permute-start(bf16[2,2,384,768]{3,2,1,0:T(8,128)(2,1)} %pad_maximum_fusion.2), channel_id=1, source_target_pairs={{0,4},{4,8},{8,12},{16,20},{20,24},{24,28},{32,36},{36,40},{40,44}... | collective-permute-start | bytes 7077896 | tf_op jit(solution)/shard_map/ppermute | solution.py:23
  64.2 56.4 %collective-permute-start.3 = (bf16[2,2,384,768]{3,2,1,0:T(8,128)(2,1)}, bf16[2,2,384,768]{3,2,1,0:T(8,128)(2,1)}, u32[]{:S(2)}, u32[]{:S(2)}) collective-permute-start(bf16[2,2,384,768]{3,2,1,0:T(8,128)(2,1)} %pad_maximum_fusion.2), channel_id=1, source_target_pairs={{4,0},{8,4},{12,8},{20,16},{24,20},{28,24},{36,32},{40,36},{44,40}... | collective-permute-start | bytes 7077896 | tf_op jit(solution)/shard_map/ppermute | solution.py:23
  65.5 72.5 %collective-permute-start.4 = (bf16[2,384,768]{2,1,0:T(8,128)(2,1)}, bf16[2,384,768]{2,1,0:T(8,128)(2,1)}, u32[]{:S(2)}, u32[]{:S(2)}) collective-permute-start(bf16[2,384,768]{2,1,0:T(8,128)(2,1)} %pad_maximum_fusion.3), channel_id=1, source_target_pairs={{0,4},{4,8},{8,12},{16,20},{20,24},{24,28},{32,36},{36,40},{40,44}... | collective-permute-start | bytes 3538952 | tf_op jit(solution)/shard_map/ppermute | solution.py:23
  71.1 72.4 %collective-permute-start.5 = (bf16[2,384,768]{2,1,0:T(8,128)(2,1)}, bf16[2,384,768]{2,1,0:T(8,128)(2,1)}, u32[]{:S(2)}, u32[]{:S(2)}) collective-permute-start(bf16[2,384,768]{2,1,0:T(8,128)(2,1)} %pad_maximum_fusion.3), channel_id=1, source_target_pairs={{4,0},{8,4},{12,8},{20,16},{24,20},{28,24},{36,32},{40,36},{44,40}... | collective-permute-start | bytes 3538952 | tf_op jit(solution)/shard_map/ppermute | solution.py:23
  96.6 20.6 %copy-start.6 = (bf16[2,384,768]{2,1,0:T(8,128)(2,1)S(1)}, bf16[2,384,768]{2,1,0:T(8,128)(2,1)}, u32[]{:S(2)}) copy-start(bf16[2,384,768]{2,1,0:T(8,128)(2,1)} %copy-done.5) | copy-start | bytes 3538948
  118.3 22.1 %copy-start.17 = (bf16[1,1,384,768]{3,2,1,0:T(8,128)(2,1)S(1)}, bf16[1,1,384,768]{3,2,1,0:T(8,128)(2,1)}, u32[]{:S(2)}) copy-start(bf16[1,1,384,768]{3,2,1,0:T(8,128)(2,1)} %param.8) | copy-start | bytes 1769476
  118.3 22.1 %copy-start.18 = (bf16[1,1,384,768]{3,2,1,0:T(8,128)(2,1)S(1)}, bf16[1,1,384,768]{3,2,1,0:T(8,128)(2,1)}, u32[]{:S(2)}) copy-start(bf16[1,1,384,768]{3,2,1,0:T(8,128)(2,1)} %param.7) | copy-start | bytes 1769476
  194.2 22.1 %collective-permute-start.10 = (bf16[3072,384]{0,1:T(8,128)(2,1)}, bf16[3072,384]{0,1:T(8,128)(2,1)S(1)}, u32[]{:S(2)}, u32[]{:S(2)}) collective-permute-start(bf16[3072,384]{0,1:T(8,128)(2,1)} %fusion.1), channel_id=1, source_target_pairs={{0,1},{1,0},{2,3},{3,2},{4,5},{5,4},{6,7},{7,6},{8,9},{9,8},{10,11... | collective-permute-start | bytes 7077896 | tf_op jit(solution)/shard_map/ppermute | solution.py:134
  203.9 100.6 %collective-permute-start.6 = (bf16[3,2,384,768]{3,2,1,0:T(8,128)(2,1)}, bf16[3,2,384,768]{3,2,1,0:T(8,128)(2,1)}, u32[]{:S(2)}, u32[]{:S(2)}) collective-permute-start(bf16[3,2,384,768]{3,2,1,0:T(8,128)(2,1)} %pad_maximum_fusion), channel_id=1, source_target_pairs={{4,0},{8,4},{12,8},{20,16},{24,20},{28,24},{36,32},{40,36},{44,40}... | collective-permute-start | bytes 10616840 | tf_op jit(solution)/shard_map/ppermute | solution.py:23
  207.7 8.5 %copy-start.19 = (bf16[384,2,1,192]{0,3,2,1:T(8,128)(2,1)S(1)}, bf16[384,2,1,192]{0,3,2,1:T(8,128)(2,1)}, u32[]{:S(2)}) copy-start(bf16[384,2,1,192]{0,3,2,1:T(8,128)(2,1)} %get-tuple-element.40) | copy-start | bytes 884740
  209.8 100.7 %collective-permute-start.7 = (bf16[3,2,384,768]{3,2,1,0:T(8,128)(2,1)}, bf16[3,2,384,768]{3,2,1,0:T(8,128)(2,1)}, u32[]{:S(2)}, u32[]{:S(2)}) collective-permute-start(bf16[3,2,384,768]{3,2,1,0:T(8,128)(2,1)} %pad_maximum_fusion.1), channel_id=1, source_target_pairs={{0,4},{4,8},{8,12},{16,20},{20,24},{24,28},{32,36},{36,40},{40,44}... | collective-permute-start | bytes 10616840 | tf_op jit(solution)/shard_map/ppermute | solution.py:23
  223.4 156.2 %all-to-all-start = ((bf16[64,48,384]{2,1,0:T(8,128)(2,1)}), bf16[64,48,384]{2,1,0:T(8,128)(2,1)}, u32[]{:S(2)}, u32[]{:S(2)}) async-start(bf16[64,48,384]{2,1,0:T(8,128)(2,1)} %bitcast.178), calls=%async_computation | async-start | bytes 4718592 | tf_op jit(solution)/shard_map/all_to_all | solution.py:138
  307.2 6.0 %copy-start.1 = (f32[3,2,384,768]{3,2,1,0:T(8,128)}, f32[3,2,384,768]{3,2,1,0:T(8,128)S(1)}, u32[]{:S(2)}) copy-start(f32[3,2,384,768]{3,2,1,0:T(8,128)S(1)} %convert_element_type.66) | copy-start | bytes 21233668
  307.2 6.0 %copy-start.7 = (bf16[1,384,768]{2,1,0:T(8,128)(2,1)S(1)}, bf16[1,384,768]{2,1,0:T(8,128)(2,1)}, u32[]{:S(2)}) copy-start(bf16[1,384,768]{2,1,0:T(8,128)(2,1)} %get-tuple-element.72) | copy-start | bytes 1769476
  307.2 6.0 %copy-start.8 = (bf16[1,384,768]{2,1,0:T(8,128)(2,1)S(1)}, bf16[1,384,768]{2,1,0:T(8,128)(2,1)}, u32[]{:S(2)}) copy-start(bf16[1,384,768]{2,1,0:T(8,128)(2,1)} %get-tuple-element.73) | copy-start | bytes 1769476
  316.7 33.7 %collective-permute-start.8 = (bf16[2,384,768]{2,1,0:T(8,128)(2,1)}, bf16[2,384,768]{2,1,0:T(8,128)(2,1)S(1)}, u32[]{:S(2)}, u32[]{:S(2)}) collective-permute-start(bf16[2,384,768]{2,1,0:T(8,128)(2,1)} %get-tuple-element.16), channel_id=1, source_target_pairs={{16,0},{20,4},{24,8},{28,12},{32,16},{36,20},{40,24},{44,28},{48,3... | collective-permute-start | bytes 3538952 | tf_op jit(solution)/shard_map/ppermute | solution.py:23
  323.7 51.2 %collective-permute-start.9 = (bf16[2,384,768]{2,1,0:T(8,128)(2,1)}, bf16[2,384,768]{2,1,0:T(8,128)(2,1)}, u32[]{:S(2)}, u32[]{:S(2)}) collective-permute-start(bf16[2,384,768]{2,1,0:T(8,128)(2,1)} %get-tuple-element.17), channel_id=1, source_target_pairs={{0,16},{4,20},{8,24},{12,28},{16,32},{20,36},{24,40},{28,44},{32,4... | collective-permute-start | bytes 3538952 | tf_op jit(solution)/shard_map/ppermute | solution.py:23
  350.4 24.5 %copy-start.20 = (bf16[2,384,768]{2,1,0:T(8,128)(2,1)}, bf16[2,384,768]{2,1,0:T(8,128)(2,1)S(1)}, u32[]{:S(2)}) copy-start(bf16[2,384,768]{2,1,0:T(8,128)(2,1)S(1)} %collective-permute-done.8) | copy-start | bytes 3538948
  384.9 8.8 %collective-permute-start.11 = (f32[48,192]{1,0:T(8,128)S(1)}, f32[48,192]{1,0:T(8,128)S(1)}, u32[]{:S(2)}, u32[]{:S(2)}) collective-permute-start(f32[48,192]{1,0:T(8,128)S(1)} %bitcast.190), channel_id=1, source_target_pairs={{0,2},{1,3},{2,0},{3,1},{4,6},{5,7},{6,4},{7,5},{8,10},{9,11},{10,... | collective-permute-start | bytes 110600 | tf_op jit(solution)/shard_map/ppermute | solution.py:146
  (13 other events, 37.1 us)

commit v5 on v4

--- a/solution.py
+++ b/solution.py
@@ -63,11 +63,17 @@
     def shifted(value, time_step, height_step, toward):
         return neighbour_shift(value, "sp", time_step, height_step, height_tiles, toward)
 
-    earlier = shifted(key_value, -1, 0, False)
-    later = shifted(key_value, 1, 0, False)
+    earlier, later, left_own, right_own = lax.optimization_barrier(
+        (
+            shifted(key_value, -1, 0, False),
+            shifted(key_value, 1, 0, False),
+            shifted(key_value, 0, -1, False),
+            shifted(key_value, 0, 1, False),
+        )
+    )
     column = [earlier, key_value, later]
     relayed = jnp.stack([earlier, later])
-    side_own = {step: shifted(key_value, 0, step, False) for step in (-1, 1)}
+    side_own = {-1: left_own, 1: right_own}
     side_relayed = {step: shifted(relayed, 0, step, False) for step in (-1, 1)}
     pieces = []
     for time_step in (-1, 0, 1):
@@ -161,22 +167,25 @@
         )
         return jnp.where(match_any[slot_number], payload, jnp.zeros_like(payload))
 
-    from_side = {
-        step: shifted(
-            jnp.stack([slot_payload(time_step * 3 + step + 4) for time_step in (-1, 0, 1)]), 0, step, True
-        ).astype(jnp.float32)
+    diagonal_sends = [
+        shifted(jnp.stack([slot_payload(step + 1), slot_payload(step + 7)]), 0, step, True)
         for step in (-1, 1)
-    }
-    column_sums = [
-        slot_payload(time_step * 3 + 4).astype(jnp.float32)
-        + from_side[-1][time_step + 1]
-        + from_side[1][time_step + 1]
-        for time_step in (-1, 0, 1)
     ]
+    own_row_parts = [slot_payload(step + 4) for step in (-1, 1)]
+    diagonal_in, own_row_parts = lax.optimization_barrier((diagonal_sends, own_row_parts))
+    diagonal_in = [part.astype(jnp.float32) for part in diagonal_in]
+    row_in = [
+        shifted(part, 0, step, True).astype(jnp.float32)
+        for part, step in zip(own_row_parts, (-1, 1))
+    ]
+    earlier_sum = slot_payload(1).astype(jnp.float32) + diagonal_in[0][0] + diagonal_in[1][0]
+    later_sum = slot_payload(7).astype(jnp.float32) + diagonal_in[0][1] + diagonal_in[1][1]
     grad_total = (
-        column_sums[1]
-        + shifted(column_sums[0].astype(jnp.bfloat16), -1, 0, True).astype(jnp.float32)
-        + shifted(column_sums[2].astype(jnp.bfloat16), 1, 0, True).astype(jnp.float32)
+        slot_payload(4).astype(jnp.float32)
+        + row_in[0]
+        + row_in[1]
+        + shifted(earlier_sum.astype(jnp.bfloat16), -1, 0, True).astype(jnp.float32)
+        + shifted(later_sum.astype(jnp.bfloat16), 1, 0, True).astype(jnp.float32)
     )
     grad_kv = grad_total.astype(jnp.bfloat16)
     return (grad_query[None, None], grad_kv[0][None, None], grad_kv[1][None, None], weight_grad)

time: 400 us -> 390 us (0.975)
  waiting for transfers between devices: 207 us -> 197 us
  local copies, waits for them, and re-layouts: 43.2 us -> 47.6 us
  other arithmetic: 35.9 us -> 31.7 us
    ppermute x10 -> x12, waiting for transfers between devices: 206 us -> 195 us  [neighbour_shift(): return lax.ppermute(value, axis, pairs)]
    dynamic_slice x1, local copies, waits for them, and re-layouts: 3.31 us -> 7.61 us  [slot_payload(): lax.dynamic_index_in_dim(value_terms, picked_slot, 0, keepdims=False)]
    ppermute x10 -> x12, starting transfers between devices: 38.3 us -> 40.1 us  [neighbour_shift(): return lax.ppermute(value, axis, pairs)]
    unnamed x58 -> x42, local copies, waits for them, and re-layouts: 15 us -> 15 us
  transfers between devices with their start and end apart: 13 -> 15, of which waited for: 11 -> 9; matrix products, arithmetic and copies ran while one was open for 13% -> 13% of each run, Pallas kernels for 0% -> 0%
where the time goes in v5:
time: 390 us; the launch traced here: 388 us
  waiting for transfers between devices  197 us (51%)
  starting transfers between devices  57.9 us (15%)
  local copies, waits for them, and re-layouts  47.6 us (12%)
  other arithmetic  31.7 us (8%)
  Pallas kernels  23.2 us (6%)
  between operations  18.2 us (5%)
  matrix products  12.5 us (3%)
    ppermute x12, waiting for transfers between devices, neighbour_shift(): return lax.ppermute(value, axis, pairs)  195 us
    ppermute x12, starting transfers between devices, neighbour_shift(): return lax.ppermute(value, axis, pairs)  40.1 us
    pallas_call x1, Pallas kernels, body(): pl.pallas_call(functools.partial(tile_attention, score_scale=score_scale)...  23.2 us
    unnamed x42, local copies, waits for them, and re-layouts  15 us
    all_to_all x1, starting transfers between devices, body(): lax.all_to_all(core_sum.reshape(sp_count, col_block, -1), 'sp', 0, 0, til...  10.9 us
    select_n x6, other arithmetic, slot_payload(): return jnp.where(match_any[slot_number], payload, jnp.zeros_like(payload))  8 us
    gather x1, local copies, waits for them, and re-layouts, body(): picked = jnp.take(window, slot_index, axis=0)  7.99 us
  transfers between devices with their start and end apart: 15, of which 9 were waited for; matrix products, arithmetic and copies ran while one was open for 13% of the time, Pallas kernels for 0%

profile of v5, /device:TPU:24, one launch (start us, length us, event | category | flops | bytes accessed | tf_op | source)
XLA Modules:
  0.0 387.7 jit_solution(7537087841202244867)
XLA Ops:
  2.2 3.8 collective-permute-start
  6.0 4.8 %collective-permute-start.1 = (bf16[2,384,768]{2,1,0:T(8,128)(2,1)S(1)}, bf16[2,384,768]{2,1,0:T(8,128)(2,1)S(1)}, u32[]{:S(2)}, u32[]{:S(2)}) collective-permute-start(bf16[2,384,768]{2,1,0:T(8,128)(2,1)S(1)} %pad_maximum_fusion.3), channel_id=1, source_target_pairs={{16,0},{20,4},{24,8},{28,12},{32,16},{36,20},{40,24},{44,28},{48,3... | collective-permute-start | bytes 3538952 | tf_op jit(solution)/shard_map/ppermute | solution.py:23
  10.8 4.4 %collective-permute-start.2 = (bf16[2,384,768]{2,1,0:T(8,128)(2,1)S(1)}, bf16[2,384,768]{2,1,0:T(8,128)(2,1)}, u32[]{:S(2)}, u32[]{:S(2)}) collective-permute-start(bf16[2,384,768]{2,1,0:T(8,128)(2,1)S(1)} %pad_maximum_fusion.3), channel_id=1, source_target_pairs={{0,4},{4,8},{8,12},{16,20},{20,24},{24,28},{32,36},{36,40},{40,44}... | collective-permute-start | bytes 3538952 | tf_op jit(solution)/shard_map/ppermute | solution.py:23
  16.5 19.2 %collective-permute-done = bf16[2,384,768]{2,1,0:T(8,128)(2,1)S(1)} collective-permute-done((bf16[2,384,768]{2,1,0:T(8,128)(2,1)S(1)}, bf16[2,384,768]{2,1,0:T(8,128)(2,1)S(1)}, u32[]{:S(2)}, u32[]{:S(2)}) %collective-permute-start) | collective-permute-done | bytes 1179680 | tf_op jit(solution)/shard_map/ppermute | solution.py:23
  35.7 20.8 %collective-permute-done.1 = bf16[2,384,768]{2,1,0:T(8,128)(2,1)S(1)} collective-permute-done((bf16[2,384,768]{2,1,0:T(8,128)(2,1)S(1)}, bf16[2,384,768]{2,1,0:T(8,128)(2,1)S(1)}, u32[]{:S(2)}, u32[]{:S(2)}) %collective-permute-start.1) | collective-permute-done | bytes 1179680 | tf_op jit(solution)/shard_map/ppermute | solution.py:23
  58.1 4.8 %collective-permute-start.4 = (bf16[2,2,384,768]{3,2,1,0:T(8,128)(2,1)}, bf16[2,2,384,768]{3,2,1,0:T(8,128)(2,1)}, u32[]{:S(2)}, u32[]{:S(2)}) collective-permute-start(bf16[2,2,384,768]{3,2,1,0:T(8,128)(2,1)} %pad_maximum_fusion), channel_id=1, source_target_pairs={{0,4},{4,8},{8,12},{16,20},{20,24},{24,28},{32,36},{36,40},{40,44}... | collective-permute-start | bytes 7077896 | tf_op jit(solution)/shard_map/ppermute | solution.py:23
  65.6 5.2 %fusion.12.grad_ref = bf16[384,768]{1,0:T(8,128)(2,1)} fusion(bf16[768,3072]{1,0:T(8,128)(2,1)} %param.11, bf16[1,1,384,3072]{3,2,1,0:T(8,128)(2,1)S(1)} %copy-done), kind=kOutput, calls=%fused_computation.25 | convolution fusion | flops 1812234240 | bytes 7667712 | tf_op jit(solution)/shard_map/dot_general | solution.py:96
  70.8 40.7 %collective-permute-done.4 = bf16[2,2,384,768]{3,2,1,0:T(8,128)(2,1)} collective-permute-done((bf16[2,2,384,768]{3,2,1,0:T(8,128)(2,1)}, bf16[2,2,384,768]{3,2,1,0:T(8,128)(2,1)}, u32[]{:S(2)}, u32[]{:S(2)}) %collective-permute-start.4) | collective-permute-done | bytes 2359328 | tf_op jit(solution)/shard_map/ppermute | solution.py:23
  131.2 8.0 %gather_fusion = bf16[5,2,384,768]{3,2,1,0:T(8,128)(2,1)} fusion(bf16[9,2,384,768]{3,2,1,0:T(8,128)(2,1)} %slice_dynamic-update-slice_fusion, s32[1024]{0:T(1024)S(1)} %pad_clamp_fusion), kind=kCustom, calls=%fused_computation | custom fusion | bytes 11796500 | tf_op jit(solution)/shard_map/jit(_take)/gather | solution.py:92
  139.2 3.3 broadcast_select_fusion
  145.5 23.2 %shard_map.93 = (bf16[384,768]{1,0:T(8,128)(2,1)}, bf16[384,768]{1,0:T(8,128)(2,1)}, bf16[1920,768]{1,0:T(8,128)(2,1)}, bf16[1920,768]{1,0:T(8,128)(2,1)}) custom-call(s32[1,1920]{1,0:T(1,128)} %bitcast.167, bf16[384,768]{1,0:T(8,128)(2,1)} %bitcast.168, bf16[1920,768]{1,0:T(8,128)(2,1)} %bitcast.158, bf16[1920,768]{1,0:T(8,128)(2,1)} %bitcast.157, ...), custom_call_target="tpu_custom_call" | custom-call | flops 5662310400 | bytes 14155776 | tf_op jit(solution)/shard_map/pallas_call | solution.py:104
  193.0 7.6 %constant_dynamic-slice_fusion.12 = (bf16[1,384,768]{2,1,0:T(8,128)(2,1)}, bf16[1,384,768]{2,1,0:T(8,128)(2,1)}, bf16[1,384,768]{2,1,0:T(8,128)(2,1)}, bf16[1,38...) fusion(bf16[5,384,768]{2,1,0:T(8,128)(2,1)} %bitcast.153, ...), kind=kLoop, calls=%fused_computation.71 | loop fusion | bytes 21233700 | tf_op jit(solution)/shard_map/jit(dynamic_index_in_dim)/dynamic_slice | solution.py:165
  203.8 4.0 %collective-permute-start.7 = (bf16[2,2,384,768]{3,2,1,0:T(8,128)(2,1)}, bf16[2,2,384,768]{3,2,1,0:T(8,128)(2,1)}, u32[]{:S(2)}, u32[]{:S(2)}) collective-permute-start(bf16[2,2,384,768]{3,2,1,0:T(8,128)(2,1)} %pad_maximum_fusion.2), channel_id=1, source_target_pairs={{0,4},{4,8},{8,12},{16,20},{20,24},{24,28},{32,36},{36,40},{40,44}... | collective-permute-start | bytes 7077896 | tf_op jit(solution)/shard_map/ppermute | solution.py:23
  208.7 4.5 %fusion = bf16[3072,384]{0,1:T(8,128)(2,1)} fusion(bf16[3072,384]{0,1:T(8,128)(2,1)} %collective-permute-done.12, bf16[384,384]{0,1:T(8,128)(2,1)S(1)} %bitcast.164, bf16[1,1,384,3072]{3,2,1,0:T(8,128)(2,1)S(1)} %copy-done), kind=kOutput, calls=%fused_computation.3 | convolution fusion | flops 909508608 | bytes 7372800 | tf_op jit(solution)/shard_map/dot_general | solution.py:138
  213.2 4.3 %copy.13 = bf16[3072,384]{1,0:T(8,128)(2,1)} copy(bf16[3072,384]{0,1:T(8,128)(2,1)} %fusion) | data formatting | bytes 4718592 | tf_op jit(solution)/shard_map/convert_element_type | solution.py:143
  217.5 10.9 %all-to-all-start = ((bf16[64,48,384]{2,1,0:T(8,128)(2,1)}), bf16[64,48,384]{2,1,0:T(8,128)(2,1)}, u32[]{:S(2)}, u32[]{:S(2)}) async-start(bf16[64,48,384]{2,1,0:T(8,128)(2,1)} %bitcast.154), calls=%async_computation | async-start | bytes 4718592 | tf_op jit(solution)/shard_map/all_to_all | solution.py:144
  235.7 40.2 %collective-permute-done.7 = bf16[2,2,384,768]{3,2,1,0:T(8,128)(2,1)} collective-permute-done((bf16[2,2,384,768]{3,2,1,0:T(8,128)(2,1)}, bf16[2,2,384,768]{3,2,1,0:T(8,128)(2,1)}, u32[]{:S(2)}, u32[]{:S(2)}) %collective-permute-start.7) | collective-permute-done | bytes 2359328 | tf_op jit(solution)/shard_map/ppermute | solution.py:23
  275.9 30.0 %collective-permute-done.6 = bf16[2,2,384,768]{3,2,1,0:T(8,128)(2,1)S(1)} collective-permute-done((bf16[2,2,384,768]{3,2,1,0:T(8,128)(2,1)S(1)}, bf16[2,2,384,768]{3,2,1,0:T(8,128)(2,1)S(1)}, u32[]{:S(2)}, u32[]{:S(2)}) %collective-permute-start.6) | collective-permute-done | bytes 2359328 | tf_op jit(solution)/shard_map/ppermute | solution.py:23
  311.6 5.4 %collective-permute-start.10 = (bf16[2,384,768]{2,1,0:T(8,128)(2,1)}, bf16[2,384,768]{2,1,0:T(8,128)(2,1)}, u32[]{:S(2)}, u32[]{:S(2)}) collective-permute-start(bf16[2,384,768]{2,1,0:T(8,128)(2,1)} %get-tuple-element.32), channel_id=1, source_target_pairs={{16,0},{20,4},{24,8},{28,12},{32,16},{36,20},{40,24},{44,28},{48,3... | collective-permute-start | bytes 3538952 | tf_op jit(solution)/shard_map/ppermute | solution.py:23
  320.3 5.6 %collective-permute-start.9 = (bf16[2,384,768]{2,1,0:T(8,128)(2,1)}, bf16[2,384,768]{2,1,0:T(8,128)(2,1)}, u32[]{:S(2)}, u32[]{:S(2)}) collective-permute-start(bf16[2,384,768]{2,1,0:T(8,128)(2,1)} %maximum_select_fusion.6), channel_id=1, source_target_pairs={{0,4},{4,8},{8,12},{16,20},{20,24},{24,28},{32,36},{36,40},{40,44}... | collective-permute-start | bytes 3538952 | tf_op jit(solution)/shard_map/ppermute | solution.py:23
  325.8 18.0 %collective-permute-done.10 = bf16[2,384,768]{2,1,0:T(8,128)(2,1)} collective-permute-done((bf16[2,384,768]{2,1,0:T(8,128)(2,1)}, bf16[2,384,768]{2,1,0:T(8,128)(2,1)}, u32[]{:S(2)}, u32[]{:S(2)}) %collective-permute-start.10) | collective-permute-done | bytes 1179680 | tf_op jit(solution)/shard_map/ppermute | solution.py:23
  343.8 24.7 %collective-permute-done.11 = bf16[2,384,768]{2,1,0:T(8,128)(2,1)} collective-permute-done((bf16[2,384,768]{2,1,0:T(8,128)(2,1)S(1)}, bf16[2,384,768]{2,1,0:T(8,128)(2,1)}, u32[]{:S(2)}, u32[]{:S(2)}) %collective-permute-start.11) | collective-permute-done | bytes 1179680 | tf_op jit(solution)/shard_map/ppermute | solution.py:23
  368.5 4.1 %add_convert_fusion = bf16[2,384,768]{2,1,0:T(8,128)(2,1)S(1)} fusion(bf16[2,384,768]{2,1,0:T(8,128)(2,1)} %collective-permute-done.11, bf16[2,384,768]{2,1,0:T(8,128)(2,1)} %collective-permute-done.10, bf16[2,384,768]{2,1,0:T(8,128)(2,1)} %collective-permute-done.9, bf16[2,384,768]{2,1,0:T(8,128)(2,1)} %collective-permute-done.8, ...), kind=kLoop, calls=%fused_computation.24 | loop fusion | flops 7077888 | bytes 7077889 | tf_op jit(solution)/shard_map/convert_element_type | solution.py:190
  378.0 6.9 %collective-permute-start.13 = (f32[48,192]{1,0:T(8,128)S(1)}, f32[48,192]{1,0:T(8,128)S(1)}, u32[]{:S(2)}, u32[]{:S(2)}) collective-permute-start(f32[48,192]{1,0:T(8,128)S(1)} %bitcast.166), channel_id=1, source_target_pairs={{0,2},{1,3},{2,0},{3,1},{4,6},{5,7},{6,4},{7,5},{8,10},{9,11},{10,... | collective-permute-start | bytes 110600 | tf_op jit(solution)/shard_map/ppermute | solution.py:152
  (87 shorter events, 65.1 us)
Async XLA Ops:
  0.6 64.9 %copy-start = (bf16[1,1,384,3072]{3,2,1,0:T(8,128)(2,1)S(1)}, bf16[1,1,384,3072]{3,2,1,0:T(8,128)(2,1)}, u32[]{:S(2)}) copy-start(bf16[1,1,384,3072]{3,2,1,0:T(8,128)(2,1)} %param.10) | copy-start | bytes 7077892
  2.2 33.5 %collective-permute-start = (bf16[2,384,768]{2,1,0:T(8,128)(2,1)S(1)}, bf16[2,384,768]{2,1,0:T(8,128)(2,1)S(1)}, u32[]{:S(2)}, u32[]{:S(2)}) collective-permute-start(bf16[2,384,768]{2,1,0:T(8,128)(2,1)S(1)} %pad_maximum_fusion.3), channel_id=1, source_target_pairs={{0,16},{4,20},{8,24},{12,28},{16,32},{20,36},{24,40},{28,44},{32,4... | collective-permute-start | bytes 3538952 | tf_op jit(solution)/shard_map/ppermute | solution.py:23
  6.0 50.5 %collective-permute-start.1 = (bf16[2,384,768]{2,1,0:T(8,128)(2,1)S(1)}, bf16[2,384,768]{2,1,0:T(8,128)(2,1)S(1)}, u32[]{:S(2)}, u32[]{:S(2)}) collective-permute-start(bf16[2,384,768]{2,1,0:T(8,128)(2,1)S(1)} %pad_maximum_fusion.3), channel_id=1, source_target_pairs={{16,0},{20,4},{24,8},{28,12},{32,16},{36,20},{40,24},{44,28},{48,3... | collective-permute-start | bytes 3538952 | tf_op jit(solution)/shard_map/ppermute | solution.py:23
  10.8 45.7 %collective-permute-start.2 = (bf16[2,384,768]{2,1,0:T(8,128)(2,1)S(1)}, bf16[2,384,768]{2,1,0:T(8,128)(2,1)}, u32[]{:S(2)}, u32[]{:S(2)}) collective-permute-start(bf16[2,384,768]{2,1,0:T(8,128)(2,1)S(1)} %pad_maximum_fusion.3), channel_id=1, source_target_pairs={{0,4},{4,8},{8,12},{16,20},{20,24},{24,28},{32,36},{36,40},{40,44}... | collective-permute-start | bytes 3538952 | tf_op jit(solution)/shard_map/ppermute | solution.py:23
  15.2 41.3 %collective-permute-start.3 = (bf16[2,384,768]{2,1,0:T(8,128)(2,1)S(1)}, bf16[2,384,768]{2,1,0:T(8,128)(2,1)}, u32[]{:S(2)}, u32[]{:S(2)}) collective-permute-start(bf16[2,384,768]{2,1,0:T(8,128)(2,1)S(1)} %pad_maximum_fusion.3), channel_id=1, source_target_pairs={{4,0},{8,4},{12,8},{20,16},{24,20},{28,24},{36,32},{40,36},{44,40}... | collective-permute-start | bytes 3538952 | tf_op jit(solution)/shard_map/ppermute | solution.py:23
  35.7 22.4 %copy-start.1 = (bf16[2,384,768]{2,1,0:T(8,128)(2,1)}, bf16[2,384,768]{2,1,0:T(8,128)(2,1)S(1)}, u32[]{:S(2)}) copy-start(bf16[2,384,768]{2,1,0:T(8,128)(2,1)S(1)} %collective-permute-done) | copy-start | bytes 3538948
  56.5 7.7 %copy-start.14 = (s32[1,5]{1,0:T(1,128)S(1)}, s32[1,5]{1,0:T(1,128)}, u32[]{:S(2)}) copy-start(s32[1,5]{1,0:T(1,128)} %param.9) | copy-start | bytes 64
  58.1 53.3 %collective-permute-start.4 = (bf16[2,2,384,768]{3,2,1,0:T(8,128)(2,1)}, bf16[2,2,384,768]{3,2,1,0:T(8,128)(2,1)}, u32[]{:S(2)}, u32[]{:S(2)}) collective-permute-start(bf16[2,2,384,768]{3,2,1,0:T(8,128)(2,1)} %pad_maximum_fusion), channel_id=1, source_target_pairs={{0,4},{4,8},{8,12},{16,20},{20,24},{24,28},{32,36},{36,40},{40,44}... | collective-permute-start | bytes 7077896 | tf_op jit(solution)/shard_map/ppermute | solution.py:23
  62.9 54.0 %collective-permute-start.5 = (bf16[2,2,384,768]{3,2,1,0:T(8,128)(2,1)}, bf16[2,2,384,768]{3,2,1,0:T(8,128)(2,1)}, u32[]{:S(2)}, u32[]{:S(2)}) collective-permute-start(bf16[2,2,384,768]{3,2,1,0:T(8,128)(2,1)} %pad_maximum_fusion), channel_id=1, source_target_pairs={{4,0},{8,4},{12,8},{20,16},{24,20},{28,24},{36,32},{40,36},{44,40}... | collective-permute-start | bytes 7077896 | tf_op jit(solution)/shard_map/ppermute | solution.py:23
  70.8 43.1 %copy-start.2 = (bf16[2,384,768]{2,1,0:T(8,128)(2,1)S(1)}, bf16[2,384,768]{2,1,0:T(8,128)(2,1)}, u32[]{:S(2)}) copy-start(bf16[2,384,768]{2,1,0:T(8,128)(2,1)} %copy-done.1) | copy-start | bytes 3538948
  115.0 6.7 %copy-start.11 = (bf16[1,1,384,768]{3,2,1,0:T(8,128)(2,1)S(1)}, bf16[1,1,384,768]{3,2,1,0:T(8,128)(2,1)}, u32[]{:S(2)}) copy-start(bf16[1,1,384,768]{3,2,1,0:T(8,128)(2,1)} %param.8) | copy-start | bytes 1769476
  115.0 6.7 %copy-start.12 = (bf16[1,1,384,768]{3,2,1,0:T(8,128)(2,1)S(1)}, bf16[1,1,384,768]{3,2,1,0:T(8,128)(2,1)}, u32[]{:S(2)}) copy-start(bf16[1,1,384,768]{3,2,1,0:T(8,128)(2,1)} %param.7) | copy-start | bytes 1769476
  173.7 35.0 %collective-permute-start.12 = (bf16[3072,384]{0,1:T(8,128)(2,1)}, bf16[3072,384]{0,1:T(8,128)(2,1)}, u32[]{:S(2)}, u32[]{:S(2)}) collective-permute-start(bf16[3072,384]{0,1:T(8,128)(2,1)} %fusion.1), channel_id=1, source_target_pairs={{0,1},{1,0},{2,3},{3,2},{4,5},{5,4},{6,7},{7,6},{8,9},{9,8},{10,11... | collective-permute-start | bytes 7077896 | tf_op jit(solution)/shard_map/ppermute | solution.py:140
  203.8 4.9 %copy-start.13 = (bf16[384,2,1,192]{0,3,2,1:T(8,128)(2,1)S(1)}, bf16[384,2,1,192]{0,3,2,1:T(8,128)(2,1)}, u32[]{:S(2)}) copy-start(bf16[384,2,1,192]{0,3,2,1:T(8,128)(2,1)} %get-tuple-element.56) | copy-start | bytes 884740
  203.8 72.1 %collective-permute-start.7 = (bf16[2,2,384,768]{3,2,1,0:T(8,128)(2,1)}, bf16[2,2,384,768]{3,2,1,0:T(8,128)(2,1)}, u32[]{:S(2)}, u32[]{:S(2)}) collective-permute-start(bf16[2,2,384,768]{3,2,1,0:T(8,128)(2,1)} %pad_maximum_fusion.2), channel_id=1, source_target_pairs={{0,4},{4,8},{8,12},{16,20},{20,24},{24,28},{32,36},{36,40},{40,44}... | collective-permute-start | bytes 7077896 | tf_op jit(solution)/shard_map/ppermute | solution.py:23
  217.5 155.1 %all-to-all-start = ((bf16[64,48,384]{2,1,0:T(8,128)(2,1)}), bf16[64,48,384]{2,1,0:T(8,128)(2,1)}, u32[]{:S(2)}, u32[]{:S(2)}) async-start(bf16[64,48,384]{2,1,0:T(8,128)(2,1)} %bitcast.154), calls=%async_computation | async-start | bytes 4718592 | tf_op jit(solution)/shard_map/all_to_all | solution.py:144
  230.6 3.3 copy-start.7
  230.6 3.3 copy-start.8
  230.6 75.2 %collective-permute-start.6 = (bf16[2,2,384,768]{3,2,1,0:T(8,128)(2,1)S(1)}, bf16[2,2,384,768]{3,2,1,0:T(8,128)(2,1)S(1)}, u32[]{:S(2)}, u32[]{:S(2)}) collective-permute-start(bf16[2,2,384,768]{3,2,1,0:T(8,128)(2,1)S(1)} %pad_maximum_fusion.1), channel_id=1, source_target_pairs={{4,0},{8,4},{12,8},{20,16},{24,20},{28,24},{36,32},{40,36},{44,40}... | collective-permute-start | bytes 7077896 | tf_op jit(solution)/shard_map/ppermute | solution.py:23
  311.6 32.2 %collective-permute-start.10 = (bf16[2,384,768]{2,1,0:T(8,128)(2,1)}, bf16[2,384,768]{2,1,0:T(8,128)(2,1)}, u32[]{:S(2)}, u32[]{:S(2)}) collective-permute-start(bf16[2,384,768]{2,1,0:T(8,128)(2,1)} %get-tuple-element.32), channel_id=1, source_target_pairs={{16,0},{20,4},{24,8},{28,12},{32,16},{36,20},{40,24},{44,28},{48,3... | collective-permute-start | bytes 3538952 | tf_op jit(solution)/shard_map/ppermute | solution.py:23
  317.0 51.4 %collective-permute-start.11 = (bf16[2,384,768]{2,1,0:T(8,128)(2,1)S(1)}, bf16[2,384,768]{2,1,0:T(8,128)(2,1)}, u32[]{:S(2)}, u32[]{:S(2)}) collective-permute-start(bf16[2,384,768]{2,1,0:T(8,128)(2,1)S(1)} %get-tuple-element.33), channel_id=1, source_target_pairs={{0,16},{4,20},{8,24},{12,28},{16,32},{20,36},{24,40},{28,44},{32,4... | collective-permute-start | bytes 3538952 | tf_op jit(solution)/shard_map/ppermute | solution.py:23
  319.0 49.5 %collective-permute-start.8 = (bf16[2,384,768]{2,1,0:T(8,128)(2,1)}, bf16[2,384,768]{2,1,0:T(8,128)(2,1)}, u32[]{:S(2)}, u32[]{:S(2)}) collective-permute-start(bf16[2,384,768]{2,1,0:T(8,128)(2,1)} %maximum_select_fusion.5), channel_id=1, source_target_pairs={{4,0},{8,4},{12,8},{20,16},{24,20},{28,24},{36,32},{40,36},{44,40}... | collective-permute-start | bytes 3538952 | tf_op jit(solution)/shard_map/ppermute | solution.py:23
  320.3 48.2 %collective-permute-start.9 = (bf16[2,384,768]{2,1,0:T(8,128)(2,1)}, bf16[2,384,768]{2,1,0:T(8,128)(2,1)}, u32[]{:S(2)}, u32[]{:S(2)}) collective-permute-start(bf16[2,384,768]{2,1,0:T(8,128)(2,1)} %maximum_select_fusion.6), channel_id=1, source_target_pairs={{0,4},{4,8},{8,12},{16,20},{20,24},{24,28},{32,36},{36,40},{40,44}... | collective-permute-start | bytes 3538952 | tf_op jit(solution)/shard_map/ppermute | solution.py:23
  378.0 9.1 %collective-permute-start.13 = (f32[48,192]{1,0:T(8,128)S(1)}, f32[48,192]{1,0:T(8,128)S(1)}, u32[]{:S(2)}, u32[]{:S(2)}) collective-permute-start(f32[48,192]{1,0:T(8,128)S(1)} %bitcast.166), channel_id=1, source_target_pairs={{0,2},{1,3},{2,0},{3,1},{4,6},{5,7},{6,4},{7,5},{8,10},{9,11},{10,... | collective-permute-start | bytes 110600 | tf_op jit(solution)/shard_map/ppermute | solution.py:152
  (7 other events, 15.3 us)

commit v6 on v5

--- a/solution.py
+++ b/solution.py
@@ -23,13 +23,35 @@
     return lax.ppermute(value, axis, pairs)
 
 
-def tile_attention(mask_ref, query_ref, key_ref, value_ref, grad_ref, attn_ref, dq_ref, dk_ref, dv_ref, *, score_scale):
+def tile_attention(mask_ref, query_ref, grad_ref, *refs, score_scale):
+    in_refs, out_refs = refs[:7], refs[7:]
+    attn_ref, dq_ref = out_refs[:2]
+
+    def by_direction(group):
+        earlier, own, later, left, right, rel_left, rel_right = group
+        return [
+            (rel_left, 0), (earlier, None), (rel_right, 0),
+            (left, None), (own, None), (right, None),
+            (rel_left, 1), (later, None), (rel_right, 1),
+        ]
+
+    def read(ref, pair, part):
+        return ref[part] if pair is None else ref[pair, part]
+
+    def write(ref, pair, part, block):
+        if pair is None:
+            ref[part] = block
+        else:
+            ref[pair, part] = block
+
+    directions = by_direction(in_refs)
+    out_directions = by_direction(out_refs[2:])
     rows_by_rows = (((1,), (1,)), ((), ()))
     cols_by_cols = (((0,), (0,)), ((), ()))
     query = query_ref[...]
-    key = key_ref[...]
-    value = value_ref[...]
     grad = grad_ref[...]
+    key = jnp.concatenate([read(ref, pair, 0) for ref, pair in directions], axis=0)
+    value = jnp.concatenate([read(ref, pair, 1) for ref, pair in directions], axis=0)
     scores = lax.dot_general(query, key, rows_by_rows, preferred_element_type=jnp.float32) * score_scale
     scores = jnp.where(mask_ref[...] > 0, scores, -1e30)
     row_peak = jnp.max(scores, axis=1, keepdims=True)
@@ -42,10 +64,15 @@
     dprobs = lax.dot_general(grad, value, rows_by_rows, preferred_element_type=jnp.float32)
     dscores = (probs * (dprobs - row_delta)).astype(jnp.bfloat16)
     dq_ref[...] = (jnp.dot(dscores, key, preferred_element_type=jnp.float32) * score_scale).astype(jnp.bfloat16)
-    dk_ref[...] = (
+    grad_key = (
         lax.dot_general(dscores, query, cols_by_cols, preferred_element_type=jnp.float32) * score_scale
     ).astype(jnp.bfloat16)
-    dv_ref[...] = lax.dot_general(probs_low, grad, cols_by_cols, preferred_element_type=jnp.float32).astype(jnp.bfloat16)
+    grad_value = lax.dot_general(probs_low, grad, cols_by_cols, preferred_element_type=jnp.float32).astype(jnp.bfloat16)
+    tile_tok = query.shape[0]
+    for number, (ref, pair) in enumerate(out_directions):
+        rows = slice(number * tile_tok, (number + 1) * tile_tok)
+        write(ref, pair, 0, grad_key[rows])
+        write(ref, pair, 1, grad_value[rows])
 
 
 def body(queries, keys, values, tile_lists, grad_out, w_out):
@@ -71,59 +98,55 @@
             shifted(key_value, 0, 1, False),
         )
     )
-    column = [earlier, key_value, later]
     relayed = jnp.stack([earlier, later])
-    side_own = {-1: left_own, 1: right_own}
     side_relayed = {step: shifted(relayed, 0, step, False) for step in (-1, 1)}
-    pieces = []
-    for time_step in (-1, 0, 1):
-        for height_step in (-1, 0, 1):
-            if height_step == 0:
-                pieces.append(column[time_step + 1])
-            elif time_step == 0:
-                pieces.append(side_own[height_step])
-            else:
-                pieces.append(side_relayed[height_step][(time_step + 1) // 2])
-    window = jnp.stack(pieces)
     valid_slot = listed >= 0
     time_gap = listed // height_tiles - own_tile // height_tiles
     height_gap = listed % height_tiles - own_tile % height_tiles
     slot_index = jnp.where(valid_slot, (time_gap + 1) * 3 + height_gap + 1, 4)
-    picked = jnp.take(window, slot_index, axis=0)
-    key_rows = picked[:, 0].reshape(slot_count * tile_tok, inner_width)
-    value_rows = picked[:, 1].reshape(slot_count * tile_tok, inner_width)
-    key_mask = jnp.repeat(valid_slot, tile_tok)
+    direction_count = 9
+    listed_direction = jnp.any(
+        (slot_index[:, None] == jnp.arange(direction_count, dtype=jnp.int32)[None, :]) & valid_slot[:, None],
+        axis=0,
+    )
+    key_count = direction_count * tile_tok
+    mask_row = jnp.repeat(listed_direction, tile_tok).astype(jnp.int32).reshape(1, key_count)
     grad_attn = lax.dot_general(
         grad_tile, w_out, (((1,), (1,)), ((), ())), preferred_element_type=jnp.float32
     ).astype(jnp.bfloat16)
-    key_count = slot_count * tile_tok
-    mask_row = key_mask.astype(jnp.int32).reshape(1, key_count)
     head_count = inner_width // HEAD
     tile_spec = pl.BlockSpec((tile_tok, HEAD), lambda head: (0, head))
-    key_spec = pl.BlockSpec((key_count, HEAD), lambda head: (0, head))
-    attn_all, grad_query, grad_key, grad_value = pl.pallas_call(
+    single_spec = pl.BlockSpec((2, tile_tok, HEAD), lambda head: (0, 0, head))
+    pair_spec = pl.BlockSpec((2, 2, tile_tok, HEAD), lambda head: (0, 0, 0, head))
+    group_specs = [single_spec] * 5 + [pair_spec] * 2
+    single_shape = jax.ShapeDtypeStruct((2, tile_tok, inner_width), jnp.bfloat16)
+    pair_shape = jax.ShapeDtypeStruct((2, 2, tile_tok, inner_width), jnp.bfloat16)
+    tile_shape = jax.ShapeDtypeStruct((tile_tok, inner_width), jnp.bfloat16)
+    outputs = pl.pallas_call(
         functools.partial(tile_attention, score_scale=score_scale),
         grid=(head_count,),
-        in_specs=[
-            pl.BlockSpec((1, key_count), lambda head: (0, 0)),
-            tile_spec,
-            key_spec,
-            key_spec,
-            tile_spec,
-        ],
-        out_specs=[tile_spec, tile_spec, key_spec, key_spec],
-        out_shape=[
-            jax.ShapeDtypeStruct((tile_tok, inner_width), jnp.bfloat16),
-            jax.ShapeDtypeStruct((tile_tok, inner_width), jnp.bfloat16),
-            jax.ShapeDtypeStruct((key_count, inner_width), jnp.bfloat16),
-            jax.ShapeDtypeStruct((key_count, inner_width), jnp.bfloat16),
-        ],
+        in_specs=[pl.BlockSpec((1, key_count), lambda head: (0, 0)), tile_spec, tile_spec, *group_specs],
+        out_specs=[tile_spec, tile_spec, *group_specs],
+        out_shape=[tile_shape, tile_shape, *[single_shape] * 5, *[pair_shape] * 2],
         cost_estimate=pl.CostEstimate(
             flops=2 * 5 * tile_tok * key_count * inner_width,
             transcendentals=head_count * tile_tok * key_count,
             bytes_accessed=2 * 2 * (2 * tile_tok + 2 * key_count) * inner_width,
         ),
-    )(mask_row, query_tile, key_rows, value_rows, grad_attn)
+    )(
+        mask_row,
+        query_tile,
+        grad_attn,
+        earlier,
+        key_value,
+        later,
+        left_own,
+        right_own,
+        side_relayed[-1],
+        side_relayed[1],
+    )
+    attn_all, grad_query = outputs[:2]
+    back_earlier, back_own, back_later, back_left, back_right, back_rel_left, back_rel_right = outputs[2:]
     dp_count = lax.axis_size("dp")
     sp_count = lax.axis_size("sp")
     dp_index = lax.axis_index("dp")
@@ -151,37 +174,17 @@
         own_half
         + lax.ppermute(other_half, "dp", [(index, (index + 2) % dp_count) for index in range(dp_count)])
     ).T
-    key_terms = grad_key.reshape(slot_count, tile_tok, inner_width)
-    value_terms = grad_value.reshape(slot_count, tile_tok, inner_width)
-    matches = (slot_index[:, None] == jnp.arange(9, dtype=jnp.int32)[None, :]) & valid_slot[:, None]
-    match_slot = jnp.argmax(matches, axis=0)
-    match_any = jnp.any(matches, axis=0)
-
-    def slot_payload(slot_number):
-        picked_slot = match_slot[slot_number]
-        payload = jnp.stack(
-            [
-                lax.dynamic_index_in_dim(key_terms, picked_slot, 0, keepdims=False),
-                lax.dynamic_index_in_dim(value_terms, picked_slot, 0, keepdims=False),
-            ]
-        )
-        return jnp.where(match_any[slot_number], payload, jnp.zeros_like(payload))
-
-    diagonal_sends = [
-        shifted(jnp.stack([slot_payload(step + 1), slot_payload(step + 7)]), 0, step, True)
-        for step in (-1, 1)
-    ]
-    own_row_parts = [slot_payload(step + 4) for step in (-1, 1)]
-    diagonal_in, own_row_parts = lax.optimization_barrier((diagonal_sends, own_row_parts))
+    diagonal_sends = [shifted(back_rel_left, 0, -1, True), shifted(back_rel_right, 0, 1, True)]
+    diagonal_in, own_row_parts = lax.optimization_barrier((diagonal_sends, [back_left, back_right]))
     diagonal_in = [part.astype(jnp.float32) for part in diagonal_in]
     row_in = [
         shifted(part, 0, step, True).astype(jnp.float32)
         for part, step in zip(own_row_parts, (-1, 1))
     ]
-    earlier_sum = slot_payload(1).astype(jnp.float32) + diagonal_in[0][0] + diagonal_in[1][0]
-    later_sum = slot_payload(7).astype(jnp.float32) + diagonal_in[0][1] + diagonal_in[1][1]
+    earlier_sum = back_earlier.astype(jnp.float32) + diagonal_in[0][0] + diagonal_in[1][0]
+    later_sum = back_later.astype(jnp.float32) + diagonal_in[0][1] + diagonal_in[1][1]
     grad_total = (
-        slot_payload(4).astype(jnp.float32)
+        back_own.astype(jnp.float32)
         + row_in[0]
         + row_in[1]
         + shifted(earlier_sum.astype(jnp.bfloat16), -1, 0, True).astype(jnp.float32)

time: 390 us -> 343 us (0.88)
  local copies, waits for them, and re-layouts: 47.6 us -> 13.9 us
  other arithmetic: 31.7 us -> 12.8 us
  between operations: 18.2 us -> 0.92 us
  Pallas kernels: 23.2 us -> 38 us
  waiting for transfers between devices: 197 us -> 209 us
    pallas_call x1, Pallas kernels: 23.2 us -> 38 us  [body(): pl.pallas_call(functools.partial(tile_attention, score_scale=score_scale)...]
    select_n x8 -> x1, other arithmetic: 11.3 us -> 0.02 us  [body(): slot_index = jnp.where(valid_slot, (time_gap + 1) * 3 + height_gap + 1, 4)]
    unnamed x42 -> x27, local copies, waits for them, and re-layouts: 15 us -> 4.41 us
    gather x1 -> x0, local copies, waits for them, and re-layouts: 7.99 us -> none  [body(): picked = jnp.take(window, slot_index, axis=0)]
    ppermute x12, waiting for transfers between devices: 195 us -> 203 us  [neighbour_shift(): return lax.ppermute(value, axis, pairs)]
    dynamic_slice x1 -> x0, local copies, waits for them, and re-layouts: 7.61 us -> none  [slot_payload(): lax.dynamic_index_in_dim(value_terms, picked_slot, 0, keepdims=False)]
    ppermute x1, waiting for transfers between devices: 0.01 us -> 4.52 us  [body(): lax.ppermute(sent_part.astype(jnp.bfloat16), 'dp', [(index, index ^ 1) fo...]
    slice x3 -> x0, local copies, waits for them, and re-layouts: 4.34 us -> none  [the longest x1 2.96 us: body(): value_rows = picked[:, 1].reshape(slot_count * tile_tok, inner_width)]
  transfers between devices with their start and end apart: 15 -> 15, of which waited for: 9 -> 9; matrix products, arithmetic and copies ran while one was open for 13% -> 4% of each run, Pallas kernels for 0% -> 0%
where the time goes in v6:
time: 343 us; the launch traced here: 342 us
  waiting for transfers between devices  209 us (61%)
  starting transfers between devices  57.8 us (17%)
  Pallas kernels  38 us (11%)
  local copies, waits for them, and re-layouts  13.9 us (4%)
  other arithmetic  12.8 us (4%)
  matrix products  9.45 us (3%)
    ppermute x12, waiting for transfers between devices, neighbour_shift(): return lax.ppermute(value, axis, pairs)  203 us
    ppermute x12, starting transfers between devices, neighbour_shift(): return lax.ppermute(value, axis, pairs)  39.8 us
    pallas_call x1, Pallas kernels, body(): pl.pallas_call(functools.partial(tile_attention, score_scale=score_scale)...  38 us
    all_to_all x1, starting transfers between devices, body(): lax.all_to_all(core_sum.reshape(sp_count, col_block, -1), 'sp', 0, 0, til...  10.8 us
    ppermute x1, starting transfers between devices, body(): lax.ppermute(other_half, 'dp', [(index, (index + 2) % dp_count) for index...  6.9 us
  transfers between devices with their start and end apart: 15, of which 9 were waited for; matrix products, arithmetic and copies ran while one was open for 4% of the time, Pallas kernels for 0%

profile of v6, /device:TPU:24, one launch (start us, length us, event | category | flops | bytes accessed | tf_op | source)
XLA Modules:
  0.0 341.7 jit_solution(13834525677989587512)
XLA Ops:
  2.2 3.8 %collective-permute-start = (bf16[2,384,768]{2,1,0:T(8,128)(2,1)S(1)}, bf16[2,384,768]{2,1,0:T(8,128)(2,1)S(1)}, u32[]{:S(2)}, u32[]{:S(2)}) collective-permute-start(bf16[2,384,768]{2,1,0:T(8,128)(2,1)S(1)} %pad_maximum_fusion.1.refs_1_), channel_id=1, source_target_pairs={{0,16},{4,20},{8,24},{12,28},{16,32},{20,36},{24,40},{28,44},{32,4... | collective-permute-start | bytes 3538952 | tf_op jit(solution)/shard_map/ppermute | solution.py:23
  6.0 4.8 %collective-permute-start.1 = (bf16[2,384,768]{2,1,0:T(8,128)(2,1)S(1)}, bf16[2,384,768]{2,1,0:T(8,128)(2,1)S(1)}, u32[]{:S(2)}, u32[]{:S(2)}) collective-permute-start(bf16[2,384,768]{2,1,0:T(8,128)(2,1)S(1)} %pad_maximum_fusion.1.refs_1_), channel_id=1, source_target_pairs={{16,0},{20,4},{24,8},{28,12},{32,16},{36,20},{40,24},{44,28},{48,3... | collective-permute-start | bytes 3538952 | tf_op jit(solution)/shard_map/ppermute | solution.py:23
  10.8 3.5 %collective-permute-start.2 = (bf16[2,384,768]{2,1,0:T(8,128)(2,1)S(1)}, bf16[2,384,768]{2,1,0:T(8,128)(2,1)S(1)}, u32[]{:S(2)}, u32[]{:S(2)}) collective-permute-start(bf16[2,384,768]{2,1,0:T(8,128)(2,1)S(1)} %pad_maximum_fusion.1.refs_1_), channel_id=1, source_target_pairs={{0,4},{4,8},{8,12},{16,20},{20,24},{24,28},{32,36},{36,40},{40,44}... | collective-permute-start | bytes 3538952 | tf_op jit(solution)/shard_map/ppermute | solution.py:23
  15.6 20.1 %collective-permute-done.refs_0_ = bf16[2,384,768]{2,1,0:T(8,128)(2,1)S(1)} collective-permute-done((bf16[2,384,768]{2,1,0:T(8,128)(2,1)S(1)}, bf16[2,384,768]{2,1,0:T(8,128)(2,1)S(1)}, u32[]{:S(2)}, u32[]{:S(2)}) %collective-permute-start) | collective-permute-done | bytes 1179680 | tf_op jit(solution)/shard_map/ppermute | solution.py:23
  35.7 20.8 %collective-permute-done.1.refs_2_ = bf16[2,384,768]{2,1,0:T(8,128)(2,1)S(1)} collective-permute-done((bf16[2,384,768]{2,1,0:T(8,128)(2,1)S(1)}, bf16[2,384,768]{2,1,0:T(8,128)(2,1)S(1)}, u32[]{:S(2)}, u32[]{:S(2)}) %collective-permute-start.1) | collective-permute-done | bytes 1179680 | tf_op jit(solution)/shard_map/ppermute | solution.py:23
  59.6 4.8 %collective-permute-start.4 = (bf16[2,2,384,768]{3,2,1,0:T(8,128)(2,1)}, bf16[2,2,384,768]{3,2,1,0:T(8,128)(2,1)}, u32[]{:S(2)}, u32[]{:S(2)}) collective-permute-start(bf16[2,2,384,768]{3,2,1,0:T(8,128)(2,1)} %pad_maximum_fusion), channel_id=1, source_target_pairs={{0,4},{4,8},{8,12},{16,20},{20,24},{24,28},{32,36},{36,40},{40,44}... | collective-permute-start | bytes 7077896 | tf_op jit(solution)/shard_map/ppermute | solution.py:23
  66.6 5.2 %fusion.12.grad_ref = bf16[384,768]{1,0:T(8,128)(2,1)} fusion(bf16[768,3072]{1,0:T(8,128)(2,1)} %param.11, bf16[1,1,384,3072]{3,2,1,0:T(8,128)(2,1)S(1)} %copy-done), kind=kOutput, calls=%fused_computation.21 | convolution fusion | flops 1812234240 | bytes 7667712 | tf_op jit(solution)/shard_map/dot_general | solution.py:114
  71.8 41.2 %collective-permute-done.4.refs_5_ = bf16[2,2,384,768]{3,2,1,0:T(8,128)(2,1)} collective-permute-done((bf16[2,2,384,768]{3,2,1,0:T(8,128)(2,1)}, bf16[2,2,384,768]{3,2,1,0:T(8,128)(2,1)}, u32[]{:S(2)}, u32[]{:S(2)}) %collective-permute-start.4) | collective-permute-done | bytes 2359328 | tf_op jit(solution)/shard_map/ppermute | solution.py:23
  112.9 5.5 %collective-permute-done.5.refs_6_ = bf16[2,2,384,768]{3,2,1,0:T(8,128)(2,1)} collective-permute-done((bf16[2,2,384,768]{3,2,1,0:T(8,128)(2,1)}, bf16[2,2,384,768]{3,2,1,0:T(8,128)(2,1)}, u32[]{:S(2)}, u32[]{:S(2)}) %collective-permute-start.5) | collective-permute-done | bytes 2359328 | tf_op jit(solution)/shard_map/ppermute | solution.py:23
  118.5 38.0 %shard_map.93 = (bf16[384,768]{1,0:T(8,128)(2,1)}, bf16[384,768]{1,0:T(8,128)(2,1)}, bf16[2,384,768]{2,1,0:T(8,128)(2,1)}, bf16[2,384,768]{2,1,0:T(8,128)(2,1)},...) custom-call(s32[1,3456]{1,0:T(1,128)} %bitcast.93, ...), custom_call_target="tpu_custom_call" | custom-call | flops 10192158720 | bytes 23592960 | tf_op jit(solution)/shard_map/pallas_call | solution.py:125
  159.6 4.5 %collective-permute-done.12 = bf16[3072,384]{0,1:T(8,128)(2,1)S(1)} collective-permute-done((bf16[3072,384]{0,1:T(8,128)(2,1)S(1)}, bf16[3072,384]{0,1:T(8,128)(2,1)S(1)}, u32[]{:S(2)}, u32[]{:S(2)}) %collective-permute-start.12) | collective-permute-done | bytes 2359328 | tf_op jit(solution)/shard_map/ppermute | solution.py:163
  164.2 2.9 fusion
  167.0 4.3 %copy.13 = bf16[3072,384]{1,0:T(8,128)(2,1)} copy(bf16[3072,384]{0,1:T(8,128)(2,1)} %fusion) | data formatting | bytes 4718592 | tf_op jit(solution)/shard_map/convert_element_type | solution.py:166
  171.3 10.8 %all-to-all-start = ((bf16[64,48,384]{2,1,0:T(8,128)(2,1)}), bf16[64,48,384]{2,1,0:T(8,128)(2,1)}, u32[]{:S(2)}, u32[]{:S(2)}) async-start(bf16[64,48,384]{2,1,0:T(8,128)(2,1)} %bitcast.19), calls=%async_computation | async-start | bytes 4718592 | tf_op jit(solution)/shard_map/all_to_all | solution.py:167
  183.4 4.7 %collective-permute-start.7 = (bf16[2,2,384,768]{3,2,1,0:T(8,128)(2,1)}, bf16[2,2,384,768]{3,2,1,0:T(8,128)(2,1)S(1)}, u32[]{:S(2)}, u32[]{:S(2)}) collective-permute-start(bf16[2,2,384,768]{3,2,1,0:T(8,128)(2,1)} %get-tuple-element.28), channel_id=1, source_target_pairs={{0,4},{4,8},{8,12},{16,20},{20,24},{24,28},{32,36},{36,40},{40,44}... | collective-permute-start | bytes 7077896 | tf_op jit(solution)/shard_map/ppermute | solution.py:23
  188.1 71.4 %collective-permute-done.6 = bf16[2,2,384,768]{3,2,1,0:T(8,128)(2,1)S(1)} collective-permute-done((bf16[2,2,384,768]{3,2,1,0:T(8,128)(2,1)}, bf16[2,2,384,768]{3,2,1,0:T(8,128)(2,1)S(1)}, u32[]{:S(2)}, u32[]{:S(2)}) %collective-permute-start.6) | collective-permute-done | bytes 2359328 | tf_op jit(solution)/shard_map/ppermute | solution.py:23
  263.5 5.4 %collective-permute-start.10 = (bf16[2,384,768]{2,1,0:T(8,128)(2,1)}, bf16[2,384,768]{2,1,0:T(8,128)(2,1)S(1)}, u32[]{:S(2)}, u32[]{:S(2)}) collective-permute-start(bf16[2,384,768]{2,1,0:T(8,128)(2,1)} %get-tuple-element.38), channel_id=1, source_target_pairs={{16,0},{20,4},{24,8},{28,12},{32,16},{36,20},{40,24},{44,28},{48,3... | collective-permute-start | bytes 3538952 | tf_op jit(solution)/shard_map/ppermute | solution.py:23
  268.9 1.9 collective-permute-start.11
  272.2 5.6 %collective-permute-start.9 = (bf16[2,384,768]{2,1,0:T(8,128)(2,1)}, bf16[2,384,768]{2,1,0:T(8,128)(2,1)}, u32[]{:S(2)}, u32[]{:S(2)}) collective-permute-start(bf16[2,384,768]{2,1,0:T(8,128)(2,1)} %get-tuple-element.32), channel_id=1, source_target_pairs={{0,4},{4,8},{8,12},{16,20},{20,24},{24,28},{32,36},{36,40},{40,44}... | collective-permute-start | bytes 3538952 | tf_op jit(solution)/shard_map/ppermute | solution.py:23
  277.7 17.9 %collective-permute-done.10 = bf16[2,384,768]{2,1,0:T(8,128)(2,1)S(1)} collective-permute-done((bf16[2,384,768]{2,1,0:T(8,128)(2,1)}, bf16[2,384,768]{2,1,0:T(8,128)(2,1)S(1)}, u32[]{:S(2)}, u32[]{:S(2)}) %collective-permute-start.10) | collective-permute-done | bytes 1179680 | tf_op jit(solution)/shard_map/ppermute | solution.py:23
  295.7 26.3 %collective-permute-done.11 = bf16[2,384,768]{2,1,0:T(8,128)(2,1)S(1)} collective-permute-done((bf16[2,384,768]{2,1,0:T(8,128)(2,1)S(1)}, bf16[2,384,768]{2,1,0:T(8,128)(2,1)S(1)}, u32[]{:S(2)}, u32[]{:S(2)}) %collective-permute-start.11) | collective-permute-done | bytes 1179680 | tf_op jit(solution)/shard_map/ppermute | solution.py:23
  323.1 3.6 %add_convert_fusion = bf16[2,384,768]{2,1,0:T(8,128)(2,1)S(1)} fusion(bf16[2,384,768]{2,1,0:T(8,128)(2,1)} %copy-done.5, bf16[2,384,768]{2,1,0:T(8,128)(2,1)} %copy-done.4, bf16[2,384,768]{2,1,0:T(8,128)(2,1)} %collective-permute-done.9, bf16[2,384,768]{2,1,0:T(8,128)(2,1)} %collective-permute-done.8, bf16[2,384,768]{2,1,0:T(8,128)(2,1)} %get-tuple-element.26), kind=kLoop, calls=%fused_computation.20 | loop fusion | flops 5898240 | bytes 7077888 | tf_op jit(solution)/shard_map/convert_element_type | solution.py:193
  326.7 2.6 convert_reduce_fusion
  332.1 6.9 %collective-permute-start.13 = (f32[48,192]{1,0:T(8,128)S(1)}, f32[48,192]{1,0:T(8,128)S(1)}, u32[]{:S(2)}, u32[]{:S(2)}) collective-permute-start(f32[48,192]{1,0:T(8,128)S(1)} %bitcast.92), channel_id=1, source_target_pairs={{0,2},{1,3},{2,0},{3,1},{4,6},{5,7},{6,4},{7,5},{8,10},{9,11},{10,... | collective-permute-start | bytes 110600 | tf_op jit(solution)/shard_map/ppermute | solution.py:175
  (55 shorter events, 24.1 us)
Async XLA Ops:
  0.6 66.0 %copy-start = (bf16[1,1,384,3072]{3,2,1,0:T(8,128)(2,1)S(1)}, bf16[1,1,384,3072]{3,2,1,0:T(8,128)(2,1)}, u32[]{:S(2)}) copy-start(bf16[1,1,384,3072]{3,2,1,0:T(8,128)(2,1)} %param.10) | copy-start | bytes 7077892
  2.2 57.5 %copy-start.6 = (bf16[2,384,768]{2,1,0:T(8,128)(2,1)}, bf16[2,384,768]{2,1,0:T(8,128)(2,1)S(1)}, u32[]{:S(2)}) copy-start(bf16[2,384,768]{2,1,0:T(8,128)(2,1)S(1)} %pad_maximum_fusion.1.refs_1_) | copy-start | bytes 3538948
  2.2 33.5 %collective-permute-start = (bf16[2,384,768]{2,1,0:T(8,128)(2,1)S(1)}, bf16[2,384,768]{2,1,0:T(8,128)(2,1)S(1)}, u32[]{:S(2)}, u32[]{:S(2)}) collective-permute-start(bf16[2,384,768]{2,1,0:T(8,128)(2,1)S(1)} %pad_maximum_fusion.1.refs_1_), channel_id=1, source_target_pairs={{0,16},{4,20},{8,24},{12,28},{16,32},{20,36},{24,40},{28,44},{32,4... | collective-permute-start | bytes 3538952 | tf_op jit(solution)/shard_map/ppermute | solution.py:23
  6.0 50.5 %collective-permute-start.1 = (bf16[2,384,768]{2,1,0:T(8,128)(2,1)S(1)}, bf16[2,384,768]{2,1,0:T(8,128)(2,1)S(1)}, u32[]{:S(2)}, u32[]{:S(2)}) collective-permute-start(bf16[2,384,768]{2,1,0:T(8,128)(2,1)S(1)} %pad_maximum_fusion.1.refs_1_), channel_id=1, source_target_pairs={{16,0},{20,4},{24,8},{28,12},{32,16},{36,20},{40,24},{44,28},{48,3... | collective-permute-start | bytes 3538952 | tf_op jit(solution)/shard_map/ppermute | solution.py:23
  10.8 45.7 %collective-permute-start.2 = (bf16[2,384,768]{2,1,0:T(8,128)(2,1)S(1)}, bf16[2,384,768]{2,1,0:T(8,128)(2,1)S(1)}, u32[]{:S(2)}, u32[]{:S(2)}) collective-permute-start(bf16[2,384,768]{2,1,0:T(8,128)(2,1)S(1)} %pad_maximum_fusion.1.refs_1_), channel_id=1, source_target_pairs={{0,4},{4,8},{8,12},{16,20},{20,24},{24,28},{32,36},{36,40},{40,44}... | collective-permute-start | bytes 3538952 | tf_op jit(solution)/shard_map/ppermute | solution.py:23
  14.3 42.2 %collective-permute-start.3 = (bf16[2,384,768]{2,1,0:T(8,128)(2,1)S(1)}, bf16[2,384,768]{2,1,0:T(8,128)(2,1)S(1)}, u32[]{:S(2)}, u32[]{:S(2)}) collective-permute-start(bf16[2,384,768]{2,1,0:T(8,128)(2,1)S(1)} %pad_maximum_fusion.1.refs_1_), channel_id=1, source_target_pairs={{4,0},{8,4},{12,8},{20,16},{24,20},{28,24},{36,32},{40,36},{44,40}... | collective-permute-start | bytes 3538952 | tf_op jit(solution)/shard_map/ppermute | solution.py:23
  35.7 23.9 %copy-start.7 = (bf16[2,384,768]{2,1,0:T(8,128)(2,1)}, bf16[2,384,768]{2,1,0:T(8,128)(2,1)S(1)}, u32[]{:S(2)}) copy-start(bf16[2,384,768]{2,1,0:T(8,128)(2,1)S(1)} %collective-permute-done.refs_0_) | copy-start | bytes 3538948
  56.5 3.1 copy-start.8
  56.5 1.4 copy-start.11
  58.0 7.8 %copy-start.9 = (s32[1,5]{1,0:T(1,128)S(1)}, s32[1,5]{1,0:T(1,128)}, u32[]{:S(2)}) copy-start(s32[1,5]{1,0:T(1,128)} %param.9) | copy-start | bytes 64
  59.6 53.3 %collective-permute-start.4 = (bf16[2,2,384,768]{3,2,1,0:T(8,128)(2,1)}, bf16[2,2,384,768]{3,2,1,0:T(8,128)(2,1)}, u32[]{:S(2)}, u32[]{:S(2)}) collective-permute-start(bf16[2,2,384,768]{3,2,1,0:T(8,128)(2,1)} %pad_maximum_fusion), channel_id=1, source_target_pairs={{0,4},{4,8},{8,12},{16,20},{20,24},{24,28},{32,36},{36,40},{40,44}... | collective-permute-start | bytes 7077896 | tf_op jit(solution)/shard_map/ppermute | solution.py:23
  64.4 54.0 %collective-permute-start.5 = (bf16[2,2,384,768]{3,2,1,0:T(8,128)(2,1)}, bf16[2,2,384,768]{3,2,1,0:T(8,128)(2,1)}, u32[]{:S(2)}, u32[]{:S(2)}) collective-permute-start(bf16[2,2,384,768]{3,2,1,0:T(8,128)(2,1)} %pad_maximum_fusion), channel_id=1, source_target_pairs={{4,0},{8,4},{12,8},{20,16},{24,20},{28,24},{36,32},{40,36},{44,40}... | collective-permute-start | bytes 7077896 | tf_op jit(solution)/shard_map/ppermute | solution.py:23
  159.3 4.8 %collective-permute-start.12 = (bf16[3072,384]{0,1:T(8,128)(2,1)S(1)}, bf16[3072,384]{0,1:T(8,128)(2,1)S(1)}, u32[]{:S(2)}, u32[]{:S(2)}) collective-permute-start(bf16[3072,384]{0,1:T(8,128)(2,1)S(1)} %fusion.1), channel_id=1, source_target_pairs={{0,1},{1,0},{2,3},{3,2},{4,5},{5,4},{6,7},{7,6},{8,9},{9,8},{10,11... | collective-permute-start | bytes 7077896 | tf_op jit(solution)/shard_map/ppermute | solution.py:163
  171.3 155.4 %all-to-all-start = ((bf16[64,48,384]{2,1,0:T(8,128)(2,1)}), bf16[64,48,384]{2,1,0:T(8,128)(2,1)}, u32[]{:S(2)}, u32[]{:S(2)}) async-start(bf16[64,48,384]{2,1,0:T(8,128)(2,1)} %bitcast.19), calls=%async_computation | async-start | bytes 4718592 | tf_op jit(solution)/shard_map/all_to_all | solution.py:167
  182.1 77.4 %collective-permute-start.6 = (bf16[2,2,384,768]{3,2,1,0:T(8,128)(2,1)}, bf16[2,2,384,768]{3,2,1,0:T(8,128)(2,1)S(1)}, u32[]{:S(2)}, u32[]{:S(2)}) collective-permute-start(bf16[2,2,384,768]{3,2,1,0:T(8,128)(2,1)} %get-tuple-element.27), channel_id=1, source_target_pairs={{4,0},{8,4},{12,8},{20,16},{24,20},{28,24},{36,32},{40,36},{44,40}... | collective-permute-start | bytes 7077896 | tf_op jit(solution)/shard_map/ppermute | solution.py:23
  183.4 76.1 %collective-permute-start.7 = (bf16[2,2,384,768]{3,2,1,0:T(8,128)(2,1)}, bf16[2,2,384,768]{3,2,1,0:T(8,128)(2,1)S(1)}, u32[]{:S(2)}, u32[]{:S(2)}) collective-permute-start(bf16[2,2,384,768]{3,2,1,0:T(8,128)(2,1)} %get-tuple-element.28), channel_id=1, source_target_pairs={{0,4},{4,8},{8,12},{16,20},{20,24},{24,28},{32,36},{36,40},{40,44}... | collective-permute-start | bytes 7077896 | tf_op jit(solution)/shard_map/ppermute | solution.py:23
  260.0 1.6 copy-start.3
  263.5 32.2 %collective-permute-start.10 = (bf16[2,384,768]{2,1,0:T(8,128)(2,1)}, bf16[2,384,768]{2,1,0:T(8,128)(2,1)S(1)}, u32[]{:S(2)}, u32[]{:S(2)}) collective-permute-start(bf16[2,384,768]{2,1,0:T(8,128)(2,1)} %get-tuple-element.38), channel_id=1, source_target_pairs={{16,0},{20,4},{24,8},{28,12},{32,16},{36,20},{40,24},{44,28},{48,3... | collective-permute-start | bytes 3538952 | tf_op jit(solution)/shard_map/ppermute | solution.py:23
  268.9 53.1 %collective-permute-start.11 = (bf16[2,384,768]{2,1,0:T(8,128)(2,1)S(1)}, bf16[2,384,768]{2,1,0:T(8,128)(2,1)S(1)}, u32[]{:S(2)}, u32[]{:S(2)}) collective-permute-start(bf16[2,384,768]{2,1,0:T(8,128)(2,1)S(1)} %get-tuple-element.39), channel_id=1, source_target_pairs={{0,16},{4,20},{8,24},{12,28},{16,32},{20,36},{24,40},{28,44},{32,4... | collective-permute-start | bytes 3538952 | tf_op jit(solution)/shard_map/ppermute | solution.py:23
  270.9 51.2 %collective-permute-start.8 = (bf16[2,384,768]{2,1,0:T(8,128)(2,1)}, bf16[2,384,768]{2,1,0:T(8,128)(2,1)}, u32[]{:S(2)}, u32[]{:S(2)}) collective-permute-start(bf16[2,384,768]{2,1,0:T(8,128)(2,1)} %get-tuple-element.31), channel_id=1, source_target_pairs={{4,0},{8,4},{12,8},{20,16},{24,20},{28,24},{36,32},{40,36},{44,40}... | collective-permute-start | bytes 3538952 | tf_op jit(solution)/shard_map/ppermute | solution.py:23
  272.2 49.9 %collective-permute-start.9 = (bf16[2,384,768]{2,1,0:T(8,128)(2,1)}, bf16[2,384,768]{2,1,0:T(8,128)(2,1)}, u32[]{:S(2)}, u32[]{:S(2)}) collective-permute-start(bf16[2,384,768]{2,1,0:T(8,128)(2,1)} %get-tuple-element.32), channel_id=1, source_target_pairs={{0,4},{4,8},{8,12},{16,20},{20,24},{24,28},{32,36},{36,40},{40,44}... | collective-permute-start | bytes 3538952 | tf_op jit(solution)/shard_map/ppermute | solution.py:23
  295.7 26.3 %copy-start.4 = (bf16[2,384,768]{2,1,0:T(8,128)(2,1)}, bf16[2,384,768]{2,1,0:T(8,128)(2,1)S(1)}, u32[]{:S(2)}) copy-start(bf16[2,384,768]{2,1,0:T(8,128)(2,1)S(1)} %collective-permute-done.10) | copy-start | bytes 3538948
  323.1 18.6 %copy-start.1 = (bf16[1,1,384,3072]{3,2,1,0:T(8,128)(2,1)S(1)}, bf16[1,1,384,3072]{3,2,1,0:T(8,128)(2,1)}, u32[]{:S(2)}) copy-start(bf16[1,1,384,3072]{3,2,1,0:T(8,128)(2,1)} %param.10) | copy-start | bytes 7077892
  332.1 9.0 %collective-permute-start.13 = (f32[48,192]{1,0:T(8,128)S(1)}, f32[48,192]{1,0:T(8,128)S(1)}, u32[]{:S(2)}, u32[]{:S(2)}) collective-permute-start(f32[48,192]{1,0:T(8,128)S(1)} %bitcast.92), channel_id=1, source_target_pairs={{0,2},{1,3},{2,0},{3,1},{4,6},{5,7},{6,4},{7,5},{8,10},{9,11},{10,... | collective-permute-start | bytes 110600 | tf_op jit(solution)/shard_map/ppermute | solution.py:175
  (3 other events, 3.4 us)

commit v7 on v6

--- a/solution.py
+++ b/solution.py
@@ -24,34 +24,15 @@
 
 
 def tile_attention(mask_ref, query_ref, grad_ref, *refs, score_scale):
-    in_refs, out_refs = refs[:7], refs[7:]
-    attn_ref, dq_ref = out_refs[:2]
-
-    def by_direction(group):
-        earlier, own, later, left, right, rel_left, rel_right = group
-        return [
-            (rel_left, 0), (earlier, None), (rel_right, 0),
-            (left, None), (own, None), (right, None),
-            (rel_left, 1), (later, None), (rel_right, 1),
-        ]
-
-    def read(ref, pair, part):
-        return ref[part] if pair is None else ref[pair, part]
-
-    def write(ref, pair, part, block):
-        if pair is None:
-            ref[part] = block
-        else:
-            ref[pair, part] = block
-
-    directions = by_direction(in_refs)
-    out_directions = by_direction(out_refs[2:])
+    directions = refs[:9]
+    attn_ref, dq_ref = refs[9:11]
+    out_directions = refs[11:]
     rows_by_rows = (((1,), (1,)), ((), ()))
     cols_by_cols = (((0,), (0,)), ((), ()))
     query = query_ref[...]
     grad = grad_ref[...]
-    key = jnp.concatenate([read(ref, pair, 0) for ref, pair in directions], axis=0)
-    value = jnp.concatenate([read(ref, pair, 1) for ref, pair in directions], axis=0)
+    key = jnp.concatenate([ref[0] for ref in directions], axis=0)
+    value = jnp.concatenate([ref[1] for ref in directions], axis=0)
     scores = lax.dot_general(query, key, rows_by_rows, preferred_element_type=jnp.float32) * score_scale
     scores = jnp.where(mask_ref[...] > 0, scores, -1e30)
     row_peak = jnp.max(scores, axis=1, keepdims=True)
@@ -69,10 +50,10 @@
     ).astype(jnp.bfloat16)
     grad_value = lax.dot_general(probs_low, grad, cols_by_cols, preferred_element_type=jnp.float32).astype(jnp.bfloat16)
     tile_tok = query.shape[0]
-    for number, (ref, pair) in enumerate(out_directions):
+    for number, ref in enumerate(out_directions):
         rows = slice(number * tile_tok, (number + 1) * tile_tok)
-        write(ref, pair, 0, grad_key[rows])
-        write(ref, pair, 1, grad_value[rows])
+        ref[0] = grad_key[rows]
+        ref[1] = grad_value[rows]
 
 
 def body(queries, keys, values, tile_lists, grad_out, w_out):
@@ -90,16 +71,19 @@
     def shifted(value, time_step, height_step, toward):
         return neighbour_shift(value, "sp", time_step, height_step, height_tiles, toward)
 
-    earlier, later, left_own, right_own = lax.optimization_barrier(
+    earlier, left_own, right_own = lax.optimization_barrier(
         (
             shifted(key_value, -1, 0, False),
-            shifted(key_value, 1, 0, False),
             shifted(key_value, 0, -1, False),
             shifted(key_value, 0, 1, False),
         )
     )
-    relayed = jnp.stack([earlier, later])
-    side_relayed = {step: shifted(relayed, 0, step, False) for step in (-1, 1)}
+    later = shifted(key_value, 1, 0, False)
+    gathered = [
+        shifted(earlier, 0, -1, False), earlier, shifted(earlier, 0, 1, False),
+        left_own, key_value, right_own,
+        shifted(later, 0, -1, False), later, shifted(later, 0, 1, False),
+    ]
     valid_slot = listed >= 0
     time_gap = listed // height_tiles - own_tile // height_tiles
     height_gap = listed % height_tiles - own_tile % height_tiles
@@ -117,17 +101,14 @@
     head_count = inner_width // HEAD
     tile_spec = pl.BlockSpec((tile_tok, HEAD), lambda head: (0, head))
     single_spec = pl.BlockSpec((2, tile_tok, HEAD), lambda head: (0, 0, head))
-    pair_spec = pl.BlockSpec((2, 2, tile_tok, HEAD), lambda head: (0, 0, 0, head))
-    group_specs = [single_spec] * 5 + [pair_spec] * 2
     single_shape = jax.ShapeDtypeStruct((2, tile_tok, inner_width), jnp.bfloat16)
-    pair_shape = jax.ShapeDtypeStruct((2, 2, tile_tok, inner_width), jnp.bfloat16)
     tile_shape = jax.ShapeDtypeStruct((tile_tok, inner_width), jnp.bfloat16)
     outputs = pl.pallas_call(
         functools.partial(tile_attention, score_scale=score_scale),
         grid=(head_count,),
-        in_specs=[pl.BlockSpec((1, key_count), lambda head: (0, 0)), tile_spec, tile_spec, *group_specs],
-        out_specs=[tile_spec, tile_spec, *group_specs],
-        out_shape=[tile_shape, tile_shape, *[single_shape] * 5, *[pair_shape] * 2],
+        in_specs=[pl.BlockSpec((1, key_count), lambda head: (0, 0)), tile_spec, tile_spec, *[single_spec] * direction_count],
+        out_specs=[tile_spec, tile_spec, *[single_spec] * direction_count],
+        out_shape=[tile_shape, tile_shape, *[single_shape] * direction_count],
         cost_estimate=pl.CostEstimate(
             flops=2 * 5 * tile_tok * key_count * inner_width,
             transcendentals=head_count * tile_tok * key_count,
@@ -137,16 +118,10 @@
         mask_row,
         query_tile,
         grad_attn,
-        earlier,
-        key_value,
-        later,
-        left_own,
-        right_own,
-        side_relayed[-1],
-        side_relayed[1],
+        *gathered,
     )
     attn_all, grad_query = outputs[:2]
-    back_earlier, back_own, back_later, back_left, back_right, back_rel_left, back_rel_right = outputs[2:]
+    back = outputs[2:]
     dp_count = lax.axis_size("dp")
     sp_count = lax.axis_size("sp")
     dp_index = lax.axis_index("dp")
@@ -174,21 +149,20 @@
         own_half
         + lax.ppermute(other_half, "dp", [(index, (index + 2) % dp_count) for index in range(dp_count)])
     ).T
-    diagonal_sends = [shifted(back_rel_left, 0, -1, True), shifted(back_rel_right, 0, 1, True)]
-    diagonal_in, own_row_parts = lax.optimization_barrier((diagonal_sends, [back_left, back_right]))
-    diagonal_in = [part.astype(jnp.float32) for part in diagonal_in]
-    row_in = [
-        shifted(part, 0, step, True).astype(jnp.float32)
-        for part, step in zip(own_row_parts, (-1, 1))
-    ]
-    earlier_sum = back_earlier.astype(jnp.float32) + diagonal_in[0][0] + diagonal_in[1][0]
-    later_sum = back_later.astype(jnp.float32) + diagonal_in[0][1] + diagonal_in[1][1]
+    early_in = [shifted(back[0], 0, -1, True), shifted(back[2], 0, 1, True)]
+    early_in, late_out, row_out = lax.optimization_barrier((early_in, [back[6], back[8]], [back[3], back[5]]))
+    earlier_sum = back[1].astype(jnp.float32) + early_in[0].astype(jnp.float32) + early_in[1].astype(jnp.float32)
+    from_later = shifted(earlier_sum.astype(jnp.bfloat16), -1, 0, True)
+    late_in = [shifted(late_out[0], 0, -1, True), shifted(late_out[1], 0, 1, True)]
+    row_in = [shifted(part, 0, step, True) for part, step in zip(row_out, (-1, 1))]
+    later_sum = back[7].astype(jnp.float32) + late_in[0].astype(jnp.float32) + late_in[1].astype(jnp.float32)
+    from_earlier = shifted(later_sum.astype(jnp.bfloat16), 1, 0, True)
     grad_total = (
-        back_own.astype(jnp.float32)
-        + row_in[0]
-        + row_in[1]
-        + shifted(earlier_sum.astype(jnp.bfloat16), -1, 0, True).astype(jnp.float32)
-        + shifted(later_sum.astype(jnp.bfloat16), 1, 0, True).astype(jnp.float32)
+        back[4].astype(jnp.float32)
+        + row_in[0].astype(jnp.float32)
+        + row_in[1].astype(jnp.float32)
+        + from_later.astype(jnp.float32)
+        + from_earlier.astype(jnp.float32)
     )
     grad_kv = grad_total.astype(jnp.bfloat16)
     return (grad_query[None, None], grad_kv[0][None, None], grad_kv[1][None, None], weight_grad)

time: 343 us -> 303 us (0.88)
  waiting for transfers between devices: 209 us -> 162 us
  starting transfers between devices: 57.8 us -> 70.1 us
  local copies, waits for them, and re-layouts: 13.9 us -> 10.2 us
    ppermute x12 -> x16, waiting for transfers between devices: 203 us -> 150 us  [neighbour_shift(): return lax.ppermute(value, axis, pairs)]
    ppermute x12 -> x16, starting transfers between devices: 39.8 us -> 52.3 us  [neighbour_shift(): return lax.ppermute(value, axis, pairs)]
    ppermute x1, starting transfers between devices: 6.9 us -> 0.09 us  [body(): lax.ppermute(other_half, 'dp', [(index, (index + 2) % dp_count) for index...]
    all_to_all x1, starting transfers between devices: 10.8 us -> 17.4 us  [body(): lax.all_to_all(core_sum.reshape(sp_count, col_block, -1), 'sp', 0, 0, til...]
    ppermute x1, waiting for transfers between devices: 0.98 us -> 6.9 us  [body(): lax.ppermute(other_half, 'dp', [(index, (index + 2) % dp_count) for index...]
    unnamed x27 -> x15, local copies, waits for them, and re-layouts: 4.41 us -> 0.72 us
  transfers between devices with their start and end apart: 15 -> 19, of which waited for: 9 -> 16; matrix products, arithmetic and copies ran while one was open for 4% -> 4% of each run, Pallas kernels for 0% -> 0%
where the time goes in v7:
time: 303 us; the launch traced here: 302 us
  waiting for transfers between devices  162 us (53%)
  starting transfers between devices  70.1 us (23%)
  Pallas kernels  38 us (13%)
  other arithmetic  11.3 us (4%)
  local copies, waits for them, and re-layouts  10.2 us (3%)
  matrix products  9.44 us (3%)
    ppermute x16, waiting for transfers between devices, neighbour_shift(): return lax.ppermute(value, axis, pairs)  150 us
    ppermute x16, starting transfers between devices, neighbour_shift(): return lax.ppermute(value, axis, pairs)  52.3 us
    pallas_call x1, Pallas kernels, body(): pl.pallas_call(functools.partial(tile_attention, score_scale=score_scale)...  38 us
    all_to_all x1, starting transfers between devices, body(): lax.all_to_all(core_sum.reshape(sp_count, col_block, -1), 'sp', 0, 0, til...  17.4 us
    ppermute x1, waiting for transfers between devices, body(): lax.ppermute(other_half, 'dp', [(index, (index + 2) % dp_count) for index...  6.9 us
  transfers between devices with their start and end apart: 19, of which 16 were waited for; matrix products, arithmetic and copies ran while one was open for 4% of the time, Pallas kernels for 0%

profile of v7, /device:TPU:24, one launch (start us, length us, event | category | flops | bytes accessed | tf_op | source)
XLA Modules:
  0.0 301.8 jit_solution(12147260894626723176)
XLA Ops:
  2.2 3.8 %collective-permute-start = (bf16[2,384,768]{2,1,0:T(8,128)(2,1)S(1)}, bf16[2,384,768]{2,1,0:T(8,128)(2,1)}, u32[]{:S(2)}, u32[]{:S(2)}) collective-permute-start(bf16[2,384,768]{2,1,0:T(8,128)(2,1)S(1)} %pad_maximum_fusion.refs_4_), channel_id=1, source_target_pairs={{0,16},{4,20},{8,24},{12,28},{16,32},{20,36},{24,40},{28,44},{32,4... | collective-permute-start | bytes 3538952 | tf_op jit(solution)/shard_map/ppermute | solution.py:23
  6.0 4.4 %collective-permute-start.1 = (bf16[2,384,768]{2,1,0:T(8,128)(2,1)S(1)}, bf16[2,384,768]{2,1,0:T(8,128)(2,1)}, u32[]{:S(2)}, u32[]{:S(2)}) collective-permute-start(bf16[2,384,768]{2,1,0:T(8,128)(2,1)S(1)} %pad_maximum_fusion.refs_4_), channel_id=1, source_target_pairs={{0,4},{4,8},{8,12},{16,20},{20,24},{24,28},{32,36},{36,40},{40,44}... | collective-permute-start | bytes 3538952 | tf_op jit(solution)/shard_map/ppermute | solution.py:23
  11.7 4.8 %collective-permute-start.5 = (bf16[2,384,768]{2,1,0:T(8,128)(2,1)S(1)}, bf16[2,384,768]{2,1,0:T(8,128)(2,1)}, u32[]{:S(2)}, u32[]{:S(2)}) collective-permute-start(bf16[2,384,768]{2,1,0:T(8,128)(2,1)S(1)} %pad_maximum_fusion.refs_4_), channel_id=1, source_target_pairs={{16,0},{20,4},{24,8},{28,12},{32,16},{36,20},{40,24},{44,28},{48,3... | collective-permute-start | bytes 3538952 | tf_op jit(solution)/shard_map/ppermute | solution.py:23
  16.6 19.2 %collective-permute-done.refs_1_ = bf16[2,384,768]{2,1,0:T(8,128)(2,1)} collective-permute-done((bf16[2,384,768]{2,1,0:T(8,128)(2,1)S(1)}, bf16[2,384,768]{2,1,0:T(8,128)(2,1)}, u32[]{:S(2)}, u32[]{:S(2)}) %collective-permute-start) | collective-permute-done | bytes 1179680 | tf_op jit(solution)/shard_map/ppermute | solution.py:23
  35.8 3.7 %collective-permute-done.2.refs_5_ = bf16[2,384,768]{2,1,0:T(8,128)(2,1)} collective-permute-done((bf16[2,384,768]{2,1,0:T(8,128)(2,1)S(1)}, bf16[2,384,768]{2,1,0:T(8,128)(2,1)}, u32[]{:S(2)}, u32[]{:S(2)}) %collective-permute-start.2) | collective-permute-done | bytes 1179680 | tf_op jit(solution)/shard_map/ppermute | solution.py:23
  44.3 12.3 %collective-permute-done.5.refs_7_ = bf16[2,384,768]{2,1,0:T(8,128)(2,1)} collective-permute-done((bf16[2,384,768]{2,1,0:T(8,128)(2,1)S(1)}, bf16[2,384,768]{2,1,0:T(8,128)(2,1)}, u32[]{:S(2)}, u32[]{:S(2)}) %collective-permute-start.5) | collective-permute-done | bytes 1179680 | tf_op jit(solution)/shard_map/ppermute | solution.py:23
  56.5 4.4 %collective-permute-start.6 = (bf16[2,384,768]{2,1,0:T(8,128)(2,1)}, bf16[2,384,768]{2,1,0:T(8,128)(2,1)}, u32[]{:S(2)}, u32[]{:S(2)}) collective-permute-start(bf16[2,384,768]{2,1,0:T(8,128)(2,1)} %collective-permute-done.5.refs_7_), channel_id=1, source_target_pairs={{0,4},{4,8},{8,12},{16,20},{20,24},{24,28},{32,36},{36,40},{40,44}... | collective-permute-start | bytes 3538952 | tf_op jit(solution)/shard_map/ppermute | solution.py:23
  63.1 5.2 %fusion.6.grad_ref = bf16[384,768]{1,0:T(8,128)(2,1)} fusion(bf16[768,3072]{1,0:T(8,128)(2,1)} %param.11, bf16[1,1,384,3072]{3,2,1,0:T(8,128)(2,1)S(1)} %copy-done), kind=kOutput, calls=%fused_computation.12 | convolution fusion | flops 1812234240 | bytes 7667712 | tf_op jit(solution)/shard_map/dot_general | solution.py:98
  68.7 5.4 %collective-permute-done.4.refs_2_ = bf16[2,384,768]{2,1,0:T(8,128)(2,1)} collective-permute-done((bf16[2,384,768]{2,1,0:T(8,128)(2,1)}, bf16[2,384,768]{2,1,0:T(8,128)(2,1)}, u32[]{:S(2)}, u32[]{:S(2)}) %collective-permute-start.4) | collective-permute-done | bytes 1179680 | tf_op jit(solution)/shard_map/ppermute | solution.py:23
  74.1 17.2 %collective-permute-done.6.refs_6_ = bf16[2,384,768]{2,1,0:T(8,128)(2,1)} collective-permute-done((bf16[2,384,768]{2,1,0:T(8,128)(2,1)}, bf16[2,384,768]{2,1,0:T(8,128)(2,1)}, u32[]{:S(2)}, u32[]{:S(2)}) %collective-permute-start.6) | collective-permute-done | bytes 1179680 | tf_op jit(solution)/shard_map/ppermute | solution.py:23
  91.3 5.1 %collective-permute-done.7.refs_8_ = bf16[2,384,768]{2,1,0:T(8,128)(2,1)} collective-permute-done((bf16[2,384,768]{2,1,0:T(8,128)(2,1)}, bf16[2,384,768]{2,1,0:T(8,128)(2,1)}, u32[]{:S(2)}, u32[]{:S(2)}) %collective-permute-start.7) | collective-permute-done | bytes 1179680 | tf_op jit(solution)/shard_map/ppermute | solution.py:23
  96.4 38.0 %shard_map.93 = (bf16[384,768]{1,0:T(8,128)(2,1)}, bf16[384,768]{1,0:T(8,128)(2,1)}, bf16[2,384,768]{2,1,0:T(8,128)(2,1)}, bf16[2,384,768]{2,1,0:T(8,128)(2,1)},...) custom-call(s32[1,3456]{1,0:T(1,128)} %bitcast.66, ...), custom_call_target="tpu_custom_call" | custom-call | flops 10192158720 | bytes 23592960 | tf_op jit(solution)/shard_map/pallas_call | solution.py:106
  137.5 4.5 %collective-permute-done.16 = bf16[3072,384]{0,1:T(8,128)(2,1)S(1)} collective-permute-done((bf16[3072,384]{0,1:T(8,128)(2,1)S(1)}, bf16[3072,384]{0,1:T(8,128)(2,1)S(1)}, u32[]{:S(2)}, u32[]{:S(2)}) %collective-permute-start.16) | collective-permute-done | bytes 2359328 | tf_op jit(solution)/shard_map/ppermute | solution.py:138
  144.9 4.3 %copy.13 = bf16[3072,384]{1,0:T(8,128)(2,1)} copy(bf16[3072,384]{0,1:T(8,128)(2,1)} %fusion) | data formatting | bytes 4718592 | tf_op jit(solution)/shard_map/convert_element_type | solution.py:141
  149.2 17.4 %all-to-all-start = ((bf16[64,48,384]{2,1,0:T(8,128)(2,1)}), bf16[64,48,384]{2,1,0:T(8,128)(2,1)}, u32[]{:S(2)}, u32[]{:S(2)}) async-start(bf16[64,48,384]{2,1,0:T(8,128)(2,1)} %bitcast.59), calls=%async_computation | async-start | bytes 4718592 | tf_op jit(solution)/shard_map/all_to_all | solution.py:142
  167.9 4.6 %collective-permute-start.9 = (bf16[2,384,768]{2,1,0:T(8,128)(2,1)}, bf16[2,384,768]{2,1,0:T(8,128)(2,1)S(1)}, u32[]{:S(2)}, u32[]{:S(2)}) collective-permute-start(bf16[2,384,768]{2,1,0:T(8,128)(2,1)} %get-tuple-element.30), channel_id=1, source_target_pairs={{0,4},{4,8},{8,12},{16,20},{20,24},{24,28},{32,36},{36,40},{40,44}... | collective-permute-start | bytes 3538952 | tf_op jit(solution)/shard_map/ppermute | solution.py:23
  172.5 46.2 %collective-permute-done.8 = bf16[2,384,768]{2,1,0:T(8,128)(2,1)S(1)} collective-permute-done((bf16[2,384,768]{2,1,0:T(8,128)(2,1)}, bf16[2,384,768]{2,1,0:T(8,128)(2,1)S(1)}, u32[]{:S(2)}, u32[]{:S(2)}) %collective-permute-start.8) | collective-permute-done | bytes 1179680 | tf_op jit(solution)/shard_map/ppermute | solution.py:23
  220.0 4.6 %collective-permute-start.14 = (bf16[2,384,768]{2,1,0:T(8,128)(2,1)}, bf16[2,384,768]{2,1,0:T(8,128)(2,1)S(1)}, u32[]{:S(2)}, u32[]{:S(2)}) collective-permute-start(bf16[2,384,768]{2,1,0:T(8,128)(2,1)} %get-tuple-element.42), channel_id=1, source_target_pairs={{0,4},{4,8},{8,12},{16,20},{20,24},{24,28},{32,36},{36,40},{40,44}... | collective-permute-start | bytes 3538952 | tf_op jit(solution)/shard_map/ppermute | solution.py:23
  226.2 5.4 %collective-permute-start.12 = (bf16[2,384,768]{2,1,0:T(8,128)(2,1)}, bf16[2,384,768]{2,1,0:T(8,128)(2,1)S(1)}, u32[]{:S(2)}, u32[]{:S(2)}) collective-permute-start(bf16[2,384,768]{2,1,0:T(8,128)(2,1)} %add_convert_fusion.2), channel_id=1, source_target_pairs={{16,0},{20,4},{24,8},{28,12},{32,16},{36,20},{40,24},{44,28},{48,3... | collective-permute-start | bytes 3538952 | tf_op jit(solution)/shard_map/ppermute | solution.py:23
  232.9 5.6 %collective-permute-start.11 = (bf16[2,384,768]{2,1,0:T(8,128)(2,1)}, bf16[2,384,768]{2,1,0:T(8,128)(2,1)}, u32[]{:S(2)}, u32[]{:S(2)}) collective-permute-start(bf16[2,384,768]{2,1,0:T(8,128)(2,1)} %get-tuple-element.36), channel_id=1, source_target_pairs={{0,4},{4,8},{8,12},{16,20},{20,24},{24,28},{32,36},{36,40},{40,44}... | collective-permute-start | bytes 3538952 | tf_op jit(solution)/shard_map/ppermute | solution.py:23
  238.6 11.2 %collective-permute-done.13 = bf16[2,384,768]{2,1,0:T(8,128)(2,1)S(1)} collective-permute-done((bf16[2,384,768]{2,1,0:T(8,128)(2,1)}, bf16[2,384,768]{2,1,0:T(8,128)(2,1)S(1)}, u32[]{:S(2)}, u32[]{:S(2)}) %collective-permute-start.13) | collective-permute-done | bytes 1179680 | tf_op jit(solution)/shard_map/ppermute | solution.py:23
  258.4 14.7 %collective-permute-done.10 = bf16[2,384,768]{2,1,0:T(8,128)(2,1)} collective-permute-done((bf16[2,384,768]{2,1,0:T(8,128)(2,1)}, bf16[2,384,768]{2,1,0:T(8,128)(2,1)}, u32[]{:S(2)}, u32[]{:S(2)}) %collective-permute-start.10) | collective-permute-done | bytes 1179680 | tf_op jit(solution)/shard_map/ppermute | solution.py:23
  274.3 10.0 %collective-permute-done.15 = bf16[2,384,768]{2,1,0:T(8,128)(2,1)} collective-permute-done((bf16[2,384,768]{2,1,0:T(8,128)(2,1)}, bf16[2,384,768]{2,1,0:T(8,128)(2,1)}, u32[]{:S(2)}, u32[]{:S(2)}) %collective-permute-start.15) | collective-permute-done | bytes 1179680 | tf_op jit(solution)/shard_map/ppermute | solution.py:23
  294.3 6.9 %collective-permute-done.17 = f32[48,192]{1,0:T(8,128)S(1)} collective-permute-done((f32[48,192]{1,0:T(8,128)S(1)}, f32[48,192]{1,0:T(8,128)S(1)}, u32[]{:S(2)}, u32[]{:S(2)}) %collective-permute-start.17) | collective-permute-done | bytes 36896 | tf_op jit(solution)/shard_map/ppermute | solution.py:150
  (49 shorter events, 41.7 us)
Async XLA Ops:
  0.6 62.4 %copy-start = (bf16[1,1,384,3072]{3,2,1,0:T(8,128)(2,1)S(1)}, bf16[1,1,384,3072]{3,2,1,0:T(8,128)(2,1)}, u32[]{:S(2)}) copy-start(bf16[1,1,384,3072]{3,2,1,0:T(8,128)(2,1)} %param.10) | copy-start | bytes 7077892
  2.2 66.1 %copy-start.2 = (bf16[2,384,768]{2,1,0:T(8,128)(2,1)}, bf16[2,384,768]{2,1,0:T(8,128)(2,1)S(1)}, u32[]{:S(2)}) copy-start(bf16[2,384,768]{2,1,0:T(8,128)(2,1)S(1)} %pad_maximum_fusion.refs_4_) | copy-start | bytes 3538948
  2.2 33.7 %collective-permute-start = (bf16[2,384,768]{2,1,0:T(8,128)(2,1)S(1)}, bf16[2,384,768]{2,1,0:T(8,128)(2,1)}, u32[]{:S(2)}, u32[]{:S(2)}) collective-permute-start(bf16[2,384,768]{2,1,0:T(8,128)(2,1)S(1)} %pad_maximum_fusion.refs_4_), channel_id=1, source_target_pairs={{0,16},{4,20},{8,24},{12,28},{16,32},{20,36},{24,40},{28,44},{32,4... | collective-permute-start | bytes 3538952 | tf_op jit(solution)/shard_map/ppermute | solution.py:23
  6.0 29.8 %collective-permute-start.1 = (bf16[2,384,768]{2,1,0:T(8,128)(2,1)S(1)}, bf16[2,384,768]{2,1,0:T(8,128)(2,1)}, u32[]{:S(2)}, u32[]{:S(2)}) collective-permute-start(bf16[2,384,768]{2,1,0:T(8,128)(2,1)S(1)} %pad_maximum_fusion.refs_4_), channel_id=1, source_target_pairs={{0,4},{4,8},{8,12},{16,20},{20,24},{24,28},{32,36},{36,40},{40,44}... | collective-permute-start | bytes 3538952 | tf_op jit(solution)/shard_map/ppermute | solution.py:23
  10.4 29.1 %collective-permute-start.2 = (bf16[2,384,768]{2,1,0:T(8,128)(2,1)S(1)}, bf16[2,384,768]{2,1,0:T(8,128)(2,1)}, u32[]{:S(2)}, u32[]{:S(2)}) collective-permute-start(bf16[2,384,768]{2,1,0:T(8,128)(2,1)S(1)} %pad_maximum_fusion.refs_4_), channel_id=1, source_target_pairs={{4,0},{8,4},{12,8},{20,16},{24,20},{28,24},{36,32},{40,36},{44,40}... | collective-permute-start | bytes 3538952 | tf_op jit(solution)/shard_map/ppermute | solution.py:23
  11.7 44.8 %collective-permute-start.5 = (bf16[2,384,768]{2,1,0:T(8,128)(2,1)S(1)}, bf16[2,384,768]{2,1,0:T(8,128)(2,1)}, u32[]{:S(2)}, u32[]{:S(2)}) collective-permute-start(bf16[2,384,768]{2,1,0:T(8,128)(2,1)S(1)} %pad_maximum_fusion.refs_4_), channel_id=1, source_target_pairs={{16,0},{20,4},{24,8},{28,12},{32,16},{36,20},{40,24},{44,28},{48,3... | collective-permute-start | bytes 3538952 | tf_op jit(solution)/shard_map/ppermute | solution.py:23
  39.6 29.1 %collective-permute-start.3 = (bf16[2,384,768]{2,1,0:T(8,128)(2,1)}, bf16[2,384,768]{2,1,0:T(8,128)(2,1)}, u32[]{:S(2)}, u32[]{:S(2)}) collective-permute-start(bf16[2,384,768]{2,1,0:T(8,128)(2,1)} %collective-permute-done.refs_1_), channel_id=1, source_target_pairs={{0,4},{4,8},{8,12},{16,20},{20,24},{24,28},{32,36},{36,40},{40,44}... | collective-permute-start | bytes 3538952 | tf_op jit(solution)/shard_map/ppermute | solution.py:23
  43.0 31.1 %collective-permute-start.4 = (bf16[2,384,768]{2,1,0:T(8,128)(2,1)}, bf16[2,384,768]{2,1,0:T(8,128)(2,1)}, u32[]{:S(2)}, u32[]{:S(2)}) collective-permute-start(bf16[2,384,768]{2,1,0:T(8,128)(2,1)} %collective-permute-done.refs_1_), channel_id=1, source_target_pairs={{4,0},{8,4},{12,8},{20,16},{24,20},{28,24},{36,32},{40,36},{44,40}... | collective-permute-start | bytes 3538952 | tf_op jit(solution)/shard_map/ppermute | solution.py:23
  56.5 34.7 %collective-permute-start.6 = (bf16[2,384,768]{2,1,0:T(8,128)(2,1)}, bf16[2,384,768]{2,1,0:T(8,128)(2,1)}, u32[]{:S(2)}, u32[]{:S(2)}) collective-permute-start(bf16[2,384,768]{2,1,0:T(8,128)(2,1)} %collective-permute-done.5.refs_7_), channel_id=1, source_target_pairs={{0,4},{4,8},{8,12},{16,20},{20,24},{24,28},{32,36},{36,40},{40,44}... | collective-permute-start | bytes 3538952 | tf_op jit(solution)/shard_map/ppermute | solution.py:23
  61.0 35.4 %collective-permute-start.7 = (bf16[2,384,768]{2,1,0:T(8,128)(2,1)}, bf16[2,384,768]{2,1,0:T(8,128)(2,1)}, u32[]{:S(2)}, u32[]{:S(2)}) collective-permute-start(bf16[2,384,768]{2,1,0:T(8,128)(2,1)} %collective-permute-done.5.refs_7_), channel_id=1, source_target_pairs={{4,0},{8,4},{12,8},{20,16},{24,20},{28,24},{36,32},{40,36},{44,40}... | collective-permute-start | bytes 3538952 | tf_op jit(solution)/shard_map/ppermute | solution.py:23
  137.2 4.8 %collective-permute-start.16 = (bf16[3072,384]{0,1:T(8,128)(2,1)S(1)}, bf16[3072,384]{0,1:T(8,128)(2,1)S(1)}, u32[]{:S(2)}, u32[]{:S(2)}) collective-permute-start(bf16[3072,384]{0,1:T(8,128)(2,1)S(1)} %fusion.1), channel_id=1, source_target_pairs={{0,1},{1,0},{2,3},{3,2},{4,5},{5,4},{6,7},{7,6},{8,9},{9,8},{10,11... | collective-permute-start | bytes 7077896 | tf_op jit(solution)/shard_map/ppermute | solution.py:138
  149.2 75.5 %copy-start.4 = (bf16[2,384,768]{2,1,0:T(8,128)(2,1)S(1)}, bf16[2,384,768]{2,1,0:T(8,128)(2,1)}, u32[]{:S(2)}) copy-start(bf16[2,384,768]{2,1,0:T(8,128)(2,1)} %get-tuple-element.37) | copy-start | bytes 3538948
  149.2 138.5 %all-to-all-start = ((bf16[64,48,384]{2,1,0:T(8,128)(2,1)}), bf16[64,48,384]{2,1,0:T(8,128)(2,1)}, u32[]{:S(2)}, u32[]{:S(2)}) async-start(bf16[64,48,384]{2,1,0:T(8,128)(2,1)} %bitcast.59), calls=%async_computation | async-start | bytes 4718592 | tf_op jit(solution)/shard_map/all_to_all | solution.py:142
  166.6 52.1 %collective-permute-start.8 = (bf16[2,384,768]{2,1,0:T(8,128)(2,1)}, bf16[2,384,768]{2,1,0:T(8,128)(2,1)S(1)}, u32[]{:S(2)}, u32[]{:S(2)}) collective-permute-start(bf16[2,384,768]{2,1,0:T(8,128)(2,1)} %get-tuple-element.29), channel_id=1, source_target_pairs={{4,0},{8,4},{12,8},{20,16},{24,20},{28,24},{36,32},{40,36},{44,40}... | collective-permute-start | bytes 3538952 | tf_op jit(solution)/shard_map/ppermute | solution.py:23
  167.9 50.8 %collective-permute-start.9 = (bf16[2,384,768]{2,1,0:T(8,128)(2,1)}, bf16[2,384,768]{2,1,0:T(8,128)(2,1)S(1)}, u32[]{:S(2)}, u32[]{:S(2)}) collective-permute-start(bf16[2,384,768]{2,1,0:T(8,128)(2,1)} %get-tuple-element.30), channel_id=1, source_target_pairs={{0,4},{4,8},{8,12},{16,20},{20,24},{24,28},{32,36},{36,40},{40,44}... | collective-permute-start | bytes 3538952 | tf_op jit(solution)/shard_map/ppermute | solution.py:23
  218.7 31.0 %collective-permute-start.13 = (bf16[2,384,768]{2,1,0:T(8,128)(2,1)}, bf16[2,384,768]{2,1,0:T(8,128)(2,1)S(1)}, u32[]{:S(2)}, u32[]{:S(2)}) collective-permute-start(bf16[2,384,768]{2,1,0:T(8,128)(2,1)} %get-tuple-element.41), channel_id=1, source_target_pairs={{4,0},{8,4},{12,8},{20,16},{24,20},{28,24},{36,32},{40,36},{44,40}... | collective-permute-start | bytes 3538952 | tf_op jit(solution)/shard_map/ppermute | solution.py:23
  220.0 31.3 %collective-permute-start.14 = (bf16[2,384,768]{2,1,0:T(8,128)(2,1)}, bf16[2,384,768]{2,1,0:T(8,128)(2,1)S(1)}, u32[]{:S(2)}, u32[]{:S(2)}) collective-permute-start(bf16[2,384,768]{2,1,0:T(8,128)(2,1)} %get-tuple-element.42), channel_id=1, source_target_pairs={{0,4},{4,8},{8,12},{16,20},{20,24},{24,28},{32,36},{36,40},{40,44}... | collective-permute-start | bytes 3538952 | tf_op jit(solution)/shard_map/ppermute | solution.py:23
  224.7 26.6 %copy-start.3 = (bf16[2,384,768]{2,1,0:T(8,128)(2,1)S(1)}, bf16[2,384,768]{2,1,0:T(8,128)(2,1)}, u32[]{:S(2)}) copy-start(bf16[2,384,768]{2,1,0:T(8,128)(2,1)} %get-tuple-element.40) | copy-start | bytes 3538948
  226.2 32.2 %collective-permute-start.12 = (bf16[2,384,768]{2,1,0:T(8,128)(2,1)}, bf16[2,384,768]{2,1,0:T(8,128)(2,1)S(1)}, u32[]{:S(2)}, u32[]{:S(2)}) collective-permute-start(bf16[2,384,768]{2,1,0:T(8,128)(2,1)} %add_convert_fusion.2), channel_id=1, source_target_pairs={{16,0},{20,4},{24,8},{28,12},{32,16},{36,20},{40,24},{44,28},{48,3... | collective-permute-start | bytes 3538952 | tf_op jit(solution)/shard_map/ppermute | solution.py:23
  231.6 41.5 %collective-permute-start.10 = (bf16[2,384,768]{2,1,0:T(8,128)(2,1)}, bf16[2,384,768]{2,1,0:T(8,128)(2,1)}, u32[]{:S(2)}, u32[]{:S(2)}) collective-permute-start(bf16[2,384,768]{2,1,0:T(8,128)(2,1)} %get-tuple-element.35), channel_id=1, source_target_pairs={{4,0},{8,4},{12,8},{20,16},{24,20},{28,24},{36,32},{40,36},{44,40}... | collective-permute-start | bytes 3538952 | tf_op jit(solution)/shard_map/ppermute | solution.py:23
  232.9 41.3 %collective-permute-start.11 = (bf16[2,384,768]{2,1,0:T(8,128)(2,1)}, bf16[2,384,768]{2,1,0:T(8,128)(2,1)}, u32[]{:S(2)}, u32[]{:S(2)}) collective-permute-start(bf16[2,384,768]{2,1,0:T(8,128)(2,1)} %get-tuple-element.36), channel_id=1, source_target_pairs={{0,4},{4,8},{8,12},{16,20},{20,24},{24,28},{32,36},{36,40},{40,44}... | collective-permute-start | bytes 3538952 | tf_op jit(solution)/shard_map/ppermute | solution.py:23
  252.8 31.5 %collective-permute-start.15 = (bf16[2,384,768]{2,1,0:T(8,128)(2,1)}, bf16[2,384,768]{2,1,0:T(8,128)(2,1)}, u32[]{:S(2)}, u32[]{:S(2)}) collective-permute-start(bf16[2,384,768]{2,1,0:T(8,128)(2,1)} %add_convert_fusion.1), channel_id=1, source_target_pairs={{0,16},{4,20},{8,24},{12,28},{16,32},{20,36},{24,40},{28,44},{32,4... | collective-permute-start | bytes 3538952 | tf_op jit(solution)/shard_map/ppermute | solution.py:23
  258.4 25.9 %copy-start.1 = (bf16[2,384,768]{2,1,0:T(8,128)(2,1)}, bf16[2,384,768]{2,1,0:T(8,128)(2,1)S(1)}, u32[]{:S(2)}) copy-start(bf16[2,384,768]{2,1,0:T(8,128)(2,1)S(1)} %collective-permute-done.12) | copy-start | bytes 3538948
  293.1 8.1 %collective-permute-start.17 = (f32[48,192]{1,0:T(8,128)S(1)}, f32[48,192]{1,0:T(8,128)S(1)}, u32[]{:S(2)}, u32[]{:S(2)}) collective-permute-start(f32[48,192]{1,0:T(8,128)S(1)} %bitcast.65), channel_id=1, source_target_pairs={{0,2},{1,3},{2,0},{3,1},{4,6},{5,7},{6,4},{7,5},{8,10},{9,11},{10,... | collective-permute-start | bytes 110600 | tf_op jit(solution)/shard_map/ppermute | solution.py:150
  (1 other events, 15.9 us)

commit v8 on v7

--- a/solution.py
+++ b/solution.py
@@ -122,6 +122,22 @@
     )
     attn_all, grad_query = outputs[:2]
     back = outputs[2:]
+    early_in = [shifted(back[0], 0, -1, True), shifted(back[2], 0, 1, True)]
+    early_in, late_out, row_out = lax.optimization_barrier((early_in, [back[6], back[8]], [back[3], back[5]]))
+    earlier_sum = back[1].astype(jnp.float32) + early_in[0].astype(jnp.float32) + early_in[1].astype(jnp.float32)
+    from_later = shifted(earlier_sum.astype(jnp.bfloat16), -1, 0, True)
+    late_in = [shifted(late_out[0], 0, -1, True), shifted(late_out[1], 0, 1, True)]
+    row_in = [shifted(part, 0, step, True) for part, step in zip(row_out, (-1, 1))]
+    later_sum = back[7].astype(jnp.float32) + late_in[0].astype(jnp.float32) + late_in[1].astype(jnp.float32)
+    from_earlier = shifted(later_sum.astype(jnp.bfloat16), 1, 0, True)
+    grad_total = (
+        back[4].astype(jnp.float32)
+        + row_in[0].astype(jnp.float32)
+        + row_in[1].astype(jnp.float32)
+        + from_later.astype(jnp.float32)
+        + from_earlier.astype(jnp.float32)
+    )
+    attn_all, grad_tile, grad_total = lax.optimization_barrier((attn_all, grad_tile, grad_total))
     dp_count = lax.axis_size("dp")
     sp_count = lax.axis_size("sp")
     dp_index = lax.axis_index("dp")
@@ -149,21 +165,6 @@
         own_half
         + lax.ppermute(other_half, "dp", [(index, (index + 2) % dp_count) for index in range(dp_count)])
     ).T
-    early_in = [shifted(back[0], 0, -1, True), shifted(back[2], 0, 1, True)]
-    early_in, late_out, row_out = lax.optimization_barrier((early_in, [back[6], back[8]], [back[3], back[5]]))
-    earlier_sum = back[1].astype(jnp.float32) + early_in[0].astype(jnp.float32) + early_in[1].astype(jnp.float32)
-    from_later = shifted(earlier_sum.astype(jnp.bfloat16), -1, 0, True)
-    late_in = [shifted(late_out[0], 0, -1, True), shifted(late_out[1], 0, 1, True)]
-    row_in = [shifted(part, 0, step, True) for part, step in zip(row_out, (-1, 1))]
-    later_sum = back[7].astype(jnp.float32) + late_in[0].astype(jnp.float32) + late_in[1].astype(jnp.float32)
-    from_earlier = shifted(later_sum.astype(jnp.bfloat16), 1, 0, True)
-    grad_total = (
-        back[4].astype(jnp.float32)
-        + row_in[0].astype(jnp.float32)
-        + row_in[1].astype(jnp.float32)
-        + from_later.astype(jnp.float32)
-        + from_earlier.astype(jnp.float32)
-    )
     grad_kv = grad_total.astype(jnp.bfloat16)
     return (grad_query[None, None], grad_kv[0][None, None], grad_kv[1][None, None], weight_grad)
 

time: 303 us -> 324 us (1.069)
  waiting for transfers between devices: 162 us -> 173 us
  starting transfers between devices: 70.1 us -> 74.6 us
    all_to_all x1, waiting for transfers between devices: 0.01 us -> 55 us  [body(): lax.all_to_all(core_sum.reshape(sp_count, col_block, -1), 'sp', 0, 0, til...]
    ppermute x16, waiting for transfers between devices: 150 us -> 113 us  [neighbour_shift(): return lax.ppermute(value, axis, pairs)]
    all_to_all x1, starting transfers between devices: 17.4 us -> 9.45 us  [body(): lax.all_to_all(core_sum.reshape(sp_count, col_block, -1), 'sp', 0, 0, til...]
    ppermute x1, starting transfers between devices: 0.09 us -> 6.61 us  [body(): lax.ppermute(other_half, 'dp', [(index, (index + 2) % dp_count) for index...]
    ppermute x16, starting transfers between devices: 52.3 us -> 58.4 us  [neighbour_shift(): return lax.ppermute(value, axis, pairs)]
    ppermute x1, waiting for transfers between devices: 6.9 us -> 0.98 us  [body(): lax.ppermute(other_half, 'dp', [(index, (index + 2) % dp_count) for index...]
    convert_element_type x1 -> x0, local copies, waits for them, and re-layouts: 4.28 us -> none  [body(): (kept_part + sibling_part.astype(jnp.float32)).astype(jnp.bfloat16)]
    unnamed x15 -> x21, local copies, waits for them, and re-layouts: 0.72 us -> 4.83 us
  transfers between devices with their start and end apart: 19 -> 19, of which waited for: 16 -> 18; matrix products, arithmetic and copies ran while one was open for 4% -> 4% of each run, Pallas kernels for 0% -> 0%
where the time goes in v8:
time: 324 us; the launch traced here: 322 us
  waiting for transfers between devices  173 us (53%)
  starting transfers between devices  74.6 us (23%)
  Pallas kernels  38 us (12%)
  other arithmetic  12.7 us (4%)
  local copies, waits for them, and re-layouts  11.9 us (4%)
  matrix products  10 us (3%)
    ppermute x16, waiting for transfers between devices, neighbour_shift(): return lax.ppermute(value, axis, pairs)  113 us
    ppermute x16, starting transfers between devices, neighbour_shift(): return lax.ppermute(value, axis, pairs)  58.4 us
    all_to_all x1, waiting for transfers between devices, body(): lax.all_to_all(core_sum.reshape(sp_count, col_block, -1), 'sp', 0, 0, til...  55 us
    pallas_call x1, Pallas kernels, body(): pl.pallas_call(functools.partial(tile_attention, score_scale=score_scale)...  38 us
    all_to_all x1, starting transfers between devices, body(): lax.all_to_all(core_sum.reshape(sp_count, col_block, -1), 'sp', 0, 0, til...  9.45 us
    ppermute x1, starting transfers between devices, body(): lax.ppermute(other_half, 'dp', [(index, (index + 2) % dp_count) for index...  6.61 us
  transfers between devices with their start and end apart: 19, of which 18 were waited for; matrix products, arithmetic and copies ran while one was open for 4% of the time, Pallas kernels for 0%

profile of v8, /device:TPU:24, one launch (start us, length us, event | category | flops | bytes accessed | tf_op | source)
XLA Modules:
  0.0 321.5 jit_solution(2625399021296400095)
XLA Ops:
  2.2 3.8 %collective-permute-start = (bf16[2,384,768]{2,1,0:T(8,128)(2,1)S(1)}, bf16[2,384,768]{2,1,0:T(8,128)(2,1)}, u32[]{:S(2)}, u32[]{:S(2)}) collective-permute-start(bf16[2,384,768]{2,1,0:T(8,128)(2,1)S(1)} %pad_maximum_fusion.refs_4_), channel_id=1, source_target_pairs={{0,16},{4,20},{8,24},{12,28},{16,32},{20,36},{24,40},{28,44},{32,4... | collective-permute-start | bytes 3538952 | tf_op jit(solution)/shard_map/ppermute | solution.py:23
  6.0 4.5 %collective-permute-start.1 = (bf16[2,384,768]{2,1,0:T(8,128)(2,1)S(1)}, bf16[2,384,768]{2,1,0:T(8,128)(2,1)}, u32[]{:S(2)}, u32[]{:S(2)}) collective-permute-start(bf16[2,384,768]{2,1,0:T(8,128)(2,1)S(1)} %pad_maximum_fusion.refs_4_), channel_id=1, source_target_pairs={{0,4},{4,8},{8,12},{16,20},{20,24},{24,28},{32,36},{36,40},{40,44}... | collective-permute-start | bytes 3538952 | tf_op jit(solution)/shard_map/ppermute | solution.py:23
  11.8 4.8 %collective-permute-start.5 = (bf16[2,384,768]{2,1,0:T(8,128)(2,1)S(1)}, bf16[2,384,768]{2,1,0:T(8,128)(2,1)}, u32[]{:S(2)}, u32[]{:S(2)}) collective-permute-start(bf16[2,384,768]{2,1,0:T(8,128)(2,1)S(1)} %pad_maximum_fusion.refs_4_), channel_id=1, source_target_pairs={{16,0},{20,4},{24,8},{28,12},{32,16},{36,20},{40,24},{44,28},{48,3... | collective-permute-start | bytes 3538952 | tf_op jit(solution)/shard_map/ppermute | solution.py:23
  16.6 19.2 %collective-permute-done.refs_1_ = bf16[2,384,768]{2,1,0:T(8,128)(2,1)} collective-permute-done((bf16[2,384,768]{2,1,0:T(8,128)(2,1)S(1)}, bf16[2,384,768]{2,1,0:T(8,128)(2,1)}, u32[]{:S(2)}, u32[]{:S(2)}) %collective-permute-start) | collective-permute-done | bytes 1179680 | tf_op jit(solution)/shard_map/ppermute | solution.py:23
  35.8 3.8 %collective-permute-done.2.refs_5_ = bf16[2,384,768]{2,1,0:T(8,128)(2,1)} collective-permute-done((bf16[2,384,768]{2,1,0:T(8,128)(2,1)S(1)}, bf16[2,384,768]{2,1,0:T(8,128)(2,1)}, u32[]{:S(2)}, u32[]{:S(2)}) %collective-permute-start.2) | collective-permute-done | bytes 1179680 | tf_op jit(solution)/shard_map/ppermute | solution.py:23
  43.3 13.2 %collective-permute-done.5.refs_7_ = bf16[2,384,768]{2,1,0:T(8,128)(2,1)} collective-permute-done((bf16[2,384,768]{2,1,0:T(8,128)(2,1)S(1)}, bf16[2,384,768]{2,1,0:T(8,128)(2,1)}, u32[]{:S(2)}, u32[]{:S(2)}) %collective-permute-start.5) | collective-permute-done | bytes 1179680 | tf_op jit(solution)/shard_map/ppermute | solution.py:23
  56.5 3.5 %collective-permute-start.6 = (bf16[2,384,768]{2,1,0:T(8,128)(2,1)}, bf16[2,384,768]{2,1,0:T(8,128)(2,1)S(1)}, u32[]{:S(2)}, u32[]{:S(2)}) collective-permute-start(bf16[2,384,768]{2,1,0:T(8,128)(2,1)} %collective-permute-done.5.refs_7_), channel_id=1, source_target_pairs={{0,4},{4,8},{8,12},{16,20},{20,24},{24,28},{32,36},{36,40},{40,44}... | collective-permute-start | bytes 3538952 | tf_op jit(solution)/shard_map/ppermute | solution.py:23
  62.1 5.2 %convolution_convert_fusion.1.grad_ref = bf16[384,768]{1,0:T(8,128)(2,1)} fusion(bf16[768,3072]{1,0:T(8,128)(2,1)} %param.11, bf16[1,1,384,3072]{3,2,1,0:T(8,128)(2,1)S(1)} %copy-done), kind=kOutput, calls=%fused_computation.6 | convolution fusion | flops 1812234240 | bytes 7667712 | tf_op jit(solution)/shard_map/dot_general | solution.py:98
  69.7 3.3 %collective-permute-done.4.refs_2_ = bf16[2,384,768]{2,1,0:T(8,128)(2,1)S(1)} collective-permute-done((bf16[2,384,768]{2,1,0:T(8,128)(2,1)}, bf16[2,384,768]{2,1,0:T(8,128)(2,1)S(1)}, u32[]{:S(2)}, u32[]{:S(2)}) %collective-permute-start.4) | collective-permute-done | bytes 1179680 | tf_op jit(solution)/shard_map/ppermute | solution.py:23
  74.1 17.2 %collective-permute-done.6.refs_6_ = bf16[2,384,768]{2,1,0:T(8,128)(2,1)S(1)} collective-permute-done((bf16[2,384,768]{2,1,0:T(8,128)(2,1)}, bf16[2,384,768]{2,1,0:T(8,128)(2,1)S(1)}, u32[]{:S(2)}, u32[]{:S(2)}) %collective-permute-start.6) | collective-permute-done | bytes 1179680 | tf_op jit(solution)/shard_map/ppermute | solution.py:23
  96.4 38.0 %shard_map.93 = (bf16[384,768]{1,0:T(8,128)(2,1)}, bf16[384,768]{1,0:T(8,128)(2,1)}, bf16[2,384,768]{2,1,0:T(8,128)(2,1)}, bf16[2,384,768]{2,1,0:T(8,128)(2,1)},...) custom-call(s32[1,3456]{1,0:T(1,128)} %bitcast.58, ...), custom_call_target="tpu_custom_call" | custom-call | flops 10192158720 | bytes 23592960 | tf_op jit(solution)/shard_map/pallas_call | solution.py:106
  135.7 4.6 %collective-permute-start.9 = (bf16[2,384,768]{2,1,0:T(8,128)(2,1)}, bf16[2,384,768]{2,1,0:T(8,128)(2,1)S(1)}, u32[]{:S(2)}, u32[]{:S(2)}) collective-permute-start(bf16[2,384,768]{2,1,0:T(8,128)(2,1)} %get-tuple-element.34), channel_id=1, source_target_pairs={{0,4},{4,8},{8,12},{16,20},{20,24},{24,28},{32,36},{36,40},{40,44}... | collective-permute-start | bytes 3538952 | tf_op jit(solution)/shard_map/ppermute | solution.py:23
  140.3 21.2 %collective-permute-done.8 = bf16[2,384,768]{2,1,0:T(8,128)(2,1)S(1)} collective-permute-done((bf16[2,384,768]{2,1,0:T(8,128)(2,1)}, bf16[2,384,768]{2,1,0:T(8,128)(2,1)S(1)}, u32[]{:S(2)}, u32[]{:S(2)}) %collective-permute-start.8) | collective-permute-done | bytes 1179680 | tf_op jit(solution)/shard_map/ppermute | solution.py:23
  164.1 5.0 %collective-permute-start.14 = (bf16[2,384,768]{2,1,0:T(8,128)(2,1)}, bf16[2,384,768]{2,1,0:T(8,128)(2,1)S(1)}, u32[]{:S(2)}, u32[]{:S(2)}) collective-permute-start(bf16[2,384,768]{2,1,0:T(8,128)(2,1)} %get-tuple-element.46), channel_id=1, source_target_pairs={{0,4},{4,8},{8,12},{16,20},{20,24},{24,28},{32,36},{36,40},{40,44}... | collective-permute-start | bytes 3538952 | tf_op jit(solution)/shard_map/ppermute | solution.py:23
  172.0 14.4 %collective-permute-start.12 = (bf16[2,384,768]{2,1,0:T(8,128)(2,1)}, bf16[2,384,768]{2,1,0:T(8,128)(2,1)S(1)}, u32[]{:S(2)}, u32[]{:S(2)}) collective-permute-start(bf16[2,384,768]{2,1,0:T(8,128)(2,1)} %add_convert_fusion.2), channel_id=1, source_target_pairs={{16,0},{20,4},{24,8},{28,12},{32,16},{36,20},{40,24},{44,28},{48,3... | collective-permute-start | bytes 3538952 | tf_op jit(solution)/shard_map/ppermute | solution.py:23
  187.7 5.6 %collective-permute-start.11 = (bf16[2,384,768]{2,1,0:T(8,128)(2,1)}, bf16[2,384,768]{2,1,0:T(8,128)(2,1)}, u32[]{:S(2)}, u32[]{:S(2)}) collective-permute-start(bf16[2,384,768]{2,1,0:T(8,128)(2,1)} %get-tuple-element.40), channel_id=1, source_target_pairs={{0,4},{4,8},{8,12},{16,20},{20,24},{24,28},{32,36},{36,40},{40,44}... | collective-permute-start | bytes 3538952 | tf_op jit(solution)/shard_map/ppermute | solution.py:23
  199.3 11.7 %collective-permute-done.12 = bf16[2,384,768]{2,1,0:T(8,128)(2,1)S(1)} collective-permute-done((bf16[2,384,768]{2,1,0:T(8,128)(2,1)}, bf16[2,384,768]{2,1,0:T(8,128)(2,1)S(1)}, u32[]{:S(2)}, u32[]{:S(2)}) %collective-permute-start.12) | collective-permute-done | bytes 1179680 | tf_op jit(solution)/shard_map/ppermute | solution.py:23
  211.0 3.7 %collective-permute-done.10 = bf16[2,384,768]{2,1,0:T(8,128)(2,1)} collective-permute-done((bf16[2,384,768]{2,1,0:T(8,128)(2,1)}, bf16[2,384,768]{2,1,0:T(8,128)(2,1)}, u32[]{:S(2)}, u32[]{:S(2)}) %collective-permute-start.10) | collective-permute-done | bytes 1179680 | tf_op jit(solution)/shard_map/ppermute | solution.py:23
  215.9 10.3 %collective-permute-done.15 = bf16[2,384,768]{2,1,0:T(8,128)(2,1)} collective-permute-done((bf16[2,384,768]{2,1,0:T(8,128)(2,1)}, bf16[2,384,768]{2,1,0:T(8,128)(2,1)}, u32[]{:S(2)}, u32[]{:S(2)}) %collective-permute-start.15) | collective-permute-done | bytes 1179680 | tf_op jit(solution)/shard_map/ppermute | solution.py:23
  226.2 3.4 %convert_add_fusion = bf16[2,384,768]{2,1,0:T(8,128)(2,1)S(1)} fusion(bf16[2,384,768]{2,1,0:T(8,128)(2,1)} %collective-permute-done.15, bf16[2,384,768]{2,1,0:T(8,128)(2,1)} %copy-done.1, bf16[2,384,768]{2,1,0:T(8,128)(2,1)} %collective-permute-done.11, bf16[2,384,768]{2,1,0:T(8,128)(2,1)} %collective-permute-done.10, bf16[2,384,768]{2,1,0:T(8,128)(2,1)} %get-tuple-element.32), kind=kLoop, calls=%fused_computation.3 | loop fusion | flops 5898240 | bytes 7077888 | tf_op jit(solution)/shard_map/add | solution.py:134
  234.6 4.5 %collective-permute-done.16 = bf16[3072,384]{1,0:T(8,128)(2,1)S(1)} collective-permute-done((bf16[3072,384]{1,0:T(8,128)(2,1)S(1)}, bf16[3072,384]{1,0:T(8,128)(2,1)S(1)}, u32[]{:S(2)}, u32[]{:S(2)}) %collective-permute-start.16) | collective-permute-done | bytes 2359328 | tf_op jit(solution)/shard_map/ppermute | solution.py:154
  242.3 9.5 %all-to-all-start = ((bf16[64,48,384]{2,1,0:T(8,128)(2,1)}), bf16[64,48,384]{2,1,0:T(8,128)(2,1)}, u32[]{:S(2)}, u32[]{:S(2)}) async-start(bf16[64,48,384]{2,1,0:T(8,128)(2,1)} %bitcast.51), calls=%async_computation | async-start | bytes 4718592 | tf_op jit(solution)/shard_map/all_to_all | solution.py:158
  251.8 55.0 %all-to-all-done = bf16[64,48,384]{2,1,0:T(8,128)(2,1)} async-done(((bf16[64,48,384]{2,1,0:T(8,128)(2,1)}), bf16[64,48,384]{2,1,0:T(8,128)(2,1)}, u32[]{:S(2)}, u32[]{:S(2)}) %all-to-all-start) | async-done | bytes 2359328 | tf_op jit(solution)/shard_map/all_to_all | solution.py:158
  312.2 6.6 %collective-permute-start.17 = (f32[48,192]{1,0:T(8,128)S(1)}, f32[48,192]{1,0:T(8,128)S(1)}, u32[]{:S(2)}, u32[]{:S(2)}) collective-permute-start(f32[48,192]{1,0:T(8,128)S(1)} %bitcast.57), channel_id=1, source_target_pairs={{0,2},{1,3},{2,0},{3,1},{4,6},{5,7},{6,4},{7,5},{8,10},{9,11},{10,... | collective-permute-start | bytes 110600 | tf_op jit(solution)/shard_map/ppermute | solution.py:166
  (54 shorter events, 48.6 us)
Async XLA Ops:
  0.6 61.5 %copy-start = (bf16[1,1,384,3072]{3,2,1,0:T(8,128)(2,1)S(1)}, bf16[1,1,384,3072]{3,2,1,0:T(8,128)(2,1)}, u32[]{:S(2)}) copy-start(bf16[1,1,384,3072]{3,2,1,0:T(8,128)(2,1)} %param.10) | copy-start | bytes 7077892
  0.6 16.0 %copy-start.4 = (s32[1,5]{1,0:T(1,128)S(1)}, s32[1,5]{1,0:T(1,128)}, u32[]{:S(2)}) copy-start(s32[1,5]{1,0:T(1,128)} %param.9) | copy-start | bytes 64
  2.2 65.1 %copy-start.2 = (bf16[2,384,768]{2,1,0:T(8,128)(2,1)}, bf16[2,384,768]{2,1,0:T(8,128)(2,1)S(1)}, u32[]{:S(2)}) copy-start(bf16[2,384,768]{2,1,0:T(8,128)(2,1)S(1)} %pad_maximum_fusion.refs_4_) | copy-start | bytes 3538948
  2.2 33.7 %collective-permute-start = (bf16[2,384,768]{2,1,0:T(8,128)(2,1)S(1)}, bf16[2,384,768]{2,1,0:T(8,128)(2,1)}, u32[]{:S(2)}, u32[]{:S(2)}) collective-permute-start(bf16[2,384,768]{2,1,0:T(8,128)(2,1)S(1)} %pad_maximum_fusion.refs_4_), channel_id=1, source_target_pairs={{0,16},{4,20},{8,24},{12,28},{16,32},{20,36},{24,40},{28,44},{32,4... | collective-permute-start | bytes 3538952 | tf_op jit(solution)/shard_map/ppermute | solution.py:23
  6.0 29.8 %collective-permute-start.1 = (bf16[2,384,768]{2,1,0:T(8,128)(2,1)S(1)}, bf16[2,384,768]{2,1,0:T(8,128)(2,1)}, u32[]{:S(2)}, u32[]{:S(2)}) collective-permute-start(bf16[2,384,768]{2,1,0:T(8,128)(2,1)S(1)} %pad_maximum_fusion.refs_4_), channel_id=1, source_target_pairs={{0,4},{4,8},{8,12},{16,20},{20,24},{24,28},{32,36},{36,40},{40,44}... | collective-permute-start | bytes 3538952 | tf_op jit(solution)/shard_map/ppermute | solution.py:23
  10.5 29.1 %collective-permute-start.2 = (bf16[2,384,768]{2,1,0:T(8,128)(2,1)S(1)}, bf16[2,384,768]{2,1,0:T(8,128)(2,1)}, u32[]{:S(2)}, u32[]{:S(2)}) collective-permute-start(bf16[2,384,768]{2,1,0:T(8,128)(2,1)S(1)} %pad_maximum_fusion.refs_4_), channel_id=1, source_target_pairs={{4,0},{8,4},{12,8},{20,16},{24,20},{28,24},{36,32},{40,36},{44,40}... | collective-permute-start | bytes 3538952 | tf_op jit(solution)/shard_map/ppermute | solution.py:23
  11.8 44.8 %collective-permute-start.5 = (bf16[2,384,768]{2,1,0:T(8,128)(2,1)S(1)}, bf16[2,384,768]{2,1,0:T(8,128)(2,1)}, u32[]{:S(2)}, u32[]{:S(2)}) collective-permute-start(bf16[2,384,768]{2,1,0:T(8,128)(2,1)S(1)} %pad_maximum_fusion.refs_4_), channel_id=1, source_target_pairs={{16,0},{20,4},{24,8},{28,12},{32,16},{36,20},{40,24},{44,28},{48,3... | collective-permute-start | bytes 3538952 | tf_op jit(solution)/shard_map/ppermute | solution.py:23
  39.6 29.0 %collective-permute-start.3 = (bf16[2,384,768]{2,1,0:T(8,128)(2,1)}, bf16[2,384,768]{2,1,0:T(8,128)(2,1)S(1)}, u32[]{:S(2)}, u32[]{:S(2)}) collective-permute-start(bf16[2,384,768]{2,1,0:T(8,128)(2,1)} %collective-permute-done.refs_1_), channel_id=1, source_target_pairs={{0,4},{4,8},{8,12},{16,20},{20,24},{24,28},{32,36},{36,40},{40,44}... | collective-permute-start | bytes 3538952 | tf_op jit(solution)/shard_map/ppermute | solution.py:23
  42.0 31.0 %collective-permute-start.4 = (bf16[2,384,768]{2,1,0:T(8,128)(2,1)}, bf16[2,384,768]{2,1,0:T(8,128)(2,1)S(1)}, u32[]{:S(2)}, u32[]{:S(2)}) collective-permute-start(bf16[2,384,768]{2,1,0:T(8,128)(2,1)} %collective-permute-done.refs_1_), channel_id=1, source_target_pairs={{4,0},{8,4},{12,8},{20,16},{24,20},{28,24},{36,32},{40,36},{44,40}... | collective-permute-start | bytes 3538952 | tf_op jit(solution)/shard_map/ppermute | solution.py:23
  56.5 34.7 %collective-permute-start.6 = (bf16[2,384,768]{2,1,0:T(8,128)(2,1)}, bf16[2,384,768]{2,1,0:T(8,128)(2,1)S(1)}, u32[]{:S(2)}, u32[]{:S(2)}) collective-permute-start(bf16[2,384,768]{2,1,0:T(8,128)(2,1)} %collective-permute-done.5.refs_7_), channel_id=1, source_target_pairs={{0,4},{4,8},{8,12},{16,20},{20,24},{24,28},{32,36},{36,40},{40,44}... | collective-permute-start | bytes 3538952 | tf_op jit(solution)/shard_map/ppermute | solution.py:23
  60.0 35.4 %collective-permute-start.7 = (bf16[2,384,768]{2,1,0:T(8,128)(2,1)}, bf16[2,384,768]{2,1,0:T(8,128)(2,1)S(1)}, u32[]{:S(2)}, u32[]{:S(2)}) collective-permute-start(bf16[2,384,768]{2,1,0:T(8,128)(2,1)} %collective-permute-done.5.refs_7_), channel_id=1, source_target_pairs={{4,0},{8,4},{12,8},{20,16},{24,20},{28,24},{36,32},{40,36},{44,40}... | collective-permute-start | bytes 3538952 | tf_op jit(solution)/shard_map/ppermute | solution.py:23
  134.4 27.1 %collective-permute-start.8 = (bf16[2,384,768]{2,1,0:T(8,128)(2,1)}, bf16[2,384,768]{2,1,0:T(8,128)(2,1)S(1)}, u32[]{:S(2)}, u32[]{:S(2)}) collective-permute-start(bf16[2,384,768]{2,1,0:T(8,128)(2,1)} %get-tuple-element.33), channel_id=1, source_target_pairs={{4,0},{8,4},{12,8},{20,16},{24,20},{28,24},{36,32},{40,36},{44,40}... | collective-permute-start | bytes 3538952 | tf_op jit(solution)/shard_map/ppermute | solution.py:23
  135.7 27.1 %collective-permute-start.9 = (bf16[2,384,768]{2,1,0:T(8,128)(2,1)}, bf16[2,384,768]{2,1,0:T(8,128)(2,1)S(1)}, u32[]{:S(2)}, u32[]{:S(2)}) collective-permute-start(bf16[2,384,768]{2,1,0:T(8,128)(2,1)} %get-tuple-element.34), channel_id=1, source_target_pairs={{0,4},{4,8},{8,12},{16,20},{20,24},{24,28},{32,36},{36,40},{40,44}... | collective-permute-start | bytes 3538952 | tf_op jit(solution)/shard_map/ppermute | solution.py:23
  162.8 31.4 %collective-permute-start.13 = (bf16[2,384,768]{2,1,0:T(8,128)(2,1)}, bf16[2,384,768]{2,1,0:T(8,128)(2,1)S(1)}, u32[]{:S(2)}, u32[]{:S(2)}) collective-permute-start(bf16[2,384,768]{2,1,0:T(8,128)(2,1)} %get-tuple-element.45), channel_id=1, source_target_pairs={{4,0},{8,4},{12,8},{20,16},{24,20},{28,24},{36,32},{40,36},{44,40}... | collective-permute-start | bytes 3538952 | tf_op jit(solution)/shard_map/ppermute | solution.py:23
  164.1 31.6 %collective-permute-start.14 = (bf16[2,384,768]{2,1,0:T(8,128)(2,1)}, bf16[2,384,768]{2,1,0:T(8,128)(2,1)S(1)}, u32[]{:S(2)}, u32[]{:S(2)}) collective-permute-start(bf16[2,384,768]{2,1,0:T(8,128)(2,1)} %get-tuple-element.46), channel_id=1, source_target_pairs={{0,4},{4,8},{8,12},{16,20},{20,24},{24,28},{32,36},{36,40},{40,44}... | collective-permute-start | bytes 3538952 | tf_op jit(solution)/shard_map/ppermute | solution.py:23
  169.1 26.6 %copy-start.3 = (bf16[2,384,768]{2,1,0:T(8,128)(2,1)S(1)}, bf16[2,384,768]{2,1,0:T(8,128)(2,1)}, u32[]{:S(2)}) copy-start(bf16[2,384,768]{2,1,0:T(8,128)(2,1)} %get-tuple-element.44) | copy-start | bytes 3538948
  172.0 39.0 %collective-permute-start.12 = (bf16[2,384,768]{2,1,0:T(8,128)(2,1)}, bf16[2,384,768]{2,1,0:T(8,128)(2,1)S(1)}, u32[]{:S(2)}, u32[]{:S(2)}) collective-permute-start(bf16[2,384,768]{2,1,0:T(8,128)(2,1)} %add_convert_fusion.2), channel_id=1, source_target_pairs={{16,0},{20,4},{24,8},{28,12},{32,16},{36,20},{40,24},{44,28},{48,3... | collective-permute-start | bytes 3538952 | tf_op jit(solution)/shard_map/ppermute | solution.py:23
  186.4 28.4 %collective-permute-start.10 = (bf16[2,384,768]{2,1,0:T(8,128)(2,1)}, bf16[2,384,768]{2,1,0:T(8,128)(2,1)}, u32[]{:S(2)}, u32[]{:S(2)}) collective-permute-start(bf16[2,384,768]{2,1,0:T(8,128)(2,1)} %get-tuple-element.39), channel_id=1, source_target_pairs={{4,0},{8,4},{12,8},{20,16},{24,20},{28,24},{36,32},{40,36},{44,40}... | collective-permute-start | bytes 3538952 | tf_op jit(solution)/shard_map/ppermute | solution.py:23
  187.7 28.2 %collective-permute-start.11 = (bf16[2,384,768]{2,1,0:T(8,128)(2,1)}, bf16[2,384,768]{2,1,0:T(8,128)(2,1)}, u32[]{:S(2)}, u32[]{:S(2)}) collective-permute-start(bf16[2,384,768]{2,1,0:T(8,128)(2,1)} %get-tuple-element.40), channel_id=1, source_target_pairs={{0,4},{4,8},{8,12},{16,20},{20,24},{24,28},{32,36},{36,40},{40,44}... | collective-permute-start | bytes 3538952 | tf_op jit(solution)/shard_map/ppermute | solution.py:23
  197.2 29.0 %collective-permute-start.15 = (bf16[2,384,768]{2,1,0:T(8,128)(2,1)}, bf16[2,384,768]{2,1,0:T(8,128)(2,1)}, u32[]{:S(2)}, u32[]{:S(2)}) collective-permute-start(bf16[2,384,768]{2,1,0:T(8,128)(2,1)} %add_convert_fusion.1), channel_id=1, source_target_pairs={{0,16},{4,20},{8,24},{12,28},{16,32},{20,36},{24,40},{28,44},{32,4... | collective-permute-start | bytes 3538952 | tf_op jit(solution)/shard_map/ppermute | solution.py:23
  211.0 15.2 %copy-start.1 = (bf16[2,384,768]{2,1,0:T(8,128)(2,1)}, bf16[2,384,768]{2,1,0:T(8,128)(2,1)S(1)}, u32[]{:S(2)}) copy-start(bf16[2,384,768]{2,1,0:T(8,128)(2,1)S(1)} %collective-permute-done.12) | copy-start | bytes 3538948
  234.5 4.6 %collective-permute-start.16 = (bf16[3072,384]{1,0:T(8,128)(2,1)S(1)}, bf16[3072,384]{1,0:T(8,128)(2,1)S(1)}, u32[]{:S(2)}, u32[]{:S(2)}) collective-permute-start(bf16[3072,384]{1,0:T(8,128)(2,1)S(1)} %convolution_convert_fusion), channel_id=1, source_target_pairs={{0,1},{1,0},{2,3},{3,2},{4,5},{5,4},{6,7},{7,6},{8,9},{9,8},{10,11... | collective-permute-start | bytes 7077896 | tf_op jit(solution)/shard_map/ppermute | solution.py:154
  242.3 64.5 %all-to-all-start = ((bf16[64,48,384]{2,1,0:T(8,128)(2,1)}), bf16[64,48,384]{2,1,0:T(8,128)(2,1)}, u32[]{:S(2)}, u32[]{:S(2)}) async-start(bf16[64,48,384]{2,1,0:T(8,128)(2,1)} %bitcast.51), calls=%async_computation | async-start | bytes 4718592 | tf_op jit(solution)/shard_map/all_to_all | solution.py:158
  312.2 8.7 %collective-permute-start.17 = (f32[48,192]{1,0:T(8,128)S(1)}, f32[48,192]{1,0:T(8,128)S(1)}, u32[]{:S(2)}, u32[]{:S(2)}) collective-permute-start(f32[48,192]{1,0:T(8,128)S(1)} %bitcast.57), channel_id=1, source_target_pairs={{0,2},{1,3},{2,0},{3,1},{4,6},{5,7},{6,4},{7,5},{8,10},{9,11},{10,... | collective-permute-start | bytes 110600 | tf_op jit(solution)/shard_map/ppermute | solution.py:166
  (4 other events, 4.1 us)

commit v9 on v7

--- a/solution.py
+++ b/solution.py
@@ -138,17 +138,15 @@
     sibling_part = lax.ppermute(
         sent_part.astype(jnp.bfloat16), "dp", [(index, index ^ 1) for index in range(dp_count)]
     )
-    core_sum = (kept_part + sibling_part.astype(jnp.float32)).astype(jnp.bfloat16)
-    by_column = lax.all_to_all(
-        core_sum.reshape(sp_count, col_block, -1), "sp", 0, 0, tiled=True
+    core_sum = (kept_part + sibling_part.astype(jnp.float32)).reshape(model_width, dp_count // 2, row_block)
+    own_half = lax.dynamic_index_in_dim(core_sum, high, 1, keepdims=False)
+    other_half = lax.dynamic_index_in_dim(core_sum, 1 - high, 1, keepdims=False).astype(jnp.bfloat16)
+    partner_half = lax.ppermute(
+        other_half, "dp", [(index, (index + 2) % dp_count) for index in range(dp_count)]
     )
-    column_sum = by_column.astype(jnp.float32).sum(0).reshape(col_block, dp_count // 2, row_block)
-    own_half = lax.dynamic_index_in_dim(column_sum, high, 1, keepdims=False)
-    other_half = lax.dynamic_index_in_dim(column_sum, 1 - high, 1, keepdims=False)
-    weight_grad = (
-        own_half
-        + lax.ppermute(other_half, "dp", [(index, (index + 2) % dp_count) for index in range(dp_count)])
-    ).T
+    clip_sum = (own_half + partner_half.astype(jnp.float32)).astype(jnp.bfloat16)
+    by_column = lax.all_to_all(clip_sum.reshape(sp_count, col_block, row_block), "sp", 0, 0, tiled=True)
+    weight_grad = by_column.astype(jnp.float32).sum(0).T
     early_in = [shifted(back[0], 0, -1, True), shifted(back[2], 0, 1, True)]
     early_in, late_out, row_out = lax.optimization_barrier((early_in, [back[6], back[8]], [back[3], back[5]]))
     earlier_sum = back[1].astype(jnp.float32) + early_in[0].astype(jnp.float32) + early_in[1].astype(jnp.float32)

time: 303 us -> 319 us (1.053)
  the two profiles are of different devices: /device:TPU:24 before, /device:TPU:32 now
where the time goes in v9:
time: 319 us; the launch traced here: 318 us
  waiting for transfers between devices  166 us (52%)
  starting transfers between devices  78.1 us (24%)
  Pallas kernels  38 us (12%)
  other arithmetic  12.5 us (4%)
  local copies, waits for them, and re-layouts  11.3 us (4%)
  matrix products  11.1 us (3%)
    ppermute x16, waiting for transfers between devices, neighbour_shift(): return lax.ppermute(value, axis, pairs)  147 us
    ppermute x16, starting transfers between devices, neighbour_shift(): return lax.ppermute(value, axis, pairs)  48.9 us
    pallas_call x1, Pallas kernels, body(): pl.pallas_call(functools.partial(tile_attention, score_scale=score_scale)...  38 us
    all_to_all x1, starting transfers between devices, body(): lax.all_to_all(clip_sum.reshape(sp_count, col_block, row_block), 'sp', 0,...  23.7 us
    ppermute x1, waiting for transfers between devices, body(): lax.ppermute(other_half, 'dp', [(index, (index + 2) % dp_count) for index...  19 us
  transfers between devices with their start and end apart: 19, of which 11 were waited for; matrix products, arithmetic and copies ran while one was open for 8% of the time, Pallas kernels for 0%

profile of v9, /device:TPU:32, one launch (start us, length us, event | category | flops | bytes accessed | tf_op | source)
XLA Modules:
  0.0 318.3 jit_solution(13124501100024222685)
XLA Ops:
  2.2 3.8 %collective-permute-start = (bf16[2,384,768]{2,1,0:T(8,128)(2,1)S(1)}, bf16[2,384,768]{2,1,0:T(8,128)(2,1)}, u32[]{:S(2)}, u32[]{:S(2)}) collective-permute-start(bf16[2,384,768]{2,1,0:T(8,128)(2,1)S(1)} %pad_maximum_fusion.refs_4_), channel_id=1, source_target_pairs={{0,16},{4,20},{8,24},{12,28},{16,32},{20,36},{24,40},{28,44},{32,4... | collective-permute-start | bytes 3538952 | tf_op jit(solution)/shard_map/ppermute | solution.py:23
  6.0 4.4 %collective-permute-start.1 = (bf16[2,384,768]{2,1,0:T(8,128)(2,1)S(1)}, bf16[2,384,768]{2,1,0:T(8,128)(2,1)}, u32[]{:S(2)}, u32[]{:S(2)}) collective-permute-start(bf16[2,384,768]{2,1,0:T(8,128)(2,1)S(1)} %pad_maximum_fusion.refs_4_), channel_id=1, source_target_pairs={{0,4},{4,8},{8,12},{16,20},{20,24},{24,28},{32,36},{36,40},{40,44}... | collective-permute-start | bytes 3538952 | tf_op jit(solution)/shard_map/ppermute | solution.py:23
  11.7 3.1 collective-permute-start.5
  14.9 17.0 %collective-permute-done.refs_1_ = bf16[2,384,768]{2,1,0:T(8,128)(2,1)} collective-permute-done((bf16[2,384,768]{2,1,0:T(8,128)(2,1)S(1)}, bf16[2,384,768]{2,1,0:T(8,128)(2,1)}, u32[]{:S(2)}, u32[]{:S(2)}) %collective-permute-start) | collective-permute-done | bytes 1179680 | tf_op jit(solution)/shard_map/ppermute | solution.py:23
  34.3 5.2 %collective-permute-done.2.refs_5_ = bf16[2,384,768]{2,1,0:T(8,128)(2,1)} collective-permute-done((bf16[2,384,768]{2,1,0:T(8,128)(2,1)S(1)}, bf16[2,384,768]{2,1,0:T(8,128)(2,1)}, u32[]{:S(2)}, u32[]{:S(2)}) %collective-permute-start.2) | collective-permute-done | bytes 1179680 | tf_op jit(solution)/shard_map/ppermute | solution.py:23
  39.6 3.4 %collective-permute-start.3 = (bf16[2,384,768]{2,1,0:T(8,128)(2,1)}, bf16[2,384,768]{2,1,0:T(8,128)(2,1)}, u32[]{:S(2)}, u32[]{:S(2)}) collective-permute-start(bf16[2,384,768]{2,1,0:T(8,128)(2,1)} %collective-permute-done.refs_1_), channel_id=1, source_target_pairs={{0,4},{4,8},{8,12},{16,20},{20,24},{24,28},{32,36},{36,40},{40,44}... | collective-permute-start | bytes 3538952 | tf_op jit(solution)/shard_map/ppermute | solution.py:23
  44.3 14.4 %collective-permute-done.5.refs_7_ = bf16[2,384,768]{2,1,0:T(8,128)(2,1)} collective-permute-done((bf16[2,384,768]{2,1,0:T(8,128)(2,1)S(1)}, bf16[2,384,768]{2,1,0:T(8,128)(2,1)}, u32[]{:S(2)}, u32[]{:S(2)}) %collective-permute-start.5) | collective-permute-done | bytes 1179680 | tf_op jit(solution)/shard_map/ppermute | solution.py:23
  58.7 4.4 %collective-permute-start.6 = (bf16[2,384,768]{2,1,0:T(8,128)(2,1)}, bf16[2,384,768]{2,1,0:T(8,128)(2,1)}, u32[]{:S(2)}, u32[]{:S(2)}) collective-permute-start(bf16[2,384,768]{2,1,0:T(8,128)(2,1)} %collective-permute-done.5.refs_7_), channel_id=1, source_target_pairs={{0,4},{4,8},{8,12},{16,20},{20,24},{24,28},{32,36},{36,40},{40,44}... | collective-permute-start | bytes 3538952 | tf_op jit(solution)/shard_map/ppermute | solution.py:23
  65.2 5.2 %fusion.6.grad_ref = bf16[384,768]{1,0:T(8,128)(2,1)} fusion(bf16[768,3072]{1,0:T(8,128)(2,1)} %param.11, bf16[1,1,384,3072]{3,2,1,0:T(8,128)(2,1)S(1)} %copy-done), kind=kOutput, calls=%fused_computation.14 | convolution fusion | flops 1812234240 | bytes 7667712 | tf_op jit(solution)/shard_map/dot_general | solution.py:98
  70.4 3.7 %collective-permute-done.4.refs_2_ = bf16[2,384,768]{2,1,0:T(8,128)(2,1)} collective-permute-done((bf16[2,384,768]{2,1,0:T(8,128)(2,1)}, bf16[2,384,768]{2,1,0:T(8,128)(2,1)}, u32[]{:S(2)}, u32[]{:S(2)}) %collective-permute-start.4) | collective-permute-done | bytes 1179680 | tf_op jit(solution)/shard_map/ppermute | solution.py:23
  74.1 17.2 %collective-permute-done.6.refs_6_ = bf16[2,384,768]{2,1,0:T(8,128)(2,1)} collective-permute-done((bf16[2,384,768]{2,1,0:T(8,128)(2,1)}, bf16[2,384,768]{2,1,0:T(8,128)(2,1)}, u32[]{:S(2)}, u32[]{:S(2)}) %collective-permute-start.6) | collective-permute-done | bytes 1179680 | tf_op jit(solution)/shard_map/ppermute | solution.py:23
  91.3 5.1 %collective-permute-done.7.refs_8_ = bf16[2,384,768]{2,1,0:T(8,128)(2,1)} collective-permute-done((bf16[2,384,768]{2,1,0:T(8,128)(2,1)}, bf16[2,384,768]{2,1,0:T(8,128)(2,1)}, u32[]{:S(2)}, u32[]{:S(2)}) %collective-permute-start.7) | collective-permute-done | bytes 1179680 | tf_op jit(solution)/shard_map/ppermute | solution.py:23
  96.4 38.0 %shard_map.93 = (bf16[384,768]{1,0:T(8,128)(2,1)}, bf16[384,768]{1,0:T(8,128)(2,1)}, bf16[2,384,768]{2,1,0:T(8,128)(2,1)}, bf16[2,384,768]{2,1,0:T(8,128)(2,1)},...) custom-call(s32[1,3456]{1,0:T(1,128)} %bitcast.64, ...), custom_call_target="tpu_custom_call" | custom-call | flops 10192158720 | bytes 23592960 | tf_op jit(solution)/shard_map/pallas_call | solution.py:106
  140.0 5.6 %collective-permute-start.9 = (bf16[2,384,768]{2,1,0:T(8,128)(2,1)}, bf16[2,384,768]{2,1,0:T(8,128)(2,1)}, u32[]{:S(2)}, u32[]{:S(2)}) collective-permute-start(bf16[2,384,768]{2,1,0:T(8,128)(2,1)} %get-tuple-element.30), channel_id=1, source_target_pairs={{0,4},{4,8},{8,12},{16,20},{20,24},{24,28},{32,36},{36,40},{40,44}... | collective-permute-start | bytes 3538952 | tf_op jit(solution)/shard_map/ppermute | solution.py:23
  145.6 3.0 bitcast_add_fusion
  150.9 5.5 %collective-permute-start.17 = (bf16[3072,192]{0,1:T(8,128)(2,1)S(1)}, bf16[3072,192]{0,1:T(8,128)(2,1)}, u32[]{:S(2)}, u32[]{:S(2)}) collective-permute-start(bf16[3072,192]{0,1:T(8,128)(2,1)S(1)} %fusion.9), channel_id=1, source_target_pairs={{0,2},{1,3},{2,0},{3,1},{4,6},{5,7},{6,4},{7,5},{8,10},{9,11},{10,... | collective-permute-start | bytes 3538952 | tf_op jit(solution)/shard_map/ppermute | solution.py:144
  156.4 12.9 %collective-permute-done.8 = bf16[2,384,768]{2,1,0:T(8,128)(2,1)} collective-permute-done((bf16[2,384,768]{2,1,0:T(8,128)(2,1)}, bf16[2,384,768]{2,1,0:T(8,128)(2,1)}, u32[]{:S(2)}, u32[]{:S(2)}) %collective-permute-start.8) | collective-permute-done | bytes 1179680 | tf_op jit(solution)/shard_map/ppermute | solution.py:23
  171.7 6.0 %collective-permute-start.14 = (bf16[2,384,768]{2,1,0:T(8,128)(2,1)}, bf16[2,384,768]{2,1,0:T(8,128)(2,1)}, u32[]{:S(2)}, u32[]{:S(2)}) collective-permute-start(bf16[2,384,768]{2,1,0:T(8,128)(2,1)} %get-tuple-element.42), channel_id=1, source_target_pairs={{0,4},{4,8},{8,12},{16,20},{20,24},{24,28},{32,36},{36,40},{40,44}... | collective-permute-start | bytes 3538952 | tf_op jit(solution)/shard_map/ppermute | solution.py:23
  182.0 19.0 %collective-permute-done.17 = bf16[3072,192]{0,1:T(8,128)(2,1)} collective-permute-done((bf16[3072,192]{0,1:T(8,128)(2,1)S(1)}, bf16[3072,192]{0,1:T(8,128)(2,1)}, u32[]{:S(2)}, u32[]{:S(2)}) %collective-permute-start.17) | collective-permute-done | bytes 1179680 | tf_op jit(solution)/shard_map/ppermute | solution.py:144
  202.6 3.4 %fusion.1 = bf16[3072,192]{1,0:T(8,128)(2,1)} fusion(f32[3072,1,192]{2,0,1:T(8,128)} %copy.17, bf16[3072,192]{1,0:T(8,128)(2,1)S(1)} %copy.18), kind=kLoop, calls=%fused_computation.4 | loop fusion | flops 1769472 | bytes 4718592 | tf_op jit(solution)/shard_map/convert_element_type | solution.py:147
  206.0 23.7 %all-to-all-start = ((bf16[64,48,192]{2,1,0:T(8,128)(2,1)}), bf16[64,48,192]{2,1,0:T(8,128)(2,1)}, u32[]{:S(2)}, u32[]{:S(2)}) async-start(bf16[64,48,192]{2,1,0:T(8,128)(2,1)} %bitcast.16), calls=%async_computation | async-start | bytes 3145728 | tf_op jit(solution)/shard_map/all_to_all | solution.py:148
  235.8 4.6 %collective-permute-start.11 = (bf16[2,384,768]{2,1,0:T(8,128)(2,1)S(1)}, bf16[2,384,768]{2,1,0:T(8,128)(2,1)S(1)}, u32[]{:S(2)}, u32[]{:S(2)}) collective-permute-start(bf16[2,384,768]{2,1,0:T(8,128)(2,1)S(1)} %copy-done.8), channel_id=1, source_target_pairs={{0,4},{4,8},{8,12},{16,20},{20,24},{24,28},{32,36},{36,40},{40,44}... | collective-permute-start | bytes 3538952 | tf_op jit(solution)/shard_map/ppermute | solution.py:23
  242.6 3.4 %collective-permute-start.15 = (bf16[2,384,768]{2,1,0:T(8,128)(2,1)S(1)}, bf16[2,384,768]{2,1,0:T(8,128)(2,1)S(1)}, u32[]{:S(2)}, u32[]{:S(2)}) collective-permute-start(bf16[2,384,768]{2,1,0:T(8,128)(2,1)S(1)} %add_convert_fusion.1), channel_id=1, source_target_pairs={{0,16},{4,20},{8,24},{12,28},{16,32},{20,36},{24,40},{28,44},{32,4... | collective-permute-start | bytes 3538952 | tf_op jit(solution)/shard_map/ppermute | solution.py:23
  246.0 68.1 %collective-permute-done.12 = bf16[2,384,768]{2,1,0:T(8,128)(2,1)S(1)} collective-permute-done((bf16[2,384,768]{2,1,0:T(8,128)(2,1)S(1)}, bf16[2,384,768]{2,1,0:T(8,128)(2,1)S(1)}, u32[]{:S(2)}, u32[]{:S(2)}) %collective-permute-start.12) | collective-permute-done | bytes 1179680 | tf_op jit(solution)/shard_map/ppermute | solution.py:23
  (57 shorter events, 37.0 us)
Async XLA Ops:
  0.6 64.6 %copy-start = (bf16[1,1,384,3072]{3,2,1,0:T(8,128)(2,1)S(1)}, bf16[1,1,384,3072]{3,2,1,0:T(8,128)(2,1)}, u32[]{:S(2)}) copy-start(bf16[1,1,384,3072]{3,2,1,0:T(8,128)(2,1)} %param.10) | copy-start | bytes 7077892
  0.6 14.2 %copy-start.7 = (s32[1,5]{1,0:T(1,128)S(1)}, s32[1,5]{1,0:T(1,128)}, u32[]{:S(2)}) copy-start(s32[1,5]{1,0:T(1,128)} %param.9) | copy-start | bytes 64
  2.2 68.3 %copy-start.4 = (bf16[2,384,768]{2,1,0:T(8,128)(2,1)}, bf16[2,384,768]{2,1,0:T(8,128)(2,1)S(1)}, u32[]{:S(2)}) copy-start(bf16[2,384,768]{2,1,0:T(8,128)(2,1)S(1)} %pad_maximum_fusion.refs_4_) | copy-start | bytes 3538948
  2.2 29.7 %collective-permute-start = (bf16[2,384,768]{2,1,0:T(8,128)(2,1)S(1)}, bf16[2,384,768]{2,1,0:T(8,128)(2,1)}, u32[]{:S(2)}, u32[]{:S(2)}) collective-permute-start(bf16[2,384,768]{2,1,0:T(8,128)(2,1)S(1)} %pad_maximum_fusion.refs_4_), channel_id=1, source_target_pairs={{0,16},{4,20},{8,24},{12,28},{16,32},{20,36},{24,40},{28,44},{32,4... | collective-permute-start | bytes 3538952 | tf_op jit(solution)/shard_map/ppermute | solution.py:23
  6.0 28.3 %collective-permute-start.1 = (bf16[2,384,768]{2,1,0:T(8,128)(2,1)S(1)}, bf16[2,384,768]{2,1,0:T(8,128)(2,1)}, u32[]{:S(2)}, u32[]{:S(2)}) collective-permute-start(bf16[2,384,768]{2,1,0:T(8,128)(2,1)S(1)} %pad_maximum_fusion.refs_4_), channel_id=1, source_target_pairs={{0,4},{4,8},{8,12},{16,20},{20,24},{24,28},{32,36},{36,40},{40,44}... | collective-permute-start | bytes 3538952 | tf_op jit(solution)/shard_map/ppermute | solution.py:23
  10.5 29.1 %collective-permute-start.2 = (bf16[2,384,768]{2,1,0:T(8,128)(2,1)S(1)}, bf16[2,384,768]{2,1,0:T(8,128)(2,1)}, u32[]{:S(2)}, u32[]{:S(2)}) collective-permute-start(bf16[2,384,768]{2,1,0:T(8,128)(2,1)S(1)} %pad_maximum_fusion.refs_4_), channel_id=1, source_target_pairs={{4,0},{8,4},{12,8},{20,16},{24,20},{28,24},{36,32},{40,36},{44,40}... | collective-permute-start | bytes 3538952 | tf_op jit(solution)/shard_map/ppermute | solution.py:23
  11.7 47.0 %collective-permute-start.5 = (bf16[2,384,768]{2,1,0:T(8,128)(2,1)S(1)}, bf16[2,384,768]{2,1,0:T(8,128)(2,1)}, u32[]{:S(2)}, u32[]{:S(2)}) collective-permute-start(bf16[2,384,768]{2,1,0:T(8,128)(2,1)S(1)} %pad_maximum_fusion.refs_4_), channel_id=1, source_target_pairs={{16,0},{20,4},{24,8},{28,12},{32,16},{36,20},{40,24},{44,28},{48,3... | collective-permute-start | bytes 3538952 | tf_op jit(solution)/shard_map/ppermute | solution.py:23
  39.6 30.8 %collective-permute-start.3 = (bf16[2,384,768]{2,1,0:T(8,128)(2,1)}, bf16[2,384,768]{2,1,0:T(8,128)(2,1)}, u32[]{:S(2)}, u32[]{:S(2)}) collective-permute-start(bf16[2,384,768]{2,1,0:T(8,128)(2,1)} %collective-permute-done.refs_1_), channel_id=1, source_target_pairs={{0,4},{4,8},{8,12},{16,20},{20,24},{24,28},{32,36},{36,40},{40,44}... | collective-permute-start | bytes 3538952 | tf_op jit(solution)/shard_map/ppermute | solution.py:23
  43.0 31.1 %collective-permute-start.4 = (bf16[2,384,768]{2,1,0:T(8,128)(2,1)}, bf16[2,384,768]{2,1,0:T(8,128)(2,1)}, u32[]{:S(2)}, u32[]{:S(2)}) collective-permute-start(bf16[2,384,768]{2,1,0:T(8,128)(2,1)} %collective-permute-done.refs_1_), channel_id=1, source_target_pairs={{4,0},{8,4},{12,8},{20,16},{24,20},{28,24},{36,32},{40,36},{44,40}... | collective-permute-start | bytes 3538952 | tf_op jit(solution)/shard_map/ppermute | solution.py:23
  58.7 32.6 %collective-permute-start.6 = (bf16[2,384,768]{2,1,0:T(8,128)(2,1)}, bf16[2,384,768]{2,1,0:T(8,128)(2,1)}, u32[]{:S(2)}, u32[]{:S(2)}) collective-permute-start(bf16[2,384,768]{2,1,0:T(8,128)(2,1)} %collective-permute-done.5.refs_7_), channel_id=1, source_target_pairs={{0,4},{4,8},{8,12},{16,20},{20,24},{24,28},{32,36},{36,40},{40,44}... | collective-permute-start | bytes 3538952 | tf_op jit(solution)/shard_map/ppermute | solution.py:23
  63.1 33.3 %collective-permute-start.7 = (bf16[2,384,768]{2,1,0:T(8,128)(2,1)}, bf16[2,384,768]{2,1,0:T(8,128)(2,1)}, u32[]{:S(2)}, u32[]{:S(2)}) collective-permute-start(bf16[2,384,768]{2,1,0:T(8,128)(2,1)} %collective-permute-done.5.refs_7_), channel_id=1, source_target_pairs={{4,0},{8,4},{12,8},{20,16},{24,20},{28,24},{36,32},{40,36},{44,40}... | collective-permute-start | bytes 3538952 | tf_op jit(solution)/shard_map/ppermute | solution.py:23
  138.7 6.9 %collective-permute-start.16 = (bf16[3072,384]{0,1:T(8,128)(2,1)}, bf16[3072,384]{0,1:T(8,128)(2,1)}, u32[]{:S(2)}, u32[]{:S(2)}) collective-permute-start(bf16[3072,384]{0,1:T(8,128)(2,1)} %fusion), channel_id=1, source_target_pairs={{0,1},{1,0},{2,3},{3,2},{4,5},{5,4},{6,7},{7,6},{8,9},{9,8},{10,11... | collective-permute-start | bytes 7077896 | tf_op jit(solution)/shard_map/ppermute | solution.py:138
  138.7 30.6 %collective-permute-start.8 = (bf16[2,384,768]{2,1,0:T(8,128)(2,1)}, bf16[2,384,768]{2,1,0:T(8,128)(2,1)}, u32[]{:S(2)}, u32[]{:S(2)}) collective-permute-start(bf16[2,384,768]{2,1,0:T(8,128)(2,1)} %get-tuple-element.29), channel_id=1, source_target_pairs={{4,0},{8,4},{12,8},{20,16},{24,20},{28,24},{36,32},{40,36},{44,40}... | collective-permute-start | bytes 3538952 | tf_op jit(solution)/shard_map/ppermute | solution.py:23
  140.0 30.5 %collective-permute-start.9 = (bf16[2,384,768]{2,1,0:T(8,128)(2,1)}, bf16[2,384,768]{2,1,0:T(8,128)(2,1)}, u32[]{:S(2)}, u32[]{:S(2)}) collective-permute-start(bf16[2,384,768]{2,1,0:T(8,128)(2,1)} %get-tuple-element.30), channel_id=1, source_target_pairs={{0,4},{4,8},{8,12},{16,20},{20,24},{24,28},{32,36},{36,40},{40,44}... | collective-permute-start | bytes 3538952 | tf_op jit(solution)/shard_map/ppermute | solution.py:23
  150.9 50.0 %collective-permute-start.17 = (bf16[3072,192]{0,1:T(8,128)(2,1)S(1)}, bf16[3072,192]{0,1:T(8,128)(2,1)}, u32[]{:S(2)}, u32[]{:S(2)}) collective-permute-start(bf16[3072,192]{0,1:T(8,128)(2,1)S(1)} %fusion.9), channel_id=1, source_target_pairs={{0,2},{1,3},{2,0},{3,1},{4,6},{5,7},{6,4},{7,5},{8,10},{9,11},{10,... | collective-permute-start | bytes 3538952 | tf_op jit(solution)/shard_map/ppermute | solution.py:144
  170.5 69.9 %collective-permute-start.13 = (bf16[2,384,768]{2,1,0:T(8,128)(2,1)}, bf16[2,384,768]{2,1,0:T(8,128)(2,1)}, u32[]{:S(2)}, u32[]{:S(2)}) collective-permute-start(bf16[2,384,768]{2,1,0:T(8,128)(2,1)} %get-tuple-element.41), channel_id=1, source_target_pairs={{4,0},{8,4},{12,8},{20,16},{24,20},{28,24},{36,32},{40,36},{44,40}... | collective-permute-start | bytes 3538952 | tf_op jit(solution)/shard_map/ppermute | solution.py:23
  171.7 68.7 %collective-permute-start.14 = (bf16[2,384,768]{2,1,0:T(8,128)(2,1)}, bf16[2,384,768]{2,1,0:T(8,128)(2,1)}, u32[]{:S(2)}, u32[]{:S(2)}) collective-permute-start(bf16[2,384,768]{2,1,0:T(8,128)(2,1)} %get-tuple-element.42), channel_id=1, source_target_pairs={{0,4},{4,8},{8,12},{16,20},{20,24},{24,28},{32,36},{36,40},{40,44}... | collective-permute-start | bytes 3538952 | tf_op jit(solution)/shard_map/ppermute | solution.py:23
  206.0 23.7 %copy-start.6 = (bf16[2,384,768]{2,1,0:T(8,128)(2,1)S(1)}, bf16[2,384,768]{2,1,0:T(8,128)(2,1)}, u32[]{:S(2)}) copy-start(bf16[2,384,768]{2,1,0:T(8,128)(2,1)} %get-tuple-element.37) | copy-start | bytes 3538948
  206.0 109.9 %all-to-all-start = ((bf16[64,48,192]{2,1,0:T(8,128)(2,1)}), bf16[64,48,192]{2,1,0:T(8,128)(2,1)}, u32[]{:S(2)}, u32[]{:S(2)}) async-start(bf16[64,48,192]{2,1,0:T(8,128)(2,1)} %bitcast.16), calls=%async_computation | async-start | bytes 3145728 | tf_op jit(solution)/shard_map/all_to_all | solution.py:148
  232.0 82.1 %collective-permute-start.12 = (bf16[2,384,768]{2,1,0:T(8,128)(2,1)S(1)}, bf16[2,384,768]{2,1,0:T(8,128)(2,1)S(1)}, u32[]{:S(2)}, u32[]{:S(2)}) collective-permute-start(bf16[2,384,768]{2,1,0:T(8,128)(2,1)S(1)} %add_convert_fusion.2), channel_id=1, source_target_pairs={{16,0},{20,4},{24,8},{28,12},{32,16},{36,20},{40,24},{44,28},{48,3... | collective-permute-start | bytes 3538952 | tf_op jit(solution)/shard_map/ppermute | solution.py:23
  234.4 79.6 %collective-permute-start.10 = (bf16[2,384,768]{2,1,0:T(8,128)(2,1)S(1)}, bf16[2,384,768]{2,1,0:T(8,128)(2,1)S(1)}, u32[]{:S(2)}, u32[]{:S(2)}) collective-permute-start(bf16[2,384,768]{2,1,0:T(8,128)(2,1)S(1)} %copy-done.9), channel_id=1, source_target_pairs={{4,0},{8,4},{12,8},{20,16},{24,20},{28,24},{36,32},{40,36},{44,40}... | collective-permute-start | bytes 3538952 | tf_op jit(solution)/shard_map/ppermute | solution.py:23
  235.8 78.3 %collective-permute-start.11 = (bf16[2,384,768]{2,1,0:T(8,128)(2,1)S(1)}, bf16[2,384,768]{2,1,0:T(8,128)(2,1)S(1)}, u32[]{:S(2)}, u32[]{:S(2)}) collective-permute-start(bf16[2,384,768]{2,1,0:T(8,128)(2,1)S(1)} %copy-done.8), channel_id=1, source_target_pairs={{0,4},{4,8},{8,12},{16,20},{20,24},{24,28},{32,36},{36,40},{40,44}... | collective-permute-start | bytes 3538952 | tf_op jit(solution)/shard_map/ppermute | solution.py:23
  240.4 73.7 %copy-start.3 = (bf16[2,384,768]{2,1,0:T(8,128)(2,1)S(1)}, bf16[2,384,768]{2,1,0:T(8,128)(2,1)}, u32[]{:S(2)}) copy-start(bf16[2,384,768]{2,1,0:T(8,128)(2,1)} %get-tuple-element.28) | copy-start | bytes 3538948
  242.6 71.5 %collective-permute-start.15 = (bf16[2,384,768]{2,1,0:T(8,128)(2,1)S(1)}, bf16[2,384,768]{2,1,0:T(8,128)(2,1)S(1)}, u32[]{:S(2)}, u32[]{:S(2)}) collective-permute-start(bf16[2,384,768]{2,1,0:T(8,128)(2,1)S(1)} %add_convert_fusion.1), channel_id=1, source_target_pairs={{0,16},{4,20},{8,24},{12,28},{16,32},{20,36},{24,40},{28,44},{32,4... | collective-permute-start | bytes 3538952 | tf_op jit(solution)/shard_map/ppermute | solution.py:23
  (5 other events, 27.6 us)

commit v10 on v7

--- a/solution.py
+++ b/solution.py
@@ -37,7 +37,7 @@
     scores = jnp.where(mask_ref[...] > 0, scores, -1e30)
     row_peak = jnp.max(scores, axis=1, keepdims=True)
     exp_scores = jnp.exp(scores - row_peak)
-    probs = exp_scores / jnp.sum(exp_scores, axis=1, keepdims=True)
+    probs = exp_scores * (1.0 / jnp.sum(exp_scores, axis=1, keepdims=True))
     probs_low = probs.astype(jnp.bfloat16)
     attn = jnp.dot(probs_low, value, preferred_element_type=jnp.float32).astype(jnp.bfloat16)
     attn_ref[...] = attn

time: 303 us -> 303 us (level)
  no operation moved by 1% of the time
where the time goes in v10:
time: 303 us; the launch traced here: 302 us
  waiting for transfers between devices  162 us (53%)
  starting transfers between devices  70.1 us (23%)
  Pallas kernels  38 us (13%)
  other arithmetic  11.3 us (4%)
  local copies, waits for them, and re-layouts  10.2 us (3%)
  matrix products  9.44 us (3%)
    ppermute x16, waiting for transfers between devices, neighbour_shift(): return lax.ppermute(value, axis, pairs)  150 us
    ppermute x16, starting transfers between devices, neighbour_shift(): return lax.ppermute(value, axis, pairs)  52.3 us
    pallas_call x1, Pallas kernels, body(): pl.pallas_call(functools.partial(tile_attention, score_scale=score_scale)...  38 us
    all_to_all x1, starting transfers between devices, body(): lax.all_to_all(core_sum.reshape(sp_count, col_block, -1), 'sp', 0, 0, til...  17.4 us
    ppermute x1, waiting for transfers between devices, body(): lax.ppermute(other_half, 'dp', [(index, (index + 2) % dp_count) for index...  6.9 us
  transfers between devices with their start and end apart: 19, of which 16 were waited for; matrix products, arithmetic and copies ran while one was open for 4% of the time, Pallas kernels for 0%

profile of v10, /device:TPU:24, one launch (start us, length us, event | category | flops | bytes accessed | tf_op | source)
XLA Modules:
  0.0 301.8 jit_solution(12147260894626723176)
XLA Ops:
  2.2 3.8 %collective-permute-start = (bf16[2,384,768]{2,1,0:T(8,128)(2,1)S(1)}, bf16[2,384,768]{2,1,0:T(8,128)(2,1)}, u32[]{:S(2)}, u32[]{:S(2)}) collective-permute-start(bf16[2,384,768]{2,1,0:T(8,128)(2,1)S(1)} %pad_maximum_fusion.refs_4_), channel_id=1, source_target_pairs={{0,16},{4,20},{8,24},{12,28},{16,32},{20,36},{24,40},{28,44},{32,4... | collective-permute-start | bytes 3538952 | tf_op jit(solution)/shard_map/ppermute | solution.py:23
  6.0 4.4 %collective-permute-start.1 = (bf16[2,384,768]{2,1,0:T(8,128)(2,1)S(1)}, bf16[2,384,768]{2,1,0:T(8,128)(2,1)}, u32[]{:S(2)}, u32[]{:S(2)}) collective-permute-start(bf16[2,384,768]{2,1,0:T(8,128)(2,1)S(1)} %pad_maximum_fusion.refs_4_), channel_id=1, source_target_pairs={{0,4},{4,8},{8,12},{16,20},{20,24},{24,28},{32,36},{36,40},{40,44}... | collective-permute-start | bytes 3538952 | tf_op jit(solution)/shard_map/ppermute | solution.py:23
  11.7 4.8 %collective-permute-start.5 = (bf16[2,384,768]{2,1,0:T(8,128)(2,1)S(1)}, bf16[2,384,768]{2,1,0:T(8,128)(2,1)}, u32[]{:S(2)}, u32[]{:S(2)}) collective-permute-start(bf16[2,384,768]{2,1,0:T(8,128)(2,1)S(1)} %pad_maximum_fusion.refs_4_), channel_id=1, source_target_pairs={{16,0},{20,4},{24,8},{28,12},{32,16},{36,20},{40,24},{44,28},{48,3... | collective-permute-start | bytes 3538952 | tf_op jit(solution)/shard_map/ppermute | solution.py:23
  16.6 19.2 %collective-permute-done.refs_1_ = bf16[2,384,768]{2,1,0:T(8,128)(2,1)} collective-permute-done((bf16[2,384,768]{2,1,0:T(8,128)(2,1)S(1)}, bf16[2,384,768]{2,1,0:T(8,128)(2,1)}, u32[]{:S(2)}, u32[]{:S(2)}) %collective-permute-start) | collective-permute-done | bytes 1179680 | tf_op jit(solution)/shard_map/ppermute | solution.py:23
  35.8 3.7 %collective-permute-done.2.refs_5_ = bf16[2,384,768]{2,1,0:T(8,128)(2,1)} collective-permute-done((bf16[2,384,768]{2,1,0:T(8,128)(2,1)S(1)}, bf16[2,384,768]{2,1,0:T(8,128)(2,1)}, u32[]{:S(2)}, u32[]{:S(2)}) %collective-permute-start.2) | collective-permute-done | bytes 1179680 | tf_op jit(solution)/shard_map/ppermute | solution.py:23
  44.3 12.3 %collective-permute-done.5.refs_7_ = bf16[2,384,768]{2,1,0:T(8,128)(2,1)} collective-permute-done((bf16[2,384,768]{2,1,0:T(8,128)(2,1)S(1)}, bf16[2,384,768]{2,1,0:T(8,128)(2,1)}, u32[]{:S(2)}, u32[]{:S(2)}) %collective-permute-start.5) | collective-permute-done | bytes 1179680 | tf_op jit(solution)/shard_map/ppermute | solution.py:23
  56.5 4.4 %collective-permute-start.6 = (bf16[2,384,768]{2,1,0:T(8,128)(2,1)}, bf16[2,384,768]{2,1,0:T(8,128)(2,1)}, u32[]{:S(2)}, u32[]{:S(2)}) collective-permute-start(bf16[2,384,768]{2,1,0:T(8,128)(2,1)} %collective-permute-done.5.refs_7_), channel_id=1, source_target_pairs={{0,4},{4,8},{8,12},{16,20},{20,24},{24,28},{32,36},{36,40},{40,44}... | collective-permute-start | bytes 3538952 | tf_op jit(solution)/shard_map/ppermute | solution.py:23
  63.1 5.2 %fusion.6.grad_ref = bf16[384,768]{1,0:T(8,128)(2,1)} fusion(bf16[768,3072]{1,0:T(8,128)(2,1)} %param.11, bf16[1,1,384,3072]{3,2,1,0:T(8,128)(2,1)S(1)} %copy-done), kind=kOutput, calls=%fused_computation.12 | convolution fusion | flops 1812234240 | bytes 7667712 | tf_op jit(solution)/shard_map/dot_general | solution.py:98
  68.7 5.4 %collective-permute-done.4.refs_2_ = bf16[2,384,768]{2,1,0:T(8,128)(2,1)} collective-permute-done((bf16[2,384,768]{2,1,0:T(8,128)(2,1)}, bf16[2,384,768]{2,1,0:T(8,128)(2,1)}, u32[]{:S(2)}, u32[]{:S(2)}) %collective-permute-start.4) | collective-permute-done | bytes 1179680 | tf_op jit(solution)/shard_map/ppermute | solution.py:23
  74.1 17.2 %collective-permute-done.6.refs_6_ = bf16[2,384,768]{2,1,0:T(8,128)(2,1)} collective-permute-done((bf16[2,384,768]{2,1,0:T(8,128)(2,1)}, bf16[2,384,768]{2,1,0:T(8,128)(2,1)}, u32[]{:S(2)}, u32[]{:S(2)}) %collective-permute-start.6) | collective-permute-done | bytes 1179680 | tf_op jit(solution)/shard_map/ppermute | solution.py:23
  91.3 5.1 %collective-permute-done.7.refs_8_ = bf16[2,384,768]{2,1,0:T(8,128)(2,1)} collective-permute-done((bf16[2,384,768]{2,1,0:T(8,128)(2,1)}, bf16[2,384,768]{2,1,0:T(8,128)(2,1)}, u32[]{:S(2)}, u32[]{:S(2)}) %collective-permute-start.7) | collective-permute-done | bytes 1179680 | tf_op jit(solution)/shard_map/ppermute | solution.py:23
  96.4 38.0 %shard_map.93 = (bf16[384,768]{1,0:T(8,128)(2,1)}, bf16[384,768]{1,0:T(8,128)(2,1)}, bf16[2,384,768]{2,1,0:T(8,128)(2,1)}, bf16[2,384,768]{2,1,0:T(8,128)(2,1)},...) custom-call(s32[1,3456]{1,0:T(1,128)} %bitcast.66, ...), custom_call_target="tpu_custom_call" | custom-call | flops 10192158720 | bytes 23592960 | tf_op jit(solution)/shard_map/pallas_call | solution.py:106
  137.5 4.5 %collective-permute-done.16 = bf16[3072,384]{0,1:T(8,128)(2,1)S(1)} collective-permute-done((bf16[3072,384]{0,1:T(8,128)(2,1)S(1)}, bf16[3072,384]{0,1:T(8,128)(2,1)S(1)}, u32[]{:S(2)}, u32[]{:S(2)}) %collective-permute-start.16) | collective-permute-done | bytes 2359328 | tf_op jit(solution)/shard_map/ppermute | solution.py:138
  144.9 4.3 %copy.13 = bf16[3072,384]{1,0:T(8,128)(2,1)} copy(bf16[3072,384]{0,1:T(8,128)(2,1)} %fusion) | data formatting | bytes 4718592 | tf_op jit(solution)/shard_map/convert_element_type | solution.py:141
  149.2 17.4 %all-to-all-start = ((bf16[64,48,384]{2,1,0:T(8,128)(2,1)}), bf16[64,48,384]{2,1,0:T(8,128)(2,1)}, u32[]{:S(2)}, u32[]{:S(2)}) async-start(bf16[64,48,384]{2,1,0:T(8,128)(2,1)} %bitcast.59), calls=%async_computation | async-start | bytes 4718592 | tf_op jit(solution)/shard_map/all_to_all | solution.py:142
  167.9 4.6 %collective-permute-start.9 = (bf16[2,384,768]{2,1,0:T(8,128)(2,1)}, bf16[2,384,768]{2,1,0:T(8,128)(2,1)S(1)}, u32[]{:S(2)}, u32[]{:S(2)}) collective-permute-start(bf16[2,384,768]{2,1,0:T(8,128)(2,1)} %get-tuple-element.30), channel_id=1, source_target_pairs={{0,4},{4,8},{8,12},{16,20},{20,24},{24,28},{32,36},{36,40},{40,44}... | collective-permute-start | bytes 3538952 | tf_op jit(solution)/shard_map/ppermute | solution.py:23
  172.5 46.2 %collective-permute-done.8 = bf16[2,384,768]{2,1,0:T(8,128)(2,1)S(1)} collective-permute-done((bf16[2,384,768]{2,1,0:T(8,128)(2,1)}, bf16[2,384,768]{2,1,0:T(8,128)(2,1)S(1)}, u32[]{:S(2)}, u32[]{:S(2)}) %collective-permute-start.8) | collective-permute-done | bytes 1179680 | tf_op jit(solution)/shard_map/ppermute | solution.py:23
  220.0 4.6 %collective-permute-start.14 = (bf16[2,384,768]{2,1,0:T(8,128)(2,1)}, bf16[2,384,768]{2,1,0:T(8,128)(2,1)S(1)}, u32[]{:S(2)}, u32[]{:S(2)}) collective-permute-start(bf16[2,384,768]{2,1,0:T(8,128)(2,1)} %get-tuple-element.42), channel_id=1, source_target_pairs={{0,4},{4,8},{8,12},{16,20},{20,24},{24,28},{32,36},{36,40},{40,44}... | collective-permute-start | bytes 3538952 | tf_op jit(solution)/shard_map/ppermute | solution.py:23
  226.2 5.4 %collective-permute-start.12 = (bf16[2,384,768]{2,1,0:T(8,128)(2,1)}, bf16[2,384,768]{2,1,0:T(8,128)(2,1)S(1)}, u32[]{:S(2)}, u32[]{:S(2)}) collective-permute-start(bf16[2,384,768]{2,1,0:T(8,128)(2,1)} %add_convert_fusion.2), channel_id=1, source_target_pairs={{16,0},{20,4},{24,8},{28,12},{32,16},{36,20},{40,24},{44,28},{48,3... | collective-permute-start | bytes 3538952 | tf_op jit(solution)/shard_map/ppermute | solution.py:23
  232.9 5.6 %collective-permute-start.11 = (bf16[2,384,768]{2,1,0:T(8,128)(2,1)}, bf16[2,384,768]{2,1,0:T(8,128)(2,1)}, u32[]{:S(2)}, u32[]{:S(2)}) collective-permute-start(bf16[2,384,768]{2,1,0:T(8,128)(2,1)} %get-tuple-element.36), channel_id=1, source_target_pairs={{0,4},{4,8},{8,12},{16,20},{20,24},{24,28},{32,36},{36,40},{40,44}... | collective-permute-start | bytes 3538952 | tf_op jit(solution)/shard_map/ppermute | solution.py:23
  238.6 11.2 %collective-permute-done.13 = bf16[2,384,768]{2,1,0:T(8,128)(2,1)S(1)} collective-permute-done((bf16[2,384,768]{2,1,0:T(8,128)(2,1)}, bf16[2,384,768]{2,1,0:T(8,128)(2,1)S(1)}, u32[]{:S(2)}, u32[]{:S(2)}) %collective-permute-start.13) | collective-permute-done | bytes 1179680 | tf_op jit(solution)/shard_map/ppermute | solution.py:23
  258.4 14.7 %collective-permute-done.10 = bf16[2,384,768]{2,1,0:T(8,128)(2,1)} collective-permute-done((bf16[2,384,768]{2,1,0:T(8,128)(2,1)}, bf16[2,384,768]{2,1,0:T(8,128)(2,1)}, u32[]{:S(2)}, u32[]{:S(2)}) %collective-permute-start.10) | collective-permute-done | bytes 1179680 | tf_op jit(solution)/shard_map/ppermute | solution.py:23
  274.3 10.0 %collective-permute-done.15 = bf16[2,384,768]{2,1,0:T(8,128)(2,1)} collective-permute-done((bf16[2,384,768]{2,1,0:T(8,128)(2,1)}, bf16[2,384,768]{2,1,0:T(8,128)(2,1)}, u32[]{:S(2)}, u32[]{:S(2)}) %collective-permute-start.15) | collective-permute-done | bytes 1179680 | tf_op jit(solution)/shard_map/ppermute | solution.py:23
  294.3 6.9 %collective-permute-done.17 = f32[48,192]{1,0:T(8,128)S(1)} collective-permute-done((f32[48,192]{1,0:T(8,128)S(1)}, f32[48,192]{1,0:T(8,128)S(1)}, u32[]{:S(2)}, u32[]{:S(2)}) %collective-permute-start.17) | collective-permute-done | bytes 36896 | tf_op jit(solution)/shard_map/ppermute | solution.py:150
  (49 shorter events, 41.7 us)
Async XLA Ops:
  0.6 62.4 %copy-start = (bf16[1,1,384,3072]{3,2,1,0:T(8,128)(2,1)S(1)}, bf16[1,1,384,3072]{3,2,1,0:T(8,128)(2,1)}, u32[]{:S(2)}) copy-start(bf16[1,1,384,3072]{3,2,1,0:T(8,128)(2,1)} %param.10) | copy-start | bytes 7077892
  2.2 66.1 %copy-start.2 = (bf16[2,384,768]{2,1,0:T(8,128)(2,1)}, bf16[2,384,768]{2,1,0:T(8,128)(2,1)S(1)}, u32[]{:S(2)}) copy-start(bf16[2,384,768]{2,1,0:T(8,128)(2,1)S(1)} %pad_maximum_fusion.refs_4_) | copy-start | bytes 3538948
  2.2 33.7 %collective-permute-start = (bf16[2,384,768]{2,1,0:T(8,128)(2,1)S(1)}, bf16[2,384,768]{2,1,0:T(8,128)(2,1)}, u32[]{:S(2)}, u32[]{:S(2)}) collective-permute-start(bf16[2,384,768]{2,1,0:T(8,128)(2,1)S(1)} %pad_maximum_fusion.refs_4_), channel_id=1, source_target_pairs={{0,16},{4,20},{8,24},{12,28},{16,32},{20,36},{24,40},{28,44},{32,4... | collective-permute-start | bytes 3538952 | tf_op jit(solution)/shard_map/ppermute | solution.py:23
  6.0 29.8 %collective-permute-start.1 = (bf16[2,384,768]{2,1,0:T(8,128)(2,1)S(1)}, bf16[2,384,768]{2,1,0:T(8,128)(2,1)}, u32[]{:S(2)}, u32[]{:S(2)}) collective-permute-start(bf16[2,384,768]{2,1,0:T(8,128)(2,1)S(1)} %pad_maximum_fusion.refs_4_), channel_id=1, source_target_pairs={{0,4},{4,8},{8,12},{16,20},{20,24},{24,28},{32,36},{36,40},{40,44}... | collective-permute-start | bytes 3538952 | tf_op jit(solution)/shard_map/ppermute | solution.py:23
  10.4 29.1 %collective-permute-start.2 = (bf16[2,384,768]{2,1,0:T(8,128)(2,1)S(1)}, bf16[2,384,768]{2,1,0:T(8,128)(2,1)}, u32[]{:S(2)}, u32[]{:S(2)}) collective-permute-start(bf16[2,384,768]{2,1,0:T(8,128)(2,1)S(1)} %pad_maximum_fusion.refs_4_), channel_id=1, source_target_pairs={{4,0},{8,4},{12,8},{20,16},{24,20},{28,24},{36,32},{40,36},{44,40}... | collective-permute-start | bytes 3538952 | tf_op jit(solution)/shard_map/ppermute | solution.py:23
  11.7 44.8 %collective-permute-start.5 = (bf16[2,384,768]{2,1,0:T(8,128)(2,1)S(1)}, bf16[2,384,768]{2,1,0:T(8,128)(2,1)}, u32[]{:S(2)}, u32[]{:S(2)}) collective-permute-start(bf16[2,384,768]{2,1,0:T(8,128)(2,1)S(1)} %pad_maximum_fusion.refs_4_), channel_id=1, source_target_pairs={{16,0},{20,4},{24,8},{28,12},{32,16},{36,20},{40,24},{44,28},{48,3... | collective-permute-start | bytes 3538952 | tf_op jit(solution)/shard_map/ppermute | solution.py:23
  39.6 29.1 %collective-permute-start.3 = (bf16[2,384,768]{2,1,0:T(8,128)(2,1)}, bf16[2,384,768]{2,1,0:T(8,128)(2,1)}, u32[]{:S(2)}, u32[]{:S(2)}) collective-permute-start(bf16[2,384,768]{2,1,0:T(8,128)(2,1)} %collective-permute-done.refs_1_), channel_id=1, source_target_pairs={{0,4},{4,8},{8,12},{16,20},{20,24},{24,28},{32,36},{36,40},{40,44}... | collective-permute-start | bytes 3538952 | tf_op jit(solution)/shard_map/ppermute | solution.py:23
  43.0 31.1 %collective-permute-start.4 = (bf16[2,384,768]{2,1,0:T(8,128)(2,1)}, bf16[2,384,768]{2,1,0:T(8,128)(2,1)}, u32[]{:S(2)}, u32[]{:S(2)}) collective-permute-start(bf16[2,384,768]{2,1,0:T(8,128)(2,1)} %collective-permute-done.refs_1_), channel_id=1, source_target_pairs={{4,0},{8,4},{12,8},{20,16},{24,20},{28,24},{36,32},{40,36},{44,40}... | collective-permute-start | bytes 3538952 | tf_op jit(solution)/shard_map/ppermute | solution.py:23
  56.5 34.7 %collective-permute-start.6 = (bf16[2,384,768]{2,1,0:T(8,128)(2,1)}, bf16[2,384,768]{2,1,0:T(8,128)(2,1)}, u32[]{:S(2)}, u32[]{:S(2)}) collective-permute-start(bf16[2,384,768]{2,1,0:T(8,128)(2,1)} %collective-permute-done.5.refs_7_), channel_id=1, source_target_pairs={{0,4},{4,8},{8,12},{16,20},{20,24},{24,28},{32,36},{36,40},{40,44}... | collective-permute-start | bytes 3538952 | tf_op jit(solution)/shard_map/ppermute | solution.py:23
  61.0 35.4 %collective-permute-start.7 = (bf16[2,384,768]{2,1,0:T(8,128)(2,1)}, bf16[2,384,768]{2,1,0:T(8,128)(2,1)}, u32[]{:S(2)}, u32[]{:S(2)}) collective-permute-start(bf16[2,384,768]{2,1,0:T(8,128)(2,1)} %collective-permute-done.5.refs_7_), channel_id=1, source_target_pairs={{4,0},{8,4},{12,8},{20,16},{24,20},{28,24},{36,32},{40,36},{44,40}... | collective-permute-start | bytes 3538952 | tf_op jit(solution)/shard_map/ppermute | solution.py:23
  137.2 4.8 %collective-permute-start.16 = (bf16[3072,384]{0,1:T(8,128)(2,1)S(1)}, bf16[3072,384]{0,1:T(8,128)(2,1)S(1)}, u32[]{:S(2)}, u32[]{:S(2)}) collective-permute-start(bf16[3072,384]{0,1:T(8,128)(2,1)S(1)} %fusion.1), channel_id=1, source_target_pairs={{0,1},{1,0},{2,3},{3,2},{4,5},{5,4},{6,7},{7,6},{8,9},{9,8},{10,11... | collective-permute-start | bytes 7077896 | tf_op jit(solution)/shard_map/ppermute | solution.py:138
  149.2 75.5 %copy-start.4 = (bf16[2,384,768]{2,1,0:T(8,128)(2,1)S(1)}, bf16[2,384,768]{2,1,0:T(8,128)(2,1)}, u32[]{:S(2)}) copy-start(bf16[2,384,768]{2,1,0:T(8,128)(2,1)} %get-tuple-element.37) | copy-start | bytes 3538948
  149.2 138.5 %all-to-all-start = ((bf16[64,48,384]{2,1,0:T(8,128)(2,1)}), bf16[64,48,384]{2,1,0:T(8,128)(2,1)}, u32[]{:S(2)}, u32[]{:S(2)}) async-start(bf16[64,48,384]{2,1,0:T(8,128)(2,1)} %bitcast.59), calls=%async_computation | async-start | bytes 4718592 | tf_op jit(solution)/shard_map/all_to_all | solution.py:142
  166.6 52.1 %collective-permute-start.8 = (bf16[2,384,768]{2,1,0:T(8,128)(2,1)}, bf16[2,384,768]{2,1,0:T(8,128)(2,1)S(1)}, u32[]{:S(2)}, u32[]{:S(2)}) collective-permute-start(bf16[2,384,768]{2,1,0:T(8,128)(2,1)} %get-tuple-element.29), channel_id=1, source_target_pairs={{4,0},{8,4},{12,8},{20,16},{24,20},{28,24},{36,32},{40,36},{44,40}... | collective-permute-start | bytes 3538952 | tf_op jit(solution)/shard_map/ppermute | solution.py:23
  167.9 50.8 %collective-permute-start.9 = (bf16[2,384,768]{2,1,0:T(8,128)(2,1)}, bf16[2,384,768]{2,1,0:T(8,128)(2,1)S(1)}, u32[]{:S(2)}, u32[]{:S(2)}) collective-permute-start(bf16[2,384,768]{2,1,0:T(8,128)(2,1)} %get-tuple-element.30), channel_id=1, source_target_pairs={{0,4},{4,8},{8,12},{16,20},{20,24},{24,28},{32,36},{36,40},{40,44}... | collective-permute-start | bytes 3538952 | tf_op jit(solution)/shard_map/ppermute | solution.py:23
  218.7 31.0 %collective-permute-start.13 = (bf16[2,384,768]{2,1,0:T(8,128)(2,1)}, bf16[2,384,768]{2,1,0:T(8,128)(2,1)S(1)}, u32[]{:S(2)}, u32[]{:S(2)}) collective-permute-start(bf16[2,384,768]{2,1,0:T(8,128)(2,1)} %get-tuple-element.41), channel_id=1, source_target_pairs={{4,0},{8,4},{12,8},{20,16},{24,20},{28,24},{36,32},{40,36},{44,40}... | collective-permute-start | bytes 3538952 | tf_op jit(solution)/shard_map/ppermute | solution.py:23
  220.0 31.3 %collective-permute-start.14 = (bf16[2,384,768]{2,1,0:T(8,128)(2,1)}, bf16[2,384,768]{2,1,0:T(8,128)(2,1)S(1)}, u32[]{:S(2)}, u32[]{:S(2)}) collective-permute-start(bf16[2,384,768]{2,1,0:T(8,128)(2,1)} %get-tuple-element.42), channel_id=1, source_target_pairs={{0,4},{4,8},{8,12},{16,20},{20,24},{24,28},{32,36},{36,40},{40,44}... | collective-permute-start | bytes 3538952 | tf_op jit(solution)/shard_map/ppermute | solution.py:23
  224.7 26.6 %copy-start.3 = (bf16[2,384,768]{2,1,0:T(8,128)(2,1)S(1)}, bf16[2,384,768]{2,1,0:T(8,128)(2,1)}, u32[]{:S(2)}) copy-start(bf16[2,384,768]{2,1,0:T(8,128)(2,1)} %get-tuple-element.40) | copy-start | bytes 3538948
  226.2 32.2 %collective-permute-start.12 = (bf16[2,384,768]{2,1,0:T(8,128)(2,1)}, bf16[2,384,768]{2,1,0:T(8,128)(2,1)S(1)}, u32[]{:S(2)}, u32[]{:S(2)}) collective-permute-start(bf16[2,384,768]{2,1,0:T(8,128)(2,1)} %add_convert_fusion.2), channel_id=1, source_target_pairs={{16,0},{20,4},{24,8},{28,12},{32,16},{36,20},{40,24},{44,28},{48,3... | collective-permute-start | bytes 3538952 | tf_op jit(solution)/shard_map/ppermute | solution.py:23
  231.6 41.5 %collective-permute-start.10 = (bf16[2,384,768]{2,1,0:T(8,128)(2,1)}, bf16[2,384,768]{2,1,0:T(8,128)(2,1)}, u32[]{:S(2)}, u32[]{:S(2)}) collective-permute-start(bf16[2,384,768]{2,1,0:T(8,128)(2,1)} %get-tuple-element.35), channel_id=1, source_target_pairs={{4,0},{8,4},{12,8},{20,16},{24,20},{28,24},{36,32},{40,36},{44,40}... | collective-permute-start | bytes 3538952 | tf_op jit(solution)/shard_map/ppermute | solution.py:23
  232.9 41.3 %collective-permute-start.11 = (bf16[2,384,768]{2,1,0:T(8,128)(2,1)}, bf16[2,384,768]{2,1,0:T(8,128)(2,1)}, u32[]{:S(2)}, u32[]{:S(2)}) collective-permute-start(bf16[2,384,768]{2,1,0:T(8,128)(2,1)} %get-tuple-element.36), channel_id=1, source_target_pairs={{0,4},{4,8},{8,12},{16,20},{20,24},{24,28},{32,36},{36,40},{40,44}... | collective-permute-start | bytes 3538952 | tf_op jit(solution)/shard_map/ppermute | solution.py:23
  252.8 31.5 %collective-permute-start.15 = (bf16[2,384,768]{2,1,0:T(8,128)(2,1)}, bf16[2,384,768]{2,1,0:T(8,128)(2,1)}, u32[]{:S(2)}, u32[]{:S(2)}) collective-permute-start(bf16[2,384,768]{2,1,0:T(8,128)(2,1)} %add_convert_fusion.1), channel_id=1, source_target_pairs={{0,16},{4,20},{8,24},{12,28},{16,32},{20,36},{24,40},{28,44},{32,4... | collective-permute-start | bytes 3538952 | tf_op jit(solution)/shard_map/ppermute | solution.py:23
  258.4 25.9 %copy-start.1 = (bf16[2,384,768]{2,1,0:T(8,128)(2,1)}, bf16[2,384,768]{2,1,0:T(8,128)(2,1)S(1)}, u32[]{:S(2)}) copy-start(bf16[2,384,768]{2,1,0:T(8,128)(2,1)S(1)} %collective-permute-done.12) | copy-start | bytes 3538948
  293.1 8.1 %collective-permute-start.17 = (f32[48,192]{1,0:T(8,128)S(1)}, f32[48,192]{1,0:T(8,128)S(1)}, u32[]{:S(2)}, u32[]{:S(2)}) collective-permute-start(f32[48,192]{1,0:T(8,128)S(1)} %bitcast.65), channel_id=1, source_target_pairs={{0,2},{1,3},{2,0},{3,1},{4,6},{5,7},{6,4},{7,5},{8,10},{9,11},{10,... | collective-permute-start | bytes 110600 | tf_op jit(solution)/shard_map/ppermute | solution.py:150
  (1 other events, 15.9 us)

commit v11 on v10

--- a/solution.py
+++ b/solution.py
@@ -139,6 +139,10 @@
         sent_part.astype(jnp.bfloat16), "dp", [(index, index ^ 1) for index in range(dp_count)]
     )
     core_sum = (kept_part + sibling_part.astype(jnp.float32)).astype(jnp.bfloat16)
+    early_in = [shifted(back[0], 0, -1, True), shifted(back[2], 0, 1, True)]
+    early_in, late_out, row_out, core_sum = lax.optimization_barrier(
+        (early_in, [back[6], back[8]], [back[3], back[5]], core_sum)
+    )
     by_column = lax.all_to_all(
         core_sum.reshape(sp_count, col_block, -1), "sp", 0, 0, tiled=True
     )
@@ -149,8 +153,6 @@
         own_half
         + lax.ppermute(other_half, "dp", [(index, (index + 2) % dp_count) for index in range(dp_count)])
     ).T
-    early_in = [shifted(back[0], 0, -1, True), shifted(back[2], 0, 1, True)]
-    early_in, late_out, row_out = lax.optimization_barrier((early_in, [back[6], back[8]], [back[3], back[5]]))
     earlier_sum = back[1].astype(jnp.float32) + early_in[0].astype(jnp.float32) + early_in[1].astype(jnp.float32)
     from_later = shifted(earlier_sum.astype(jnp.bfloat16), -1, 0, True)
     late_in = [shifted(late_out[0], 0, -1, True), shifted(late_out[1], 0, 1, True)]

time: 303 us -> 315 us (1.040)
  the two profiles are of different devices: /device:TPU:24 before, /device:TPU:32 now
where the time goes in v11:
time: 315 us; the launch traced here: 314 us
  waiting for transfers between devices  175 us (56%)
  starting transfers between devices  66.5 us (21%)
  Pallas kernels  38 us (12%)
  other arithmetic  13 us (4%)
  local copies, waits for them, and re-layouts  11.3 us (4%)
  matrix products  9.45 us (3%)
    ppermute x16, waiting for transfers between devices, neighbour_shift(): return lax.ppermute(value, axis, pairs)  168 us
    ppermute x16, starting transfers between devices, neighbour_shift(): return lax.ppermute(value, axis, pairs)  47.2 us
    pallas_call x1, Pallas kernels, body(): pl.pallas_call(functools.partial(tile_attention, score_scale=score_scale)...  38 us
    all_to_all x1, starting transfers between devices, body(): lax.all_to_all(core_sum.reshape(sp_count, col_block, -1), 'sp', 0, 0, til...  19.2 us
    ppermute x1, waiting for transfers between devices, body(): lax.ppermute(other_half, 'dp', [(index, (index + 2) % dp_count) for index...  6.9 us
  transfers between devices with their start and end apart: 19, of which 12 were waited for; matrix products, arithmetic and copies ran while one was open for 6% of the time, Pallas kernels for 0%

profile of v11, /device:TPU:32, one launch (start us, length us, event | category | flops | bytes accessed | tf_op | source)
XLA Modules:
  0.0 314.0 jit_solution(14430692570320609461)
XLA Ops:
  2.2 3.8 %collective-permute-start = (bf16[2,384,768]{2,1,0:T(8,128)(2,1)S(1)}, bf16[2,384,768]{2,1,0:T(8,128)(2,1)}, u32[]{:S(2)}, u32[]{:S(2)}) collective-permute-start(bf16[2,384,768]{2,1,0:T(8,128)(2,1)S(1)} %pad_maximum_fusion.refs_4_), channel_id=1, source_target_pairs={{0,16},{4,20},{8,24},{12,28},{16,32},{20,36},{24,40},{28,44},{32,4... | collective-permute-start | bytes 3538952 | tf_op jit(solution)/shard_map/ppermute | solution.py:23
  6.0 4.4 %collective-permute-start.1 = (bf16[2,384,768]{2,1,0:T(8,128)(2,1)S(1)}, bf16[2,384,768]{2,1,0:T(8,128)(2,1)}, u32[]{:S(2)}, u32[]{:S(2)}) collective-permute-start(bf16[2,384,768]{2,1,0:T(8,128)(2,1)S(1)} %pad_maximum_fusion.refs_4_), channel_id=1, source_target_pairs={{0,4},{4,8},{8,12},{16,20},{20,24},{24,28},{32,36},{36,40},{40,44}... | collective-permute-start | bytes 3538952 | tf_op jit(solution)/shard_map/ppermute | solution.py:23
  11.7 3.0 collective-permute-start.5
  14.8 17.1 %collective-permute-done.refs_1_ = bf16[2,384,768]{2,1,0:T(8,128)(2,1)} collective-permute-done((bf16[2,384,768]{2,1,0:T(8,128)(2,1)S(1)}, bf16[2,384,768]{2,1,0:T(8,128)(2,1)}, u32[]{:S(2)}, u32[]{:S(2)}) %collective-permute-start) | collective-permute-done | bytes 1179680 | tf_op jit(solution)/shard_map/ppermute | solution.py:23
  34.3 5.2 %collective-permute-done.2.refs_5_ = bf16[2,384,768]{2,1,0:T(8,128)(2,1)} collective-permute-done((bf16[2,384,768]{2,1,0:T(8,128)(2,1)S(1)}, bf16[2,384,768]{2,1,0:T(8,128)(2,1)}, u32[]{:S(2)}, u32[]{:S(2)}) %collective-permute-start.2) | collective-permute-done | bytes 1179680 | tf_op jit(solution)/shard_map/ppermute | solution.py:23
  39.6 3.4 %collective-permute-start.3 = (bf16[2,384,768]{2,1,0:T(8,128)(2,1)}, bf16[2,384,768]{2,1,0:T(8,128)(2,1)}, u32[]{:S(2)}, u32[]{:S(2)}) collective-permute-start(bf16[2,384,768]{2,1,0:T(8,128)(2,1)} %collective-permute-done.refs_1_), channel_id=1, source_target_pairs={{0,4},{4,8},{8,12},{16,20},{20,24},{24,28},{32,36},{36,40},{40,44}... | collective-permute-start | bytes 3538952 | tf_op jit(solution)/shard_map/ppermute | solution.py:23
  44.3 14.4 %collective-permute-done.5.refs_7_ = bf16[2,384,768]{2,1,0:T(8,128)(2,1)} collective-permute-done((bf16[2,384,768]{2,1,0:T(8,128)(2,1)S(1)}, bf16[2,384,768]{2,1,0:T(8,128)(2,1)}, u32[]{:S(2)}, u32[]{:S(2)}) %collective-permute-start.5) | collective-permute-done | bytes 1179680 | tf_op jit(solution)/shard_map/ppermute | solution.py:23
  58.7 4.4 %collective-permute-start.6 = (bf16[2,384,768]{2,1,0:T(8,128)(2,1)}, bf16[2,384,768]{2,1,0:T(8,128)(2,1)}, u32[]{:S(2)}, u32[]{:S(2)}) collective-permute-start(bf16[2,384,768]{2,1,0:T(8,128)(2,1)} %collective-permute-done.5.refs_7_), channel_id=1, source_target_pairs={{0,4},{4,8},{8,12},{16,20},{20,24},{24,28},{32,36},{36,40},{40,44}... | collective-permute-start | bytes 3538952 | tf_op jit(solution)/shard_map/ppermute | solution.py:23
  65.2 5.2 %fusion.6.grad_ref = bf16[384,768]{1,0:T(8,128)(2,1)} fusion(bf16[768,3072]{1,0:T(8,128)(2,1)} %param.11, bf16[1,1,384,3072]{3,2,1,0:T(8,128)(2,1)S(1)} %copy-done), kind=kOutput, calls=%fused_computation.12 | convolution fusion | flops 1812234240 | bytes 7667712 | tf_op jit(solution)/shard_map/dot_general | solution.py:98
  70.4 3.7 %collective-permute-done.4.refs_2_ = bf16[2,384,768]{2,1,0:T(8,128)(2,1)} collective-permute-done((bf16[2,384,768]{2,1,0:T(8,128)(2,1)}, bf16[2,384,768]{2,1,0:T(8,128)(2,1)}, u32[]{:S(2)}, u32[]{:S(2)}) %collective-permute-start.4) | collective-permute-done | bytes 1179680 | tf_op jit(solution)/shard_map/ppermute | solution.py:23
  74.1 17.2 %collective-permute-done.6.refs_6_ = bf16[2,384,768]{2,1,0:T(8,128)(2,1)} collective-permute-done((bf16[2,384,768]{2,1,0:T(8,128)(2,1)}, bf16[2,384,768]{2,1,0:T(8,128)(2,1)}, u32[]{:S(2)}, u32[]{:S(2)}) %collective-permute-start.6) | collective-permute-done | bytes 1179680 | tf_op jit(solution)/shard_map/ppermute | solution.py:23
  91.3 5.1 %collective-permute-done.7.refs_8_ = bf16[2,384,768]{2,1,0:T(8,128)(2,1)} collective-permute-done((bf16[2,384,768]{2,1,0:T(8,128)(2,1)}, bf16[2,384,768]{2,1,0:T(8,128)(2,1)}, u32[]{:S(2)}, u32[]{:S(2)}) %collective-permute-start.7) | collective-permute-done | bytes 1179680 | tf_op jit(solution)/shard_map/ppermute | solution.py:23
  96.4 38.0 %shard_map.93 = (bf16[384,768]{1,0:T(8,128)(2,1)}, bf16[384,768]{1,0:T(8,128)(2,1)}, bf16[2,384,768]{2,1,0:T(8,128)(2,1)}, bf16[2,384,768]{2,1,0:T(8,128)(2,1)},...) custom-call(s32[1,3456]{1,0:T(1,128)} %bitcast.66, ...), custom_call_target="tpu_custom_call" | custom-call | flops 10192158720 | bytes 23592960 | tf_op jit(solution)/shard_map/pallas_call | solution.py:106
  138.7 5.6 %collective-permute-start.9 = (bf16[2,384,768]{2,1,0:T(8,128)(2,1)S(1)}, bf16[2,384,768]{2,1,0:T(8,128)(2,1)}, u32[]{:S(2)}, u32[]{:S(2)}) collective-permute-start(bf16[2,384,768]{2,1,0:T(8,128)(2,1)S(1)} %copy-done.6), channel_id=1, source_target_pairs={{0,4},{4,8},{8,12},{16,20},{20,24},{24,28},{32,36},{36,40},{40,44}... | collective-permute-start | bytes 3538952 | tf_op jit(solution)/shard_map/ppermute | solution.py:23
  147.1 20.6 %collective-permute-done.8 = bf16[2,384,768]{2,1,0:T(8,128)(2,1)} collective-permute-done((bf16[2,384,768]{2,1,0:T(8,128)(2,1)S(1)}, bf16[2,384,768]{2,1,0:T(8,128)(2,1)}, u32[]{:S(2)}, u32[]{:S(2)}) %collective-permute-start.8) | collective-permute-done | bytes 1179680 | tf_op jit(solution)/shard_map/ppermute | solution.py:23
  168.8 4.3 %copy.13 = bf16[3072,384]{1,0:T(8,128)(2,1)} copy(bf16[3072,384]{0,1:T(8,128)(2,1)} %fusion) | data formatting | bytes 4718592 | tf_op jit(solution)/shard_map/optimization_barrier | solution.py:143
  173.1 19.2 %all-to-all-start = ((bf16[64,48,384]{2,1,0:T(8,128)(2,1)}), bf16[64,48,384]{2,1,0:T(8,128)(2,1)}, u32[]{:S(2)}, u32[]{:S(2)}) async-start(bf16[64,48,384]{2,1,0:T(8,128)(2,1)} %bitcast.59), calls=%async_computation | async-start | bytes 4718592 | tf_op jit(solution)/shard_map/all_to_all | solution.py:146
  193.6 4.6 %collective-permute-start.15 = (bf16[2,384,768]{2,1,0:T(8,128)(2,1)}, bf16[2,384,768]{2,1,0:T(8,128)(2,1)S(1)}, u32[]{:S(2)}, u32[]{:S(2)}) collective-permute-start(bf16[2,384,768]{2,1,0:T(8,128)(2,1)} %get-tuple-element.44), channel_id=1, source_target_pairs={{0,4},{4,8},{8,12},{16,20},{20,24},{24,28},{32,36},{36,40},{40,44}... | collective-permute-start | bytes 3538952 | tf_op jit(solution)/shard_map/ppermute | solution.py:23
  198.3 3.2 %add_convert_fusion.2 = bf16[2,384,768]{2,1,0:T(8,128)(2,1)} fusion(bf16[2,384,768]{2,1,0:T(8,128)(2,1)} %collective-permute-done.9, bf16[2,384,768]{2,1,0:T(8,128)(2,1)} %collective-permute-done.8, bf16[2,384,768]{2,1,0:T(8,128)(2,1)S(1)} %copy-done.4), kind=kLoop, calls=%fused_computation.11 | loop fusion | flops 3538944 | bytes 4718592 | tf_op jit(solution)/shard_map/convert_element_type | solution.py:157
  205.2 5.6 %collective-permute-start.12 = (bf16[2,384,768]{2,1,0:T(8,128)(2,1)}, bf16[2,384,768]{2,1,0:T(8,128)(2,1)}, u32[]{:S(2)}, u32[]{:S(2)}) collective-permute-start(bf16[2,384,768]{2,1,0:T(8,128)(2,1)} %get-tuple-element.38), channel_id=1, source_target_pairs={{0,4},{4,8},{8,12},{16,20},{20,24},{24,28},{32,36},{36,40},{40,44}... | collective-permute-start | bytes 3538952 | tf_op jit(solution)/shard_map/ppermute | solution.py:23
  210.8 35.3 %collective-permute-done.14 = bf16[2,384,768]{2,1,0:T(8,128)(2,1)S(1)} collective-permute-done((bf16[2,384,768]{2,1,0:T(8,128)(2,1)}, bf16[2,384,768]{2,1,0:T(8,128)(2,1)S(1)}, u32[]{:S(2)}, u32[]{:S(2)}) %collective-permute-start.14) | collective-permute-done | bytes 1179680 | tf_op jit(solution)/shard_map/ppermute | solution.py:23
  249.7 45.7 %collective-permute-done.13 = bf16[2,384,768]{2,1,0:T(8,128)(2,1)S(1)} collective-permute-done((bf16[2,384,768]{2,1,0:T(8,128)(2,1)}, bf16[2,384,768]{2,1,0:T(8,128)(2,1)S(1)}, u32[]{:S(2)}, u32[]{:S(2)}) %collective-permute-start.13) | collective-permute-done | bytes 1179680 | tf_op jit(solution)/shard_map/ppermute | solution.py:23
  296.4 3.4 %add_convert_fusion = bf16[2,384,768]{2,1,0:T(8,128)(2,1)S(1)} fusion(bf16[2,384,768]{2,1,0:T(8,128)(2,1)} %collective-permute-done.16, bf16[2,384,768]{2,1,0:T(8,128)(2,1)} %copy-done.1, bf16[2,384,768]{2,1,0:T(8,128)(2,1)} %collective-permute-done.12, bf16[2,384,768]{2,1,0:T(8,128)(2,1)} %collective-permute-done.11, bf16[2,384,768]{2,1,0:T(8,128)(2,1)} %get-tuple-element.29), kind=kLoop, calls=%fused_computation.9 | loop fusion | flops 5898240 | bytes 7077888 | tf_op jit(solution)/shard_map/convert_element_type | solution.py:169
  306.4 6.9 %collective-permute-done.17 = f32[48,192]{1,0:T(8,128)S(1)} collective-permute-done((f32[48,192]{1,0:T(8,128)S(1)}, f32[48,192]{1,0:T(8,128)S(1)}, u32[]{:S(2)}, u32[]{:S(2)}) %collective-permute-start.17) | collective-permute-done | bytes 36896 | tf_op jit(solution)/shard_map/ppermute | solution.py:154
  (53 shorter events, 33.6 us)
Async XLA Ops:
  0.6 64.6 %copy-start = (bf16[1,1,384,3072]{3,2,1,0:T(8,128)(2,1)S(1)}, bf16[1,1,384,3072]{3,2,1,0:T(8,128)(2,1)}, u32[]{:S(2)}) copy-start(bf16[1,1,384,3072]{3,2,1,0:T(8,128)(2,1)} %param.10) | copy-start | bytes 7077892
  0.6 14.1 %copy-start.5 = (s32[1,5]{1,0:T(1,128)S(1)}, s32[1,5]{1,0:T(1,128)}, u32[]{:S(2)}) copy-start(s32[1,5]{1,0:T(1,128)} %param.9) | copy-start | bytes 64
  2.2 68.2 %copy-start.2 = (bf16[2,384,768]{2,1,0:T(8,128)(2,1)}, bf16[2,384,768]{2,1,0:T(8,128)(2,1)S(1)}, u32[]{:S(2)}) copy-start(bf16[2,384,768]{2,1,0:T(8,128)(2,1)S(1)} %pad_maximum_fusion.refs_4_) | copy-start | bytes 3538948
  2.2 29.7 %collective-permute-start = (bf16[2,384,768]{2,1,0:T(8,128)(2,1)S(1)}, bf16[2,384,768]{2,1,0:T(8,128)(2,1)}, u32[]{:S(2)}, u32[]{:S(2)}) collective-permute-start(bf16[2,384,768]{2,1,0:T(8,128)(2,1)S(1)} %pad_maximum_fusion.refs_4_), channel_id=1, source_target_pairs={{0,16},{4,20},{8,24},{12,28},{16,32},{20,36},{24,40},{28,44},{32,4... | collective-permute-start | bytes 3538952 | tf_op jit(solution)/shard_map/ppermute | solution.py:23
  6.0 28.3 %collective-permute-start.1 = (bf16[2,384,768]{2,1,0:T(8,128)(2,1)S(1)}, bf16[2,384,768]{2,1,0:T(8,128)(2,1)}, u32[]{:S(2)}, u32[]{:S(2)}) collective-permute-start(bf16[2,384,768]{2,1,0:T(8,128)(2,1)S(1)} %pad_maximum_fusion.refs_4_), channel_id=1, source_target_pairs={{0,4},{4,8},{8,12},{16,20},{20,24},{24,28},{32,36},{36,40},{40,44}... | collective-permute-start | bytes 3538952 | tf_op jit(solution)/shard_map/ppermute | solution.py:23
  10.4 29.1 %collective-permute-start.2 = (bf16[2,384,768]{2,1,0:T(8,128)(2,1)S(1)}, bf16[2,384,768]{2,1,0:T(8,128)(2,1)}, u32[]{:S(2)}, u32[]{:S(2)}) collective-permute-start(bf16[2,384,768]{2,1,0:T(8,128)(2,1)S(1)} %pad_maximum_fusion.refs_4_), channel_id=1, source_target_pairs={{4,0},{8,4},{12,8},{20,16},{24,20},{28,24},{36,32},{40,36},{44,40}... | collective-permute-start | bytes 3538952 | tf_op jit(solution)/shard_map/ppermute | solution.py:23
  11.7 47.0 %collective-permute-start.5 = (bf16[2,384,768]{2,1,0:T(8,128)(2,1)S(1)}, bf16[2,384,768]{2,1,0:T(8,128)(2,1)}, u32[]{:S(2)}, u32[]{:S(2)}) collective-permute-start(bf16[2,384,768]{2,1,0:T(8,128)(2,1)S(1)} %pad_maximum_fusion.refs_4_), channel_id=1, source_target_pairs={{16,0},{20,4},{24,8},{28,12},{32,16},{36,20},{40,24},{44,28},{48,3... | collective-permute-start | bytes 3538952 | tf_op jit(solution)/shard_map/ppermute | solution.py:23
  39.6 30.9 %collective-permute-start.3 = (bf16[2,384,768]{2,1,0:T(8,128)(2,1)}, bf16[2,384,768]{2,1,0:T(8,128)(2,1)}, u32[]{:S(2)}, u32[]{:S(2)}) collective-permute-start(bf16[2,384,768]{2,1,0:T(8,128)(2,1)} %collective-permute-done.refs_1_), channel_id=1, source_target_pairs={{0,4},{4,8},{8,12},{16,20},{20,24},{24,28},{32,36},{36,40},{40,44}... | collective-permute-start | bytes 3538952 | tf_op jit(solution)/shard_map/ppermute | solution.py:23
  43.0 31.1 %collective-permute-start.4 = (bf16[2,384,768]{2,1,0:T(8,128)(2,1)}, bf16[2,384,768]{2,1,0:T(8,128)(2,1)}, u32[]{:S(2)}, u32[]{:S(2)}) collective-permute-start(bf16[2,384,768]{2,1,0:T(8,128)(2,1)} %collective-permute-done.refs_1_), channel_id=1, source_target_pairs={{4,0},{8,4},{12,8},{20,16},{24,20},{28,24},{36,32},{40,36},{44,40}... | collective-permute-start | bytes 3538952 | tf_op jit(solution)/shard_map/ppermute | solution.py:23
  58.7 32.6 %collective-permute-start.6 = (bf16[2,384,768]{2,1,0:T(8,128)(2,1)}, bf16[2,384,768]{2,1,0:T(8,128)(2,1)}, u32[]{:S(2)}, u32[]{:S(2)}) collective-permute-start(bf16[2,384,768]{2,1,0:T(8,128)(2,1)} %collective-permute-done.5.refs_7_), channel_id=1, source_target_pairs={{0,4},{4,8},{8,12},{16,20},{20,24},{24,28},{32,36},{36,40},{40,44}... | collective-permute-start | bytes 3538952 | tf_op jit(solution)/shard_map/ppermute | solution.py:23
  63.1 33.3 %collective-permute-start.7 = (bf16[2,384,768]{2,1,0:T(8,128)(2,1)}, bf16[2,384,768]{2,1,0:T(8,128)(2,1)}, u32[]{:S(2)}, u32[]{:S(2)}) collective-permute-start(bf16[2,384,768]{2,1,0:T(8,128)(2,1)} %collective-permute-done.5.refs_7_), channel_id=1, source_target_pairs={{4,0},{8,4},{12,8},{20,16},{24,20},{28,24},{36,32},{40,36},{44,40}... | collective-permute-start | bytes 3538952 | tf_op jit(solution)/shard_map/ppermute | solution.py:23
  137.3 7.0 %collective-permute-start.10 = (bf16[3072,384]{0,1:T(8,128)(2,1)S(1)}, bf16[3072,384]{0,1:T(8,128)(2,1)S(1)}, u32[]{:S(2)}, u32[]{:S(2)}) collective-permute-start(bf16[3072,384]{0,1:T(8,128)(2,1)S(1)} %fusion.1), channel_id=1, source_target_pairs={{0,1},{1,0},{2,3},{3,2},{4,5},{5,4},{6,7},{7,6},{8,9},{9,8},{10,11... | collective-permute-start | bytes 7077896 | tf_op jit(solution)/shard_map/ppermute | solution.py:138
  137.4 30.4 %collective-permute-start.8 = (bf16[2,384,768]{2,1,0:T(8,128)(2,1)S(1)}, bf16[2,384,768]{2,1,0:T(8,128)(2,1)}, u32[]{:S(2)}, u32[]{:S(2)}) collective-permute-start(bf16[2,384,768]{2,1,0:T(8,128)(2,1)S(1)} %copy-done.7), channel_id=1, source_target_pairs={{4,0},{8,4},{12,8},{20,16},{24,20},{28,24},{36,32},{40,36},{44,40}... | collective-permute-start | bytes 3538952 | tf_op jit(solution)/shard_map/ppermute | solution.py:23
  138.7 30.1 %collective-permute-start.9 = (bf16[2,384,768]{2,1,0:T(8,128)(2,1)S(1)}, bf16[2,384,768]{2,1,0:T(8,128)(2,1)}, u32[]{:S(2)}, u32[]{:S(2)}) collective-permute-start(bf16[2,384,768]{2,1,0:T(8,128)(2,1)S(1)} %copy-done.6), channel_id=1, source_target_pairs={{0,4},{4,8},{8,12},{16,20},{20,24},{24,28},{32,36},{36,40},{40,44}... | collective-permute-start | bytes 3538952 | tf_op jit(solution)/shard_map/ppermute | solution.py:23
  173.1 25.1 %copy-start.4 = (bf16[2,384,768]{2,1,0:T(8,128)(2,1)S(1)}, bf16[2,384,768]{2,1,0:T(8,128)(2,1)}, u32[]{:S(2)}) copy-start(bf16[2,384,768]{2,1,0:T(8,128)(2,1)} %get-tuple-element.39) | copy-start | bytes 3538948
  173.1 126.8 %all-to-all-start = ((bf16[64,48,384]{2,1,0:T(8,128)(2,1)}), bf16[64,48,384]{2,1,0:T(8,128)(2,1)}, u32[]{:S(2)}, u32[]{:S(2)}) async-start(bf16[64,48,384]{2,1,0:T(8,128)(2,1)} %bitcast.59), calls=%async_computation | async-start | bytes 4718592 | tf_op jit(solution)/shard_map/all_to_all | solution.py:146
  192.3 53.8 %collective-permute-start.14 = (bf16[2,384,768]{2,1,0:T(8,128)(2,1)}, bf16[2,384,768]{2,1,0:T(8,128)(2,1)S(1)}, u32[]{:S(2)}, u32[]{:S(2)}) collective-permute-start(bf16[2,384,768]{2,1,0:T(8,128)(2,1)} %get-tuple-element.43), channel_id=1, source_target_pairs={{4,0},{8,4},{12,8},{20,16},{24,20},{28,24},{36,32},{40,36},{44,40}... | collective-permute-start | bytes 3538952 | tf_op jit(solution)/shard_map/ppermute | solution.py:23
  193.6 52.5 %collective-permute-start.15 = (bf16[2,384,768]{2,1,0:T(8,128)(2,1)}, bf16[2,384,768]{2,1,0:T(8,128)(2,1)S(1)}, u32[]{:S(2)}, u32[]{:S(2)}) collective-permute-start(bf16[2,384,768]{2,1,0:T(8,128)(2,1)} %get-tuple-element.44), channel_id=1, source_target_pairs={{0,4},{4,8},{8,12},{16,20},{20,24},{24,28},{32,36},{36,40},{40,44}... | collective-permute-start | bytes 3538952 | tf_op jit(solution)/shard_map/ppermute | solution.py:23
  198.3 47.9 %copy-start.3 = (bf16[2,384,768]{2,1,0:T(8,128)(2,1)S(1)}, bf16[2,384,768]{2,1,0:T(8,128)(2,1)}, u32[]{:S(2)}) copy-start(bf16[2,384,768]{2,1,0:T(8,128)(2,1)} %get-tuple-element.42) | copy-start | bytes 3538948
  201.4 93.9 %collective-permute-start.13 = (bf16[2,384,768]{2,1,0:T(8,128)(2,1)}, bf16[2,384,768]{2,1,0:T(8,128)(2,1)S(1)}, u32[]{:S(2)}, u32[]{:S(2)}) collective-permute-start(bf16[2,384,768]{2,1,0:T(8,128)(2,1)} %add_convert_fusion.2), channel_id=1, source_target_pairs={{16,0},{20,4},{24,8},{28,12},{32,16},{36,20},{40,24},{44,28},{48,3... | collective-permute-start | bytes 3538952 | tf_op jit(solution)/shard_map/ppermute | solution.py:23
  203.9 91.5 %collective-permute-start.11 = (bf16[2,384,768]{2,1,0:T(8,128)(2,1)}, bf16[2,384,768]{2,1,0:T(8,128)(2,1)}, u32[]{:S(2)}, u32[]{:S(2)}) collective-permute-start(bf16[2,384,768]{2,1,0:T(8,128)(2,1)} %get-tuple-element.37), channel_id=1, source_target_pairs={{4,0},{8,4},{12,8},{20,16},{24,20},{28,24},{36,32},{40,36},{44,40}... | collective-permute-start | bytes 3538952 | tf_op jit(solution)/shard_map/ppermute | solution.py:23
  205.2 90.2 %collective-permute-start.12 = (bf16[2,384,768]{2,1,0:T(8,128)(2,1)}, bf16[2,384,768]{2,1,0:T(8,128)(2,1)}, u32[]{:S(2)}, u32[]{:S(2)}) collective-permute-start(bf16[2,384,768]{2,1,0:T(8,128)(2,1)} %get-tuple-element.38), channel_id=1, source_target_pairs={{0,4},{4,8},{8,12},{16,20},{20,24},{24,28},{32,36},{36,40},{40,44}... | collective-permute-start | bytes 3538952 | tf_op jit(solution)/shard_map/ppermute | solution.py:23
  247.6 47.8 %collective-permute-start.16 = (bf16[2,384,768]{2,1,0:T(8,128)(2,1)}, bf16[2,384,768]{2,1,0:T(8,128)(2,1)}, u32[]{:S(2)}, u32[]{:S(2)}) collective-permute-start(bf16[2,384,768]{2,1,0:T(8,128)(2,1)} %add_convert_fusion.1), channel_id=1, source_target_pairs={{0,16},{4,20},{8,24},{12,28},{16,32},{20,36},{24,40},{28,44},{32,4... | collective-permute-start | bytes 3538952 | tf_op jit(solution)/shard_map/ppermute | solution.py:23
  305.2 8.1 %collective-permute-start.17 = (f32[48,192]{1,0:T(8,128)S(1)}, f32[48,192]{1,0:T(8,128)S(1)}, u32[]{:S(2)}, u32[]{:S(2)}) collective-permute-start(f32[48,192]{1,0:T(8,128)S(1)} %bitcast.65), channel_id=1, source_target_pairs={{0,2},{1,3},{2,0},{3,1},{4,6},{5,7},{6,4},{7,5},{8,10},{9,11},{10,... | collective-permute-start | bytes 110600 | tf_op jit(solution)/shard_map/ppermute | solution.py:154
  (3 other events, 5.4 us)

commit v12 on v10

--- a/solution.py
+++ b/solution.py
@@ -150,10 +150,11 @@
         + lax.ppermute(other_half, "dp", [(index, (index + 2) % dp_count) for index in range(dp_count)])
     ).T
     early_in = [shifted(back[0], 0, -1, True), shifted(back[2], 0, 1, True)]
-    early_in, late_out, row_out = lax.optimization_barrier((early_in, [back[6], back[8]], [back[3], back[5]]))
+    early_in, late_out = lax.optimization_barrier((early_in, [back[6], back[8]]))
     earlier_sum = back[1].astype(jnp.float32) + early_in[0].astype(jnp.float32) + early_in[1].astype(jnp.float32)
     from_later = shifted(earlier_sum.astype(jnp.bfloat16), -1, 0, True)
     late_in = [shifted(late_out[0], 0, -1, True), shifted(late_out[1], 0, 1, True)]
+    late_in, row_out = lax.optimization_barrier((late_in, [back[3], back[5]]))
     row_in = [shifted(part, 0, step, True) for part, step in zip(row_out, (-1, 1))]
     later_sum = back[7].astype(jnp.float32) + late_in[0].astype(jnp.float32) + late_in[1].astype(jnp.float32)
     from_earlier = shifted(later_sum.astype(jnp.bfloat16), 1, 0, True)

time: 303 us -> 306 us (level)
  transfers between devices with their start and end apart: 19 -> 19, of which waited for: 16 -> 13; matrix products, arithmetic and copies ran while one was open for 4% -> 4% of each run, Pallas kernels for 0% -> 0%
where the time goes in v12:
time: 306 us; the launch traced here: 302 us
  waiting for transfers between devices  161 us (53%)
  starting transfers between devices  70.6 us (23%)
  Pallas kernels  38 us (12%)
  other arithmetic  11.4 us (4%)
  local copies, waits for them, and re-layouts  10.2 us (3%)
  matrix products  9.44 us (3%)
    ppermute x16, waiting for transfers between devices, neighbour_shift(): return lax.ppermute(value, axis, pairs)  150 us
    ppermute x16, starting transfers between devices, neighbour_shift(): return lax.ppermute(value, axis, pairs)  52.8 us
    pallas_call x1, Pallas kernels, body(): pl.pallas_call(functools.partial(tile_attention, score_scale=score_scale)...  38 us
    all_to_all x1, starting transfers between devices, body(): lax.all_to_all(core_sum.reshape(sp_count, col_block, -1), 'sp', 0, 0, til...  17.4 us
    ppermute x1, waiting for transfers between devices, body(): lax.ppermute(other_half, 'dp', [(index, (index + 2) % dp_count) for index...  7 us
  transfers between devices with their start and end apart: 19, of which 13 were waited for; matrix products, arithmetic and copies ran while one was open for 4% of the time, Pallas kernels for 0%

profile of v12, /device:TPU:24, one launch (start us, length us, event | category | flops | bytes accessed | tf_op | source)
XLA Modules:
  0.0 302.0 jit_solution(3090231252783249185)
XLA Ops:
  2.2 3.8 %collective-permute-start = (bf16[2,384,768]{2,1,0:T(8,128)(2,1)S(1)}, bf16[2,384,768]{2,1,0:T(8,128)(2,1)}, u32[]{:S(2)}, u32[]{:S(2)}) collective-permute-start(bf16[2,384,768]{2,1,0:T(8,128)(2,1)S(1)} %pad_maximum_fusion.refs_4_), channel_id=1, source_target_pairs={{0,16},{4,20},{8,24},{12,28},{16,32},{20,36},{24,40},{28,44},{32,4... | collective-permute-start | bytes 3538952 | tf_op jit(solution)/shard_map/ppermute | solution.py:23
  6.0 4.4 %collective-permute-start.1 = (bf16[2,384,768]{2,1,0:T(8,128)(2,1)S(1)}, bf16[2,384,768]{2,1,0:T(8,128)(2,1)}, u32[]{:S(2)}, u32[]{:S(2)}) collective-permute-start(bf16[2,384,768]{2,1,0:T(8,128)(2,1)S(1)} %pad_maximum_fusion.refs_4_), channel_id=1, source_target_pairs={{0,4},{4,8},{8,12},{16,20},{20,24},{24,28},{32,36},{36,40},{40,44}... | collective-permute-start | bytes 3538952 | tf_op jit(solution)/shard_map/ppermute | solution.py:23
  11.7 4.8 %collective-permute-start.5 = (bf16[2,384,768]{2,1,0:T(8,128)(2,1)S(1)}, bf16[2,384,768]{2,1,0:T(8,128)(2,1)}, u32[]{:S(2)}, u32[]{:S(2)}) collective-permute-start(bf16[2,384,768]{2,1,0:T(8,128)(2,1)S(1)} %pad_maximum_fusion.refs_4_), channel_id=1, source_target_pairs={{16,0},{20,4},{24,8},{28,12},{32,16},{36,20},{40,24},{44,28},{48,3... | collective-permute-start | bytes 3538952 | tf_op jit(solution)/shard_map/ppermute | solution.py:23
  16.6 19.2 %collective-permute-done.refs_1_ = bf16[2,384,768]{2,1,0:T(8,128)(2,1)} collective-permute-done((bf16[2,384,768]{2,1,0:T(8,128)(2,1)S(1)}, bf16[2,384,768]{2,1,0:T(8,128)(2,1)}, u32[]{:S(2)}, u32[]{:S(2)}) %collective-permute-start) | collective-permute-done | bytes 1179680 | tf_op jit(solution)/shard_map/ppermute | solution.py:23
  35.8 3.7 %collective-permute-done.2.refs_5_ = bf16[2,384,768]{2,1,0:T(8,128)(2,1)} collective-permute-done((bf16[2,384,768]{2,1,0:T(8,128)(2,1)S(1)}, bf16[2,384,768]{2,1,0:T(8,128)(2,1)}, u32[]{:S(2)}, u32[]{:S(2)}) %collective-permute-start.2) | collective-permute-done | bytes 1179680 | tf_op jit(solution)/shard_map/ppermute | solution.py:23
  44.3 12.3 %collective-permute-done.5.refs_7_ = bf16[2,384,768]{2,1,0:T(8,128)(2,1)} collective-permute-done((bf16[2,384,768]{2,1,0:T(8,128)(2,1)S(1)}, bf16[2,384,768]{2,1,0:T(8,128)(2,1)}, u32[]{:S(2)}, u32[]{:S(2)}) %collective-permute-start.5) | collective-permute-done | bytes 1179680 | tf_op jit(solution)/shard_map/ppermute | solution.py:23
  56.5 4.4 %collective-permute-start.6 = (bf16[2,384,768]{2,1,0:T(8,128)(2,1)}, bf16[2,384,768]{2,1,0:T(8,128)(2,1)}, u32[]{:S(2)}, u32[]{:S(2)}) collective-permute-start(bf16[2,384,768]{2,1,0:T(8,128)(2,1)} %collective-permute-done.5.refs_7_), channel_id=1, source_target_pairs={{0,4},{4,8},{8,12},{16,20},{20,24},{24,28},{32,36},{36,40},{40,44}... | collective-permute-start | bytes 3538952 | tf_op jit(solution)/shard_map/ppermute | solution.py:23
  63.1 5.2 %fusion.6.grad_ref = bf16[384,768]{1,0:T(8,128)(2,1)} fusion(bf16[768,3072]{1,0:T(8,128)(2,1)} %param.11, bf16[1,1,384,3072]{3,2,1,0:T(8,128)(2,1)S(1)} %copy-done), kind=kOutput, calls=%fused_computation.12 | convolution fusion | flops 1812234240 | bytes 7667712 | tf_op jit(solution)/shard_map/dot_general | solution.py:98
  68.7 5.4 %collective-permute-done.4.refs_2_ = bf16[2,384,768]{2,1,0:T(8,128)(2,1)} collective-permute-done((bf16[2,384,768]{2,1,0:T(8,128)(2,1)}, bf16[2,384,768]{2,1,0:T(8,128)(2,1)}, u32[]{:S(2)}, u32[]{:S(2)}) %collective-permute-start.4) | collective-permute-done | bytes 1179680 | tf_op jit(solution)/shard_map/ppermute | solution.py:23
  74.1 17.2 %collective-permute-done.6.refs_6_ = bf16[2,384,768]{2,1,0:T(8,128)(2,1)} collective-permute-done((bf16[2,384,768]{2,1,0:T(8,128)(2,1)}, bf16[2,384,768]{2,1,0:T(8,128)(2,1)}, u32[]{:S(2)}, u32[]{:S(2)}) %collective-permute-start.6) | collective-permute-done | bytes 1179680 | tf_op jit(solution)/shard_map/ppermute | solution.py:23
  91.3 5.1 %collective-permute-done.7.refs_8_ = bf16[2,384,768]{2,1,0:T(8,128)(2,1)} collective-permute-done((bf16[2,384,768]{2,1,0:T(8,128)(2,1)}, bf16[2,384,768]{2,1,0:T(8,128)(2,1)}, u32[]{:S(2)}, u32[]{:S(2)}) %collective-permute-start.7) | collective-permute-done | bytes 1179680 | tf_op jit(solution)/shard_map/ppermute | solution.py:23
  96.4 38.0 %shard_map.93 = (bf16[384,768]{1,0:T(8,128)(2,1)}, bf16[384,768]{1,0:T(8,128)(2,1)}, bf16[2,384,768]{2,1,0:T(8,128)(2,1)}, bf16[2,384,768]{2,1,0:T(8,128)(2,1)},...) custom-call(s32[1,3456]{1,0:T(1,128)} %bitcast.66, ...), custom_call_target="tpu_custom_call" | custom-call | flops 10192158720 | bytes 23592960 | tf_op jit(solution)/shard_map/pallas_call | solution.py:106
  137.5 4.5 %collective-permute-done.16 = bf16[3072,384]{0,1:T(8,128)(2,1)S(1)} collective-permute-done((bf16[3072,384]{0,1:T(8,128)(2,1)S(1)}, bf16[3072,384]{0,1:T(8,128)(2,1)S(1)}, u32[]{:S(2)}, u32[]{:S(2)}) %collective-permute-start.16) | collective-permute-done | bytes 2359328 | tf_op jit(solution)/shard_map/ppermute | solution.py:138
  144.9 4.3 %copy.13 = bf16[3072,384]{1,0:T(8,128)(2,1)} copy(bf16[3072,384]{0,1:T(8,128)(2,1)} %fusion) | data formatting | bytes 4718592 | tf_op jit(solution)/shard_map/convert_element_type | solution.py:141
  149.2 17.4 %all-to-all-start = ((bf16[64,48,384]{2,1,0:T(8,128)(2,1)}), bf16[64,48,384]{2,1,0:T(8,128)(2,1)}, u32[]{:S(2)}, u32[]{:S(2)}) async-start(bf16[64,48,384]{2,1,0:T(8,128)(2,1)} %bitcast.59), calls=%async_computation | async-start | bytes 4718592 | tf_op jit(solution)/shard_map/all_to_all | solution.py:142
  167.9 4.6 %collective-permute-start.9 = (bf16[2,384,768]{2,1,0:T(8,128)(2,1)}, bf16[2,384,768]{2,1,0:T(8,128)(2,1)S(1)}, u32[]{:S(2)}, u32[]{:S(2)}) collective-permute-start(bf16[2,384,768]{2,1,0:T(8,128)(2,1)} %get-tuple-element.32), channel_id=1, source_target_pairs={{0,4},{4,8},{8,12},{16,20},{20,24},{24,28},{32,36},{36,40},{40,44}... | collective-permute-start | bytes 3538952 | tf_op jit(solution)/shard_map/ppermute | solution.py:23
  172.5 46.2 %collective-permute-done.8 = bf16[2,384,768]{2,1,0:T(8,128)(2,1)S(1)} collective-permute-done((bf16[2,384,768]{2,1,0:T(8,128)(2,1)}, bf16[2,384,768]{2,1,0:T(8,128)(2,1)S(1)}, u32[]{:S(2)}, u32[]{:S(2)}) %collective-permute-start.8) | collective-permute-done | bytes 1179680 | tf_op jit(solution)/shard_map/ppermute | solution.py:23
  220.0 4.6 %collective-permute-start.11 = (bf16[2,384,768]{2,1,0:T(8,128)(2,1)}, bf16[2,384,768]{2,1,0:T(8,128)(2,1)S(1)}, u32[]{:S(2)}, u32[]{:S(2)}) collective-permute-start(bf16[2,384,768]{2,1,0:T(8,128)(2,1)} %get-tuple-element.36), channel_id=1, source_target_pairs={{0,4},{4,8},{8,12},{16,20},{20,24},{24,28},{32,36},{36,40},{40,44}... | collective-permute-start | bytes 3538952 | tf_op jit(solution)/shard_map/ppermute | solution.py:23
  226.2 5.4 %collective-permute-start.14 = (bf16[2,384,768]{2,1,0:T(8,128)(2,1)}, bf16[2,384,768]{2,1,0:T(8,128)(2,1)S(1)}, u32[]{:S(2)}, u32[]{:S(2)}) collective-permute-start(bf16[2,384,768]{2,1,0:T(8,128)(2,1)} %add_convert_fusion.2), channel_id=1, source_target_pairs={{16,0},{20,4},{24,8},{28,12},{32,16},{36,20},{40,24},{44,28},{48,3... | collective-permute-start | bytes 3538952 | tf_op jit(solution)/shard_map/ppermute | solution.py:23
  231.7 16.0 %collective-permute-done.10 = bf16[2,384,768]{2,1,0:T(8,128)(2,1)S(1)} collective-permute-done((bf16[2,384,768]{2,1,0:T(8,128)(2,1)}, bf16[2,384,768]{2,1,0:T(8,128)(2,1)S(1)}, u32[]{:S(2)}, u32[]{:S(2)}) %collective-permute-start.10) | collective-permute-done | bytes 1179680 | tf_op jit(solution)/shard_map/ppermute | solution.py:23
  250.5 3.6 %collective-permute-start.15 = (bf16[2,384,768]{2,1,0:T(8,128)(2,1)}, bf16[2,384,768]{2,1,0:T(8,128)(2,1)}, u32[]{:S(2)}, u32[]{:S(2)}) collective-permute-start(bf16[2,384,768]{2,1,0:T(8,128)(2,1)} %add_convert_fusion.1), channel_id=1, source_target_pairs={{0,16},{4,20},{8,24},{12,28},{16,32},{20,36},{24,40},{28,44},{32,4... | collective-permute-start | bytes 3538952 | tf_op jit(solution)/shard_map/ppermute | solution.py:23
  255.4 6.0 %collective-permute-start.13 = (bf16[2,384,768]{2,1,0:T(8,128)(2,1)}, bf16[2,384,768]{2,1,0:T(8,128)(2,1)}, u32[]{:S(2)}, u32[]{:S(2)}) collective-permute-start(bf16[2,384,768]{2,1,0:T(8,128)(2,1)} %get-tuple-element.40), channel_id=1, source_target_pairs={{0,4},{4,8},{8,12},{16,20},{20,24},{24,28},{32,36},{36,40},{40,44}... | collective-permute-start | bytes 3538952 | tf_op jit(solution)/shard_map/ppermute | solution.py:23
  261.4 22.9 %collective-permute-done.15 = bf16[2,384,768]{2,1,0:T(8,128)(2,1)} collective-permute-done((bf16[2,384,768]{2,1,0:T(8,128)(2,1)}, bf16[2,384,768]{2,1,0:T(8,128)(2,1)}, u32[]{:S(2)}, u32[]{:S(2)}) %collective-permute-start.15) | collective-permute-done | bytes 1179680 | tf_op jit(solution)/shard_map/ppermute | solution.py:23
  294.3 7.0 %collective-permute-done.17 = f32[48,192]{1,0:T(8,128)S(1)} collective-permute-done((f32[48,192]{1,0:T(8,128)S(1)}, f32[48,192]{1,0:T(8,128)S(1)}, u32[]{:S(2)}, u32[]{:S(2)}) %collective-permute-start.17) | collective-permute-done | bytes 36896 | tf_op jit(solution)/shard_map/ppermute | solution.py:150
  (49 shorter events, 34.8 us)
Async XLA Ops:
  0.6 62.4 %copy-start = (bf16[1,1,384,3072]{3,2,1,0:T(8,128)(2,1)S(1)}, bf16[1,1,384,3072]{3,2,1,0:T(8,128)(2,1)}, u32[]{:S(2)}) copy-start(bf16[1,1,384,3072]{3,2,1,0:T(8,128)(2,1)} %param.10) | copy-start | bytes 7077892
  2.2 66.1 %copy-start.2 = (bf16[2,384,768]{2,1,0:T(8,128)(2,1)}, bf16[2,384,768]{2,1,0:T(8,128)(2,1)S(1)}, u32[]{:S(2)}) copy-start(bf16[2,384,768]{2,1,0:T(8,128)(2,1)S(1)} %pad_maximum_fusion.refs_4_) | copy-start | bytes 3538948
  2.2 33.7 %collective-permute-start = (bf16[2,384,768]{2,1,0:T(8,128)(2,1)S(1)}, bf16[2,384,768]{2,1,0:T(8,128)(2,1)}, u32[]{:S(2)}, u32[]{:S(2)}) collective-permute-start(bf16[2,384,768]{2,1,0:T(8,128)(2,1)S(1)} %pad_maximum_fusion.refs_4_), channel_id=1, source_target_pairs={{0,16},{4,20},{8,24},{12,28},{16,32},{20,36},{24,40},{28,44},{32,4... | collective-permute-start | bytes 3538952 | tf_op jit(solution)/shard_map/ppermute | solution.py:23
  6.0 29.8 %collective-permute-start.1 = (bf16[2,384,768]{2,1,0:T(8,128)(2,1)S(1)}, bf16[2,384,768]{2,1,0:T(8,128)(2,1)}, u32[]{:S(2)}, u32[]{:S(2)}) collective-permute-start(bf16[2,384,768]{2,1,0:T(8,128)(2,1)S(1)} %pad_maximum_fusion.refs_4_), channel_id=1, source_target_pairs={{0,4},{4,8},{8,12},{16,20},{20,24},{24,28},{32,36},{36,40},{40,44}... | collective-permute-start | bytes 3538952 | tf_op jit(solution)/shard_map/ppermute | solution.py:23
  10.4 29.1 %collective-permute-start.2 = (bf16[2,384,768]{2,1,0:T(8,128)(2,1)S(1)}, bf16[2,384,768]{2,1,0:T(8,128)(2,1)}, u32[]{:S(2)}, u32[]{:S(2)}) collective-permute-start(bf16[2,384,768]{2,1,0:T(8,128)(2,1)S(1)} %pad_maximum_fusion.refs_4_), channel_id=1, source_target_pairs={{4,0},{8,4},{12,8},{20,16},{24,20},{28,24},{36,32},{40,36},{44,40}... | collective-permute-start | bytes 3538952 | tf_op jit(solution)/shard_map/ppermute | solution.py:23
  11.7 44.8 %collective-permute-start.5 = (bf16[2,384,768]{2,1,0:T(8,128)(2,1)S(1)}, bf16[2,384,768]{2,1,0:T(8,128)(2,1)}, u32[]{:S(2)}, u32[]{:S(2)}) collective-permute-start(bf16[2,384,768]{2,1,0:T(8,128)(2,1)S(1)} %pad_maximum_fusion.refs_4_), channel_id=1, source_target_pairs={{16,0},{20,4},{24,8},{28,12},{32,16},{36,20},{40,24},{44,28},{48,3... | collective-permute-start | bytes 3538952 | tf_op jit(solution)/shard_map/ppermute | solution.py:23
  39.6 29.1 %collective-permute-start.3 = (bf16[2,384,768]{2,1,0:T(8,128)(2,1)}, bf16[2,384,768]{2,1,0:T(8,128)(2,1)}, u32[]{:S(2)}, u32[]{:S(2)}) collective-permute-start(bf16[2,384,768]{2,1,0:T(8,128)(2,1)} %collective-permute-done.refs_1_), channel_id=1, source_target_pairs={{0,4},{4,8},{8,12},{16,20},{20,24},{24,28},{32,36},{36,40},{40,44}... | collective-permute-start | bytes 3538952 | tf_op jit(solution)/shard_map/ppermute | solution.py:23
  43.0 31.1 %collective-permute-start.4 = (bf16[2,384,768]{2,1,0:T(8,128)(2,1)}, bf16[2,384,768]{2,1,0:T(8,128)(2,1)}, u32[]{:S(2)}, u32[]{:S(2)}) collective-permute-start(bf16[2,384,768]{2,1,0:T(8,128)(2,1)} %collective-permute-done.refs_1_), channel_id=1, source_target_pairs={{4,0},{8,4},{12,8},{20,16},{24,20},{28,24},{36,32},{40,36},{44,40}... | collective-permute-start | bytes 3538952 | tf_op jit(solution)/shard_map/ppermute | solution.py:23
  56.5 34.7 %collective-permute-start.6 = (bf16[2,384,768]{2,1,0:T(8,128)(2,1)}, bf16[2,384,768]{2,1,0:T(8,128)(2,1)}, u32[]{:S(2)}, u32[]{:S(2)}) collective-permute-start(bf16[2,384,768]{2,1,0:T(8,128)(2,1)} %collective-permute-done.5.refs_7_), channel_id=1, source_target_pairs={{0,4},{4,8},{8,12},{16,20},{20,24},{24,28},{32,36},{36,40},{40,44}... | collective-permute-start | bytes 3538952 | tf_op jit(solution)/shard_map/ppermute | solution.py:23
  61.0 35.4 %collective-permute-start.7 = (bf16[2,384,768]{2,1,0:T(8,128)(2,1)}, bf16[2,384,768]{2,1,0:T(8,128)(2,1)}, u32[]{:S(2)}, u32[]{:S(2)}) collective-permute-start(bf16[2,384,768]{2,1,0:T(8,128)(2,1)} %collective-permute-done.5.refs_7_), channel_id=1, source_target_pairs={{4,0},{8,4},{12,8},{20,16},{24,20},{28,24},{36,32},{40,36},{44,40}... | collective-permute-start | bytes 3538952 | tf_op jit(solution)/shard_map/ppermute | solution.py:23
  137.2 4.8 %collective-permute-start.16 = (bf16[3072,384]{0,1:T(8,128)(2,1)S(1)}, bf16[3072,384]{0,1:T(8,128)(2,1)S(1)}, u32[]{:S(2)}, u32[]{:S(2)}) collective-permute-start(bf16[3072,384]{0,1:T(8,128)(2,1)S(1)} %fusion.1), channel_id=1, source_target_pairs={{0,1},{1,0},{2,3},{3,2},{4,5},{5,4},{6,7},{7,6},{8,9},{9,8},{10,11... | collective-permute-start | bytes 7077896 | tf_op jit(solution)/shard_map/ppermute | solution.py:138
  149.2 75.5 %copy-start.4 = (bf16[2,384,768]{2,1,0:T(8,128)(2,1)S(1)}, bf16[2,384,768]{2,1,0:T(8,128)(2,1)}, u32[]{:S(2)}) copy-start(bf16[2,384,768]{2,1,0:T(8,128)(2,1)} %get-tuple-element.41) | copy-start | bytes 3538948
  149.2 138.6 %all-to-all-start = ((bf16[64,48,384]{2,1,0:T(8,128)(2,1)}), bf16[64,48,384]{2,1,0:T(8,128)(2,1)}, u32[]{:S(2)}, u32[]{:S(2)}) async-start(bf16[64,48,384]{2,1,0:T(8,128)(2,1)} %bitcast.59), calls=%async_computation | async-start | bytes 4718592 | tf_op jit(solution)/shard_map/all_to_all | solution.py:142
  166.6 52.1 %collective-permute-start.8 = (bf16[2,384,768]{2,1,0:T(8,128)(2,1)}, bf16[2,384,768]{2,1,0:T(8,128)(2,1)S(1)}, u32[]{:S(2)}, u32[]{:S(2)}) collective-permute-start(bf16[2,384,768]{2,1,0:T(8,128)(2,1)} %get-tuple-element.31), channel_id=1, source_target_pairs={{4,0},{8,4},{12,8},{20,16},{24,20},{28,24},{36,32},{40,36},{44,40}... | collective-permute-start | bytes 3538952 | tf_op jit(solution)/shard_map/ppermute | solution.py:23
  167.9 50.8 %collective-permute-start.9 = (bf16[2,384,768]{2,1,0:T(8,128)(2,1)}, bf16[2,384,768]{2,1,0:T(8,128)(2,1)S(1)}, u32[]{:S(2)}, u32[]{:S(2)}) collective-permute-start(bf16[2,384,768]{2,1,0:T(8,128)(2,1)} %get-tuple-element.32), channel_id=1, source_target_pairs={{0,4},{4,8},{8,12},{16,20},{20,24},{24,28},{32,36},{36,40},{40,44}... | collective-permute-start | bytes 3538952 | tf_op jit(solution)/shard_map/ppermute | solution.py:23
  218.7 29.0 %collective-permute-start.10 = (bf16[2,384,768]{2,1,0:T(8,128)(2,1)}, bf16[2,384,768]{2,1,0:T(8,128)(2,1)S(1)}, u32[]{:S(2)}, u32[]{:S(2)}) collective-permute-start(bf16[2,384,768]{2,1,0:T(8,128)(2,1)} %get-tuple-element.35), channel_id=1, source_target_pairs={{4,0},{8,4},{12,8},{20,16},{24,20},{28,24},{36,32},{40,36},{44,40}... | collective-permute-start | bytes 3538952 | tf_op jit(solution)/shard_map/ppermute | solution.py:23
  220.0 29.0 %collective-permute-start.11 = (bf16[2,384,768]{2,1,0:T(8,128)(2,1)}, bf16[2,384,768]{2,1,0:T(8,128)(2,1)S(1)}, u32[]{:S(2)}, u32[]{:S(2)}) collective-permute-start(bf16[2,384,768]{2,1,0:T(8,128)(2,1)} %get-tuple-element.36), channel_id=1, source_target_pairs={{0,4},{4,8},{8,12},{16,20},{20,24},{24,28},{32,36},{36,40},{40,44}... | collective-permute-start | bytes 3538952 | tf_op jit(solution)/shard_map/ppermute | solution.py:23
  224.7 24.4 %copy-start.3 = (bf16[2,384,768]{2,1,0:T(8,128)(2,1)S(1)}, bf16[2,384,768]{2,1,0:T(8,128)(2,1)}, u32[]{:S(2)}) copy-start(bf16[2,384,768]{2,1,0:T(8,128)(2,1)} %get-tuple-element.44) | copy-start | bytes 3538948
  226.2 35.1 %collective-permute-start.14 = (bf16[2,384,768]{2,1,0:T(8,128)(2,1)}, bf16[2,384,768]{2,1,0:T(8,128)(2,1)S(1)}, u32[]{:S(2)}, u32[]{:S(2)}) collective-permute-start(bf16[2,384,768]{2,1,0:T(8,128)(2,1)} %add_convert_fusion.2), channel_id=1, source_target_pairs={{16,0},{20,4},{24,8},{28,12},{32,16},{36,20},{40,24},{44,28},{48,3... | collective-permute-start | bytes 3538952 | tf_op jit(solution)/shard_map/ppermute | solution.py:23
  250.5 33.8 %collective-permute-start.15 = (bf16[2,384,768]{2,1,0:T(8,128)(2,1)}, bf16[2,384,768]{2,1,0:T(8,128)(2,1)}, u32[]{:S(2)}, u32[]{:S(2)}) collective-permute-start(bf16[2,384,768]{2,1,0:T(8,128)(2,1)} %add_convert_fusion.1), channel_id=1, source_target_pairs={{0,16},{4,20},{8,24},{12,28},{16,32},{20,36},{24,40},{28,44},{32,4... | collective-permute-start | bytes 3538952 | tf_op jit(solution)/shard_map/ppermute | solution.py:23
  254.1 30.2 %collective-permute-start.12 = (bf16[2,384,768]{2,1,0:T(8,128)(2,1)}, bf16[2,384,768]{2,1,0:T(8,128)(2,1)}, u32[]{:S(2)}, u32[]{:S(2)}) collective-permute-start(bf16[2,384,768]{2,1,0:T(8,128)(2,1)} %get-tuple-element.39), channel_id=1, source_target_pairs={{4,0},{8,4},{12,8},{20,16},{24,20},{28,24},{36,32},{40,36},{44,40}... | collective-permute-start | bytes 3538952 | tf_op jit(solution)/shard_map/ppermute | solution.py:23
  255.4 28.9 %collective-permute-start.13 = (bf16[2,384,768]{2,1,0:T(8,128)(2,1)}, bf16[2,384,768]{2,1,0:T(8,128)(2,1)}, u32[]{:S(2)}, u32[]{:S(2)}) collective-permute-start(bf16[2,384,768]{2,1,0:T(8,128)(2,1)} %get-tuple-element.40), channel_id=1, source_target_pairs={{0,4},{4,8},{8,12},{16,20},{20,24},{24,28},{32,36},{36,40},{40,44}... | collective-permute-start | bytes 3538952 | tf_op jit(solution)/shard_map/ppermute | solution.py:23
  261.4 23.0 %copy-start.1 = (bf16[2,384,768]{2,1,0:T(8,128)(2,1)}, bf16[2,384,768]{2,1,0:T(8,128)(2,1)S(1)}, u32[]{:S(2)}) copy-start(bf16[2,384,768]{2,1,0:T(8,128)(2,1)S(1)} %collective-permute-done.14) | copy-start | bytes 3538948
  293.1 8.2 %collective-permute-start.17 = (f32[48,192]{1,0:T(8,128)S(1)}, f32[48,192]{1,0:T(8,128)S(1)}, u32[]{:S(2)}, u32[]{:S(2)}) collective-permute-start(f32[48,192]{1,0:T(8,128)S(1)} %bitcast.65), channel_id=1, source_target_pairs={{0,2},{1,3},{2,0},{3,1},{4,6},{5,7},{6,4},{7,5},{8,10},{9,11},{10,... | collective-permute-start | bytes 110600 | tf_op jit(solution)/shard_map/ppermute | solution.py:150
  (1 other events, 15.9 us)
